TPU v7x, 512 devices: a whole 4x8x8 slice. The times are simulated.
512 devices in a mesh: seq: 64 (over y, x, core), ch: 8 (over z).
Axes of the slice: x: 4, y: 8, z: 8, core: 2. Of those that a mesh axis runs over, the one named last changes fastest.
Arguments:
- signal: bfloat16 [1536, 32768], P('ch', 'seq'), may hold values from -16 to 16
- input_norm_gain: float32 [1536], P('ch'), may hold values from 0.25 to 1.75
- value_weight: bfloat16 [1536, 1536], P('seq', 'ch'), may hold values from -0.15625 to 0.15625
- gate_weight: bfloat16 [1536, 1536], P('seq', 'ch'), may hold values from -0.15625 to 0.15625
- depth_taps: float32 [31, 1536], P(None, 'ch'), may hold values from -1 to 1
- cotangent: bfloat16 [1536, 32768], P('ch', 'seq'), may hold values from -6 to 6
Outputs:
- output: bfloat16 [1536, 32768], P('ch', 'seq')
- signal_gradient: bfloat16 [1536, 32768], P('ch', 'seq')
- grad_value: float32 [1536, 1536], P('seq', 'ch')
- grad_gate: float32 [1536, 1536], P('seq', 'ch')
- grad_taps: float32 [31, 1536], P(None, 'ch')
- gain_gradient: float32 [1536], P('ch')
All inputs are finite; a program needn't handle non-finite values.
Results may differ from a plain program's by a relative error of at most 0.02.
Values may be sent and summed in bfloat16 or wider, within the bound.
No kernel may reach another device: no remote copies, remote signals or barrier semaphores. Data moves between devices by JAX's collectives and lax.ppermute only.
A program may use at most 64 MiB of HBM per device.

v0:
```python
import jax
import jax.numpy as jnp
from jax import lax
from jax.sharding import PartitionSpec as P


def extended(cells, sides, width):
    for axis, dim in sides:
        count = lax.axis_size(axis)
        ends = count - 1
        head = lax.slice_in_dim(cells, 0, width, axis=dim)
        tail = lax.slice_in_dim(cells, cells.shape[dim] - width, cells.shape[dim], axis=dim)
        cells = jnp.concatenate(
            [
                lax.ppermute(tail, axis, [(i, (i + 1) % count) for i in range(ends)]),
                cells,
                lax.ppermute(head, axis, [((i + 1) % count, i) for i in range(ends)]),
            ],
            axis=dim,
        )
    return cells


def standardize_rows(columns_in):
    values = columns_in.astype(jnp.float32)
    average = jnp.mean(values, 0, keepdims=True)
    centred = values - average
    spread = jnp.mean(centred * centred, 0, keepdims=True)
    inverse_deviation = lax.rsqrt(spread + 1e-05)
    return (centred * inverse_deviation, inverse_deviation)


def depthwise(padded, kernel):
    channels = padded.shape[0]
    result = lax.conv_general_dilated(
        padded[None],
        kernel,
        (1,),
        "VALID",
        dimension_numbers=("NCH", "OIH", "NCH"),
        feature_group_count=channels,
        precision=lax.Precision.HIGHEST,
    )
    return result[0]


def shards(signal, input_norm_gain, value_weight, gate_weight, depth_taps, cotangent):
    local_cols = signal.shape[0]
    frames = signal.shape[1]
    groups = lax.axis_size("ch")
    block_of_rows = frames // groups
    channel_position = lax.axis_index("ch")
    reach = depth_taps.shape[0] // 2
    complete_signal, complete_gain = (
        lax.all_gather(signal, "ch", axis=0, tiled=True),
        lax.all_gather(input_norm_gain.astype(jnp.bfloat16), "ch", axis=0, tiled=True).astype(
            input_norm_gain.dtype
        ),
    )
    centered_unit, inverse_deviation = standardize_rows(complete_signal)
    normalized_signal = (centered_unit * complete_gain[:, None]).astype(jnp.bfloat16)
    centered_unit_rows = lax.dynamic_slice_in_dim(
        centered_unit, channel_position * block_of_rows, block_of_rows, 1
    )
    row_inverse_deviation = lax.dynamic_slice_in_dim(
        inverse_deviation, channel_position * block_of_rows, block_of_rows, 1
    )
    stacked = jnp.concatenate([value_weight, gate_weight], 1)
    gathered = lax.all_gather(stacked, "seq", axis=0, tiled=True)
    mixed = lax.dot_general(
        gathered, normalized_signal, (((0,), (0,)), ((), ())), preferred_element_type=jnp.float32
    )
    value = mixed[:local_cols]
    gate = mixed[local_cols:]
    sig_gate = jax.nn.sigmoid(gate)
    glued = (value * sig_gate).astype(jnp.bfloat16)
    glued_pad = extended(glued, (("seq", 1),), reach).astype(jnp.float32)
    forward_kernel = depth_taps.T[:, None, :]
    pre = depthwise(glued_pad, forward_kernel)
    sig_pre = jax.nn.sigmoid(pre)
    output = (pre * sig_pre).astype(jnp.bfloat16)
    grad_pre = (cotangent.astype(jnp.float32) * sig_pre * (1.0 + pre * (1.0 - sig_pre))).astype(
        jnp.bfloat16
    )
    grad_pre_f = grad_pre.astype(jnp.float32)
    grad_pad = extended(grad_pre, (("seq", 1),), reach).astype(jnp.float32)
    grad_glued = depthwise(grad_pad, forward_kernel[:, :, ::-1])
    tap_partial = depthwise(glued_pad, grad_pre_f[:, None, :]).T
    grad_taps = lax.psum(tap_partial, "seq")
    grad_v = (grad_glued * sig_gate).astype(jnp.bfloat16)
    grad_g = (grad_glued * value * sig_gate * (1.0 - sig_gate)).astype(jnp.bfloat16)
    grad_both = jnp.concatenate([grad_v, grad_g], 0)
    weight_sums = lax.psum_scatter(
        lax.dot_general(
            normalized_signal,
            grad_both,
            (((1,), (1,)), ((), ())),
            preferred_element_type=jnp.float32,
        ),
        "seq",
        scatter_dimension=0,
        tiled=True,
    )
    grad_value = weight_sums[:, :local_cols]
    grad_gate = weight_sums[:, local_cols:]
    normed_term = jnp.dot(gathered, grad_both, preferred_element_type=jnp.float32)
    normalized_gradient = lax.psum_scatter(
        normed_term.astype(jnp.bfloat16), "ch", scatter_dimension=1, tiled=True
    ).astype(jnp.float32)
    scaled_signal = normalized_gradient * complete_gain[:, None]
    first_moment = jnp.mean(scaled_signal, 0, keepdims=True)
    second_moment = jnp.mean(scaled_signal * centered_unit_rows, 0, keepdims=True)
    gradient_rows = (
        row_inverse_deviation * (scaled_signal - first_moment - centered_unit_rows * second_moment)
    ).astype(jnp.bfloat16)
    signal_gradient = lax.all_to_all(gradient_rows, "ch", split_axis=0, concat_axis=1, tiled=True)
    gain_portion = jnp.sum(normalized_gradient * centered_unit_rows, 1)
    gain_whole = lax.psum(gain_portion, ("seq", "ch"))
    gain_gradient = lax.dynamic_slice_in_dim(
        gain_whole, channel_position * local_cols, local_cols, 0
    )
    return (output, signal_gradient, grad_value, grad_gate, grad_taps, gain_gradient)


def solution(mesh):
    placed = (
        P("ch", "seq"),
        P("ch"),
        P("seq", "ch"),
        P("seq", "ch"),
        P(None, "ch"),
        P("ch", "seq"),
    )
    return jax.shard_map(
        shards,
        mesh=mesh,
        in_specs=placed,
        out_specs=(
            P("ch", "seq"),
            P("ch", "seq"),
            P("seq", "ch"),
            P("seq", "ch"),
            P(None, "ch"),
            P("ch"),
        ),
        check_vma=False,
    )
```

profile of v0, /device:TPU:1, one launch (start us, length us, event | category | flops | bytes accessed | tf_op | source)
XLA Modules:
  0.0 592.0 jit_solution(6644750311934210366)
XLA Ops:
  8.0 1.4 pad_maximum_fusion.4
  12.3 20.2 %all-reduce = bf16[1536]{0:T(1024)(128)(2,1)S(1)} all-reduce(bf16[1536]{0:T(1024)(128)(2,1)S(1)} %dynamic-update-slice), channel_id=1, replica_groups=mesh['seq'=64,'ch'=8] {'ch'}, use_global_device_ids=true, to_apply=%add | all-reduce | flops 1536 | bytes 6144
  32.6 22.6 %all-gather.5.cloned.1.call-done = bf16[1536,512]{1,0:T(8,128)(2,1)} async-done(((bf16[192,512]{1,0:T(8,128)(2,1)}), bf16[1536,512]{1,0:T(8,128)(2,1)}) %all-gather.5.cloned.1.call-update) | async-done | bytes 1572880 | tf_op jit(solution)/shard_map/all_gather | solution.py:55
  55.2 1.7 copy.41
  57.8 85.3 %all-gather.3.cloned.1.call-done = bf16[1536,384]{1,0:T(8,128)(2,1)} async-done(((bf16[24,384]{1,0:T(8,128)(2,1)}), bf16[1536,384]{1,0:T(8,128)(2,1)}) %all-gather.3.cloned.1.call-update) | async-done | bytes 1179664 | tf_op jit(solution)/shard_map/all_gather | solution.py:69
  143.1 2.2 fusion.6
  145.6 2.1 collective-permute-start.1
  147.7 3.4 collective-permute-start
  154.1 2.0 convolution_select_fusion.1
  156.1 1.4 copy.58
  158.5 2.0 multiply_convert_fusion.5
  160.6 1.9 collective-permute-start.3
  162.5 4.2 collective-permute-start.2
  168.9 2.0 convolution_select_fusion
  171.0 1.4 copy.59
  174.6 3.5 convolution_convert_fusion
  180.4 2.1 fusion
  183.8 2.7 fusion.5
  186.5 38.9 %reduce-scatter.2.cloned.1.call-done = bf16[1536,64]{0,1:T(8,128)(2,1)} async-done(((bf16[1536,512]{0,1:T(8,128)(2,1)}), bf16[1536,64]{0,1:T(8,128)(2,1)}) %reduce-scatter.2.cloned.1.call-update) | async-done | bytes 196624 | tf_op jit(solution)/shard_map/reduce_scatter | solution.py:107
  228.9 4.7 all-to-all-start
  233.6 2.2 fusion.49
  235.9 245.9 %psum.14 = f32[31,192]{1,0:T(8,128)} all-reduce(f32[31,192]{1,0:T(8,128)S(1)} %bitcast.60), channel_id=1, replica_groups=mesh['seq'=64,'ch'=8] {'seq'}, use_global_device_ids=true, to_apply=%region_6.0 | all-reduce | flops 5952 | bytes 47616 | tf_op jit(solution)/shard_map/psum | solution.py:89
  481.8 1.5 fusion.46
  483.3 100.8 %psum.15 = f32[1536]{0:T(1024)S(1)} all-reduce(f32[1536]{0:T(1024)S(1)} %get-tuple-element.18), channel_id=1, replica_groups=mesh['seq'=64,'ch'=8] {'seq','ch'}, use_global_device_ids=true, to_apply=%region_8.0 | all-reduce | flops 1536 | bytes 12288 | tf_op jit(solution)/shard_map/psum | solution.py:118
  (57 shorter events, 20.3 us)
Async XLA Ops:
  7.2 146.9 %copy-start = (f32[31,192]{1,0:T(8,128)S(1)}, f32[31,192]{1,0:T(8,128)}, u32[]{:S(2)}) copy-start(f32[31,192]{1,0:T(8,128)} %param.10) | copy-start | bytes 71428
  7.2 48.0 %all-gather.5.cloned.1.call-start = ((), (), s32[]{:S(2)}) async-start(), calls=%async_computation.3 | async-start | bytes 1769472 | tf_op jit(solution)/shard_map/all_gather | solution.py:55
  7.9 135.2 %all-gather.3.cloned.1.call-start = ((), (), s32[]{:S(2)}) async-start(), calls=%async_computation.2 | async-start | bytes 1198080 | tf_op jit(solution)/shard_map/all_gather | solution.py:69
  9.4 216.0 %reduce-scatter.2.cloned.1.call-start = ((), (), s32[]{:S(2)}) async-start(), calls=%async_computation.4 | async-start | bytes 1769472 | tf_op jit(solution)/shard_map/reduce_scatter | solution.py:107
  145.3 8.7 %copy-start.2 = (pred[8,68]{0,1:T(8,128)(4,1)S(1)}, pred[8,68]{0,1:T(8,128)(4,1)}, u32[]{:S(2)}) copy-start(pred[8,68]{0,1:T(8,128)(4,1)} %constant.43) | copy-start | bytes 1636
  145.6 5.6 collective-permute-start.1
  147.7 4.6 collective-permute-start
  160.6 6.2 %collective-permute-start.3 = (bf16[192,15]{1,0:T(8,128)(2,1)S(1)}, bf16[192,15]{1,0:T(8,128)(2,1)S(1)}, u32[]{:S(2)}, u32[]{:S(2)}) collective-permute-start(bf16[192,15]{1,0:T(8,128)(2,1)S(1)} %get-tuple-element.30), channel_id=1, source_target_pairs={{8,0},{16,8},{24,16},{32,24},{40,32},{48,40},{56,48},{64,56},{72,6... | collective-permute-start | bytes 17288 | tf_op jit(solution)/shard_map/ppermute | solution.py:17
  162.5 5.4 collective-permute-start.2
  178.1 4.3 copy-start.1
  178.1 303.6 %all-reduce.4.cloned.1.call-start = ((), (), s32[]{:S(2)}) async-start(), calls=%async_computation.5 | async-start | bytes 4718592
  228.9 355.8 %all-to-all-start = ((bf16[8,192,64]{1,2,0:T(8,128)(2,1)}), bf16[8,192,64]{1,2,0:T(8,128)(2,1)S(1)}, u32[]{:S(2)}, u32[]{:S(2)}) async-start(bf16[8,192,64]{1,2,0:T(8,128)(2,1)} %copy.54), calls=%async_computation.1 | async-start | bytes 524288 | tf_op jit(solution)/shard_map/all_to_all | solution.py:116
Sparse Core Ops, SparseCore 0:
  10.1 45.0 all-gather.4
  59.0 84.0 all-gather.2
  178.3 47.0 reduce-scatter.1
  228.6 202.0 all-reduce.3
where the time goes:
time: 593 us; the launch traced here: 592 us
  blocking collectives  367 us (62%)
  waiting for transfers between devices  150 us (25%)
  starting transfers between devices  16.8 us (3%)
  local copies, waits for them, and re-layouts  16.6 us (3%)
  between operations  15.3 us (3%)
  matrix products  14.7 us (2%)
  other arithmetic  11.8 us (2%)
    psum x1, blocking collectives, shards(): grad_taps = lax.psum(tap_partial, 'seq')  246 us
    psum x1, blocking collectives, shards(): gain_whole = lax.psum(gain_portion, ('seq', 'ch'))  101 us
    all_gather x1, waiting for transfers between devices, shards(): gathered = lax.all_gather(stacked, 'seq', axis=0, tiled=True)  85.3 us
    reduce_scatter x1, waiting for transfers between devices, shards(): lax.psum_scatter(normed_term.astype(jnp.bfloat16), 'ch', scatter_dimensio...  38.9 us
    all_gather x1, waiting for transfers between devices, shards(): lax.all_gather(signal, 'ch', axis=0, tiled=True)  22.6 us
    unnamed x1, blocking collectives  20.2 us
  transfers between devices with their start and end apart: 9, of which 5 were waited for; matrix products, arithmetic and copies ran while one was open for 4% of the time, Pallas kernels for 0%

commit v1 on v0

--- a/solution.py
+++ b/solution.py
@@ -46,24 +46,15 @@
 
 def shards(signal, input_norm_gain, value_weight, gate_weight, depth_taps, cotangent):
     local_cols = signal.shape[0]
-    frames = signal.shape[1]
-    groups = lax.axis_size("ch")
-    block_of_rows = frames // groups
+    seq_position = lax.axis_index("seq")
     channel_position = lax.axis_index("ch")
     reach = depth_taps.shape[0] // 2
-    complete_signal, complete_gain = (
-        lax.all_gather(signal, "ch", axis=0, tiled=True),
-        lax.all_gather(input_norm_gain.astype(jnp.bfloat16), "ch", axis=0, tiled=True).astype(
-            input_norm_gain.dtype
-        ),
-    )
+    complete_signal = lax.all_gather(signal, "ch", axis=0, tiled=True)
+    complete_gain = lax.all_gather(input_norm_gain, "ch", axis=0, tiled=True)
     centered_unit, inverse_deviation = standardize_rows(complete_signal)
     normalized_signal = (centered_unit * complete_gain[:, None]).astype(jnp.bfloat16)
     centered_unit_rows = lax.dynamic_slice_in_dim(
-        centered_unit, channel_position * block_of_rows, block_of_rows, 1
-    )
-    row_inverse_deviation = lax.dynamic_slice_in_dim(
-        inverse_deviation, channel_position * block_of_rows, block_of_rows, 1
+        centered_unit, channel_position * local_cols, local_cols, 0
     )
     stacked = jnp.concatenate([value_weight, gate_weight], 1)
     gathered = lax.all_gather(stacked, "seq", axis=0, tiled=True)
@@ -86,39 +77,44 @@
     grad_pad = extended(grad_pre, (("seq", 1),), reach).astype(jnp.float32)
     grad_glued = depthwise(grad_pad, forward_kernel[:, :, ::-1])
     tap_partial = depthwise(glued_pad, grad_pre_f[:, None, :]).T
-    grad_taps = lax.psum(tap_partial, "seq")
     grad_v = (grad_glued * sig_gate).astype(jnp.bfloat16)
     grad_g = (grad_glued * value * sig_gate * (1.0 - sig_gate)).astype(jnp.bfloat16)
     grad_both = jnp.concatenate([grad_v, grad_g], 0)
-    weight_sums = lax.psum_scatter(
-        lax.dot_general(
-            normalized_signal,
-            grad_both,
-            (((1,), (1,)), ((), ())),
-            preferred_element_type=jnp.float32,
-        ),
-        "seq",
-        scatter_dimension=0,
-        tiled=True,
+    weight_partial = lax.dot_general(
+        normalized_signal,
+        grad_both,
+        (((1,), (1,)), ((), ())),
+        preferred_element_type=jnp.float32,
     )
+    normed_term = jnp.dot(gathered, grad_both, preferred_element_type=jnp.float32)
+    normalized_gradient = lax.psum_scatter(
+        normed_term.astype(jnp.bfloat16), "ch", scatter_dimension=0, tiled=True
+    ).astype(jnp.float32)
+    scaled_signal = normalized_gradient * input_norm_gain[:, None]
+    moments = jnp.concatenate(
+        [
+            jnp.sum(scaled_signal, 0, keepdims=True),
+            jnp.sum(scaled_signal * centered_unit_rows, 0, keepdims=True),
+        ],
+        0,
+    )
+    moments = lax.psum(moments, "ch") * (1.0 / complete_signal.shape[0])
+    inverse_rows = inverse_deviation
+    signal_gradient = (
+        inverse_rows * (scaled_signal - moments[0:1] - centered_unit_rows * moments[1:2])
+    ).astype(jnp.bfloat16)
+    gain_portion = jnp.sum(normalized_gradient * centered_unit_rows, 1)
+    extra = jnp.concatenate([tap_partial, gain_portion[None]], 0)
+    extra = jnp.pad(extra, ((0, 0), (0, weight_partial.shape[1] - extra.shape[1])))
+    summed = lax.psum(jnp.concatenate([weight_partial, extra], 0), "seq")
+    rows = value_weight.shape[0]
+    weight_sums = lax.dynamic_slice_in_dim(summed, seq_position * rows, rows, 0)
     grad_value = weight_sums[:, :local_cols]
     grad_gate = weight_sums[:, local_cols:]
-    normed_term = jnp.dot(gathered, grad_both, preferred_element_type=jnp.float32)
-    normalized_gradient = lax.psum_scatter(
-        normed_term.astype(jnp.bfloat16), "ch", scatter_dimension=1, tiled=True
-    ).astype(jnp.float32)
-    scaled_signal = normalized_gradient * complete_gain[:, None]
-    first_moment = jnp.mean(scaled_signal, 0, keepdims=True)
-    second_moment = jnp.mean(scaled_signal * centered_unit_rows, 0, keepdims=True)
-    gradient_rows = (
-        row_inverse_deviation * (scaled_signal - first_moment - centered_unit_rows * second_moment)
-    ).astype(jnp.bfloat16)
-    signal_gradient = lax.all_to_all(gradient_rows, "ch", split_axis=0, concat_axis=1, tiled=True)
-    gain_portion = jnp.sum(normalized_gradient * centered_unit_rows, 1)
-    gain_whole = lax.psum(gain_portion, ("seq", "ch"))
-    gain_gradient = lax.dynamic_slice_in_dim(
-        gain_whole, channel_position * local_cols, local_cols, 0
-    )
+    taps_rows = depth_taps.shape[0]
+    full_rows = weight_partial.shape[0]
+    grad_taps = summed[full_rows : full_rows + taps_rows, :local_cols]
+    gain_gradient = summed[full_rows + taps_rows, :local_cols]
     return (output, signal_gradient, grad_value, grad_gate, grad_taps, gain_gradient)
 
 

time: 593 us -> 445 us (0.75)
  blocking collectives: 367 us -> 32.7 us
  waiting for transfers between devices: 150 us -> 338 us
    psum x2 -> x1, blocking collectives: 347 us -> 12.2 us  [shards(): moments = lax.psum(moments, 'ch') * (1.0 / complete_signal.shape[0])]
    psum x0 -> x1, waiting for transfers between devices: none -> 188 us  [shards(): summed = lax.psum(jnp.concatenate([weight_partial, extra], 0), 'seq')]
  transfers between devices with their start and end apart: 9 -> 8, of which waited for: 5 -> 6; matrix products, arithmetic and copies ran while one was open for 4% -> 4% of each run, Pallas kernels for 0% -> 0%
where the time goes in v1:
time: 445 us; the launch traced here: 443 us
  waiting for transfers between devices  338 us (76%)
  blocking collectives  32.7 us (7%)
  other arithmetic  16.4 us (4%)
  between operations  14.7 us (3%)
  local copies, waits for them, and re-layouts  14.5 us (3%)
  matrix products  14.2 us (3%)
  starting transfers between devices  12.1 us (3%)
    psum x1, waiting for transfers between devices, shards(): summed = lax.psum(jnp.concatenate([weight_partial, extra], 0), 'seq')  188 us
    all_gather x1, waiting for transfers between devices, shards(): gathered = lax.all_gather(stacked, 'seq', axis=0, tiled=True)  85.5 us
    reduce_scatter x1, waiting for transfers between devices, shards(): lax.psum_scatter(normed_term.astype(jnp.bfloat16), 'ch', scatter_dimensio...  38.9 us
    all_gather x1, waiting for transfers between devices, shards(): complete_signal = lax.all_gather(signal, 'ch', axis=0, tiled=True)  22.4 us
    unnamed x1, blocking collectives  20.5 us
    psum x1, blocking collectives, shards(): moments = lax.psum(moments, 'ch') * (1.0 / complete_signal.shape[0])  12.2 us
  transfers between devices with their start and end apart: 8, of which 6 were waited for; matrix products, arithmetic and copies ran while one was open for 4% of the time, Pallas kernels for 0%

profile of v1, /device:TPU:1, one launch (start us, length us, event | category | flops | bytes accessed | tf_op | source)
XLA Modules:
  0.0 442.7 jit_solution(922992032706214905)
XLA Ops:
  12.3 20.5 %all-reduce.1 = f32[1536]{0:T(1024)S(1)} all-reduce(f32[1536]{0:T(1024)S(1)} %dynamic-update-slice), channel_id=1, replica_groups=mesh['seq'=64,'ch'=8] {'ch'}, use_global_device_ids=true, to_apply=%add.1 | all-reduce | flops 1536 | bytes 12288
  32.8 22.4 %all-gather.5.cloned.1.call-done = bf16[1536,512]{1,0:T(8,128)(2,1)} async-done(((bf16[192,512]{1,0:T(8,128)(2,1)}), bf16[1536,512]{1,0:T(8,128)(2,1)}) %all-gather.5.cloned.1.call-update) | async-done | bytes 1572880 | tf_op jit(solution)/shard_map/all_gather | solution.py:52
  55.2 1.8 convert_reduce_fusion
  57.6 85.5 %all-gather.3.cloned.1.call-done = bf16[1536,384]{1,0:T(8,128)(2,1)} async-done(((bf16[24,384]{1,0:T(8,128)(2,1)}), bf16[1536,384]{1,0:T(8,128)(2,1)}) %all-gather.3.cloned.1.call-update) | async-done | bytes 1179664 | tf_op jit(solution)/shard_map/all_gather | solution.py:60
  143.1 2.1 fusion.29
  145.5 2.2 collective-permute-start.1
  147.6 3.4 collective-permute-start
  153.9 2.0 convolution_select_fusion.1
  155.9 1.4 copy.36
  158.4 2.0 multiply_convert_fusion.3
  160.4 1.9 collective-permute-start.3
  162.4 4.2 collective-permute-start.2
  168.8 2.0 convolution_select_fusion
  170.9 1.4 copy.37
  174.5 3.4 convolution_convert_fusion
  178.1 2.1 fusion
  181.6 2.2 fusion.48
  183.9 2.4 fusion.28
  186.3 38.9 %reduce-scatter.2.cloned.1.call-done = bf16[192,512]{1,0:T(8,128)(2,1)} async-done(((bf16[1536,512]{1,0:T(8,128)(2,1)}), bf16[192,512]{1,0:T(8,128)(2,1)}) %reduce-scatter.2.cloned.1.call-update) | async-done | bytes 196624 | tf_op jit(solution)/shard_map/reduce_scatter | solution.py:90
  226.4 3.3 pad_maximum_fusion
  229.8 12.2 %psum.14 = f32[2,512]{1,0:T(2,128)S(1)} all-reduce(f32[2,512]{1,0:T(2,128)S(1)} %pad_maximum_fusion.6), channel_id=1, replica_groups=mesh['seq'=64,'ch'=8] {'ch'}, use_global_device_ids=true, to_apply=%region_5.0 | all-reduce | flops 1024 | bytes 8192 | tf_op jit(solution)/shard_map/psum | solution.py:101
  242.0 1.8 fusion.23
  243.8 188.2 %all-reduce.4.cloned.1.call-done = f32[1568,384]{1,0:T(8,128)} async-done(((f32[1568,384]{1,0:T(8,128)}), f32[1568,384]{1,0:T(8,128)}) %all-reduce.4.cloned.1.call-update) | async-done | bytes 2408464 | tf_op jit(solution)/shard_map/psum | solution.py:109
  434.6 1.5 fusion.44
  (57 shorter events, 19.0 us)
Async XLA Ops:
  7.2 146.7 %copy-start = (f32[31,192]{1,0:T(8,128)S(1)}, f32[31,192]{1,0:T(8,128)}, u32[]{:S(2)}) copy-start(f32[31,192]{1,0:T(8,128)} %param.10) | copy-start | bytes 71428
  7.2 48.0 %all-gather.5.cloned.1.call-start = ((), (), s32[]{:S(2)}) async-start(), calls=%async_computation.2 | async-start | bytes 1769472 | tf_op jit(solution)/shard_map/all_gather | solution.py:52
  7.9 135.2 %all-gather.3.cloned.1.call-start = ((), (), s32[]{:S(2)}) async-start(), calls=%async_computation.1 | async-start | bytes 1198080 | tf_op jit(solution)/shard_map/all_gather | solution.py:60
  9.4 215.7 %reduce-scatter.2.cloned.1.call-start = ((), (), s32[]{:S(2)}) async-start(), calls=%async_computation.3 | async-start | bytes 1769472 | tf_op jit(solution)/shard_map/reduce_scatter | solution.py:90
  55.2 1.9 copy-start.1
  145.2 8.7 %copy-start.5 = (pred[8,68]{0,1:T(8,128)(4,1)S(1)}, pred[8,68]{0,1:T(8,128)(4,1)}, u32[]{:S(2)}) copy-start(pred[8,68]{0,1:T(8,128)(4,1)} %constant.49) | copy-start | bytes 1636
  145.5 5.6 %collective-permute-start.1 = (bf16[192,15]{1,0:T(8,128)(2,1)S(1)}, bf16[192,15]{1,0:T(8,128)(2,1)S(1)}, u32[]{:S(2)}, u32[]{:S(2)}) collective-permute-start(bf16[192,15]{1,0:T(8,128)(2,1)S(1)} %get-tuple-element.20), channel_id=1, source_target_pairs={{8,0},{16,8},{24,16},{32,24},{40,32},{48,40},{56,48},{64,56},{72,6... | collective-permute-start | bytes 17288 | tf_op jit(solution)/shard_map/ppermute | solution.py:17
  147.6 4.6 %collective-permute-start = (bf16[192,15]{1,0:T(8,128)(2,1)S(1)}, bf16[192,15]{1,0:T(8,128)(2,1)S(1)}, u32[]{:S(2)}, u32[]{:S(2)}) collective-permute-start(bf16[192,15]{1,0:T(8,128)(2,1)S(1)} %get-tuple-element.19), channel_id=1, source_target_pairs={{0,8},{8,16},{16,24},{24,32},{32,40},{40,48},{48,56},{56,64},{64,7... | collective-permute-start | bytes 17288 | tf_op jit(solution)/shard_map/ppermute | solution.py:15
  160.4 6.2 %collective-permute-start.3 = (bf16[192,15]{1,0:T(8,128)(2,1)S(1)}, bf16[192,15]{1,0:T(8,128)(2,1)S(1)}, u32[]{:S(2)}, u32[]{:S(2)}) collective-permute-start(bf16[192,15]{1,0:T(8,128)(2,1)S(1)} %get-tuple-element.18), channel_id=1, source_target_pairs={{8,0},{16,8},{24,16},{32,24},{40,32},{48,40},{56,48},{64,56},{72,6... | collective-permute-start | bytes 17288 | tf_op jit(solution)/shard_map/ppermute | solution.py:17
  162.4 5.4 %collective-permute-start.2 = (bf16[192,15]{1,0:T(8,128)(2,1)S(1)}, bf16[192,15]{1,0:T(8,128)(2,1)S(1)}, u32[]{:S(2)}, u32[]{:S(2)}) collective-permute-start(bf16[192,15]{1,0:T(8,128)(2,1)S(1)} %get-tuple-element.17), channel_id=1, source_target_pairs={{0,8},{8,16},{16,24},{24,32},{32,40},{40,48},{48,56},{56,64},{64,7... | collective-permute-start | bytes 17288 | tf_op jit(solution)/shard_map/ppermute | solution.py:15
  177.9 2.4 copy-start.2
  177.9 254.1 %all-reduce.4.cloned.1.call-start = ((), (), s32[]{:S(2)}) async-start(), calls=%async_computation.4 | async-start | bytes 4816896 | tf_op jit(solution)/shard_map/psum | solution.py:109
  183.8 41.3 %copy-start.4 = (f32[192]{0:T(256)S(1)}, f32[192]{0:T(256)}, u32[]{:S(2)}) copy-start(f32[192]{0:T(256)} %param.7) | copy-start | bytes 2308
  229.7 12.3 %copy-start.3 = (bf16[192,512]{1,0:T(8,128)(2,1)S(1)}, bf16[192,512]{1,0:T(8,128)(2,1)}, u32[]{:S(2)}) copy-start(bf16[192,512]{1,0:T(8,128)(2,1)} %reduce-scatter.2.cloned.1.call-done) | copy-start | bytes 589828
Sparse Core Ops, SparseCore 0:
  10.1 45.0 all-gather.4
  59.1 83.9 all-gather.2
  178.0 47.0 reduce-scatter.1
  229.9 202.0 all-reduce.3

commit v2 on v1

--- a/solution.py
+++ b/solution.py
@@ -44,20 +44,41 @@
     return result[0]
 
 
+def gather_by_exchange(block, axis):
+    count = lax.axis_size(axis)
+    copies = jnp.broadcast_to(block[None], (count,) + block.shape)
+    return lax.all_to_all(copies, axis, 0, 0, tiled=False)
+
+
+def bf16_pieces(values, pieces):
+    parts = []
+    rest = values
+    for _ in range(pieces):
+        part = rest.astype(jnp.bfloat16)
+        parts.append(part)
+        rest = rest - part.astype(jnp.float32)
+    return parts
+
+
 def shards(signal, input_norm_gain, value_weight, gate_weight, depth_taps, cotangent):
-    local_cols = signal.shape[0]
-    seq_position = lax.axis_index("seq")
+    local_cols, frames = signal.shape
+    groups = lax.axis_size("ch")
+    blocks = lax.axis_size("seq")
     channel_position = lax.axis_index("ch")
     reach = depth_taps.shape[0] // 2
-    complete_signal = lax.all_gather(signal, "ch", axis=0, tiled=True)
-    complete_gain = lax.all_gather(input_norm_gain, "ch", axis=0, tiled=True)
+    gain_rows = jnp.stack(bf16_pieces(input_norm_gain, 3), 0)
+    gain_rows = jnp.pad(gain_rows, ((0, 13), (0, frames - local_cols)))
+    arrived = gather_by_exchange(jnp.concatenate([signal, gain_rows], 0), "ch")
+    complete_signal = arrived[:, :local_cols].reshape(groups * local_cols, frames)
+    gain_parts = arrived[:, local_cols : local_cols + 3, :local_cols].astype(jnp.float32)
+    complete_gain = ((gain_parts[:, 0] + gain_parts[:, 1]) + gain_parts[:, 2]).reshape(-1)
     centered_unit, inverse_deviation = standardize_rows(complete_signal)
     normalized_signal = (centered_unit * complete_gain[:, None]).astype(jnp.bfloat16)
     centered_unit_rows = lax.dynamic_slice_in_dim(
         centered_unit, channel_position * local_cols, local_cols, 0
     )
     stacked = jnp.concatenate([value_weight, gate_weight], 1)
-    gathered = lax.all_gather(stacked, "seq", axis=0, tiled=True)
+    gathered = gather_by_exchange(stacked, "seq").reshape(-1, stacked.shape[1])
     mixed = lax.dot_general(
         gathered, normalized_signal, (((0,), (0,)), ((), ())), preferred_element_type=jnp.float32
     )
@@ -86,35 +107,51 @@
         (((1,), (1,)), ((), ())),
         preferred_element_type=jnp.float32,
     )
-    normed_term = jnp.dot(gathered, grad_both, preferred_element_type=jnp.float32)
-    normalized_gradient = lax.psum_scatter(
-        normed_term.astype(jnp.bfloat16), "ch", scatter_dimension=0, tiled=True
-    ).astype(jnp.float32)
+    normed_term = jnp.dot(gathered, grad_both, preferred_element_type=jnp.float32).astype(
+        jnp.bfloat16
+    )
+    gain_portion = jnp.sum(normed_term.astype(jnp.float32) * centered_unit, 1)
+    width = weight_partial.shape[1]
+    taps_rows = depth_taps.shape[0]
+    extra = jnp.pad(tap_partial, ((0, 1), (0, 0))).reshape(-1, width)
+    extra = jnp.concatenate([extra, gain_portion.reshape(-1, width)], 0)
+    rows = value_weight.shape[0]
+    outgoing = jnp.concatenate(
+        [
+            weight_partial.reshape(blocks, rows, width),
+            jnp.broadcast_to(extra[None], (blocks,) + extra.shape),
+        ],
+        1,
+    )
+    summed = jnp.sum(lax.all_to_all(outgoing, "seq", 0, 0, tiled=False), 0)
+    grad_value = summed[:rows, :local_cols]
+    grad_gate = summed[:rows, local_cols:]
+    taps_end = rows + (taps_rows + 1) * local_cols // width
+    grad_taps = summed[rows:taps_end].reshape(taps_rows + 1, local_cols)[:taps_rows]
+    gain_seq_sum = summed[taps_end:].reshape(-1)
+    partials = lax.all_to_all(
+        normed_term.reshape(groups, local_cols, frames), "ch", 0, 0, tiled=False
+    )
+    normalized_gradient = jnp.sum(partials.astype(jnp.float32), 0)
     scaled_signal = normalized_gradient * input_norm_gain[:, None]
     moments = jnp.concatenate(
         [
-            jnp.sum(scaled_signal, 0, keepdims=True),
-            jnp.sum(scaled_signal * centered_unit_rows, 0, keepdims=True),
+            jnp.sum(scaled_signal, 0),
+            jnp.sum(scaled_signal * centered_unit_rows, 0),
+            gain_seq_sum,
         ],
         0,
     )
-    moments = lax.psum(moments, "ch") * (1.0 / complete_signal.shape[0])
-    inverse_rows = inverse_deviation
+    moments = lax.psum(moments, "ch")
+    first_moment = moments[:frames] * (1.0 / complete_signal.shape[0])
+    second_moment = moments[frames : 2 * frames] * (1.0 / complete_signal.shape[0])
     signal_gradient = (
-        inverse_rows * (scaled_signal - moments[0:1] - centered_unit_rows * moments[1:2])
+        inverse_deviation
+        * (scaled_signal - first_moment[None] - centered_unit_rows * second_moment[None])
     ).astype(jnp.bfloat16)
-    gain_portion = jnp.sum(normalized_gradient * centered_unit_rows, 1)
-    extra = jnp.concatenate([tap_partial, gain_portion[None]], 0)
-    extra = jnp.pad(extra, ((0, 0), (0, weight_partial.shape[1] - extra.shape[1])))
-    summed = lax.psum(jnp.concatenate([weight_partial, extra], 0), "seq")
-    rows = value_weight.shape[0]
-    weight_sums = lax.dynamic_slice_in_dim(summed, seq_position * rows, rows, 0)
-    grad_value = weight_sums[:, :local_cols]
-    grad_gate = weight_sums[:, local_cols:]
-    taps_rows = depth_taps.shape[0]
-    full_rows = weight_partial.shape[0]
-    grad_taps = summed[full_rows : full_rows + taps_rows, :local_cols]
-    gain_gradient = summed[full_rows + taps_rows, :local_cols]
+    gain_gradient = lax.dynamic_slice_in_dim(
+        moments[2 * frames :], channel_position * local_cols, local_cols, 0
+    )
     return (output, signal_gradient, grad_value, grad_gate, grad_taps, gain_gradient)
 
 

time: 445 us -> 342 us (0.77)
  the two profiles are of different devices: /device:TPU:1 before, /device:TPU:2 now
where the time goes in v2:
time: 342 us; the launch traced here: 341 us
  waiting for transfers between devices  205 us (60%)
  starting transfers between devices  44.2 us (13%)
  blocking collectives  29.4 us (9%)
  local copies, waits for them, and re-layouts  23.4 us (7%)
  other arithmetic  21.1 us (6%)
  matrix products  16.7 us (5%)
    all_to_all x1, waiting for transfers between devices, shards(): summed = jnp.sum(lax.all_to_all(outgoing, 'seq', 0, 0, tiled=False), 0)  105 us
    all_to_all x2, waiting for transfers between devices, gather_by_exchange(): return lax.all_to_all(copies, axis, 0, 0, tiled=False)  70.6 us
    psum x1, blocking collectives, shards(): moments = lax.psum(moments, 'ch')  29.4 us
    all_to_all x1, waiting for transfers between devices, shards(): lax.all_to_all(normed_term.reshape(groups, local_cols, frames), 'ch', 0,...  24 us
    all_to_all x2, starting transfers between devices, gather_by_exchange(): return lax.all_to_all(copies, axis, 0, 0, tiled=False)  21 us
    conv_general_dilated x10, local copies, waits for them, and re-layouts, depthwise(): lax.conv_general_dilated(padded[None], kernel, (1,), 'VALID', dimension_n...  13.8 us
    all_to_all x1, starting transfers between devices, shards(): summed = jnp.sum(lax.all_to_all(outgoing, 'seq', 0, 0, tiled=False), 0)  9.97 us
    conv_general_dilated x3, matrix products, depthwise(): lax.conv_general_dilated(padded[None], kernel, (1,), 'VALID', dimension_n...  9.18 us
  transfers between devices with their start and end apart: 8, of which 6 were waited for; matrix products, arithmetic and copies ran while one was open for 6% of the time, Pallas kernels for 0%

profile of v2, /device:TPU:2, one launch (start us, length us, event | category | flops | bytes accessed | tf_op | source)
XLA Modules:
  0.0 340.9 jit_solution(9039355976572360150)
XLA Ops:
  3.8 10.3 %all-to-all-start.1 = ((bf16[8,208,512]{2,1,0:T(8,128)(2,1)}), bf16[8,208,512]{2,1,0:T(8,128)(2,1)S(1)}, u32[]{:S(2)}, u32[]{:S(2)}) async-start(bf16[8,208,512]{2,1,0:T(8,128)(2,1)} %broadcast_in_dim.15), calls=%async_computation.1 | async-start | bytes 3407872 | tf_op jit(solution)/shard_map/all_to_all | solution.py:50
  14.2 42.7 %all-to-all-done.1 = bf16[8,208,512]{2,1,0:T(8,128)(2,1)S(1)} async-done(((bf16[8,208,512]{2,1,0:T(8,128)(2,1)}), bf16[8,208,512]{2,1,0:T(8,128)(2,1)S(1)}, u32[]{:S(2)}, u32[]{:S(2)}) %all-to-all-start.1) | async-done | bytes 1703968 | tf_op jit(solution)/shard_map/all_to_all | solution.py:50
  58.0 10.7 %all-to-all-start = ((bf16[64,24,384]{2,1,0:T(8,128)(2,1)}), bf16[64,24,384]{2,1,0:T(8,128)(2,1)S(1)}, u32[]{:S(2)}, u32[]{:S(2)}) async-start(bf16[64,24,384]{2,1,0:T(8,128)(2,1)} %broadcast_in_dim.14), calls=%async_computation | async-start | bytes 2359296 | tf_op jit(solution)/shard_map/all_to_all | solution.py:50
  72.3 27.9 %all-to-all-done = bf16[64,24,384]{2,1,0:T(8,128)(2,1)S(1)} async-done(((bf16[64,24,384]{2,1,0:T(8,128)(2,1)}), bf16[64,24,384]{2,1,0:T(8,128)(2,1)S(1)}, u32[]{:S(2)}, u32[]{:S(2)}) %all-to-all-start) | async-done | bytes 1179680 | tf_op jit(solution)/shard_map/all_to_all | solution.py:50
  100.3 2.2 fusion.53
  105.5 2.4 collective-permute-start
  107.9 3.0 collective-permute-done
  114.2 2.2 convolution_select_fusion.1
  117.7 2.2 reshape.146
  123.9 2.4 collective-permute-start.2
  126.3 3.0 collective-permute-done.2
  133.6 3.0 convolution_select_fusion
  136.6 2.3 copy.53
  138.9 2.2 reshape.147
  142.5 3.3 multiply_reduce_fusion
  145.8 4.6 %all-to-all-start.2 = ((bf16[8,192,512]{2,1,0:T(8,128)(2,1)}), bf16[8,192,512]{2,1,0:T(8,128)(2,1)}, u32[]{:S(2)}, u32[]{:S(2)}) async-start(bf16[8,192,512]{2,1,0:T(8,128)(2,1)} %bitcast.73), calls=%async_computation.2 | async-start | bytes 3145728 | tf_op jit(solution)/shard_map/all_to_all | solution.py:132
  150.5 2.1 slice_convert_fusion
  155.0 4.0 %fusion.52 = f32[1,192,31]{1,0,2:T(1,128)S(1)} fusion(bf16[1,192,542]{1,0,2:T(2,128)(2,1)} %copy.50, bf16[192,1,512]{0,1,2:T(2,128)(2,1)} %copy.51), kind=kOutput, calls=%fused_computation.95 | convolution fusion | flops 6094848 | bytes 428544 | tf_op jit(solution)/shard_map/conv_general_dilated | solution.py:35
  161.2 2.5 pad_maximum_fusion
  163.7 24.0 %all-to-all-done.2 = bf16[8,192,512]{2,1,0:T(8,128)(2,1)} async-done(((bf16[8,192,512]{2,1,0:T(8,128)(2,1)}), bf16[8,192,512]{2,1,0:T(8,128)(2,1)}, u32[]{:S(2)}, u32[]{:S(2)}) %all-to-all-start.2) | async-done | bytes 1572896 | tf_op jit(solution)/shard_map/all_to_all | solution.py:132
  187.7 10.0 %all-to-all-start.3 = ((f32[64,44,384]{2,1,0:T(8,128)}), f32[64,44,384]{2,1,0:T(8,128)}, u32[]{:S(2)}, u32[]{:S(2)}) async-start(f32[64,44,384]{2,1,0:T(8,128)} %pad_maximum_fusion), calls=%async_computation.3 | async-start | bytes 9437184 | tf_op jit(solution)/shard_map/all_to_all | solution.py:126
  200.5 104.6 %all-to-all-done.3 = f32[64,44,384]{2,1,0:T(8,128)} async-done(((f32[64,44,384]{2,1,0:T(8,128)}), f32[64,44,384]{2,1,0:T(8,128)}, u32[]{:S(2)}, u32[]{:S(2)}) %all-to-all-start.3) | async-done | bytes 4325408 | tf_op jit(solution)/shard_map/all_to_all | solution.py:126
  305.1 2.6 reduce_sum.69
  308.4 29.4 %psum.7 = f32[2560]{0:T(1024)S(1)} all-reduce(f32[2560]{0:T(1024)S(1)} %pad_maximum_fusion.8), channel_id=1, replica_groups=mesh['seq'=64,'ch'=8] {'ch'}, use_global_device_ids=true, to_apply=%region_7.8 | all-reduce | flops 2560 | bytes 20480 | tf_op jit(solution)/shard_map/psum | solution.py:145
  (87 shorter events, 36.5 us)
Async XLA Ops:
  0.6 113.6 %copy-start = (f32[31,192]{1,0:T(8,128)S(1)}, f32[31,192]{1,0:T(8,128)}, u32[]{:S(2)}) copy-start(f32[31,192]{1,0:T(8,128)} %param.10) | copy-start | bytes 71428
  0.6 13.4 %copy-start.10 = (bf16[24,192]{1,0:T(8,128)(2,1)S(1)}, bf16[24,192]{1,0:T(8,128)(2,1)}, u32[]{:S(2)}) copy-start(bf16[24,192]{1,0:T(8,128)(2,1)} %param.9) | copy-start | bytes 27652
  0.7 13.4 %copy-start.11 = (bf16[24,192]{1,0:T(8,128)(2,1)S(1)}, bf16[24,192]{1,0:T(8,128)(2,1)}, u32[]{:S(2)}) copy-start(bf16[24,192]{1,0:T(8,128)(2,1)} %param.8) | copy-start | bytes 27652
  3.8 53.1 %all-to-all-start.1 = ((bf16[8,208,512]{2,1,0:T(8,128)(2,1)}), bf16[8,208,512]{2,1,0:T(8,128)(2,1)S(1)}, u32[]{:S(2)}, u32[]{:S(2)}) async-start(bf16[8,208,512]{2,1,0:T(8,128)(2,1)} %broadcast_in_dim.15), calls=%async_computation.1 | async-start | bytes 3407872 | tf_op jit(solution)/shard_map/all_to_all | solution.py:50
  58.0 42.3 %all-to-all-start = ((bf16[64,24,384]{2,1,0:T(8,128)(2,1)}), bf16[64,24,384]{2,1,0:T(8,128)(2,1)S(1)}, u32[]{:S(2)}, u32[]{:S(2)}) async-start(bf16[64,24,384]{2,1,0:T(8,128)(2,1)} %broadcast_in_dim.14), calls=%async_computation | async-start | bytes 2359296 | tf_op jit(solution)/shard_map/all_to_all | solution.py:50
  69.6 0.6 copy-start.7
  70.1 0.6 copy-start.5
  102.5 0.9 copy-start.2
  103.6 4.3 %collective-permute-start.1 = (bf16[192,15]{1,0:T(8,128)(2,1)S(1)}, bf16[192,15]{1,0:T(8,128)(2,1)S(1)}, u32[]{:S(2)}, u32[]{:S(2)}) collective-permute-start(bf16[192,15]{1,0:T(8,128)(2,1)S(1)} %get-tuple-element.21), channel_id=1, source_target_pairs={{8,0},{16,8},{24,16},{32,24},{40,32},{48,40},{56,48},{64,56},{72,6... | collective-permute-start | bytes 17288 | tf_op jit(solution)/shard_map/ppermute | solution.py:17
  105.5 5.4 %collective-permute-start = (bf16[192,15]{1,0:T(8,128)(2,1)S(1)}, bf16[192,15]{1,0:T(8,128)(2,1)S(1)}, u32[]{:S(2)}, u32[]{:S(2)}) collective-permute-start(bf16[192,15]{1,0:T(8,128)(2,1)S(1)} %get-tuple-element.20), channel_id=1, source_target_pairs={{0,8},{8,16},{16,24},{24,32},{32,40},{40,48},{48,56},{56,64},{64,7... | collective-permute-start | bytes 17288 | tf_op jit(solution)/shard_map/ppermute | solution.py:15
  116.4 17.1 %copy-start.13 = (pred[8,68]{0,1:T(8,128)(4,1)S(1)}, pred[8,68]{0,1:T(8,128)(4,1)}, u32[]{:S(2)}) copy-start(pred[8,68]{0,1:T(8,128)(4,1)} %constant.44) | copy-start | bytes 1636
  121.9 4.3 %collective-permute-start.3 = (bf16[192,15]{1,0:T(8,128)(2,1)S(1)}, bf16[192,15]{1,0:T(8,128)(2,1)S(1)}, u32[]{:S(2)}, u32[]{:S(2)}) collective-permute-start(bf16[192,15]{1,0:T(8,128)(2,1)S(1)} %get-tuple-element.19), channel_id=1, source_target_pairs={{8,0},{16,8},{24,16},{32,24},{40,32},{48,40},{56,48},{64,56},{72,6... | collective-permute-start | bytes 17288 | tf_op jit(solution)/shard_map/ppermute | solution.py:17
  123.9 5.4 %collective-permute-start.2 = (bf16[192,15]{1,0:T(8,128)(2,1)S(1)}, bf16[192,15]{1,0:T(8,128)(2,1)S(1)}, u32[]{:S(2)}, u32[]{:S(2)}) collective-permute-start(bf16[192,15]{1,0:T(8,128)(2,1)S(1)} %get-tuple-element.18), channel_id=1, source_target_pairs={{0,8},{8,16},{16,24},{24,32},{32,40},{40,48},{48,56},{56,64},{64,7... | collective-permute-start | bytes 17288 | tf_op jit(solution)/shard_map/ppermute | solution.py:15
  136.6 5.9 %copy-start.6 = (f32[512]{0:T(512)S(1)}, f32[512]{0:T(512)}, u32[]{:S(2)}) copy-start(f32[512]{0:T(512)} %copy-done.5) | copy-start | bytes 6148
  136.6 5.9 %copy-start.8 = (f32[512]{0:T(512)S(1)}, f32[512]{0:T(512)}, u32[]{:S(2)}) copy-start(f32[512]{0:T(512)} %copy-done.7) | copy-start | bytes 6148
  142.5 3.3 copy-start.3
  145.8 4.6 %copy-start.9 = (f32[8,192]{1,0:T(8,128)S(1)}, f32[8,192]{1,0:T(8,128)}, u32[]{:S(2)}) copy-start(f32[8,192]{1,0:T(8,128)} %get-tuple-element.8) | copy-start | bytes 18436
  145.8 41.9 %all-to-all-start.2 = ((bf16[8,192,512]{2,1,0:T(8,128)(2,1)}), bf16[8,192,512]{2,1,0:T(8,128)(2,1)}, u32[]{:S(2)}, u32[]{:S(2)}) async-start(bf16[8,192,512]{2,1,0:T(8,128)(2,1)} %bitcast.73), calls=%async_computation.2 | async-start | bytes 3145728 | tf_op jit(solution)/shard_map/all_to_all | solution.py:132
  150.4 2.2 copy-start.4
  155.0 4.1 %copy-start.1 = (f32[8,192,512]{2,1,0:T(8,128)S(1)}, f32[8,192,512]{2,1,0:T(8,128)}, u32[]{:S(2)}) copy-start(f32[8,192,512]{2,1,0:T(8,128)} %slice_convert_fusion) | copy-start | bytes 9437188
  163.7 35.6 %copy-start.12 = (f32[192]{0:T(256)S(1)}, f32[192]{0:T(256)}, u32[]{:S(2)}) copy-start(f32[192]{0:T(256)} %param.7) | copy-start | bytes 2308
  187.7 117.4 %all-to-all-start.3 = ((f32[64,44,384]{2,1,0:T(8,128)}), f32[64,44,384]{2,1,0:T(8,128)}, u32[]{:S(2)}, u32[]{:S(2)}) async-start(f32[64,44,384]{2,1,0:T(8,128)} %pad_maximum_fusion), calls=%async_computation.3 | async-start | bytes 9437184 | tf_op jit(solution)/shard_map/all_to_all | solution.py:126

commit v3 on v2

--- a/solution.py
+++ b/solution.py
@@ -60,6 +60,28 @@
     return parts
 
 
+def gather_by_shifts(block, axis):
+    count = lax.axis_size(axis)
+    position = lax.axis_index(axis)
+    pieces = [block]
+    for shift in range(1, count):
+        pieces.append(
+            lax.ppermute(block, axis, [(i, (i - shift) % count) for i in range(count)])
+        )
+    return jnp.roll(jnp.stack(pieces, 0), position, axis=0)
+
+
+def reduce_by_shifts(blocks, axis):
+    count = lax.axis_size(axis)
+    position = lax.axis_index(axis)
+    total = lax.dynamic_index_in_dim(blocks, position, 0, keepdims=False).astype(jnp.float32)
+    for shift in range(1, count):
+        outgoing = lax.dynamic_index_in_dim(blocks, (position + shift) % count, 0, keepdims=False)
+        arrived = lax.ppermute(outgoing, axis, [(i, (i + shift) % count) for i in range(count)])
+        total = total + arrived.astype(jnp.float32)
+    return total
+
+
 def shards(signal, input_norm_gain, value_weight, gate_weight, depth_taps, cotangent):
     local_cols, frames = signal.shape
     groups = lax.axis_size("ch")
@@ -68,7 +90,7 @@
     reach = depth_taps.shape[0] // 2
     gain_rows = jnp.stack(bf16_pieces(input_norm_gain, 3), 0)
     gain_rows = jnp.pad(gain_rows, ((0, 13), (0, frames - local_cols)))
-    arrived = gather_by_exchange(jnp.concatenate([signal, gain_rows], 0), "ch")
+    arrived = gather_by_shifts(jnp.concatenate([signal, gain_rows], 0), "ch")
     complete_signal = arrived[:, :local_cols].reshape(groups * local_cols, frames)
     gain_parts = arrived[:, local_cols : local_cols + 3, :local_cols].astype(jnp.float32)
     complete_gain = ((gain_parts[:, 0] + gain_parts[:, 1]) + gain_parts[:, 2]).reshape(-1)
@@ -129,10 +151,9 @@
     taps_end = rows + (taps_rows + 1) * local_cols // width
     grad_taps = summed[rows:taps_end].reshape(taps_rows + 1, local_cols)[:taps_rows]
     gain_seq_sum = summed[taps_end:].reshape(-1)
-    partials = lax.all_to_all(
-        normed_term.reshape(groups, local_cols, frames), "ch", 0, 0, tiled=False
-    )
-    normalized_gradient = jnp.sum(partials.astype(jnp.float32), 0)
+    normalized_gradient = reduce_by_shifts(
+        normed_term.reshape(groups, local_cols, frames), "ch"
+    )
     scaled_signal = normalized_gradient * input_norm_gain[:, None]
     moments = jnp.concatenate(
         [

time: 342 us -> 314 us (0.918)
  waiting for transfers between devices: 205 us -> 87.9 us
  starting transfers between devices: 44.2 us -> 107 us
  local copies, waits for them, and re-layouts: 23.4 us -> 41.7 us
    all_to_all x2 -> x1, waiting for transfers between devices: 70.6 us -> 0.01 us  [gather_by_exchange(): return lax.all_to_all(copies, axis, 0, 0, tiled=False)]
    ppermute x0 -> x14, starting transfers between devices: none -> 70 us  [the longest x7 40.9 us: gather_by_shifts(): lax.ppermute(block, axis, [(i, (i - shift) % count) for i in range(count)])]
    all_to_all x1, waiting for transfers between devices: 105 us -> 59 us  [shards(): summed = jnp.sum(lax.all_to_all(outgoing, 'seq', 0, 0, tiled=False), 0)]
    ppermute x0 -> x14, waiting for transfers between devices: none -> 28.9 us  [the longest x7 17.5 us: reduce_by_shifts(): lax.ppermute(outgoing, axis, [(i, (i + shift) % count) for i in range(cou...]
    all_to_all x1 -> x0, waiting for transfers between devices: 24 us -> none  [shards(): lax.all_to_all(normed_term.reshape(groups, local_cols, frames), 'ch', 0,...]
    unnamed x30 -> x33, local copies, waits for them, and re-layouts: 1.51 us -> 11.8 us
    all_to_all x2 -> x1, starting transfers between devices: 21 us -> 10.8 us  [gather_by_exchange(): return lax.all_to_all(copies, axis, 0, 0, tiled=False)]
    ppermute x2, waiting for transfers between devices: 5.97 us -> 0.01 us  [extended(): lax.ppermute(tail, axis, [(i, (i + 1) % count) for i in range(ends)])]
  transfers between devices with their start and end apart: 8 -> 20, of which waited for: 6 -> 8; matrix products, arithmetic and copies ran while one was open for 6% -> 9% of each run, Pallas kernels for 0% -> 0%
where the time goes in v3:
time: 314 us; the launch traced here: 312 us
  starting transfers between devices  107 us (34%)
  waiting for transfers between devices  87.9 us (28%)
  local copies, waits for them, and re-layouts  41.7 us (13%)
  blocking collectives  29.3 us (9%)
  other arithmetic  24.4 us (8%)
  matrix products  20.1 us (6%)
    all_to_all x1, waiting for transfers between devices, shards(): summed = jnp.sum(lax.all_to_all(outgoing, 'seq', 0, 0, tiled=False), 0)  59 us
    ppermute x7, starting transfers between devices, gather_by_shifts(): lax.ppermute(block, axis, [(i, (i - shift) % count) for i in range(count)])  40.9 us
    psum x1, blocking collectives, shards(): moments = lax.psum(moments, 'ch')  29.3 us
    ppermute x7, starting transfers between devices, reduce_by_shifts(): lax.ppermute(outgoing, axis, [(i, (i + shift) % count) for i in range(cou...  29 us
    conv_general_dilated x10, local copies, waits for them, and re-layouts, depthwise(): lax.conv_general_dilated(padded[None], kernel, (1,), 'VALID', dimension_n...  19.4 us
    ppermute x7, waiting for transfers between devices, reduce_by_shifts(): lax.ppermute(outgoing, axis, [(i, (i + shift) % count) for i in range(cou...  17.5 us
    all_to_all x1, starting transfers between devices, shards(): summed = jnp.sum(lax.all_to_all(outgoing, 'seq', 0, 0, tiled=False), 0)  15.1 us
    unnamed x33, local copies, waits for them, and re-layouts  11.8 us
  transfers between devices with their start and end apart: 20, of which 8 were waited for; matrix products, arithmetic and copies ran while one was open for 9% of the time, Pallas kernels for 0%

profile of v3, /device:TPU:2, one launch (start us, length us, event | category | flops | bytes accessed | tf_op | source)
XLA Modules:
  0.0 311.9 jit_solution(8395790140859634718)
XLA Ops:
  3.1 6.1 %collective-permute-start.5 = (bf16[208,512]{1,0:T(8,128)(2,1)}, bf16[208,512]{1,0:T(8,128)(2,1)}, u32[]{:S(2)}, u32[]{:S(2)}) collective-permute-start(bf16[208,512]{1,0:T(8,128)(2,1)} %pad_maximum_fusion.5), channel_id=1, source_target_pairs={{0,2},{1,3},{2,4},{3,5},{4,6},{5,7},{6,0},{7,1},{8,10},{9,11},{10,... | collective-permute-start | bytes 638984 | tf_op jit(solution)/shard_map/ppermute | solution.py:69
  9.2 8.2 %collective-permute-start.4 = (bf16[208,512]{1,0:T(8,128)(2,1)}, bf16[208,512]{1,0:T(8,128)(2,1)}, u32[]{:S(2)}, u32[]{:S(2)}) collective-permute-start(bf16[208,512]{1,0:T(8,128)(2,1)} %pad_maximum_fusion.5), channel_id=1, source_target_pairs={{0,3},{1,4},{2,5},{3,6},{4,7},{5,0},{6,1},{7,2},{8,11},{9,12},{10,... | collective-permute-start | bytes 638984 | tf_op jit(solution)/shard_map/ppermute | solution.py:69
  17.4 3.7 %collective-permute-start.3 = (bf16[208,512]{1,0:T(8,128)(2,1)}, bf16[208,512]{1,0:T(8,128)(2,1)}, u32[]{:S(2)}, u32[]{:S(2)}) collective-permute-start(bf16[208,512]{1,0:T(8,128)(2,1)} %pad_maximum_fusion.5), channel_id=1, source_target_pairs={{0,4},{1,5},{2,6},{3,7},{4,0},{5,1},{6,2},{7,3},{8,12},{9,13},{10,... | collective-permute-start | bytes 638984 | tf_op jit(solution)/shard_map/ppermute | solution.py:69
  21.1 6.0 %collective-permute-start.2 = (bf16[208,512]{1,0:T(8,128)(2,1)}, bf16[208,512]{1,0:T(8,128)(2,1)}, u32[]{:S(2)}, u32[]{:S(2)}) collective-permute-start(bf16[208,512]{1,0:T(8,128)(2,1)} %pad_maximum_fusion.5), channel_id=1, source_target_pairs={{0,5},{1,6},{2,7},{3,0},{4,1},{5,2},{6,3},{7,4},{8,13},{9,14},{10,... | collective-permute-start | bytes 638984 | tf_op jit(solution)/shard_map/ppermute | solution.py:69
  31.6 10.8 %all-to-all-start = ((bf16[64,24,384]{2,1,0:T(8,128)(2,1)}), bf16[64,24,384]{2,1,0:T(8,128)(2,1)}, u32[]{:S(2)}, u32[]{:S(2)}) async-start(bf16[64,24,384]{2,1,0:T(8,128)(2,1)} %broadcast_in_dim.12), calls=%async_computation | async-start | bytes 2359296 | tf_op jit(solution)/shard_map/all_to_all | solution.py:50
  43.3 6.2 %collective-permute-done = bf16[208,512]{1,0:T(8,128)(2,1)} collective-permute-done((bf16[208,512]{1,0:T(8,128)(2,1)}, bf16[208,512]{1,0:T(8,128)(2,1)}, u32[]{:S(2)}, u32[]{:S(2)}) %collective-permute-start) | collective-permute-done | bytes 213024 | tf_op jit(solution)/shard_map/ppermute | solution.py:69
  49.6 4.6 %collective-permute-start.1 = (bf16[208,512]{1,0:T(8,128)(2,1)}, bf16[208,512]{1,0:T(8,128)(2,1)S(1)}, u32[]{:S(2)}, u32[]{:S(2)}) collective-permute-start(bf16[208,512]{1,0:T(8,128)(2,1)} %pad_maximum_fusion.5), channel_id=1, source_target_pairs={{0,6},{1,7},{2,0},{3,1},{4,2},{5,3},{6,4},{7,5},{8,14},{9,15},{10,... | collective-permute-start | bytes 638984 | tf_op jit(solution)/shard_map/ppermute | solution.py:69
  55.1 4.1 %collective-permute-done.1 = bf16[208,512]{1,0:T(8,128)(2,1)S(1)} collective-permute-done((bf16[208,512]{1,0:T(8,128)(2,1)}, bf16[208,512]{1,0:T(8,128)(2,1)S(1)}, u32[]{:S(2)}, u32[]{:S(2)}) %collective-permute-start.1) | collective-permute-done | bytes 213024 | tf_op jit(solution)/shard_map/ppermute | solution.py:69
  59.3 9.8 %collective-permute-start.6 = (bf16[208,512]{1,0:T(8,128)(2,1)}, bf16[208,512]{1,0:T(8,128)(2,1)S(1)}, u32[]{:S(2)}, u32[]{:S(2)}) collective-permute-start(bf16[208,512]{1,0:T(8,128)(2,1)} %pad_maximum_fusion.5), channel_id=1, source_target_pairs={{0,1},{1,2},{2,3},{3,4},{4,5},{5,6},{6,7},{7,0},{8,9},{9,10},{10,1... | collective-permute-start | bytes 638984 | tf_op jit(solution)/shard_map/ppermute | solution.py:69
  89.2 3.6 %collective-permute-start.8 = (bf16[192,15]{1,0:T(8,128)(2,1)}, bf16[192,15]{1,0:T(8,128)(2,1)}, u32[]{:S(2)}, u32[]{:S(2)}) collective-permute-start(bf16[192,15]{1,0:T(8,128)(2,1)} %get-tuple-element.29), channel_id=1, source_target_pairs={{8,0},{16,8},{24,16},{32,24},{40,32},{48,40},{56,48},{64,56},{72,6... | collective-permute-start | bytes 17288 | tf_op jit(solution)/shard_map/ppermute | solution.py:17
  102.8 3.0 convolution_select_fusion.1
  113.6 3.4 %collective-permute-start.9 = (bf16[192,15]{1,0:T(8,128)(2,1)}, bf16[192,15]{1,0:T(8,128)(2,1)}, u32[]{:S(2)}, u32[]{:S(2)}) collective-permute-start(bf16[192,15]{1,0:T(8,128)(2,1)} %get-tuple-element.26), channel_id=1, source_target_pairs={{0,8},{8,16},{16,24},{24,32},{32,40},{40,48},{48,56},{56,64},{64,7... | collective-permute-start | bytes 17288 | tf_op jit(solution)/shard_map/ppermute | solution.py:15
  123.4 3.8 %fusion.61 = f32[1,192,31]{1,0,2:T(1,128)S(1)} fusion(bf16[1,192,542]{1,0,2:T(2,128)(2,1)} %copy.34, bf16[192,1,512]{0,1,2:T(2,128)(2,1)} %copy.35), kind=kOutput, calls=%fused_computation.125 | convolution fusion | flops 6094848 | bytes 428544 | tf_op jit(solution)/shard_map/conv_general_dilated | solution.py:35
  143.3 4.7 %multiply_reduce_fusion = (f32[1536]{0:T(1024)S(1)}, f32[1536,512]{1,0:T(8,128)}, bf16[1536,512]{1,0:T(8,128)(2,1)}) fusion(f32[512]{0:T(512)S(1)} %add_rsqrt_fusion, f32[512]{0:T(512)S(1)} %broadcast_multiply_fusion, bf16[16,208,512]{2,1,0:T(8,128)(2,1)S(1)} %bitcast_dynamic-update-slice_fusion.1, s32[]{:T(128)S(6)} %select_n.73, ...), kind=kOutput, calls=%fused_computation.3 | convolution fusion | flops 610269696 | bytes 7874564 | tf_op jit(solution)/shard_map/dot_general | solution.py:132
  153.7 15.1 %all-to-all-start.1 = ((f32[64,44,384]{2,1,0:T(8,128)}), f32[64,44,384]{2,1,0:T(8,128)}, u32[]{:S(2)}, u32[]{:S(2)}) async-start(f32[64,44,384]{2,1,0:T(8,128)} %pad_maximum_fusion), calls=%async_computation.1 | async-start | bytes 9437184 | tf_op jit(solution)/shard_map/all_to_all | solution.py:148
  169.1 4.3 %collective-permute-start.11 = (bf16[192,512]{1,0:T(8,128)(2,1)S(1)}, bf16[192,512]{1,0:T(8,128)(2,1)S(1)}, u32[]{:S(2)}, u32[]{:S(2)}) collective-permute-start(bf16[192,512]{1,0:T(8,128)(2,1)S(1)} %get-tuple-element.13), channel_id=1, source_target_pairs={{0,1},{1,2},{2,3},{3,4},{4,5},{5,6},{6,7},{7,0},{8,9},{9,10},{10,1... | collective-permute-start | bytes 589832 | tf_op jit(solution)/shard_map/ppermute | solution.py:80
  178.6 6.4 %collective-permute-start.15 = (bf16[192,512]{1,0:T(8,128)(2,1)S(1)}, bf16[192,512]{1,0:T(8,128)(2,1)S(1)}, u32[]{:S(2)}, u32[]{:S(2)}) collective-permute-start(bf16[192,512]{1,0:T(8,128)(2,1)S(1)} %get-tuple-element.16), channel_id=1, source_target_pairs={{0,5},{1,6},{2,7},{3,0},{4,1},{5,2},{6,3},{7,4},{8,13},{9,14},{10,... | collective-permute-start | bytes 589832 | tf_op jit(solution)/shard_map/ppermute | solution.py:80
  185.0 3.3 %collective-permute-start.14 = (bf16[192,512]{1,0:T(8,128)(2,1)S(1)}, bf16[192,512]{1,0:T(8,128)(2,1)}, u32[]{:S(2)}, u32[]{:S(2)}) collective-permute-start(bf16[192,512]{1,0:T(8,128)(2,1)S(1)} %get-tuple-element.17), channel_id=1, source_target_pairs={{0,4},{1,5},{2,6},{3,7},{4,0},{5,1},{6,2},{7,3},{8,12},{9,13},{10,... | collective-permute-start | bytes 589832 | tf_op jit(solution)/shard_map/ppermute | solution.py:80
  188.3 3.9 %collective-permute-start.13 = (bf16[192,512]{1,0:T(8,128)(2,1)S(1)}, bf16[192,512]{1,0:T(8,128)(2,1)}, u32[]{:S(2)}, u32[]{:S(2)}) collective-permute-start(bf16[192,512]{1,0:T(8,128)(2,1)S(1)} %get-tuple-element.18), channel_id=1, source_target_pairs={{0,3},{1,4},{2,5},{3,6},{4,7},{5,0},{6,1},{7,2},{8,11},{9,12},{10,... | collective-permute-start | bytes 589832 | tf_op jit(solution)/shard_map/ppermute | solution.py:80
  192.2 6.0 %collective-permute-start.12 = (bf16[192,512]{1,0:T(8,128)(2,1)S(1)}, bf16[192,512]{1,0:T(8,128)(2,1)}, u32[]{:S(2)}, u32[]{:S(2)}) collective-permute-start(bf16[192,512]{1,0:T(8,128)(2,1)S(1)} %get-tuple-element.19), channel_id=1, source_target_pairs={{0,2},{1,3},{2,4},{3,5},{4,6},{5,7},{6,0},{7,1},{8,10},{9,11},{10,... | collective-permute-start | bytes 589832 | tf_op jit(solution)/shard_map/ppermute | solution.py:80
  198.2 5.1 %collective-permute-done.15 = bf16[192,512]{1,0:T(8,128)(2,1)S(1)} collective-permute-done((bf16[192,512]{1,0:T(8,128)(2,1)S(1)}, bf16[192,512]{1,0:T(8,128)(2,1)S(1)}, u32[]{:S(2)}, u32[]{:S(2)}) %collective-permute-start.15) | collective-permute-done | bytes 196640 | tf_op jit(solution)/shard_map/ppermute | solution.py:80
  204.9 10.2 %collective-permute-done.13 = bf16[192,512]{1,0:T(8,128)(2,1)} collective-permute-done((bf16[192,512]{1,0:T(8,128)(2,1)S(1)}, bf16[192,512]{1,0:T(8,128)(2,1)}, u32[]{:S(2)}, u32[]{:S(2)}) %collective-permute-start.13) | collective-permute-done | bytes 196640 | tf_op jit(solution)/shard_map/ppermute | solution.py:80
  217.2 59.0 %all-to-all-done.1 = f32[64,44,384]{2,1,0:T(8,128)} async-done(((f32[64,44,384]{2,1,0:T(8,128)}), f32[64,44,384]{2,1,0:T(8,128)}, u32[]{:S(2)}, u32[]{:S(2)}) %all-to-all-start.1) | async-done | bytes 4325408 | tf_op jit(solution)/shard_map/all_to_all | solution.py:148
  278.8 29.3 %psum.7 = f32[2560]{0:T(1024)S(1)} all-reduce(f32[2560]{0:T(1024)S(1)} %pad_maximum_fusion.8), channel_id=1, replica_groups=mesh['seq'=64,'ch'=8] {'ch'}, use_global_device_ids=true, to_apply=%region_6.7 | all-reduce | flops 2560 | bytes 20480 | tf_op jit(solution)/shard_map/psum | solution.py:166
  (116 shorter events, 89.9 us)
Async XLA Ops:
  0.6 102.1 %copy-start = (f32[31,192]{1,0:T(8,128)S(1)}, f32[31,192]{1,0:T(8,128)}, u32[]{:S(2)}) copy-start(f32[31,192]{1,0:T(8,128)} %param.10) | copy-start | bytes 71428
  3.1 68.9 %collective-permute-start.5 = (bf16[208,512]{1,0:T(8,128)(2,1)}, bf16[208,512]{1,0:T(8,128)(2,1)}, u32[]{:S(2)}, u32[]{:S(2)}) collective-permute-start(bf16[208,512]{1,0:T(8,128)(2,1)} %pad_maximum_fusion.5), channel_id=1, source_target_pairs={{0,2},{1,3},{2,4},{3,5},{4,6},{5,7},{6,0},{7,1},{8,10},{9,11},{10,... | collective-permute-start | bytes 638984 | tf_op jit(solution)/shard_map/ppermute | solution.py:69
  9.2 61.9 %collective-permute-start.4 = (bf16[208,512]{1,0:T(8,128)(2,1)}, bf16[208,512]{1,0:T(8,128)(2,1)}, u32[]{:S(2)}, u32[]{:S(2)}) collective-permute-start(bf16[208,512]{1,0:T(8,128)(2,1)} %pad_maximum_fusion.5), channel_id=1, source_target_pairs={{0,3},{1,4},{2,5},{3,6},{4,7},{5,0},{6,1},{7,2},{8,11},{9,12},{10,... | collective-permute-start | bytes 638984 | tf_op jit(solution)/shard_map/ppermute | solution.py:69
  17.4 52.7 %collective-permute-start.3 = (bf16[208,512]{1,0:T(8,128)(2,1)}, bf16[208,512]{1,0:T(8,128)(2,1)}, u32[]{:S(2)}, u32[]{:S(2)}) collective-permute-start(bf16[208,512]{1,0:T(8,128)(2,1)} %pad_maximum_fusion.5), channel_id=1, source_target_pairs={{0,4},{1,5},{2,6},{3,7},{4,0},{5,1},{6,2},{7,3},{8,12},{9,13},{10,... | collective-permute-start | bytes 638984 | tf_op jit(solution)/shard_map/ppermute | solution.py:69
  21.1 48.0 %collective-permute-start.2 = (bf16[208,512]{1,0:T(8,128)(2,1)}, bf16[208,512]{1,0:T(8,128)(2,1)}, u32[]{:S(2)}, u32[]{:S(2)}) collective-permute-start(bf16[208,512]{1,0:T(8,128)(2,1)} %pad_maximum_fusion.5), channel_id=1, source_target_pairs={{0,5},{1,6},{2,7},{3,0},{4,1},{5,2},{6,3},{7,4},{8,13},{9,14},{10,... | collective-permute-start | bytes 638984 | tf_op jit(solution)/shard_map/ppermute | solution.py:69
  27.2 22.4 %collective-permute-start = (bf16[208,512]{1,0:T(8,128)(2,1)}, bf16[208,512]{1,0:T(8,128)(2,1)}, u32[]{:S(2)}, u32[]{:S(2)}) collective-permute-start(bf16[208,512]{1,0:T(8,128)(2,1)} %pad_maximum_fusion.5), channel_id=1, source_target_pairs={{0,7},{1,0},{2,1},{3,2},{4,3},{5,4},{6,5},{7,6},{8,15},{9,8},{10,9... | collective-permute-start | bytes 638984 | tf_op jit(solution)/shard_map/ppermute | solution.py:69
  31.6 50.7 %all-to-all-start = ((bf16[64,24,384]{2,1,0:T(8,128)(2,1)}), bf16[64,24,384]{2,1,0:T(8,128)(2,1)}, u32[]{:S(2)}, u32[]{:S(2)}) async-start(bf16[64,24,384]{2,1,0:T(8,128)(2,1)} %broadcast_in_dim.12), calls=%async_computation | async-start | bytes 2359296 | tf_op jit(solution)/shard_map/all_to_all | solution.py:50
  49.6 9.7 %collective-permute-start.1 = (bf16[208,512]{1,0:T(8,128)(2,1)}, bf16[208,512]{1,0:T(8,128)(2,1)S(1)}, u32[]{:S(2)}, u32[]{:S(2)}) collective-permute-start(bf16[208,512]{1,0:T(8,128)(2,1)} %pad_maximum_fusion.5), channel_id=1, source_target_pairs={{0,6},{1,7},{2,0},{3,1},{4,2},{5,3},{6,4},{7,5},{8,14},{9,15},{10,... | collective-permute-start | bytes 638984 | tf_op jit(solution)/shard_map/ppermute | solution.py:69
  59.3 14.7 %collective-permute-start.6 = (bf16[208,512]{1,0:T(8,128)(2,1)}, bf16[208,512]{1,0:T(8,128)(2,1)S(1)}, u32[]{:S(2)}, u32[]{:S(2)}) collective-permute-start(bf16[208,512]{1,0:T(8,128)(2,1)} %pad_maximum_fusion.5), channel_id=1, source_target_pairs={{0,1},{1,2},{2,3},{3,4},{4,5},{5,6},{6,7},{7,0},{8,9},{9,10},{10,1... | collective-permute-start | bytes 638984 | tf_op jit(solution)/shard_map/ppermute | solution.py:69
  87.3 7.8 %collective-permute-start.7 = (bf16[192,15]{1,0:T(8,128)(2,1)}, bf16[192,15]{1,0:T(8,128)(2,1)S(1)}, u32[]{:S(2)}, u32[]{:S(2)}) collective-permute-start(bf16[192,15]{1,0:T(8,128)(2,1)} %get-tuple-element.28), channel_id=1, source_target_pairs={{0,8},{8,16},{16,24},{24,32},{32,40},{40,48},{48,56},{56,64},{64,7... | collective-permute-start | bytes 17288 | tf_op jit(solution)/shard_map/ppermute | solution.py:15
  89.2 13.6 %copy-start.8 = (pred[8,68]{0,1:T(8,128)(4,1)S(1)}, pred[8,68]{0,1:T(8,128)(4,1)}, u32[]{:S(2)}) copy-start(pred[8,68]{0,1:T(8,128)(4,1)} %constant.127) | copy-start | bytes 1636
  89.2 5.8 %collective-permute-start.8 = (bf16[192,15]{1,0:T(8,128)(2,1)}, bf16[192,15]{1,0:T(8,128)(2,1)}, u32[]{:S(2)}, u32[]{:S(2)}) collective-permute-start(bf16[192,15]{1,0:T(8,128)(2,1)} %get-tuple-element.29), channel_id=1, source_target_pairs={{8,0},{16,8},{24,16},{32,24},{40,32},{48,40},{56,48},{64,56},{72,6... | collective-permute-start | bytes 17288 | tf_op jit(solution)/shard_map/ppermute | solution.py:17
  113.6 13.7 %collective-permute-start.9 = (bf16[192,15]{1,0:T(8,128)(2,1)}, bf16[192,15]{1,0:T(8,128)(2,1)}, u32[]{:S(2)}, u32[]{:S(2)}) collective-permute-start(bf16[192,15]{1,0:T(8,128)(2,1)} %get-tuple-element.26), channel_id=1, source_target_pairs={{0,8},{8,16},{16,24},{24,32},{32,40},{40,48},{48,56},{56,64},{64,7... | collective-permute-start | bytes 17288 | tf_op jit(solution)/shard_map/ppermute | solution.py:15
  117.0 10.3 %collective-permute-start.10 = (bf16[192,15]{1,0:T(8,128)(2,1)}, bf16[192,15]{1,0:T(8,128)(2,1)}, u32[]{:S(2)}, u32[]{:S(2)}) collective-permute-start(bf16[192,15]{1,0:T(8,128)(2,1)} %get-tuple-element.27), channel_id=1, source_target_pairs={{8,0},{16,8},{24,16},{32,24},{40,32},{48,40},{56,48},{64,56},{72,6... | collective-permute-start | bytes 17288 | tf_op jit(solution)/shard_map/ppermute | solution.py:17
  153.7 15.2 %copy-start.2 = (bf16[1536,512]{1,0:T(8,128)(2,1)S(1)}, bf16[1536,512]{1,0:T(8,128)(2,1)}, u32[]{:S(2)}) copy-start(bf16[1536,512]{1,0:T(8,128)(2,1)} %get-tuple-element.37) | copy-start | bytes 4718596
  153.7 62.0 %copy-start.7 = (f32[192]{0:T(256)S(1)}, f32[192]{0:T(256)}, u32[]{:S(2)}) copy-start(f32[192]{0:T(256)} %param.7) | copy-start | bytes 2308
  153.7 122.5 %all-to-all-start.1 = ((f32[64,44,384]{2,1,0:T(8,128)}), f32[64,44,384]{2,1,0:T(8,128)}, u32[]{:S(2)}, u32[]{:S(2)}) async-start(f32[64,44,384]{2,1,0:T(8,128)} %pad_maximum_fusion), calls=%async_computation.1 | async-start | bytes 9437184 | tf_op jit(solution)/shard_map/all_to_all | solution.py:148
  169.1 19.2 %collective-permute-start.11 = (bf16[192,512]{1,0:T(8,128)(2,1)S(1)}, bf16[192,512]{1,0:T(8,128)(2,1)S(1)}, u32[]{:S(2)}, u32[]{:S(2)}) collective-permute-start(bf16[192,512]{1,0:T(8,128)(2,1)S(1)} %get-tuple-element.13), channel_id=1, source_target_pairs={{0,1},{1,2},{2,3},{3,4},{4,5},{5,6},{6,7},{7,0},{8,9},{9,10},{10,1... | collective-permute-start | bytes 589832 | tf_op jit(solution)/shard_map/ppermute | solution.py:80
  173.4 18.8 %collective-permute-start.17 = (bf16[192,512]{1,0:T(8,128)(2,1)S(1)}, bf16[192,512]{1,0:T(8,128)(2,1)S(1)}, u32[]{:S(2)}, u32[]{:S(2)}) collective-permute-start(bf16[192,512]{1,0:T(8,128)(2,1)S(1)} %get-tuple-element.14), channel_id=1, source_target_pairs={{0,7},{1,0},{2,1},{3,2},{4,3},{5,4},{6,5},{7,6},{8,15},{9,8},{10,9... | collective-permute-start | bytes 589832 | tf_op jit(solution)/shard_map/ppermute | solution.py:80
  176.2 22.1 %collective-permute-start.16 = (bf16[192,512]{1,0:T(8,128)(2,1)S(1)}, bf16[192,512]{1,0:T(8,128)(2,1)S(1)}, u32[]{:S(2)}, u32[]{:S(2)}) collective-permute-start(bf16[192,512]{1,0:T(8,128)(2,1)S(1)} %get-tuple-element.15), channel_id=1, source_target_pairs={{0,6},{1,7},{2,0},{3,1},{4,2},{5,3},{6,4},{7,5},{8,14},{9,15},{10,... | collective-permute-start | bytes 589832 | tf_op jit(solution)/shard_map/ppermute | solution.py:80
  178.6 24.7 %collective-permute-start.15 = (bf16[192,512]{1,0:T(8,128)(2,1)S(1)}, bf16[192,512]{1,0:T(8,128)(2,1)S(1)}, u32[]{:S(2)}, u32[]{:S(2)}) collective-permute-start(bf16[192,512]{1,0:T(8,128)(2,1)S(1)} %get-tuple-element.16), channel_id=1, source_target_pairs={{0,5},{1,6},{2,7},{3,0},{4,1},{5,2},{6,3},{7,4},{8,13},{9,14},{10,... | collective-permute-start | bytes 589832 | tf_op jit(solution)/shard_map/ppermute | solution.py:80
  185.0 19.9 %collective-permute-start.14 = (bf16[192,512]{1,0:T(8,128)(2,1)S(1)}, bf16[192,512]{1,0:T(8,128)(2,1)}, u32[]{:S(2)}, u32[]{:S(2)}) collective-permute-start(bf16[192,512]{1,0:T(8,128)(2,1)S(1)} %get-tuple-element.17), channel_id=1, source_target_pairs={{0,4},{1,5},{2,6},{3,7},{4,0},{5,1},{6,2},{7,3},{8,12},{9,13},{10,... | collective-permute-start | bytes 589832 | tf_op jit(solution)/shard_map/ppermute | solution.py:80
  188.3 26.8 %collective-permute-start.13 = (bf16[192,512]{1,0:T(8,128)(2,1)S(1)}, bf16[192,512]{1,0:T(8,128)(2,1)}, u32[]{:S(2)}, u32[]{:S(2)}) collective-permute-start(bf16[192,512]{1,0:T(8,128)(2,1)S(1)} %get-tuple-element.18), channel_id=1, source_target_pairs={{0,3},{1,4},{2,5},{3,6},{4,7},{5,0},{6,1},{7,2},{8,11},{9,12},{10,... | collective-permute-start | bytes 589832 | tf_op jit(solution)/shard_map/ppermute | solution.py:80
  192.2 23.6 %collective-permute-start.12 = (bf16[192,512]{1,0:T(8,128)(2,1)S(1)}, bf16[192,512]{1,0:T(8,128)(2,1)}, u32[]{:S(2)}, u32[]{:S(2)}) collective-permute-start(bf16[192,512]{1,0:T(8,128)(2,1)S(1)} %get-tuple-element.19), channel_id=1, source_target_pairs={{0,2},{1,3},{2,4},{3,5},{4,6},{5,7},{6,0},{7,1},{8,10},{9,11},{10,... | collective-permute-start | bytes 589832 | tf_op jit(solution)/shard_map/ppermute | solution.py:80
  (5 other events, 11.7 us)

commit v4 on v3

--- a/solution.py
+++ b/solution.py
@@ -132,47 +132,39 @@
     normed_term = jnp.dot(gathered, grad_both, preferred_element_type=jnp.float32).astype(
         jnp.bfloat16
     )
-    gain_portion = jnp.sum(normed_term.astype(jnp.float32) * centered_unit, 1)
     width = weight_partial.shape[1]
+    rows = value_weight.shape[0]
     taps_rows = depth_taps.shape[0]
-    extra = jnp.pad(tap_partial, ((0, 1), (0, 0))).reshape(-1, width)
-    extra = jnp.concatenate([extra, gain_portion.reshape(-1, width)], 0)
-    rows = value_weight.shape[0]
-    outgoing = jnp.concatenate(
-        [
-            weight_partial.reshape(blocks, rows, width),
-            jnp.broadcast_to(extra[None], (blocks,) + extra.shape),
-        ],
-        1,
-    )
+    taps_flat = jnp.pad(tap_partial, ((0, 1), (0, 0))).reshape(blocks, -1)
+    piece = taps_flat.shape[1]
+    outgoing = jnp.concatenate([weight_partial.reshape(blocks, rows * width), taps_flat], 1)
     summed = jnp.sum(lax.all_to_all(outgoing, "seq", 0, 0, tiled=False), 0)
-    grad_value = summed[:rows, :local_cols]
-    grad_gate = summed[:rows, local_cols:]
-    taps_end = rows + (taps_rows + 1) * local_cols // width
-    grad_taps = summed[rows:taps_end].reshape(taps_rows + 1, local_cols)[:taps_rows]
-    gain_seq_sum = summed[taps_end:].reshape(-1)
+    weight_sums = summed[: rows * width].reshape(rows, width)
+    grad_value = weight_sums[:, :local_cols]
+    grad_gate = weight_sums[:, local_cols:]
     normalized_gradient = reduce_by_shifts(
         normed_term.reshape(groups, local_cols, frames), "ch"
     )
     scaled_signal = normalized_gradient * input_norm_gain[:, None]
-    moments = jnp.concatenate(
+    moments = jnp.stack(
         [
             jnp.sum(scaled_signal, 0),
             jnp.sum(scaled_signal * centered_unit_rows, 0),
-            gain_seq_sum,
         ],
         0,
     )
-    moments = lax.psum(moments, "ch")
-    first_moment = moments[:frames] * (1.0 / complete_signal.shape[0])
-    second_moment = moments[frames : 2 * frames] * (1.0 / complete_signal.shape[0])
+    moments = lax.psum(moments, "ch") * (1.0 / complete_signal.shape[0])
     signal_gradient = (
         inverse_deviation
-        * (scaled_signal - first_moment[None] - centered_unit_rows * second_moment[None])
+        * (scaled_signal - moments[0:1] - centered_unit_rows * moments[1:2])
     ).astype(jnp.bfloat16)
-    gain_gradient = lax.dynamic_slice_in_dim(
-        moments[2 * frames :], channel_position * local_cols, local_cols, 0
+    gain_portion = jnp.sum(normalized_gradient * centered_unit_rows, 1)
+    last = jnp.concatenate([summed[rows * width :], gain_portion], 0)
+    finished = gather_by_exchange(last, "seq")
+    grad_taps = finished[:, :piece].reshape(-1)[: taps_rows * local_cols].reshape(
+        taps_rows, local_cols
     )
+    gain_gradient = jnp.sum(finished[:, piece:], 0)
     return (output, signal_gradient, grad_value, grad_gate, grad_taps, gain_gradient)
 
 

time: 314 us -> 249 us (0.79)
  the two profiles are of different devices: /device:TPU:2 before, /device:TPU:1 now
where the time goes in v4:
time: 249 us; the launch traced here: 248 us
  starting transfers between devices  108 us (43%)
  waiting for transfers between devices  57.4 us (23%)
  local copies, waits for them, and re-layouts  32.7 us (13%)
  other arithmetic  20.1 us (8%)
  matrix products  16.1 us (6%)
  blocking collectives  11.8 us (5%)
    ppermute x7, starting transfers between devices, gather_by_shifts(): lax.ppermute(block, axis, [(i, (i - shift) % count) for i in range(count)])  31.5 us
    all_to_all x2, starting transfers between devices, gather_by_exchange(): return lax.all_to_all(copies, axis, 0, 0, tiled=False)  26.6 us
    ppermute x7, waiting for transfers between devices, reduce_by_shifts(): lax.ppermute(outgoing, axis, [(i, (i + shift) % count) for i in range(cou...  26.4 us
    ppermute x7, starting transfers between devices, reduce_by_shifts(): lax.ppermute(outgoing, axis, [(i, (i + shift) % count) for i in range(cou...  26.1 us
    all_to_all x2, waiting for transfers between devices, gather_by_exchange(): return lax.all_to_all(copies, axis, 0, 0, tiled=False)  15.9 us
    ppermute x7, waiting for transfers between devices, gather_by_shifts(): lax.ppermute(block, axis, [(i, (i - shift) % count) for i in range(count)])  15.1 us
    conv_general_dilated x10, local copies, waits for them, and re-layouts, depthwise(): lax.conv_general_dilated(padded[None], kernel, (1,), 'VALID', dimension_n...  14.2 us
    psum x1, blocking collectives, shards(): moments = lax.psum(moments, 'ch') * (1.0 / complete_signal.shape[0])  11.8 us
  transfers between devices with their start and end apart: 21, of which 9 were waited for; matrix products, arithmetic and copies ran while one was open for 8% of the time, Pallas kernels for 0%

profile of v4, /device:TPU:1, one launch (start us, length us, event | category | flops | bytes accessed | tf_op | source)
XLA Modules:
  0.0 247.5 jit_solution(7085087173060739771)
XLA Ops:
  2.4 11.5 %collective-permute-start = (bf16[208,512]{1,0:T(8,128)(2,1)S(1)}, bf16[208,512]{1,0:T(8,128)(2,1)S(1)}, u32[]{:S(2)}, u32[]{:S(2)}) collective-permute-start(bf16[208,512]{1,0:T(8,128)(2,1)S(1)} %pad_maximum_fusion.5), channel_id=1, source_target_pairs={{0,7},{1,0},{2,1},{3,2},{4,3},{5,4},{6,5},{7,6},{8,15},{9,8},{10,9... | collective-permute-start | bytes 638984 | tf_op jit(solution)/shard_map/ppermute | solution.py:69
  18.0 7.3 %collective-permute-start.3 = (bf16[208,512]{1,0:T(8,128)(2,1)S(1)}, bf16[208,512]{1,0:T(8,128)(2,1)S(1)}, u32[]{:S(2)}, u32[]{:S(2)}) collective-permute-start(bf16[208,512]{1,0:T(8,128)(2,1)S(1)} %pad_maximum_fusion.5), channel_id=1, source_target_pairs={{0,4},{1,5},{2,6},{3,7},{4,0},{5,1},{6,2},{7,3},{8,12},{9,13},{10,... | collective-permute-start | bytes 638984 | tf_op jit(solution)/shard_map/ppermute | solution.py:69
  29.2 12.1 %all-to-all-start = ((bf16[64,24,384]{2,1,0:T(8,128)(2,1)}), bf16[64,24,384]{2,1,0:T(8,128)(2,1)}, u32[]{:S(2)}, u32[]{:S(2)}) async-start(bf16[64,24,384]{2,1,0:T(8,128)(2,1)} %broadcast_in_dim.12), calls=%async_computation | async-start | bytes 2359296 | tf_op jit(solution)/shard_map/all_to_all | solution.py:50
  41.3 3.1 %collective-permute-start.5 = (bf16[208,512]{1,0:T(8,128)(2,1)S(1)}, bf16[208,512]{1,0:T(8,128)(2,1)S(1)}, u32[]{:S(2)}, u32[]{:S(2)}) collective-permute-start(bf16[208,512]{1,0:T(8,128)(2,1)S(1)} %pad_maximum_fusion.5), channel_id=1, source_target_pairs={{0,2},{1,3},{2,4},{3,5},{4,6},{5,7},{6,0},{7,1},{8,10},{9,11},{10,... | collective-permute-start | bytes 638984 | tf_op jit(solution)/shard_map/ppermute | solution.py:69
  44.5 3.6 %collective-permute-start.6 = (bf16[208,512]{1,0:T(8,128)(2,1)S(1)}, bf16[208,512]{1,0:T(8,128)(2,1)S(1)}, u32[]{:S(2)}, u32[]{:S(2)}) collective-permute-start(bf16[208,512]{1,0:T(8,128)(2,1)S(1)} %pad_maximum_fusion.5), channel_id=1, source_target_pairs={{0,1},{1,2},{2,3},{3,4},{4,5},{5,6},{6,7},{7,0},{8,9},{9,10},{10,1... | collective-permute-start | bytes 638984 | tf_op jit(solution)/shard_map/ppermute | solution.py:69
  49.8 8.9 %collective-permute-done.5 = bf16[208,512]{1,0:T(8,128)(2,1)S(1)} collective-permute-done((bf16[208,512]{1,0:T(8,128)(2,1)S(1)}, bf16[208,512]{1,0:T(8,128)(2,1)S(1)}, u32[]{:S(2)}, u32[]{:S(2)}) %collective-permute-start.5) | collective-permute-done | bytes 213024 | tf_op jit(solution)/shard_map/ppermute | solution.py:69
  58.7 4.7 %collective-permute-done.6 = bf16[208,512]{1,0:T(8,128)(2,1)S(1)} collective-permute-done((bf16[208,512]{1,0:T(8,128)(2,1)S(1)}, bf16[208,512]{1,0:T(8,128)(2,1)S(1)}, u32[]{:S(2)}, u32[]{:S(2)}) %collective-permute-start.6) | collective-permute-done | bytes 213024 | tf_op jit(solution)/shard_map/ppermute | solution.py:69
  65.8 6.0 %all-to-all-done = bf16[64,24,384]{2,1,0:T(8,128)(2,1)} async-done(((bf16[64,24,384]{2,1,0:T(8,128)(2,1)}), bf16[64,24,384]{2,1,0:T(8,128)(2,1)}, u32[]{:S(2)}, u32[]{:S(2)}) %all-to-all-start) | async-done | bytes 1179680 | tf_op jit(solution)/shard_map/all_to_all | solution.py:50
  74.8 3.5 %collective-permute-start.8 = (bf16[192,15]{1,0:T(8,128)(2,1)}, bf16[192,15]{1,0:T(8,128)(2,1)S(1)}, u32[]{:S(2)}, u32[]{:S(2)}) collective-permute-start(bf16[192,15]{1,0:T(8,128)(2,1)} %get-tuple-element.28), channel_id=1, source_target_pairs={{8,0},{16,8},{24,16},{32,24},{40,32},{48,40},{56,48},{64,56},{72,6... | collective-permute-start | bytes 17288 | tf_op jit(solution)/shard_map/ppermute | solution.py:17
  98.5 3.8 %collective-permute-start.9 = (bf16[192,15]{1,0:T(8,128)(2,1)}, bf16[192,15]{1,0:T(8,128)(2,1)S(1)}, u32[]{:S(2)}, u32[]{:S(2)}) collective-permute-start(bf16[192,15]{1,0:T(8,128)(2,1)} %get-tuple-element.25), channel_id=1, source_target_pairs={{0,8},{8,16},{16,24},{24,32},{32,40},{40,48},{48,56},{56,64},{64,7... | collective-permute-start | bytes 17288 | tf_op jit(solution)/shard_map/ppermute | solution.py:15
  105.5 3.8 %fusion.57 = f32[1,192,31]{1,0,2:T(1,128)S(1)} fusion(bf16[1,192,542]{1,0,2:T(2,128)(2,1)} %copy.48, bf16[192,1,512]{0,1,2:T(2,128)(2,1)} %copy.49), kind=kOutput, calls=%fused_computation.122 | convolution fusion | flops 6094848 | bytes 428544 | tf_op jit(solution)/shard_map/conv_general_dilated | solution.py:35
  128.7 3.1 %all_to_all.16 = f32[64,1,9312]{2,1,0:T(1,128)} reshape(f32[64,9312]{1,0:T(8,128)S(1)} %pad_maximum_fusion) | data formatting | bytes 4767744 | tf_op jit(solution)/shard_map/all_to_all | solution.py:141
  131.8 11.5 %all-to-all-start.1 = ((f32[64,1,9312]{2,1,0:T(1,128)}), f32[64,1,9312]{2,1,0:T(1,128)}, u32[]{:S(2)}, u32[]{:S(2)}) async-start(f32[64,1,9312]{2,1,0:T(1,128)} %all_to_all.16), calls=%async_computation.1 | async-start | bytes 4784128 | tf_op jit(solution)/shard_map/all_to_all | solution.py:141
  150.0 6.7 %collective-permute-start.16 = (bf16[192,512]{1,0:T(8,128)(2,1)S(1)}, bf16[192,512]{1,0:T(8,128)(2,1)S(1)}, u32[]{:S(2)}, u32[]{:S(2)}) collective-permute-start(bf16[192,512]{1,0:T(8,128)(2,1)S(1)} %get-tuple-element.14), channel_id=1, source_target_pairs={{0,6},{1,7},{2,0},{3,1},{4,2},{5,3},{6,4},{7,5},{8,14},{9,15},{10,... | collective-permute-start | bytes 589832 | tf_op jit(solution)/shard_map/ppermute | solution.py:80
  158.6 7.3 %collective-permute-start.14 = (bf16[192,512]{1,0:T(8,128)(2,1)}, bf16[192,512]{1,0:T(8,128)(2,1)}, u32[]{:S(2)}, u32[]{:S(2)}) collective-permute-start(bf16[192,512]{1,0:T(8,128)(2,1)} %get-tuple-element.16), channel_id=1, source_target_pairs={{0,4},{1,5},{2,6},{3,7},{4,0},{5,1},{6,2},{7,3},{8,12},{9,13},{10,... | collective-permute-start | bytes 589832 | tf_op jit(solution)/shard_map/ppermute | solution.py:80
  167.8 3.3 %collective-permute-start.12 = (bf16[192,512]{1,0:T(8,128)(2,1)}, bf16[192,512]{1,0:T(8,128)(2,1)}, u32[]{:S(2)}, u32[]{:S(2)}) collective-permute-start(bf16[192,512]{1,0:T(8,128)(2,1)} %get-tuple-element.18), channel_id=1, source_target_pairs={{0,2},{1,3},{2,4},{3,5},{4,6},{5,7},{6,0},{7,1},{8,10},{9,11},{10,... | collective-permute-start | bytes 589832 | tf_op jit(solution)/shard_map/ppermute | solution.py:80
  174.7 4.3 %collective-permute-done.15 = bf16[192,512]{1,0:T(8,128)(2,1)} collective-permute-done((bf16[192,512]{1,0:T(8,128)(2,1)}, bf16[192,512]{1,0:T(8,128)(2,1)}, u32[]{:S(2)}, u32[]{:S(2)}) %collective-permute-start.15) | collective-permute-done | bytes 196640 | tf_op jit(solution)/shard_map/ppermute | solution.py:80
  179.0 8.4 %collective-permute-done.13 = bf16[192,512]{1,0:T(8,128)(2,1)} collective-permute-done((bf16[192,512]{1,0:T(8,128)(2,1)}, bf16[192,512]{1,0:T(8,128)(2,1)}, u32[]{:S(2)}, u32[]{:S(2)}) %collective-permute-start.13) | collective-permute-done | bytes 196640 | tf_op jit(solution)/shard_map/ppermute | solution.py:80
  187.3 6.1 %collective-permute-done.12 = bf16[192,512]{1,0:T(8,128)(2,1)} collective-permute-done((bf16[192,512]{1,0:T(8,128)(2,1)}, bf16[192,512]{1,0:T(8,128)(2,1)}, u32[]{:S(2)}, u32[]{:S(2)}) %collective-permute-start.12) | collective-permute-done | bytes 196640 | tf_op jit(solution)/shard_map/ppermute | solution.py:80
  193.4 7.6 %collective-permute-done.11 = bf16[192,512]{1,0:T(8,128)(2,1)} collective-permute-done((bf16[192,512]{1,0:T(8,128)(2,1)S(1)}, bf16[192,512]{1,0:T(8,128)(2,1)}, u32[]{:S(2)}, u32[]{:S(2)}) %collective-permute-start.11) | collective-permute-done | bytes 196640 | tf_op jit(solution)/shard_map/ppermute | solution.py:80
  203.5 11.8 %psum.7 = f32[2,512]{1,0:T(2,128)S(1)} all-reduce(f32[2,512]{1,0:T(2,128)S(1)} %pad_maximum_fusion.7), channel_id=1, replica_groups=mesh['seq'=64,'ch'=8] {'ch'}, use_global_device_ids=true, to_apply=%region_4.5 | all-reduce | flops 1024 | bytes 8192 | tf_op jit(solution)/shard_map/psum | solution.py:156
  217.1 3.1 %reduce_sum.67 = f32[9312]{0:T(1024)S(1)} reduce(f32[64,1,9312]{2,1,0:T(1,128)} %all-to-all-done.1, f32[]{:T(128)} %constant.101.clone.1), dimensions={0,1}, to_apply=%region_5.6 | reduce | flops 586656 | bytes 2421124 | tf_op jit(solution)/shard_map/reduce_sum | solution.py:141
  221.0 14.5 %all-to-all-start.2 = ((f32[64,1,288]{2,1,0:T(1,128)}), f32[64,1,288]{2,1,0:T(1,128)S(1)}, u32[]{:S(2)}, u32[]{:S(2)}) async-start(f32[64,1,288]{2,1,0:T(1,128)} %broadcast_in_dim.33), calls=%async_computation.2 | async-start | bytes 196608 | tf_op jit(solution)/shard_map/all_to_all | solution.py:50
  236.3 9.9 %all-to-all-done.2 = f32[64,1,288]{2,1,0:T(1,128)S(1)} async-done(((f32[64,1,288]{2,1,0:T(1,128)}), f32[64,1,288]{2,1,0:T(1,128)S(1)}, u32[]{:S(2)}, u32[]{:S(2)}) %all-to-all-start.2) | async-done | bytes 73760 | tf_op jit(solution)/shard_map/all_to_all | solution.py:50
  (121 shorter events, 80.3 us)
Async XLA Ops:
  0.6 86.1 %copy-start = (f32[31,192]{1,0:T(8,128)S(1)}, f32[31,192]{1,0:T(8,128)}, u32[]{:S(2)}) copy-start(f32[31,192]{1,0:T(8,128)} %param.10) | copy-start | bytes 71428
  0.6 40.6 %copy-start.3 = (bf16[192,512]{1,0:T(8,128)(2,1)S(1)}, bf16[192,512]{1,0:T(8,128)(2,1)}, u32[]{:S(2)}) copy-start(bf16[192,512]{1,0:T(8,128)(2,1)} %param.6) | copy-start | bytes 589828
  2.4 38.9 %collective-permute-start = (bf16[208,512]{1,0:T(8,128)(2,1)S(1)}, bf16[208,512]{1,0:T(8,128)(2,1)S(1)}, u32[]{:S(2)}, u32[]{:S(2)}) collective-permute-start(bf16[208,512]{1,0:T(8,128)(2,1)S(1)} %pad_maximum_fusion.5), channel_id=1, source_target_pairs={{0,7},{1,0},{2,1},{3,2},{4,3},{5,4},{6,5},{7,6},{8,15},{9,8},{10,9... | collective-permute-start | bytes 638984 | tf_op jit(solution)/shard_map/ppermute | solution.py:69
  13.9 30.6 %collective-permute-start.1 = (bf16[208,512]{1,0:T(8,128)(2,1)S(1)}, bf16[208,512]{1,0:T(8,128)(2,1)S(1)}, u32[]{:S(2)}, u32[]{:S(2)}) collective-permute-start(bf16[208,512]{1,0:T(8,128)(2,1)S(1)} %pad_maximum_fusion.5), channel_id=1, source_target_pairs={{0,6},{1,7},{2,0},{3,1},{4,2},{5,3},{6,4},{7,5},{8,14},{9,15},{10,... | collective-permute-start | bytes 638984 | tf_op jit(solution)/shard_map/ppermute | solution.py:69
  16.1 33.6 %collective-permute-start.2 = (bf16[208,512]{1,0:T(8,128)(2,1)S(1)}, bf16[208,512]{1,0:T(8,128)(2,1)S(1)}, u32[]{:S(2)}, u32[]{:S(2)}) collective-permute-start(bf16[208,512]{1,0:T(8,128)(2,1)S(1)} %pad_maximum_fusion.5), channel_id=1, source_target_pairs={{0,5},{1,6},{2,7},{3,0},{4,1},{5,2},{6,3},{7,4},{8,13},{9,14},{10,... | collective-permute-start | bytes 638984 | tf_op jit(solution)/shard_map/ppermute | solution.py:69
  18.0 31.7 %collective-permute-start.3 = (bf16[208,512]{1,0:T(8,128)(2,1)S(1)}, bf16[208,512]{1,0:T(8,128)(2,1)S(1)}, u32[]{:S(2)}, u32[]{:S(2)}) collective-permute-start(bf16[208,512]{1,0:T(8,128)(2,1)S(1)} %pad_maximum_fusion.5), channel_id=1, source_target_pairs={{0,4},{1,5},{2,6},{3,7},{4,0},{5,1},{6,2},{7,3},{8,12},{9,13},{10,... | collective-permute-start | bytes 638984 | tf_op jit(solution)/shard_map/ppermute | solution.py:69
  25.3 24.4 %collective-permute-start.4 = (bf16[208,512]{1,0:T(8,128)(2,1)S(1)}, bf16[208,512]{1,0:T(8,128)(2,1)S(1)}, u32[]{:S(2)}, u32[]{:S(2)}) collective-permute-start(bf16[208,512]{1,0:T(8,128)(2,1)S(1)} %pad_maximum_fusion.5), channel_id=1, source_target_pairs={{0,3},{1,4},{2,5},{3,6},{4,7},{5,0},{6,1},{7,2},{8,11},{9,12},{10,... | collective-permute-start | bytes 638984 | tf_op jit(solution)/shard_map/ppermute | solution.py:69
  29.2 42.6 %all-to-all-start = ((bf16[64,24,384]{2,1,0:T(8,128)(2,1)}), bf16[64,24,384]{2,1,0:T(8,128)(2,1)}, u32[]{:S(2)}, u32[]{:S(2)}) async-start(bf16[64,24,384]{2,1,0:T(8,128)(2,1)} %broadcast_in_dim.12), calls=%async_computation | async-start | bytes 2359296 | tf_op jit(solution)/shard_map/all_to_all | solution.py:50
  41.3 17.3 %collective-permute-start.5 = (bf16[208,512]{1,0:T(8,128)(2,1)S(1)}, bf16[208,512]{1,0:T(8,128)(2,1)S(1)}, u32[]{:S(2)}, u32[]{:S(2)}) collective-permute-start(bf16[208,512]{1,0:T(8,128)(2,1)S(1)} %pad_maximum_fusion.5), channel_id=1, source_target_pairs={{0,2},{1,3},{2,4},{3,5},{4,6},{5,7},{6,0},{7,1},{8,10},{9,11},{10,... | collective-permute-start | bytes 638984 | tf_op jit(solution)/shard_map/ppermute | solution.py:69
  44.5 18.9 %collective-permute-start.6 = (bf16[208,512]{1,0:T(8,128)(2,1)S(1)}, bf16[208,512]{1,0:T(8,128)(2,1)S(1)}, u32[]{:S(2)}, u32[]{:S(2)}) collective-permute-start(bf16[208,512]{1,0:T(8,128)(2,1)S(1)} %pad_maximum_fusion.5), channel_id=1, source_target_pairs={{0,1},{1,2},{2,3},{3,4},{4,5},{5,6},{6,7},{7,0},{8,9},{9,10},{10,1... | collective-permute-start | bytes 638984 | tf_op jit(solution)/shard_map/ppermute | solution.py:69
  74.8 8.5 %collective-permute-start.8 = (bf16[192,15]{1,0:T(8,128)(2,1)}, bf16[192,15]{1,0:T(8,128)(2,1)S(1)}, u32[]{:S(2)}, u32[]{:S(2)}) collective-permute-start(bf16[192,15]{1,0:T(8,128)(2,1)} %get-tuple-element.28), channel_id=1, source_target_pairs={{8,0},{16,8},{24,16},{32,24},{40,32},{48,40},{56,48},{64,56},{72,6... | collective-permute-start | bytes 17288 | tf_op jit(solution)/shard_map/ppermute | solution.py:17
  78.2 5.0 %collective-permute-start.7 = (bf16[192,15]{1,0:T(8,128)(2,1)S(1)}, bf16[192,15]{1,0:T(8,128)(2,1)S(1)}, u32[]{:S(2)}, u32[]{:S(2)}) collective-permute-start(bf16[192,15]{1,0:T(8,128)(2,1)S(1)} %get-tuple-element.27), channel_id=1, source_target_pairs={{0,8},{8,16},{16,24},{24,32},{32,40},{40,48},{48,56},{56,64},{64,7... | collective-permute-start | bytes 17288 | tf_op jit(solution)/shard_map/ppermute | solution.py:15
  96.6 12.9 %collective-permute-start.10 = (bf16[192,15]{1,0:T(8,128)(2,1)}, bf16[192,15]{1,0:T(8,128)(2,1)S(1)}, u32[]{:S(2)}, u32[]{:S(2)}) collective-permute-start(bf16[192,15]{1,0:T(8,128)(2,1)} %get-tuple-element.26), channel_id=1, source_target_pairs={{8,0},{16,8},{24,16},{32,24},{40,32},{48,40},{56,48},{64,56},{72,6... | collective-permute-start | bytes 17288 | tf_op jit(solution)/shard_map/ppermute | solution.py:17
  98.5 10.9 %collective-permute-start.9 = (bf16[192,15]{1,0:T(8,128)(2,1)}, bf16[192,15]{1,0:T(8,128)(2,1)S(1)}, u32[]{:S(2)}, u32[]{:S(2)}) collective-permute-start(bf16[192,15]{1,0:T(8,128)(2,1)} %get-tuple-element.25), channel_id=1, source_target_pairs={{0,8},{8,16},{16,24},{24,32},{32,40},{40,48},{48,56},{56,64},{64,7... | collective-permute-start | bytes 17288 | tf_op jit(solution)/shard_map/ppermute | solution.py:15
  131.8 85.3 %all-to-all-start.1 = ((f32[64,1,9312]{2,1,0:T(1,128)}), f32[64,1,9312]{2,1,0:T(1,128)}, u32[]{:S(2)}, u32[]{:S(2)}) async-start(f32[64,1,9312]{2,1,0:T(1,128)} %all_to_all.16), calls=%async_computation.1 | async-start | bytes 4784128 | tf_op jit(solution)/shard_map/all_to_all | solution.py:141
  143.3 57.7 %copy-start.8 = (f32[192]{0:T(256)S(1)}, f32[192]{0:T(256)}, u32[]{:S(2)}) copy-start(f32[192]{0:T(256)} %param.7) | copy-start | bytes 2308
  147.8 20.0 %collective-permute-start.17 = (bf16[192,512]{1,0:T(8,128)(2,1)S(1)}, bf16[192,512]{1,0:T(8,128)(2,1)S(1)}, u32[]{:S(2)}, u32[]{:S(2)}) collective-permute-start(bf16[192,512]{1,0:T(8,128)(2,1)S(1)} %get-tuple-element.13), channel_id=1, source_target_pairs={{0,7},{1,0},{2,1},{3,2},{4,3},{5,4},{6,5},{7,6},{8,15},{9,8},{10,9... | collective-permute-start | bytes 589832 | tf_op jit(solution)/shard_map/ppermute | solution.py:80
  150.0 21.2 %collective-permute-start.16 = (bf16[192,512]{1,0:T(8,128)(2,1)S(1)}, bf16[192,512]{1,0:T(8,128)(2,1)S(1)}, u32[]{:S(2)}, u32[]{:S(2)}) collective-permute-start(bf16[192,512]{1,0:T(8,128)(2,1)S(1)} %get-tuple-element.14), channel_id=1, source_target_pairs={{0,6},{1,7},{2,0},{3,1},{4,2},{5,3},{6,4},{7,5},{8,14},{9,15},{10,... | collective-permute-start | bytes 589832 | tf_op jit(solution)/shard_map/ppermute | solution.py:80
  156.6 22.3 %collective-permute-start.15 = (bf16[192,512]{1,0:T(8,128)(2,1)}, bf16[192,512]{1,0:T(8,128)(2,1)}, u32[]{:S(2)}, u32[]{:S(2)}) collective-permute-start(bf16[192,512]{1,0:T(8,128)(2,1)} %get-tuple-element.15), channel_id=1, source_target_pairs={{0,5},{1,6},{2,7},{3,0},{4,1},{5,2},{6,3},{7,4},{8,13},{9,14},{10,... | collective-permute-start | bytes 589832 | tf_op jit(solution)/shard_map/ppermute | solution.py:80
  158.6 20.4 %collective-permute-start.14 = (bf16[192,512]{1,0:T(8,128)(2,1)}, bf16[192,512]{1,0:T(8,128)(2,1)}, u32[]{:S(2)}, u32[]{:S(2)}) collective-permute-start(bf16[192,512]{1,0:T(8,128)(2,1)} %get-tuple-element.16), channel_id=1, source_target_pairs={{0,4},{1,5},{2,6},{3,7},{4,0},{5,1},{6,2},{7,3},{8,12},{9,13},{10,... | collective-permute-start | bytes 589832 | tf_op jit(solution)/shard_map/ppermute | solution.py:80
  165.8 21.5 %collective-permute-start.13 = (bf16[192,512]{1,0:T(8,128)(2,1)}, bf16[192,512]{1,0:T(8,128)(2,1)}, u32[]{:S(2)}, u32[]{:S(2)}) collective-permute-start(bf16[192,512]{1,0:T(8,128)(2,1)} %get-tuple-element.17), channel_id=1, source_target_pairs={{0,3},{1,4},{2,5},{3,6},{4,7},{5,0},{6,1},{7,2},{8,11},{9,12},{10,... | collective-permute-start | bytes 589832 | tf_op jit(solution)/shard_map/ppermute | solution.py:80
  167.8 25.6 %collective-permute-start.12 = (bf16[192,512]{1,0:T(8,128)(2,1)}, bf16[192,512]{1,0:T(8,128)(2,1)}, u32[]{:S(2)}, u32[]{:S(2)}) collective-permute-start(bf16[192,512]{1,0:T(8,128)(2,1)} %get-tuple-element.18), channel_id=1, source_target_pairs={{0,2},{1,3},{2,4},{3,5},{4,6},{5,7},{6,0},{7,1},{8,10},{9,11},{10,... | collective-permute-start | bytes 589832 | tf_op jit(solution)/shard_map/ppermute | solution.py:80
  171.8 29.2 %collective-permute-start.11 = (bf16[192,512]{1,0:T(8,128)(2,1)S(1)}, bf16[192,512]{1,0:T(8,128)(2,1)}, u32[]{:S(2)}, u32[]{:S(2)}) collective-permute-start(bf16[192,512]{1,0:T(8,128)(2,1)S(1)} %get-tuple-element.12), channel_id=1, source_target_pairs={{0,1},{1,2},{2,3},{3,4},{4,5},{5,6},{6,7},{7,0},{8,9},{9,10},{10,1... | collective-permute-start | bytes 589832 | tf_op jit(solution)/shard_map/ppermute | solution.py:80
  221.0 25.1 %all-to-all-start.2 = ((f32[64,1,288]{2,1,0:T(1,128)}), f32[64,1,288]{2,1,0:T(1,128)S(1)}, u32[]{:S(2)}, u32[]{:S(2)}) async-start(f32[64,1,288]{2,1,0:T(1,128)} %broadcast_in_dim.33), calls=%async_computation.2 | async-start | bytes 196608 | tf_op jit(solution)/shard_map/all_to_all | solution.py:50
  (6 other events, 12.0 us)

commit v5 on v4

--- a/solution.py
+++ b/solution.py
@@ -79,6 +79,13 @@
         outgoing = lax.dynamic_index_in_dim(blocks, (position + shift) % count, 0, keepdims=False)
         arrived = lax.ppermute(outgoing, axis, [(i, (i + shift) % count) for i in range(count)])
         total = total + arrived.astype(jnp.float32)
+    return total
+
+
+def shifted_sum(padded, taps, span):
+    total = taps[0][:, None] * padded[:, 0:span]
+    for k in range(1, taps.shape[0]):
+        total = total + taps[k][:, None] * padded[:, k : k + span]
     return total
 
 
@@ -109,8 +116,9 @@
     sig_gate = jax.nn.sigmoid(gate)
     glued = (value * sig_gate).astype(jnp.bfloat16)
     glued_pad = extended(glued, (("seq", 1),), reach).astype(jnp.float32)
-    forward_kernel = depth_taps.T[:, None, :]
-    pre = depthwise(glued_pad, forward_kernel)
+    span = glued.shape[1]
+    taps_count = depth_taps.shape[0]
+    pre = shifted_sum(glued_pad, depth_taps, span)
     sig_pre = jax.nn.sigmoid(pre)
     output = (pre * sig_pre).astype(jnp.bfloat16)
     grad_pre = (cotangent.astype(jnp.float32) * sig_pre * (1.0 + pre * (1.0 - sig_pre))).astype(
@@ -118,8 +126,10 @@
     )
     grad_pre_f = grad_pre.astype(jnp.float32)
     grad_pad = extended(grad_pre, (("seq", 1),), reach).astype(jnp.float32)
-    grad_glued = depthwise(grad_pad, forward_kernel[:, :, ::-1])
-    tap_partial = depthwise(glued_pad, grad_pre_f[:, None, :]).T
+    grad_glued = shifted_sum(grad_pad, depth_taps[::-1], span)
+    tap_partial = jnp.stack(
+        [jnp.sum(glued_pad[:, k : k + span] * grad_pre_f, 1) for k in range(taps_count)], 0
+    )
     grad_v = (grad_glued * sig_gate).astype(jnp.bfloat16)
     grad_g = (grad_glued * value * sig_gate * (1.0 - sig_gate)).astype(jnp.bfloat16)
     grad_both = jnp.concatenate([grad_v, grad_g], 0)

time: 249 us -> 238 us (0.956)
  other arithmetic: 20.1 us -> 35.3 us
  waiting for transfers between devices: 57.4 us -> 44.4 us
  matrix products: 16.1 us -> 7.33 us
  local copies, waits for them, and re-layouts: 32.7 us -> 27.9 us
    conv_general_dilated x10 -> x0, local copies, waits for them, and re-layouts: 14.2 us -> none  [depthwise(): lax.conv_general_dilated(padded[None], kernel, (1,), 'VALID', dimension_n...]
    conv_general_dilated x3 -> x0, matrix products: 9.29 us -> none  [depthwise(): lax.conv_general_dilated(padded[None], kernel, (1,), 'VALID', dimension_n...]
    reduce_sum x0 -> x2, other arithmetic: none -> 9 us  [shards(): jnp.sum(glued_pad[:, k:k + span] * grad_pre_f, 1)]
    unnamed x34 -> x57, local copies, waits for them, and re-layouts: 3.62 us -> 11.4 us
    ppermute x7, waiting for transfers between devices: 15.1 us -> 8.22 us  [gather_by_shifts(): lax.ppermute(block, axis, [(i, (i - shift) % count) for i in range(count)])]
    all_to_all x2, waiting for transfers between devices: 15.9 us -> 10.1 us  [gather_by_exchange(): return lax.all_to_all(copies, axis, 0, 0, tiled=False)]
    convert_element_type x1, other arithmetic: 1.4 us -> 5.53 us  [shards(): grad_v = (grad_glued * sig_gate).astype(jnp.bfloat16)]
    broadcast_in_dim x4 -> x0, local copies, waits for them, and re-layouts: 3.21 us -> none  [the longest x3 2.15 us: depthwise(): padded[None]]
  transfers between devices with their start and end apart: 21 -> 21, of which waited for: 9 -> 9; matrix products, arithmetic and copies ran while one was open for 8% -> 14% of each run, Pallas kernels for 0% -> 0%
where the time goes in v5:
time: 238 us; the launch traced here: 237 us
  starting transfers between devices  109 us (46%)
  waiting for transfers between devices  44.4 us (19%)
  other arithmetic  35.3 us (15%)
  local copies, waits for them, and re-layouts  27.9 us (12%)
  blocking collectives  10.9 us (5%)
  matrix products  7.33 us (3%)
    ppermute x7, starting transfers between devices, gather_by_shifts(): lax.ppermute(block, axis, [(i, (i - shift) % count) for i in range(count)])  31.5 us
    all_to_all x2, starting transfers between devices, gather_by_exchange(): return lax.all_to_all(copies, axis, 0, 0, tiled=False)  26.3 us
    ppermute x7, waiting for transfers between devices, reduce_by_shifts(): lax.ppermute(outgoing, axis, [(i, (i + shift) % count) for i in range(cou...  26.1 us
    ppermute x7, starting transfers between devices, reduce_by_shifts(): lax.ppermute(outgoing, axis, [(i, (i + shift) % count) for i in range(cou...  26 us
    all_to_all x1, starting transfers between devices, shards(): summed = jnp.sum(lax.all_to_all(outgoing, 'seq', 0, 0, tiled=False), 0)  13.4 us
    unnamed x57, local copies, waits for them, and re-layouts  11.4 us
    psum x1, blocking collectives, shards(): moments = lax.psum(moments, 'ch') * (1.0 / complete_signal.shape[0])  10.9 us
    all_to_all x2, waiting for transfers between devices, gather_by_exchange(): return lax.all_to_all(copies, axis, 0, 0, tiled=False)  10.1 us
  transfers between devices with their start and end apart: 21, of which 9 were waited for; matrix products, arithmetic and copies ran while one was open for 14% of the time, Pallas kernels for 0%

profile of v5, /device:TPU:1, one launch (start us, length us, event | category | flops | bytes accessed | tf_op | source)
XLA Modules:
  0.0 236.7 jit_solution(17849011928314103144)
XLA Ops:
  3.1 11.5 %collective-permute-start = (bf16[208,512]{1,0:T(8,128)(2,1)}, bf16[208,512]{1,0:T(8,128)(2,1)}, u32[]{:S(2)}, u32[]{:S(2)}) collective-permute-start(bf16[208,512]{1,0:T(8,128)(2,1)} %pad_maximum_fusion.4), channel_id=1, source_target_pairs={{0,7},{1,0},{2,1},{3,2},{4,3},{5,4},{6,5},{7,6},{8,15},{9,8},{10,9... | collective-permute-start | bytes 638984 | tf_op jit(solution)/shard_map/ppermute | solution.py:69
  18.7 7.3 %collective-permute-start.3 = (bf16[208,512]{1,0:T(8,128)(2,1)}, bf16[208,512]{1,0:T(8,128)(2,1)}, u32[]{:S(2)}, u32[]{:S(2)}) collective-permute-start(bf16[208,512]{1,0:T(8,128)(2,1)} %pad_maximum_fusion.4), channel_id=1, source_target_pairs={{0,4},{1,5},{2,6},{3,7},{4,0},{5,1},{6,2},{7,3},{8,12},{9,13},{10,... | collective-permute-start | bytes 638984 | tf_op jit(solution)/shard_map/ppermute | solution.py:69
  29.8 12.1 %all-to-all-start = ((bf16[64,24,384]{2,1,0:T(8,128)(2,1)}), bf16[64,24,384]{2,1,0:T(8,128)(2,1)}, u32[]{:S(2)}, u32[]{:S(2)}) async-start(bf16[64,24,384]{2,1,0:T(8,128)(2,1)} %broadcast_in_dim.4), calls=%async_computation | async-start | bytes 2359296 | tf_op jit(solution)/shard_map/all_to_all | solution.py:50
  44.2 3.1 %collective-permute-start.5 = (bf16[208,512]{1,0:T(8,128)(2,1)}, bf16[208,512]{1,0:T(8,128)(2,1)S(1)}, u32[]{:S(2)}, u32[]{:S(2)}) collective-permute-start(bf16[208,512]{1,0:T(8,128)(2,1)} %pad_maximum_fusion.4), channel_id=1, source_target_pairs={{0,2},{1,3},{2,4},{3,5},{4,6},{5,7},{6,0},{7,1},{8,10},{9,11},{10,... | collective-permute-start | bytes 638984 | tf_op jit(solution)/shard_map/ppermute | solution.py:69
  48.3 3.6 %collective-permute-start.6 = (bf16[208,512]{1,0:T(8,128)(2,1)}, bf16[208,512]{1,0:T(8,128)(2,1)S(1)}, u32[]{:S(2)}, u32[]{:S(2)}) collective-permute-start(bf16[208,512]{1,0:T(8,128)(2,1)} %pad_maximum_fusion.4), channel_id=1, source_target_pairs={{0,1},{1,2},{2,3},{3,4},{4,5},{5,6},{6,7},{7,0},{8,9},{9,10},{10,1... | collective-permute-start | bytes 638984 | tf_op jit(solution)/shard_map/ppermute | solution.py:69
  55.7 5.8 %collective-permute-done.5 = bf16[208,512]{1,0:T(8,128)(2,1)S(1)} collective-permute-done((bf16[208,512]{1,0:T(8,128)(2,1)}, bf16[208,512]{1,0:T(8,128)(2,1)S(1)}, u32[]{:S(2)}, u32[]{:S(2)}) %collective-permute-start.5) | collective-permute-done | bytes 213024 | tf_op jit(solution)/shard_map/ppermute | solution.py:69
  75.9 3.5 %collective-permute-start.8 = (bf16[192,15]{1,0:T(8,128)(2,1)}, bf16[192,15]{1,0:T(8,128)(2,1)}, u32[]{:S(2)}, u32[]{:S(2)}) collective-permute-start(bf16[192,15]{1,0:T(8,128)(2,1)} %get-tuple-element.57), channel_id=1, source_target_pairs={{8,0},{16,8},{24,16},{32,24},{40,32},{48,40},{56,48},{64,56},{72,6... | collective-permute-start | bytes 17288 | tf_op jit(solution)/shard_map/ppermute | solution.py:17
  85.9 6.5 %fusion.33 = (f32[192]{0:T(256)}, f32[192]{0:T(256)}, f32[192]{0:T(256)}, f32[192]{0:T(256)}, f32[192]{0:T(256)}, /*index=5*/f32[192]{0:T(256)}, f32[192]{0:T(25...) fusion(f32[192,542]{1,0:T(8,128)S(1)} %maximum_convert_fusion, ...), kind=kLoop, calls=%fused_computation.71 | loop fusion | flops 10613376 | bytes 13013760 | tf_op jit(solution)/shard_map/reduce_sum | solution.py:131
  95.1 3.8 %collective-permute-start.9 = (bf16[192,15]{1,0:T(8,128)(2,1)S(1)}, bf16[192,15]{1,0:T(8,128)(2,1)S(1)}, u32[]{:S(2)}, u32[]{:S(2)}) collective-permute-start(bf16[192,15]{1,0:T(8,128)(2,1)S(1)} %get-tuple-element.54), channel_id=1, source_target_pairs={{0,8},{8,16},{16,24},{24,32},{32,40},{40,48},{48,56},{56,64},{64,7... | collective-permute-start | bytes 17288 | tf_op jit(solution)/shard_map/ppermute | solution.py:15
  104.5 5.5 %multiply_convert_fusion.5 = (bf16[192,512]{1,0:T(8,128)(2,1)S(1)}, f32[192,512]{1,0:T(8,128)S(1)}) fusion(f32[384,512]{1,0:T(8,128)} %copy-done.1, f32[192,542]{1,0:T(8,128)S(1)} %maximum_convert_fusion.1, f32[192]{0:T(256)} %bitcast.131, f32[192]{0:T(256)} %bitcast.169, f32[192]{0:T(256)} %bitcast.187, f32[192]{0:T(256)} %bitcast.185, f32[192]{0:T(256)} %bitcast.183, ...), kind=kLoop, calls=%fused_computation.149 | loop fusion | flops 6488064 | bytes 13196544 | tf_op jit(solution)/shard_map/convert_element_type | solution.py:133
  121.1 13.4 %all-to-all-start.1 = ((f32[64,1,9312]{2,1,0:T(1,128)}), f32[64,1,9312]{2,1,0:T(1,128)}, u32[]{:S(2)}, u32[]{:S(2)}) async-start(f32[64,1,9312]{2,1,0:T(1,128)} %all_to_all.16), calls=%async_computation.1 | async-start | bytes 4784128 | tf_op jit(solution)/shard_map/all_to_all | solution.py:151
  139.2 4.3 %collective-permute-start.17 = (bf16[192,512]{1,0:T(8,128)(2,1)}, bf16[192,512]{1,0:T(8,128)(2,1)}, u32[]{:S(2)}, u32[]{:S(2)}) collective-permute-start(bf16[192,512]{1,0:T(8,128)(2,1)} %get-tuple-element.48), channel_id=1, source_target_pairs={{0,7},{1,0},{2,1},{3,2},{4,3},{5,4},{6,5},{7,6},{8,15},{9,8},{10,9... | collective-permute-start | bytes 589832 | tf_op jit(solution)/shard_map/ppermute | solution.py:80
  143.5 3.5 %collective-permute-start.16 = (bf16[192,512]{1,0:T(8,128)(2,1)}, bf16[192,512]{1,0:T(8,128)(2,1)}, u32[]{:S(2)}, u32[]{:S(2)}) collective-permute-start(bf16[192,512]{1,0:T(8,128)(2,1)} %get-tuple-element.49), channel_id=1, source_target_pairs={{0,6},{1,7},{2,0},{3,1},{4,2},{5,3},{6,4},{7,5},{8,14},{9,15},{10,... | collective-permute-start | bytes 589832 | tf_op jit(solution)/shard_map/ppermute | solution.py:80
  147.0 3.9 %collective-permute-start.15 = (bf16[192,512]{1,0:T(8,128)(2,1)}, bf16[192,512]{1,0:T(8,128)(2,1)S(1)}, u32[]{:S(2)}, u32[]{:S(2)}) collective-permute-start(bf16[192,512]{1,0:T(8,128)(2,1)} %get-tuple-element.50), channel_id=1, source_target_pairs={{0,5},{1,6},{2,7},{3,0},{4,1},{5,2},{6,3},{7,4},{8,13},{9,14},{10,... | collective-permute-start | bytes 589832 | tf_op jit(solution)/shard_map/ppermute | solution.py:80
  150.9 4.5 %collective-permute-start.14 = (bf16[192,512]{1,0:T(8,128)(2,1)}, bf16[192,512]{1,0:T(8,128)(2,1)S(1)}, u32[]{:S(2)}, u32[]{:S(2)}) collective-permute-start(bf16[192,512]{1,0:T(8,128)(2,1)} %get-tuple-element.51), channel_id=1, source_target_pairs={{0,4},{1,5},{2,6},{3,7},{4,0},{5,1},{6,2},{7,3},{8,12},{9,13},{10,... | collective-permute-start | bytes 589832 | tf_op jit(solution)/shard_map/ppermute | solution.py:80
  158.0 3.9 %collective-permute-start.12 = (bf16[192,512]{1,0:T(8,128)(2,1)}, bf16[192,512]{1,0:T(8,128)(2,1)S(1)}, u32[]{:S(2)}, u32[]{:S(2)}) collective-permute-start(bf16[192,512]{1,0:T(8,128)(2,1)} %get-tuple-element.53), channel_id=1, source_target_pairs={{0,2},{1,3},{2,4},{3,5},{4,6},{5,7},{6,0},{7,1},{8,10},{9,11},{10,... | collective-permute-start | bytes 589832 | tf_op jit(solution)/shard_map/ppermute | solution.py:80
  161.9 3.4 %collective-permute-start.11 = (bf16[192,512]{1,0:T(8,128)(2,1)}, bf16[192,512]{1,0:T(8,128)(2,1)S(1)}, u32[]{:S(2)}, u32[]{:S(2)}) collective-permute-start(bf16[192,512]{1,0:T(8,128)(2,1)} %get-tuple-element.47), channel_id=1, source_target_pairs={{0,1},{1,2},{2,3},{3,4},{4,5},{5,6},{6,7},{7,0},{8,9},{9,10},{10,1... | collective-permute-start | bytes 589832 | tf_op jit(solution)/shard_map/ppermute | solution.py:80
  167.6 3.4 %collective-permute-done.14 = bf16[192,512]{1,0:T(8,128)(2,1)S(1)} collective-permute-done((bf16[192,512]{1,0:T(8,128)(2,1)}, bf16[192,512]{1,0:T(8,128)(2,1)S(1)}, u32[]{:S(2)}, u32[]{:S(2)}) %collective-permute-start.14) | collective-permute-done | bytes 196640 | tf_op jit(solution)/shard_map/ppermute | solution.py:80
  171.0 9.3 %collective-permute-done.13 = bf16[192,512]{1,0:T(8,128)(2,1)S(1)} collective-permute-done((bf16[192,512]{1,0:T(8,128)(2,1)}, bf16[192,512]{1,0:T(8,128)(2,1)S(1)}, u32[]{:S(2)}, u32[]{:S(2)}) %collective-permute-start.13) | collective-permute-done | bytes 196640 | tf_op jit(solution)/shard_map/ppermute | solution.py:80
  183.1 9.1 %collective-permute-done.11 = bf16[192,512]{1,0:T(8,128)(2,1)S(1)} collective-permute-done((bf16[192,512]{1,0:T(8,128)(2,1)}, bf16[192,512]{1,0:T(8,128)(2,1)S(1)}, u32[]{:S(2)}, u32[]{:S(2)}) %collective-permute-start.11) | collective-permute-done | bytes 196640 | tf_op jit(solution)/shard_map/ppermute | solution.py:80
  194.2 10.9 %psum.7 = f32[2,512]{1,0:T(2,128)S(1)} all-reduce(f32[2,512]{1,0:T(2,128)S(1)} %pad_maximum_fusion.6), channel_id=1, replica_groups=mesh['seq'=64,'ch'=8] {'ch'}, use_global_device_ids=true, to_apply=%region_4.5 | all-reduce | flops 1024 | bytes 8192 | tf_op jit(solution)/shard_map/psum | solution.py:166
  205.9 3.1 %reduce_sum.377 = f32[9312]{0:T(1024)S(1)} reduce(f32[64,1,9312]{2,1,0:T(1,128)} %all-to-all-done.1, f32[]{:T(128)} %constant.95.clone.1), dimensions={0,1}, to_apply=%region_36.37 | reduce | flops 586656 | bytes 2421124 | tf_op jit(solution)/shard_map/reduce_sum | solution.py:151
  210.5 14.3 %all-to-all-start.2 = ((f32[64,1,288]{2,1,0:T(1,128)}), f32[64,1,288]{2,1,0:T(1,128)S(1)}, u32[]{:S(2)}, u32[]{:S(2)}) async-start(f32[64,1,288]{2,1,0:T(1,128)} %broadcast_in_dim.5), calls=%async_computation.2 | async-start | bytes 196608 | tf_op jit(solution)/shard_map/all_to_all | solution.py:50
  225.5 9.9 %all-to-all-done.2 = f32[64,1,288]{2,1,0:T(1,128)S(1)} async-done(((f32[64,1,288]{2,1,0:T(1,128)}), f32[64,1,288]{2,1,0:T(1,128)S(1)}, u32[]{:S(2)}, u32[]{:S(2)}) %all-to-all-start.2) | async-done | bytes 73760 | tf_op jit(solution)/shard_map/all_to_all | solution.py:50
  (133 shorter events, 75.9 us)
Async XLA Ops:
  0.6 42.3 %copy-start.11 = (f32[31,192]{1,0:T(8,128)S(1)}, f32[31,192]{1,0:T(8,128)}, u32[]{:S(2)}) copy-start(f32[31,192]{1,0:T(8,128)} %param.10) | copy-start | bytes 71428
  3.1 41.2 %collective-permute-start = (bf16[208,512]{1,0:T(8,128)(2,1)}, bf16[208,512]{1,0:T(8,128)(2,1)}, u32[]{:S(2)}, u32[]{:S(2)}) collective-permute-start(bf16[208,512]{1,0:T(8,128)(2,1)} %pad_maximum_fusion.4), channel_id=1, source_target_pairs={{0,7},{1,0},{2,1},{3,2},{4,3},{5,4},{6,5},{7,6},{8,15},{9,8},{10,9... | collective-permute-start | bytes 638984 | tf_op jit(solution)/shard_map/ppermute | solution.py:69
  14.6 33.7 %collective-permute-start.1 = (bf16[208,512]{1,0:T(8,128)(2,1)}, bf16[208,512]{1,0:T(8,128)(2,1)}, u32[]{:S(2)}, u32[]{:S(2)}) collective-permute-start(bf16[208,512]{1,0:T(8,128)(2,1)} %pad_maximum_fusion.4), channel_id=1, source_target_pairs={{0,6},{1,7},{2,0},{3,1},{4,2},{5,3},{6,4},{7,5},{8,14},{9,15},{10,... | collective-permute-start | bytes 638984 | tf_op jit(solution)/shard_map/ppermute | solution.py:69
  16.7 36.1 %collective-permute-start.2 = (bf16[208,512]{1,0:T(8,128)(2,1)}, bf16[208,512]{1,0:T(8,128)(2,1)}, u32[]{:S(2)}, u32[]{:S(2)}) collective-permute-start(bf16[208,512]{1,0:T(8,128)(2,1)} %pad_maximum_fusion.4), channel_id=1, source_target_pairs={{0,5},{1,6},{2,7},{3,0},{4,1},{5,2},{6,3},{7,4},{8,13},{9,14},{10,... | collective-permute-start | bytes 638984 | tf_op jit(solution)/shard_map/ppermute | solution.py:69
  18.7 35.2 %collective-permute-start.3 = (bf16[208,512]{1,0:T(8,128)(2,1)}, bf16[208,512]{1,0:T(8,128)(2,1)}, u32[]{:S(2)}, u32[]{:S(2)}) collective-permute-start(bf16[208,512]{1,0:T(8,128)(2,1)} %pad_maximum_fusion.4), channel_id=1, source_target_pairs={{0,4},{1,5},{2,6},{3,7},{4,0},{5,1},{6,2},{7,3},{8,12},{9,13},{10,... | collective-permute-start | bytes 638984 | tf_op jit(solution)/shard_map/ppermute | solution.py:69
  26.0 28.8 %collective-permute-start.4 = (bf16[208,512]{1,0:T(8,128)(2,1)}, bf16[208,512]{1,0:T(8,128)(2,1)}, u32[]{:S(2)}, u32[]{:S(2)}) collective-permute-start(bf16[208,512]{1,0:T(8,128)(2,1)} %pad_maximum_fusion.4), channel_id=1, source_target_pairs={{0,3},{1,4},{2,5},{3,6},{4,7},{5,0},{6,1},{7,2},{8,11},{9,12},{10,... | collective-permute-start | bytes 638984 | tf_op jit(solution)/shard_map/ppermute | solution.py:69
  29.8 42.6 %all-to-all-start = ((bf16[64,24,384]{2,1,0:T(8,128)(2,1)}), bf16[64,24,384]{2,1,0:T(8,128)(2,1)}, u32[]{:S(2)}, u32[]{:S(2)}) async-start(bf16[64,24,384]{2,1,0:T(8,128)(2,1)} %broadcast_in_dim.4), calls=%async_computation | async-start | bytes 2359296 | tf_op jit(solution)/shard_map/all_to_all | solution.py:50
  44.2 17.4 %collective-permute-start.5 = (bf16[208,512]{1,0:T(8,128)(2,1)}, bf16[208,512]{1,0:T(8,128)(2,1)S(1)}, u32[]{:S(2)}, u32[]{:S(2)}) collective-permute-start(bf16[208,512]{1,0:T(8,128)(2,1)} %pad_maximum_fusion.4), channel_id=1, source_target_pairs={{0,2},{1,3},{2,4},{3,5},{4,6},{5,7},{6,0},{7,1},{8,10},{9,11},{10,... | collective-permute-start | bytes 638984 | tf_op jit(solution)/shard_map/ppermute | solution.py:69
  48.3 15.7 %collective-permute-start.6 = (bf16[208,512]{1,0:T(8,128)(2,1)}, bf16[208,512]{1,0:T(8,128)(2,1)S(1)}, u32[]{:S(2)}, u32[]{:S(2)}) collective-permute-start(bf16[208,512]{1,0:T(8,128)(2,1)} %pad_maximum_fusion.4), channel_id=1, source_target_pairs={{0,1},{1,2},{2,3},{3,4},{4,5},{5,6},{6,7},{7,0},{8,9},{9,10},{10,1... | collective-permute-start | bytes 638984 | tf_op jit(solution)/shard_map/ppermute | solution.py:69
  75.9 9.1 %collective-permute-start.8 = (bf16[192,15]{1,0:T(8,128)(2,1)}, bf16[192,15]{1,0:T(8,128)(2,1)}, u32[]{:S(2)}, u32[]{:S(2)}) collective-permute-start(bf16[192,15]{1,0:T(8,128)(2,1)} %get-tuple-element.57), channel_id=1, source_target_pairs={{8,0},{16,8},{24,16},{32,24},{40,32},{48,40},{56,48},{64,56},{72,6... | collective-permute-start | bytes 17288 | tf_op jit(solution)/shard_map/ppermute | solution.py:17
  79.4 5.6 %collective-permute-start.7 = (bf16[192,15]{1,0:T(8,128)(2,1)}, bf16[192,15]{1,0:T(8,128)(2,1)}, u32[]{:S(2)}, u32[]{:S(2)}) collective-permute-start(bf16[192,15]{1,0:T(8,128)(2,1)} %get-tuple-element.56), channel_id=1, source_target_pairs={{0,8},{8,16},{16,24},{24,32},{32,40},{40,48},{48,56},{56,64},{64,7... | collective-permute-start | bytes 17288 | tf_op jit(solution)/shard_map/ppermute | solution.py:15
  93.1 11.2 %collective-permute-start.10 = (bf16[192,15]{1,0:T(8,128)(2,1)}, bf16[192,15]{1,0:T(8,128)(2,1)S(1)}, u32[]{:S(2)}, u32[]{:S(2)}) collective-permute-start(bf16[192,15]{1,0:T(8,128)(2,1)} %get-tuple-element.55), channel_id=1, source_target_pairs={{8,0},{16,8},{24,16},{32,24},{40,32},{48,40},{56,48},{64,56},{72,6... | collective-permute-start | bytes 17288 | tf_op jit(solution)/shard_map/ppermute | solution.py:17
  95.1 9.3 %collective-permute-start.9 = (bf16[192,15]{1,0:T(8,128)(2,1)S(1)}, bf16[192,15]{1,0:T(8,128)(2,1)S(1)}, u32[]{:S(2)}, u32[]{:S(2)}) collective-permute-start(bf16[192,15]{1,0:T(8,128)(2,1)S(1)} %get-tuple-element.54), channel_id=1, source_target_pairs={{0,8},{8,16},{16,24},{24,32},{32,40},{40,48},{48,56},{56,64},{64,7... | collective-permute-start | bytes 17288 | tf_op jit(solution)/shard_map/ppermute | solution.py:15
  121.1 84.9 %all-to-all-start.1 = ((f32[64,1,9312]{2,1,0:T(1,128)}), f32[64,1,9312]{2,1,0:T(1,128)}, u32[]{:S(2)}, u32[]{:S(2)}) async-start(f32[64,1,9312]{2,1,0:T(1,128)} %all_to_all.16), calls=%async_computation.1 | async-start | bytes 4784128 | tf_op jit(solution)/shard_map/all_to_all | solution.py:151
  134.6 57.6 %copy-start.12 = (f32[192]{0:T(256)S(1)}, f32[192]{0:T(256)}, u32[]{:S(2)}) copy-start(f32[192]{0:T(256)} %param.7) | copy-start | bytes 2308
  136.9 68.2 %copy-start.10 = (f32[512]{0:T(512)S(1)}, f32[512]{0:T(512)}, u32[]{:S(2)}) copy-start(f32[512]{0:T(512)} %copy-done.9) | copy-start | bytes 6148
  139.2 18.9 %collective-permute-start.17 = (bf16[192,512]{1,0:T(8,128)(2,1)}, bf16[192,512]{1,0:T(8,128)(2,1)}, u32[]{:S(2)}, u32[]{:S(2)}) collective-permute-start(bf16[192,512]{1,0:T(8,128)(2,1)} %get-tuple-element.48), channel_id=1, source_target_pairs={{0,7},{1,0},{2,1},{3,2},{4,3},{5,4},{6,5},{7,6},{8,15},{9,8},{10,9... | collective-permute-start | bytes 589832 | tf_op jit(solution)/shard_map/ppermute | solution.py:80
  143.5 18.4 %collective-permute-start.16 = (bf16[192,512]{1,0:T(8,128)(2,1)}, bf16[192,512]{1,0:T(8,128)(2,1)}, u32[]{:S(2)}, u32[]{:S(2)}) collective-permute-start(bf16[192,512]{1,0:T(8,128)(2,1)} %get-tuple-element.49), channel_id=1, source_target_pairs={{0,6},{1,7},{2,0},{3,1},{4,2},{5,3},{6,4},{7,5},{8,14},{9,15},{10,... | collective-permute-start | bytes 589832 | tf_op jit(solution)/shard_map/ppermute | solution.py:80
  147.0 20.7 %collective-permute-start.15 = (bf16[192,512]{1,0:T(8,128)(2,1)}, bf16[192,512]{1,0:T(8,128)(2,1)S(1)}, u32[]{:S(2)}, u32[]{:S(2)}) collective-permute-start(bf16[192,512]{1,0:T(8,128)(2,1)} %get-tuple-element.50), channel_id=1, source_target_pairs={{0,5},{1,6},{2,7},{3,0},{4,1},{5,2},{6,3},{7,4},{8,13},{9,14},{10,... | collective-permute-start | bytes 589832 | tf_op jit(solution)/shard_map/ppermute | solution.py:80
  150.9 20.1 %collective-permute-start.14 = (bf16[192,512]{1,0:T(8,128)(2,1)}, bf16[192,512]{1,0:T(8,128)(2,1)S(1)}, u32[]{:S(2)}, u32[]{:S(2)}) collective-permute-start(bf16[192,512]{1,0:T(8,128)(2,1)} %get-tuple-element.51), channel_id=1, source_target_pairs={{0,4},{1,5},{2,6},{3,7},{4,0},{5,1},{6,2},{7,3},{8,12},{9,13},{10,... | collective-permute-start | bytes 589832 | tf_op jit(solution)/shard_map/ppermute | solution.py:80
  155.4 25.0 %collective-permute-start.13 = (bf16[192,512]{1,0:T(8,128)(2,1)}, bf16[192,512]{1,0:T(8,128)(2,1)S(1)}, u32[]{:S(2)}, u32[]{:S(2)}) collective-permute-start(bf16[192,512]{1,0:T(8,128)(2,1)} %get-tuple-element.52), channel_id=1, source_target_pairs={{0,3},{1,4},{2,5},{3,6},{4,7},{5,0},{6,1},{7,2},{8,11},{9,12},{10,... | collective-permute-start | bytes 589832 | tf_op jit(solution)/shard_map/ppermute | solution.py:80
  158.0 25.1 %collective-permute-start.12 = (bf16[192,512]{1,0:T(8,128)(2,1)}, bf16[192,512]{1,0:T(8,128)(2,1)S(1)}, u32[]{:S(2)}, u32[]{:S(2)}) collective-permute-start(bf16[192,512]{1,0:T(8,128)(2,1)} %get-tuple-element.53), channel_id=1, source_target_pairs={{0,2},{1,3},{2,4},{3,5},{4,6},{5,7},{6,0},{7,1},{8,10},{9,11},{10,... | collective-permute-start | bytes 589832 | tf_op jit(solution)/shard_map/ppermute | solution.py:80
  161.9 30.3 %collective-permute-start.11 = (bf16[192,512]{1,0:T(8,128)(2,1)}, bf16[192,512]{1,0:T(8,128)(2,1)S(1)}, u32[]{:S(2)}, u32[]{:S(2)}) collective-permute-start(bf16[192,512]{1,0:T(8,128)(2,1)} %get-tuple-element.47), channel_id=1, source_target_pairs={{0,1},{1,2},{2,3},{3,4},{4,5},{5,6},{6,7},{7,0},{8,9},{9,10},{10,1... | collective-permute-start | bytes 589832 | tf_op jit(solution)/shard_map/ppermute | solution.py:80
  210.5 24.8 %all-to-all-start.2 = ((f32[64,1,288]{2,1,0:T(1,128)}), f32[64,1,288]{2,1,0:T(1,128)S(1)}, u32[]{:S(2)}, u32[]{:S(2)}) async-start(f32[64,1,288]{2,1,0:T(1,128)} %broadcast_in_dim.5), calls=%async_computation.2 | async-start | bytes 196608 | tf_op jit(solution)/shard_map/all_to_all | solution.py:50
  (18 other events, 145.9 us)

commit v6 on v5

--- a/solution.py
+++ b/solution.py
@@ -71,15 +71,19 @@
     return jnp.roll(jnp.stack(pieces, 0), position, axis=0)
 
 
-def reduce_by_shifts(blocks, axis):
+def reduce_by_shifts(blocks, rider, axis):
     count = lax.axis_size(axis)
     position = lax.axis_index(axis)
     total = lax.dynamic_index_in_dim(blocks, position, 0, keepdims=False).astype(jnp.float32)
+    riders = rider.astype(jnp.float32)
+    rows = blocks.shape[1]
     for shift in range(1, count):
         outgoing = lax.dynamic_index_in_dim(blocks, (position + shift) % count, 0, keepdims=False)
+        outgoing = jnp.concatenate([outgoing, rider], 0)
         arrived = lax.ppermute(outgoing, axis, [(i, (i + shift) % count) for i in range(count)])
-        total = total + arrived.astype(jnp.float32)
-    return total
+        total = total + arrived[:rows].astype(jnp.float32)
+        riders = riders + arrived[rows:].astype(jnp.float32)
+    return total, riders
 
 
 def shifted_sum(padded, taps, span):
@@ -97,7 +101,7 @@
     reach = depth_taps.shape[0] // 2
     gain_rows = jnp.stack(bf16_pieces(input_norm_gain, 3), 0)
     gain_rows = jnp.pad(gain_rows, ((0, 13), (0, frames - local_cols)))
-    arrived = gather_by_shifts(jnp.concatenate([signal, gain_rows], 0), "ch")
+    arrived = lax.all_gather(jnp.concatenate([signal, gain_rows], 0), "ch", axis=0)
     complete_signal = arrived[:, :local_cols].reshape(groups * local_cols, frames)
     gain_parts = arrived[:, local_cols : local_cols + 3, :local_cols].astype(jnp.float32)
     complete_gain = ((gain_parts[:, 0] + gain_parts[:, 1]) + gain_parts[:, 2]).reshape(-1)
@@ -152,18 +156,18 @@
     weight_sums = summed[: rows * width].reshape(rows, width)
     grad_value = weight_sums[:, :local_cols]
     grad_gate = weight_sums[:, local_cols:]
-    normalized_gradient = reduce_by_shifts(
-        normed_term.reshape(groups, local_cols, frames), "ch"
+    normed_f = normed_term.astype(jnp.float32)
+    weighted = normed_f * complete_gain[:, None]
+    own_moments = jnp.stack([jnp.sum(weighted, 0), jnp.sum(weighted * centered_unit, 0)], 0)
+    moment_rows = jnp.concatenate(bf16_pieces(own_moments, 3), 0)
+    moment_rows = jnp.pad(moment_rows, ((0, 16 - moment_rows.shape[0]), (0, 0)))
+    normalized_gradient, moment_total = reduce_by_shifts(
+        normed_term.reshape(groups, local_cols, frames), moment_rows, "ch"
     )
     scaled_signal = normalized_gradient * input_norm_gain[:, None]
-    moments = jnp.stack(
-        [
-            jnp.sum(scaled_signal, 0),
-            jnp.sum(scaled_signal * centered_unit_rows, 0),
-        ],
-        0,
-    )
-    moments = lax.psum(moments, "ch") * (1.0 / complete_signal.shape[0])
+    moments = ((moment_total[0:2] + moment_total[2:4]) + moment_total[4:6]) * (
+        1.0 / complete_signal.shape[0]
+    )
     signal_gradient = (
         inverse_deviation
         * (scaled_signal - moments[0:1] - centered_unit_rows * moments[1:2])

time: 238 us -> 213 us (0.89)
  starting transfers between devices: 109 us -> 75.2 us
  waiting for transfers between devices: 44.4 us -> 69.7 us
  local copies, waits for them, and re-layouts: 27.9 us -> 14 us
  between operations: 1.41 us -> 14.5 us
  blocking collectives: 10.9 us -> 0 us
  other arithmetic: 35.3 us -> 32.2 us
    all_gather x0 -> x1, waiting for transfers between devices: none -> 32.1 us  [shards(): lax.all_gather(jnp.concatenate([signal, gain_rows], 0), 'ch', axis=0)]
    ppermute x7 -> x0, starting transfers between devices: 31.5 us -> none  [gather_by_shifts(): lax.ppermute(block, axis, [(i, (i - shift) % count) for i in range(count)])]
    psum x1 -> x0, blocking collectives: 10.9 us -> none  [shards(): moments = lax.psum(moments, 'ch') * (1.0 / complete_signal.shape[0])]
    unnamed x57 -> x18, local copies, waits for them, and re-layouts: 11.4 us -> 2.72 us
    ppermute x7 -> x0, waiting for transfers between devices: 8.22 us -> none  [gather_by_shifts(): lax.ppermute(block, axis, [(i, (i - shift) % count) for i in range(count)])]
    ppermute x2, waiting for transfers between devices: 0.01 us -> 3.39 us  [extended(): lax.ppermute(head, axis, [((i + 1) % count, i) for i in range(ends)])]
    all_to_all x2, starting transfers between devices: 26.3 us -> 23.1 us  [gather_by_exchange(): return lax.all_to_all(copies, axis, 0, 0, tiled=False)]
    ppermute x2, starting transfers between devices: 6.82 us -> 9.54 us  [extended(): lax.ppermute(tail, axis, [(i, (i + 1) % count) for i in range(ends)])]
  transfers between devices with their start and end apart: 21 -> 15, of which waited for: 9 -> 8; matrix products, arithmetic and copies ran while one was open for 14% -> 10% of each run, Pallas kernels for 0% -> 0%
where the time goes in v6:
time: 213 us; the launch traced here: 212 us
  starting transfers between devices  75.2 us (35%)
  waiting for transfers between devices  69.7 us (33%)
  other arithmetic  32.2 us (15%)
  between operations  14.5 us (7%)
  local copies, waits for them, and re-layouts  14 us (7%)
  matrix products  6.16 us (3%)
    all_gather x1, waiting for transfers between devices, shards(): lax.all_gather(jnp.concatenate([signal, gain_rows], 0), 'ch', axis=0)  32.1 us
    ppermute x7, waiting for transfers between devices, reduce_by_shifts(): lax.ppermute(outgoing, axis, [(i, (i + shift) % count) for i in range(cou...  24.3 us
    ppermute x7, starting transfers between devices, reduce_by_shifts(): lax.ppermute(outgoing, axis, [(i, (i + shift) % count) for i in range(cou...  23.9 us
    all_to_all x2, starting transfers between devices, gather_by_exchange(): return lax.all_to_all(copies, axis, 0, 0, tiled=False)  23.1 us
    all_to_all x1, starting transfers between devices, shards(): summed = jnp.sum(lax.all_to_all(outgoing, 'seq', 0, 0, tiled=False), 0)  14.1 us
    all_to_all x2, waiting for transfers between devices, gather_by_exchange(): return lax.all_to_all(copies, axis, 0, 0, tiled=False)  9.88 us
    ppermute x2, starting transfers between devices, extended(): lax.ppermute(tail, axis, [(i, (i + 1) % count) for i in range(ends)])  9.54 us
    reduce_sum x2, other arithmetic, shards(): jnp.sum(glued_pad[:, k:k + span] * grad_pre_f, 1)  7.95 us
  transfers between devices with their start and end apart: 15, of which 8 were waited for; matrix products, arithmetic and copies ran while one was open for 10% of the time, Pallas kernels for 0%

profile of v6, /device:TPU:1, one launch (start us, length us, event | category | flops | bytes accessed | tf_op | source)
XLA Modules:
  0.0 211.8 jit_solution(1128467306315349419)
XLA Ops:
  11.6 11.6 %all-to-all-start = ((bf16[64,24,384]{2,1,0:T(8,128)(2,1)}), bf16[64,24,384]{2,1,0:T(8,128)(2,1)S(1)}, u32[]{:S(2)}, u32[]{:S(2)}) async-start(bf16[64,24,384]{2,1,0:T(8,128)(2,1)} %broadcast_in_dim.4), calls=%async_computation | async-start | bytes 2359296 | tf_op jit(solution)/shard_map/all_to_all | solution.py:50
  23.3 32.1 %all-gather.3.cloned.1.call-done = bf16[1664,512]{1,0:T(8,128)(2,1)} async-done(((bf16[208,512]{1,0:T(8,128)(2,1)}), bf16[1664,512]{1,0:T(8,128)(2,1)}) %all-gather.3.cloned.1.call-update) | async-done | bytes 1703952 | tf_op jit(solution)/shard_map/all_gather | solution.py:104
  62.6 2.6 %fusion.104 = f32[384,512]{1,0:T(8,128)S(1)} fusion(bf16[1536,384]{1,0:T(8,128)(2,1)} %bitcast.109, bf16[1536,512]{1,0:T(8,128)(2,1)} %bitcast.108), kind=kOutput, calls=%fused_computation.223 | convolution fusion | flops 603979776 | bytes 3538944 | tf_op jit(solution)/shard_map/dot_general | solution.py:115
  65.4 7.6 %collective-permute-start = (bf16[192,15]{1,0:T(8,128)(2,1)S(1)}, bf16[192,15]{1,0:T(8,128)(2,1)S(1)}, u32[]{:S(2)}, u32[]{:S(2)}) collective-permute-start(bf16[192,15]{1,0:T(8,128)(2,1)S(1)} %get-tuple-element.57), channel_id=1, source_target_pairs={{0,8},{8,16},{16,24},{24,32},{32,40},{40,48},{48,56},{56,64},{64,7... | collective-permute-start | bytes 17288 | tf_op jit(solution)/shard_map/ppermute | solution.py:15
  73.0 1.9 collective-permute-start.1
  75.0 3.4 %collective-permute-done.1 = bf16[192,15]{1,0:T(8,128)(2,1)S(1)} collective-permute-done((bf16[192,15]{1,0:T(8,128)(2,1)S(1)}, bf16[192,15]{1,0:T(8,128)(2,1)S(1)}, u32[]{:S(2)}, u32[]{:S(2)}) %collective-permute-start.1) | collective-permute-done | bytes 5792 | tf_op jit(solution)/shard_map/ppermute | solution.py:17
  78.6 5.4 %fusion.34 = (f32[192]{0:T(256)S(1)}, f32[192]{0:T(256)S(1)}, f32[192]{0:T(256)S(1)}, f32[192]{0:T(256)S(1)}, f32[192]{0:T(256)S(1)}, /*index=5*/f32[192]{0:T(25...) fusion(f32[192,542]{1,0:T(8,128)S(1)} %maximum_convert_fusion, ...), kind=kLoop, calls=%fused_computation.81 | loop fusion | flops 10613376 | bytes 13013760 | tf_op jit(solution)/shard_map/reduce_sum | solution.py:135
  86.0 2.6 %collective-permute-start.3 = (bf16[192,15]{1,0:T(8,128)(2,1)S(1)}, bf16[192,15]{1,0:T(8,128)(2,1)S(1)}, u32[]{:S(2)}, u32[]{:S(2)}) collective-permute-start(bf16[192,15]{1,0:T(8,128)(2,1)S(1)} %get-tuple-element.56), channel_id=1, source_target_pairs={{8,0},{16,8},{24,16},{32,24},{40,32},{48,40},{56,48},{64,56},{72,6... | collective-permute-start | bytes 17288 | tf_op jit(solution)/shard_map/ppermute | solution.py:17
  88.6 2.5 %fusion.33 = (f32[192]{0:T(256)S(1)}, f32[192]{0:T(256)S(1)}, f32[192]{0:T(256)S(1)}, f32[192]{0:T(256)S(1)}, f32[192]{0:T(256)S(1)}, /*index=5*/f32[192]{0:T(25...) fusion(bf16[192,512]{1,0:T(8,128)(2,1)S(1)} %get-tuple-element., ...), kind=kLoop, calls=%fused_computation.80 | loop fusion | flops 2651712 | bytes 5318400 | tf_op jit(solution)/shard_map/reduce_sum | solution.py:135
  92.9 4.4 %multiply_convert_fusion.5 = (bf16[192,512]{1,0:T(8,128)(2,1)S(1)}, f32[192,512]{1,0:T(8,128)S(1)}) fusion(f32[384,512]{1,0:T(8,128)S(1)} %fusion.104, f32[192,542]{1,0:T(8,128)S(1)} %maximum_convert_fusion.1, f32[192]{0:T(256)S(1)} %bitcast.117, f32[192]{0:T(256)S(1)} %bitcast.155, f32[192]{0:T(256)S(1)} %bitcast.173, f32[192]{0:T(256)S(1)} %bitcast.171, ...), kind=kLoop, calls=%fused_computation.158 | loop fusion | flops 6488064 | bytes 13196544 | tf_op jit(solution)/shard_map/convert_element_type | solution.py:137
  97.6 2.5 %fusion.1 = (f32[512]{0:T(512)S(1)}, f32[512]{0:T(512)S(1)}, f32[1536,512]{1,0:T(8,128)S(1)}, bf16[1536,512]{1,0:T(8,128)(2,1)}) fusion(f32[1536]{0:T(1024)S(1)} %add.421, f32[512]{0:T(512)S(1)} %add_rsqrt_fusion, f32[512]{0:T(512)S(1)} %broadcast_multiply_fusion, bf16[8,208,512]{2,1,0:T(8,128)(2,1)S(1)} %bitcast.107, bf16[1536,384]{1,0:T(8,128)(2,1)S(1)} %bitcast.110, ...), kind=kOutput, calls=%fused_computation.36 | convolution fusion | flops 611843072 | bytes 7878656 | tf_op jit(solution)/shard_map/dot_general | solution.py:146
  106.3 3.1 %all_to_all.16 = f32[64,1,9312]{2,1,0:T(1,128)} reshape(f32[64,9312]{1,0:T(8,128)S(1)} %pad_maximum_fusion) | data formatting | bytes 4767744 | tf_op jit(solution)/shard_map/all_to_all | solution.py:155
  109.3 14.1 %all-to-all-start.1 = ((f32[64,1,9312]{2,1,0:T(1,128)}), f32[64,1,9312]{2,1,0:T(1,128)S(1)}, u32[]{:S(2)}, u32[]{:S(2)}) async-start(f32[64,1,9312]{2,1,0:T(1,128)} %all_to_all.16), calls=%async_computation.1 | async-start | bytes 4784128 | tf_op jit(solution)/shard_map/all_to_all | solution.py:155
  126.2 2.7 %collective-permute-start.4 = (bf16[208,512]{1,0:T(8,128)(2,1)}, bf16[208,512]{1,0:T(8,128)(2,1)S(1)}, u32[]{:S(2)}, u32[]{:S(2)}) collective-permute-start(bf16[208,512]{1,0:T(8,128)(2,1)} %get-tuple-element.92), channel_id=1, source_target_pairs={{0,1},{1,2},{2,3},{3,4},{4,5},{5,6},{6,7},{7,0},{8,9},{9,10},{10,1... | collective-permute-start | bytes 638984 | tf_op jit(solution)/shard_map/ppermute | solution.py:83
  128.9 4.0 %collective-permute-start.6 = (bf16[208,512]{1,0:T(8,128)(2,1)}, bf16[208,512]{1,0:T(8,128)(2,1)}, u32[]{:S(2)}, u32[]{:S(2)}) collective-permute-start(bf16[208,512]{1,0:T(8,128)(2,1)} %get-tuple-element.93), channel_id=1, source_target_pairs={{0,3},{1,4},{2,5},{3,6},{4,7},{5,0},{6,1},{7,2},{8,11},{9,12},{10,... | collective-permute-start | bytes 638984 | tf_op jit(solution)/shard_map/ppermute | solution.py:83
  132.9 4.6 %collective-permute-start.7 = (bf16[208,512]{1,0:T(8,128)(2,1)}, bf16[208,512]{1,0:T(8,128)(2,1)S(1)}, u32[]{:S(2)}, u32[]{:S(2)}) collective-permute-start(bf16[208,512]{1,0:T(8,128)(2,1)} %get-tuple-element.94), channel_id=1, source_target_pairs={{0,4},{1,5},{2,6},{3,7},{4,0},{5,1},{6,2},{7,3},{8,12},{9,13},{10,... | collective-permute-start | bytes 638984 | tf_op jit(solution)/shard_map/ppermute | solution.py:83
  137.6 4.4 %collective-permute-start.8 = (bf16[208,512]{1,0:T(8,128)(2,1)}, bf16[208,512]{1,0:T(8,128)(2,1)S(1)}, u32[]{:S(2)}, u32[]{:S(2)}) collective-permute-start(bf16[208,512]{1,0:T(8,128)(2,1)} %get-tuple-element.95), channel_id=1, source_target_pairs={{0,5},{1,6},{2,7},{3,0},{4,1},{5,2},{6,3},{7,4},{8,13},{9,14},{10,... | collective-permute-start | bytes 638984 | tf_op jit(solution)/shard_map/ppermute | solution.py:83
  141.9 4.3 %collective-permute-start.9 = (bf16[208,512]{1,0:T(8,128)(2,1)}, bf16[208,512]{1,0:T(8,128)(2,1)S(1)}, u32[]{:S(2)}, u32[]{:S(2)}) collective-permute-start(bf16[208,512]{1,0:T(8,128)(2,1)} %get-tuple-element.96), channel_id=1, source_target_pairs={{0,6},{1,7},{2,0},{3,1},{4,2},{5,3},{6,4},{7,5},{8,14},{9,15},{10,... | collective-permute-start | bytes 638984 | tf_op jit(solution)/shard_map/ppermute | solution.py:83
  148.2 3.2 %collective-permute-done.6 = bf16[208,512]{1,0:T(8,128)(2,1)} collective-permute-done((bf16[208,512]{1,0:T(8,128)(2,1)}, bf16[208,512]{1,0:T(8,128)(2,1)}, u32[]{:S(2)}, u32[]{:S(2)}) %collective-permute-start.6) | collective-permute-done | bytes 213024 | tf_op jit(solution)/shard_map/ppermute | solution.py:83
  155.6 6.5 %collective-permute-done.8 = bf16[208,512]{1,0:T(8,128)(2,1)S(1)} collective-permute-done((bf16[208,512]{1,0:T(8,128)(2,1)}, bf16[208,512]{1,0:T(8,128)(2,1)S(1)}, u32[]{:S(2)}, u32[]{:S(2)}) %collective-permute-start.8) | collective-permute-done | bytes 213024 | tf_op jit(solution)/shard_map/ppermute | solution.py:83
  162.2 11.0 %collective-permute-done.9 = bf16[208,512]{1,0:T(8,128)(2,1)S(1)} collective-permute-done((bf16[208,512]{1,0:T(8,128)(2,1)}, bf16[208,512]{1,0:T(8,128)(2,1)S(1)}, u32[]{:S(2)}, u32[]{:S(2)}) %collective-permute-start.9) | collective-permute-done | bytes 213024 | tf_op jit(solution)/shard_map/ppermute | solution.py:83
  173.2 2.0 collective-permute-done.10
  181.5 11.5 %all-to-all-start.2 = ((f32[64,1,288]{2,1,0:T(1,128)}), f32[64,1,288]{2,1,0:T(1,128)S(1)}, u32[]{:S(2)}, u32[]{:S(2)}) async-start(f32[64,1,288]{2,1,0:T(1,128)} %broadcast_in_dim.5), calls=%async_computation.2 | async-start | bytes 196608 | tf_op jit(solution)/shard_map/all_to_all | solution.py:50
  193.7 9.9 %all-to-all-done.2 = f32[64,1,288]{2,1,0:T(1,128)S(1)} async-done(((f32[64,1,288]{2,1,0:T(1,128)}), f32[64,1,288]{2,1,0:T(1,128)S(1)}, u32[]{:S(2)}, u32[]{:S(2)}) %all-to-all-start.2) | async-done | bytes 73760 | tf_op jit(solution)/shard_map/all_to_all | solution.py:50
  (82 shorter events, 39.1 us)
Async XLA Ops:
  7.2 16.1 %copy-start.5 = (f32[31,192]{1,0:T(8,128)S(1)}, f32[31,192]{1,0:T(8,128)}, u32[]{:S(2)}) copy-start(f32[31,192]{1,0:T(8,128)} %param.10) | copy-start | bytes 71428
  7.2 48.2 %all-gather.3.cloned.1.call-start = ((), (), s32[]{:S(2)}) async-start(), calls=%async_computation.3 | async-start | bytes 1916928 | tf_op jit(solution)/shard_map/all_gather | solution.py:104
  11.6 49.9 %all-to-all-start = ((bf16[64,24,384]{2,1,0:T(8,128)(2,1)}), bf16[64,24,384]{2,1,0:T(8,128)(2,1)S(1)}, u32[]{:S(2)}, u32[]{:S(2)}) async-start(bf16[64,24,384]{2,1,0:T(8,128)(2,1)} %broadcast_in_dim.4), calls=%async_computation | async-start | bytes 2359296 | tf_op jit(solution)/shard_map/all_to_all | solution.py:50
  55.3 4.5 %copy-start = (bf16[1664,512]{1,0:T(8,128)(2,1)S(1)}, bf16[1664,512]{1,0:T(8,128)(2,1)}, u32[]{:S(2)}) copy-start(bf16[1664,512]{1,0:T(8,128)(2,1)} %all-gather.3.cloned.1.call-done) | copy-start | bytes 5111812
  61.5 1.0 copy-start.2
  62.6 16.0 %copy-start.4 = (bf16[192,512]{1,0:T(8,128)(2,1)S(1)}, bf16[192,512]{1,0:T(8,128)(2,1)}, u32[]{:S(2)}) copy-start(bf16[192,512]{1,0:T(8,128)(2,1)} %param.11) | copy-start | bytes 589828
  65.4 9.7 %collective-permute-start = (bf16[192,15]{1,0:T(8,128)(2,1)S(1)}, bf16[192,15]{1,0:T(8,128)(2,1)S(1)}, u32[]{:S(2)}, u32[]{:S(2)}) collective-permute-start(bf16[192,15]{1,0:T(8,128)(2,1)S(1)} %get-tuple-element.57), channel_id=1, source_target_pairs={{0,8},{8,16},{16,24},{24,32},{32,40},{40,48},{48,56},{56,64},{64,7... | collective-permute-start | bytes 17288 | tf_op jit(solution)/shard_map/ppermute | solution.py:15
  73.0 5.4 %collective-permute-start.1 = (bf16[192,15]{1,0:T(8,128)(2,1)S(1)}, bf16[192,15]{1,0:T(8,128)(2,1)S(1)}, u32[]{:S(2)}, u32[]{:S(2)}) collective-permute-start(bf16[192,15]{1,0:T(8,128)(2,1)S(1)} %get-tuple-element.58), channel_id=1, source_target_pairs={{8,0},{16,8},{24,16},{32,24},{40,32},{48,40},{56,48},{64,56},{72,6... | collective-permute-start | bytes 17288 | tf_op jit(solution)/shard_map/ppermute | solution.py:17
  84.1 8.7 %collective-permute-start.2 = (bf16[192,15]{1,0:T(8,128)(2,1)S(1)}, bf16[192,15]{1,0:T(8,128)(2,1)S(1)}, u32[]{:S(2)}, u32[]{:S(2)}) collective-permute-start(bf16[192,15]{1,0:T(8,128)(2,1)S(1)} %get-tuple-element.55), channel_id=1, source_target_pairs={{0,8},{8,16},{16,24},{24,32},{32,40},{40,48},{48,56},{56,64},{64,7... | collective-permute-start | bytes 17288 | tf_op jit(solution)/shard_map/ppermute | solution.py:15
  86.0 5.1 %copy-start.6 = (f32[192]{0:T(256)S(1)}, f32[192]{0:T(256)}, u32[]{:S(2)}) copy-start(f32[192]{0:T(256)} %get-tuple-element.25) | copy-start | bytes 2308
  86.0 6.7 %collective-permute-start.3 = (bf16[192,15]{1,0:T(8,128)(2,1)S(1)}, bf16[192,15]{1,0:T(8,128)(2,1)S(1)}, u32[]{:S(2)}, u32[]{:S(2)}) collective-permute-start(bf16[192,15]{1,0:T(8,128)(2,1)S(1)} %get-tuple-element.56), channel_id=1, source_target_pairs={{8,0},{16,8},{24,16},{32,24},{40,32},{48,40},{56,48},{64,56},{72,6... | collective-permute-start | bytes 17288 | tf_op jit(solution)/shard_map/ppermute | solution.py:17
  92.9 4.6 %copy-start.3 = (bf16[64,24,384]{2,1,0:T(8,128)(2,1)S(1)}, bf16[64,24,384]{2,1,0:T(8,128)(2,1)}, u32[]{:S(2)}) copy-start(bf16[64,24,384]{2,1,0:T(8,128)(2,1)} %copy-done.2) | copy-start | bytes 3538948
  100.1 1.7 copy-start.1
  109.3 70.0 %all-to-all-start.1 = ((f32[64,1,9312]{2,1,0:T(1,128)}), f32[64,1,9312]{2,1,0:T(1,128)S(1)}, u32[]{:S(2)}, u32[]{:S(2)}) async-start(f32[64,1,9312]{2,1,0:T(1,128)} %all_to_all.16), calls=%async_computation.1 | async-start | bytes 4784128 | tf_op jit(solution)/shard_map/all_to_all | solution.py:155
  125.1 52.3 %copy-start.7 = (f32[192]{0:T(256)S(1)}, f32[192]{0:T(256)}, u32[]{:S(2)}) copy-start(f32[192]{0:T(256)} %param.7) | copy-start | bytes 2308
  126.2 20.1 %collective-permute-start.4 = (bf16[208,512]{1,0:T(8,128)(2,1)}, bf16[208,512]{1,0:T(8,128)(2,1)S(1)}, u32[]{:S(2)}, u32[]{:S(2)}) collective-permute-start(bf16[208,512]{1,0:T(8,128)(2,1)} %get-tuple-element.92), channel_id=1, source_target_pairs={{0,1},{1,2},{2,3},{3,4},{4,5},{5,6},{6,7},{7,0},{8,9},{9,10},{10,1... | collective-permute-start | bytes 638984 | tf_op jit(solution)/shard_map/ppermute | solution.py:83
  128.9 22.5 %collective-permute-start.6 = (bf16[208,512]{1,0:T(8,128)(2,1)}, bf16[208,512]{1,0:T(8,128)(2,1)}, u32[]{:S(2)}, u32[]{:S(2)}) collective-permute-start(bf16[208,512]{1,0:T(8,128)(2,1)} %get-tuple-element.93), channel_id=1, source_target_pairs={{0,3},{1,4},{2,5},{3,6},{4,7},{5,0},{6,1},{7,2},{8,11},{9,12},{10,... | collective-permute-start | bytes 638984 | tf_op jit(solution)/shard_map/ppermute | solution.py:83
  132.9 22.7 %collective-permute-start.7 = (bf16[208,512]{1,0:T(8,128)(2,1)}, bf16[208,512]{1,0:T(8,128)(2,1)S(1)}, u32[]{:S(2)}, u32[]{:S(2)}) collective-permute-start(bf16[208,512]{1,0:T(8,128)(2,1)} %get-tuple-element.94), channel_id=1, source_target_pairs={{0,4},{1,5},{2,6},{3,7},{4,0},{5,1},{6,2},{7,3},{8,12},{9,13},{10,... | collective-permute-start | bytes 638984 | tf_op jit(solution)/shard_map/ppermute | solution.py:83
  137.6 24.6 %collective-permute-start.8 = (bf16[208,512]{1,0:T(8,128)(2,1)}, bf16[208,512]{1,0:T(8,128)(2,1)S(1)}, u32[]{:S(2)}, u32[]{:S(2)}) collective-permute-start(bf16[208,512]{1,0:T(8,128)(2,1)} %get-tuple-element.95), channel_id=1, source_target_pairs={{0,5},{1,6},{2,7},{3,0},{4,1},{5,2},{6,3},{7,4},{8,13},{9,14},{10,... | collective-permute-start | bytes 638984 | tf_op jit(solution)/shard_map/ppermute | solution.py:83
  141.9 31.3 %collective-permute-start.9 = (bf16[208,512]{1,0:T(8,128)(2,1)}, bf16[208,512]{1,0:T(8,128)(2,1)S(1)}, u32[]{:S(2)}, u32[]{:S(2)}) collective-permute-start(bf16[208,512]{1,0:T(8,128)(2,1)} %get-tuple-element.96), channel_id=1, source_target_pairs={{0,6},{1,7},{2,0},{3,1},{4,2},{5,3},{6,4},{7,5},{8,14},{9,15},{10,... | collective-permute-start | bytes 638984 | tf_op jit(solution)/shard_map/ppermute | solution.py:83
  146.3 29.0 %collective-permute-start.10 = (bf16[208,512]{1,0:T(8,128)(2,1)S(1)}, bf16[208,512]{1,0:T(8,128)(2,1)S(1)}, u32[]{:S(2)}, u32[]{:S(2)}) collective-permute-start(bf16[208,512]{1,0:T(8,128)(2,1)S(1)} %get-tuple-element.97), channel_id=1, source_target_pairs={{0,7},{1,0},{2,1},{3,2},{4,3},{5,4},{6,5},{7,6},{8,15},{9,8},{10,9... | collective-permute-start | bytes 638984 | tf_op jit(solution)/shard_map/ppermute | solution.py:83
  151.4 23.8 %collective-permute-start.5 = (bf16[208,512]{1,0:T(8,128)(2,1)S(1)}, bf16[208,512]{1,0:T(8,128)(2,1)S(1)}, u32[]{:S(2)}, u32[]{:S(2)}) collective-permute-start(bf16[208,512]{1,0:T(8,128)(2,1)S(1)} %get-tuple-element.98), channel_id=1, source_target_pairs={{0,2},{1,3},{2,4},{3,5},{4,6},{5,7},{6,0},{7,1},{8,10},{9,11},{10,... | collective-permute-start | bytes 638984 | tf_op jit(solution)/shard_map/ppermute | solution.py:83
  181.5 22.0 %all-to-all-start.2 = ((f32[64,1,288]{2,1,0:T(1,128)}), f32[64,1,288]{2,1,0:T(1,128)S(1)}, u32[]{:S(2)}, u32[]{:S(2)}) async-start(f32[64,1,288]{2,1,0:T(1,128)} %broadcast_in_dim.5), calls=%async_computation.2 | async-start | bytes 196608 | tf_op jit(solution)/shard_map/all_to_all | solution.py:50
Sparse Core Ops, SparseCore 0:
  10.1 45.2 all-gather.2

commit v7 on v6

--- a/solution.py
+++ b/solution.py
@@ -151,8 +151,17 @@
     taps_rows = depth_taps.shape[0]
     taps_flat = jnp.pad(tap_partial, ((0, 1), (0, 0))).reshape(blocks, -1)
     piece = taps_flat.shape[1]
-    outgoing = jnp.concatenate([weight_partial.reshape(blocks, rows * width), taps_flat], 1)
-    summed = jnp.sum(lax.all_to_all(outgoing, "seq", 0, 0, tiled=False), 0)
+    outgoing = jnp.concatenate(
+        [weight_partial.astype(jnp.bfloat16).reshape(blocks, rows * width)]
+        + bf16_pieces(taps_flat, 3),
+        1,
+    )
+    arrived = lax.all_to_all(outgoing, "seq", 0, 0, tiled=False).astype(jnp.float32)
+    summed = jnp.sum(arrived, 0)
+    taps_summed = (
+        summed[rows * width : rows * width + piece]
+        + summed[rows * width + piece : rows * width + 2 * piece]
+    ) + summed[rows * width + 2 * piece :]
     weight_sums = summed[: rows * width].reshape(rows, width)
     grad_value = weight_sums[:, :local_cols]
     grad_gate = weight_sums[:, local_cols:]
@@ -173,7 +182,7 @@
         * (scaled_signal - moments[0:1] - centered_unit_rows * moments[1:2])
     ).astype(jnp.bfloat16)
     gain_portion = jnp.sum(normalized_gradient * centered_unit_rows, 1)
-    last = jnp.concatenate([summed[rows * width :], gain_portion], 0)
+    last = jnp.concatenate([taps_summed, gain_portion], 0)
     finished = gather_by_exchange(last, "seq")
     grad_taps = finished[:, :piece].reshape(-1)[: taps_rows * local_cols].reshape(
         taps_rows, local_cols

time: 213 us -> 221 us (1.038)
  local copies, waits for them, and re-layouts: 14 us -> 18.8 us
  waiting for transfers between devices: 69.7 us -> 72.5 us
    unnamed x18 -> x20, local copies, waits for them, and re-layouts: 2.72 us -> 13.1 us
    ppermute x2, waiting for transfers between devices: 3.39 us -> 6.17 us  [extended(): lax.ppermute(head, axis, [((i + 1) % count, i) for i in range(ends)])]
    all_to_all x1, local copies, waits for them, and re-layouts: 3.08 us -> 0.51 us  [shards(): lax.all_to_all(outgoing, 'seq', 0, 0, tiled=False).astype(jnp.float32)]
  transfers between devices with their start and end apart: 15 -> 15, of which waited for: 8 -> 9; matrix products, arithmetic and copies ran while one was open for 10% -> 6% of each run, Pallas kernels for 0% -> 0%
where the time goes in v7:
time: 221 us; the launch traced here: 220 us
  starting transfers between devices  76.8 us (35%)
  waiting for transfers between devices  72.5 us (33%)
  other arithmetic  31.1 us (14%)
  local copies, waits for them, and re-layouts  18.8 us (9%)
  between operations  14.5 us (7%)
  matrix products  6.08 us (3%)
    all_gather x1, waiting for transfers between devices, shards(): lax.all_gather(jnp.concatenate([signal, gain_rows], 0), 'ch', axis=0)  32.1 us
    ppermute x7, waiting for transfers between devices, reduce_by_shifts(): lax.ppermute(outgoing, axis, [(i, (i + shift) % count) for i in range(cou...  24.4 us
    ppermute x7, starting transfers between devices, reduce_by_shifts(): lax.ppermute(outgoing, axis, [(i, (i + shift) % count) for i in range(cou...  24 us
    all_to_all x2, starting transfers between devices, gather_by_exchange(): return lax.all_to_all(copies, axis, 0, 0, tiled=False)  23.1 us
    all_to_all x1, starting transfers between devices, shards(): lax.all_to_all(outgoing, 'seq', 0, 0, tiled=False).astype(jnp.float32)  15.6 us
    unnamed x20, local copies, waits for them, and re-layouts  13.1 us
    all_to_all x2, waiting for transfers between devices, gather_by_exchange(): return lax.all_to_all(copies, axis, 0, 0, tiled=False)  9.88 us
    ppermute x2, starting transfers between devices, extended(): lax.ppermute(tail, axis, [(i, (i + 1) % count) for i in range(ends)])  9.54 us
  transfers between devices with their start and end apart: 15, of which 9 were waited for; matrix products, arithmetic and copies ran while one was open for 6% of the time, Pallas kernels for 0%

profile of v7, /device:TPU:1, one launch (start us, length us, event | category | flops | bytes accessed | tf_op | source)
XLA Modules:
  0.0 219.8 jit_solution(9095031179345452866)
XLA Ops:
  11.6 11.6 %all-to-all-start = ((bf16[64,24,384]{2,1,0:T(8,128)(2,1)}), bf16[64,24,384]{2,1,0:T(8,128)(2,1)S(1)}, u32[]{:S(2)}, u32[]{:S(2)}) async-start(bf16[64,24,384]{2,1,0:T(8,128)(2,1)} %broadcast_in_dim.4), calls=%async_computation | async-start | bytes 2359296 | tf_op jit(solution)/shard_map/all_to_all | solution.py:50
  23.3 32.1 %all-gather.3.cloned.1.call-done = bf16[1664,512]{1,0:T(8,128)(2,1)} async-done(((bf16[208,512]{1,0:T(8,128)(2,1)}), bf16[1664,512]{1,0:T(8,128)(2,1)}) %all-gather.3.cloned.1.call-update) | async-done | bytes 1703952 | tf_op jit(solution)/shard_map/all_gather | solution.py:104
  62.5 2.6 %fusion.104 = f32[384,512]{1,0:T(8,128)S(1)} fusion(bf16[1536,384]{1,0:T(8,128)(2,1)} %bitcast.111, bf16[1536,512]{1,0:T(8,128)(2,1)} %bitcast.109), kind=kOutput, calls=%fused_computation.228 | convolution fusion | flops 603979776 | bytes 3538944 | tf_op jit(solution)/shard_map/dot_general | solution.py:115
  65.3 7.6 %collective-permute-start = (bf16[192,15]{1,0:T(8,128)(2,1)S(1)}, bf16[192,15]{1,0:T(8,128)(2,1)S(1)}, u32[]{:S(2)}, u32[]{:S(2)}) collective-permute-start(bf16[192,15]{1,0:T(8,128)(2,1)S(1)} %get-tuple-element.57), channel_id=1, source_target_pairs={{0,8},{8,16},{16,24},{24,32},{32,40},{40,48},{48,56},{56,64},{64,7... | collective-permute-start | bytes 17288 | tf_op jit(solution)/shard_map/ppermute | solution.py:15
  75.0 3.4 %collective-permute-done.1 = bf16[192,15]{1,0:T(8,128)(2,1)S(1)} collective-permute-done((bf16[192,15]{1,0:T(8,128)(2,1)S(1)}, bf16[192,15]{1,0:T(8,128)(2,1)S(1)}, u32[]{:S(2)}, u32[]{:S(2)}) %collective-permute-start.1) | collective-permute-done | bytes 5792 | tf_op jit(solution)/shard_map/ppermute | solution.py:17
  78.5 4.9 %fusion.33 = (f32[192]{0:T(256)S(1)}, f32[192]{0:T(256)S(1)}, f32[192]{0:T(256)S(1)}, f32[192]{0:T(256)S(1)}, f32[192]{0:T(256)S(1)}, /*index=5*/f32[192]{0:T(25...) fusion(f32[192,542]{1,0:T(8,128)S(1)} %maximum_convert_fusion, ...), kind=kLoop, calls=%fused_computation.81 | loop fusion | flops 10613376 | bytes 13013760 | tf_op jit(solution)/shard_map/reduce_sum | solution.py:135
  87.6 2.6 %collective-permute-start.3 = (bf16[192,15]{1,0:T(8,128)(2,1)S(1)}, bf16[192,15]{1,0:T(8,128)(2,1)S(1)}, u32[]{:S(2)}, u32[]{:S(2)}) collective-permute-start(bf16[192,15]{1,0:T(8,128)(2,1)S(1)} %get-tuple-element.56), channel_id=1, source_target_pairs={{8,0},{16,8},{24,16},{32,24},{40,32},{48,40},{56,48},{64,56},{72,6... | collective-permute-start | bytes 17288 | tf_op jit(solution)/shard_map/ppermute | solution.py:17
  90.2 2.8 %collective-permute-done.3 = bf16[192,15]{1,0:T(8,128)(2,1)S(1)} collective-permute-done((bf16[192,15]{1,0:T(8,128)(2,1)S(1)}, bf16[192,15]{1,0:T(8,128)(2,1)S(1)}, u32[]{:S(2)}, u32[]{:S(2)}) %collective-permute-start.3) | collective-permute-done | bytes 5792 | tf_op jit(solution)/shard_map/ppermute | solution.py:17
  93.1 4.4 %multiply_convert_fusion.5 = (bf16[192,512]{1,0:T(8,128)(2,1)S(1)}, f32[192,512]{1,0:T(8,128)S(1)}) fusion(f32[384,512]{1,0:T(8,128)S(1)} %fusion.104, f32[192,542]{1,0:T(8,128)S(1)} %maximum_convert_fusion.1, f32[192]{0:T(256)S(1)} %bitcast.119, f32[192]{0:T(256)S(1)} %bitcast.157, f32[192]{0:T(256)S(1)} %bitcast.175, f32[192]{0:T(256)S(1)} %bitcast.173, ...), kind=kLoop, calls=%fused_computation.158 | loop fusion | flops 6488064 | bytes 13196544 | tf_op jit(solution)/shard_map/convert_element_type | solution.py:137
  97.8 2.5 %fusion.1 = (f32[512]{0:T(512)S(1)}, f32[512]{0:T(512)S(1)}, f32[1536,512]{1,0:T(8,128)S(1)}, bf16[1536,512]{1,0:T(8,128)(2,1)}) fusion(f32[1536]{0:T(1024)S(1)} %add.427, f32[512]{0:T(512)S(1)} %add_rsqrt_fusion, f32[512]{0:T(512)S(1)} %broadcast_multiply_fusion, bf16[8,208,512]{2,1,0:T(8,128)(2,1)S(1)} %bitcast.108, bf16[1536,384]{1,0:T(8,128)(2,1)S(1)} %bitcast.112, ...), kind=kOutput, calls=%fused_computation.36 | convolution fusion | flops 611843072 | bytes 7878656 | tf_op jit(solution)/shard_map/dot_general | solution.py:146
  106.4 2.4 %reshape.175 = bf16[64,2,4752]{2,1,0:T(2,128)(2,1)} reshape(bf16[64,9504]{1,0:T(8,128)(2,1)S(1)} %reduce.5) | data formatting | bytes 2433024
  108.8 15.6 %all-to-all-start.1 = ((bf16[64,2,4752]{2,1,0:T(2,128)(2,1)}), bf16[64,2,4752]{2,1,0:T(2,128)(2,1)}, u32[]{:S(2)}, u32[]{:S(2)}) async-start(bf16[64,2,4752]{2,1,0:T(2,128)(2,1)} %reshape.175), calls=%async_computation.1 | async-start | bytes 2490368 | tf_op jit(solution)/shard_map/all_to_all | solution.py:159
  125.7 2.9 %collective-permute-start.4 = (bf16[208,512]{1,0:T(8,128)(2,1)}, bf16[208,512]{1,0:T(8,128)(2,1)S(1)}, u32[]{:S(2)}, u32[]{:S(2)}) collective-permute-start(bf16[208,512]{1,0:T(8,128)(2,1)} %get-tuple-element.95), channel_id=1, source_target_pairs={{0,1},{1,2},{2,3},{3,4},{4,5},{5,6},{6,7},{7,0},{8,9},{9,10},{10,1... | collective-permute-start | bytes 638984 | tf_op jit(solution)/shard_map/ppermute | solution.py:83
  128.6 4.0 %collective-permute-start.6 = (bf16[208,512]{1,0:T(8,128)(2,1)}, bf16[208,512]{1,0:T(8,128)(2,1)S(1)}, u32[]{:S(2)}, u32[]{:S(2)}) collective-permute-start(bf16[208,512]{1,0:T(8,128)(2,1)} %get-tuple-element.96), channel_id=1, source_target_pairs={{0,3},{1,4},{2,5},{3,6},{4,7},{5,0},{6,1},{7,2},{8,11},{9,12},{10,... | collective-permute-start | bytes 638984 | tf_op jit(solution)/shard_map/ppermute | solution.py:83
  132.6 4.6 %collective-permute-start.7 = (bf16[208,512]{1,0:T(8,128)(2,1)}, bf16[208,512]{1,0:T(8,128)(2,1)S(1)}, u32[]{:S(2)}, u32[]{:S(2)}) collective-permute-start(bf16[208,512]{1,0:T(8,128)(2,1)} %get-tuple-element.97), channel_id=1, source_target_pairs={{0,4},{1,5},{2,6},{3,7},{4,0},{5,1},{6,2},{7,3},{8,12},{9,13},{10,... | collective-permute-start | bytes 638984 | tf_op jit(solution)/shard_map/ppermute | solution.py:83
  137.2 4.4 %collective-permute-start.8 = (bf16[208,512]{1,0:T(8,128)(2,1)}, bf16[208,512]{1,0:T(8,128)(2,1)S(1)}, u32[]{:S(2)}, u32[]{:S(2)}) collective-permute-start(bf16[208,512]{1,0:T(8,128)(2,1)} %get-tuple-element.98), channel_id=1, source_target_pairs={{0,5},{1,6},{2,7},{3,0},{4,1},{5,2},{6,3},{7,4},{8,13},{9,14},{10,... | collective-permute-start | bytes 638984 | tf_op jit(solution)/shard_map/ppermute | solution.py:83
  141.6 4.3 %collective-permute-start.9 = (bf16[208,512]{1,0:T(8,128)(2,1)}, bf16[208,512]{1,0:T(8,128)(2,1)S(1)}, u32[]{:S(2)}, u32[]{:S(2)}) collective-permute-start(bf16[208,512]{1,0:T(8,128)(2,1)} %get-tuple-element.99), channel_id=1, source_target_pairs={{0,6},{1,7},{2,0},{3,1},{4,2},{5,3},{6,4},{7,5},{8,14},{9,15},{10,... | collective-permute-start | bytes 638984 | tf_op jit(solution)/shard_map/ppermute | solution.py:83
  147.9 3.3 %collective-permute-done.6 = bf16[208,512]{1,0:T(8,128)(2,1)S(1)} collective-permute-done((bf16[208,512]{1,0:T(8,128)(2,1)}, bf16[208,512]{1,0:T(8,128)(2,1)S(1)}, u32[]{:S(2)}, u32[]{:S(2)}) %collective-permute-start.6) | collective-permute-done | bytes 213024 | tf_op jit(solution)/shard_map/ppermute | solution.py:83
  155.4 6.5 %collective-permute-done.8 = bf16[208,512]{1,0:T(8,128)(2,1)S(1)} collective-permute-done((bf16[208,512]{1,0:T(8,128)(2,1)}, bf16[208,512]{1,0:T(8,128)(2,1)S(1)}, u32[]{:S(2)}, u32[]{:S(2)}) %collective-permute-start.8) | collective-permute-done | bytes 213024 | tf_op jit(solution)/shard_map/ppermute | solution.py:83
  161.9 11.0 %collective-permute-done.9 = bf16[208,512]{1,0:T(8,128)(2,1)S(1)} collective-permute-done((bf16[208,512]{1,0:T(8,128)(2,1)}, bf16[208,512]{1,0:T(8,128)(2,1)S(1)}, u32[]{:S(2)}, u32[]{:S(2)}) %collective-permute-start.9) | collective-permute-done | bytes 213024 | tf_op jit(solution)/shard_map/ppermute | solution.py:83
  178.1 8.0 %reshape.176 = bf16[64,1,9504]{2,1,0:T(2,128)(2,1)S(1)} reshape(bf16[64,2,4752]{2,1,0:T(2,128)(2,1)} %all-to-all-done.1) | data formatting | bytes 2433024
  186.1 2.5 %convert_reduce_fusion.1 = f32[9504]{0:T(1024)S(1)} fusion(bf16[64,1,9504]{2,1,0:T(2,128)(2,1)S(1)} %reshape.176), kind=kLoop, calls=%fused_computation.42 | loop fusion | flops 1207008 | bytes 1254528 | tf_op jit(solution)/shard_map/reduce_sum | solution.py:160
  189.5 11.5 %all-to-all-start.2 = ((f32[64,1,288]{2,1,0:T(1,128)}), f32[64,1,288]{2,1,0:T(1,128)S(1)}, u32[]{:S(2)}, u32[]{:S(2)}) async-start(f32[64,1,288]{2,1,0:T(1,128)} %broadcast_in_dim.5), calls=%async_computation.2 | async-start | bytes 196608 | tf_op jit(solution)/shard_map/all_to_all | solution.py:50
  201.7 9.9 %all-to-all-done.2 = f32[64,1,288]{2,1,0:T(1,128)S(1)} async-done(((f32[64,1,288]{2,1,0:T(1,128)}), f32[64,1,288]{2,1,0:T(1,128)S(1)}, u32[]{:S(2)}, u32[]{:S(2)}) %all-to-all-start.2) | async-done | bytes 73760 | tf_op jit(solution)/shard_map/all_to_all | solution.py:50
  (86 shorter events, 40.0 us)
Async XLA Ops:
  7.2 48.2 %all-gather.3.cloned.1.call-start = ((), (), s32[]{:S(2)}) async-start(), calls=%async_computation.3 | async-start | bytes 1916928 | tf_op jit(solution)/shard_map/all_gather | solution.py:104
  10.5 12.8 %copy-start.6 = (f32[31,192]{1,0:T(8,128)S(1)}, f32[31,192]{1,0:T(8,128)}, u32[]{:S(2)}) copy-start(f32[31,192]{1,0:T(8,128)} %param.10) | copy-start | bytes 71428
  11.6 49.9 %all-to-all-start = ((bf16[64,24,384]{2,1,0:T(8,128)(2,1)}), bf16[64,24,384]{2,1,0:T(8,128)(2,1)S(1)}, u32[]{:S(2)}, u32[]{:S(2)}) async-start(bf16[64,24,384]{2,1,0:T(8,128)(2,1)} %broadcast_in_dim.4), calls=%async_computation | async-start | bytes 2359296 | tf_op jit(solution)/shard_map/all_to_all | solution.py:50
  55.3 4.5 %copy-start = (bf16[1664,512]{1,0:T(8,128)(2,1)S(1)}, bf16[1664,512]{1,0:T(8,128)(2,1)}, u32[]{:S(2)}) copy-start(bf16[1664,512]{1,0:T(8,128)(2,1)} %all-gather.3.cloned.1.call-done) | copy-start | bytes 5111812
  61.5 1.0 copy-start.2
  65.1 13.4 %copy-start.5 = (bf16[192,512]{1,0:T(8,128)(2,1)S(1)}, bf16[192,512]{1,0:T(8,128)(2,1)}, u32[]{:S(2)}) copy-start(bf16[192,512]{1,0:T(8,128)(2,1)} %param.11) | copy-start | bytes 589828
  65.3 9.7 %collective-permute-start = (bf16[192,15]{1,0:T(8,128)(2,1)S(1)}, bf16[192,15]{1,0:T(8,128)(2,1)S(1)}, u32[]{:S(2)}, u32[]{:S(2)}) collective-permute-start(bf16[192,15]{1,0:T(8,128)(2,1)S(1)} %get-tuple-element.57), channel_id=1, source_target_pairs={{0,8},{8,16},{16,24},{24,32},{32,40},{40,48},{48,56},{56,64},{64,7... | collective-permute-start | bytes 17288 | tf_op jit(solution)/shard_map/ppermute | solution.py:15
  73.0 5.4 %collective-permute-start.1 = (bf16[192,15]{1,0:T(8,128)(2,1)S(1)}, bf16[192,15]{1,0:T(8,128)(2,1)S(1)}, u32[]{:S(2)}, u32[]{:S(2)}) collective-permute-start(bf16[192,15]{1,0:T(8,128)(2,1)S(1)} %get-tuple-element.58), channel_id=1, source_target_pairs={{8,0},{16,8},{24,16},{32,24},{40,32},{48,40},{56,48},{64,56},{72,6... | collective-permute-start | bytes 17288 | tf_op jit(solution)/shard_map/ppermute | solution.py:17
  85.7 4.5 %collective-permute-start.2 = (bf16[192,15]{1,0:T(8,128)(2,1)S(1)}, bf16[192,15]{1,0:T(8,128)(2,1)S(1)}, u32[]{:S(2)}, u32[]{:S(2)}) collective-permute-start(bf16[192,15]{1,0:T(8,128)(2,1)S(1)} %get-tuple-element.55), channel_id=1, source_target_pairs={{0,8},{8,16},{16,24},{24,32},{32,40},{40,48},{48,56},{56,64},{64,7... | collective-permute-start | bytes 17288 | tf_op jit(solution)/shard_map/ppermute | solution.py:15
  87.6 5.4 %collective-permute-start.3 = (bf16[192,15]{1,0:T(8,128)(2,1)S(1)}, bf16[192,15]{1,0:T(8,128)(2,1)S(1)}, u32[]{:S(2)}, u32[]{:S(2)}) collective-permute-start(bf16[192,15]{1,0:T(8,128)(2,1)S(1)} %get-tuple-element.56), channel_id=1, source_target_pairs={{8,0},{16,8},{24,16},{32,24},{40,32},{48,40},{56,48},{64,56},{72,6... | collective-permute-start | bytes 17288 | tf_op jit(solution)/shard_map/ppermute | solution.py:17
  93.1 4.6 %copy-start.3 = (bf16[64,24,384]{2,1,0:T(8,128)(2,1)S(1)}, bf16[64,24,384]{2,1,0:T(8,128)(2,1)}, u32[]{:S(2)}) copy-start(bf16[64,24,384]{2,1,0:T(8,128)(2,1)} %copy-done.2) | copy-start | bytes 3538948
  100.3 1.7 copy-start.1
  108.8 15.7 %copy-start.4 = (bf16[1536,512]{1,0:T(8,128)(2,1)S(1)}, bf16[1536,512]{1,0:T(8,128)(2,1)}, u32[]{:S(2)}) copy-start(bf16[1536,512]{1,0:T(8,128)(2,1)} %get-tuple-element.109) | copy-start | bytes 4718596
  108.8 69.3 %all-to-all-start.1 = ((bf16[64,2,4752]{2,1,0:T(2,128)(2,1)}), bf16[64,2,4752]{2,1,0:T(2,128)(2,1)}, u32[]{:S(2)}, u32[]{:S(2)}) async-start(bf16[64,2,4752]{2,1,0:T(2,128)(2,1)} %reshape.175), calls=%async_computation.1 | async-start | bytes 2490368 | tf_op jit(solution)/shard_map/all_to_all | solution.py:159
  125.7 50.6 %copy-start.7 = (f32[192]{0:T(256)S(1)}, f32[192]{0:T(256)}, u32[]{:S(2)}) copy-start(f32[192]{0:T(256)} %param.7) | copy-start | bytes 2308
  125.7 20.2 %collective-permute-start.4 = (bf16[208,512]{1,0:T(8,128)(2,1)}, bf16[208,512]{1,0:T(8,128)(2,1)S(1)}, u32[]{:S(2)}, u32[]{:S(2)}) collective-permute-start(bf16[208,512]{1,0:T(8,128)(2,1)} %get-tuple-element.95), channel_id=1, source_target_pairs={{0,1},{1,2},{2,3},{3,4},{4,5},{5,6},{6,7},{7,0},{8,9},{9,10},{10,1... | collective-permute-start | bytes 638984 | tf_op jit(solution)/shard_map/ppermute | solution.py:83
  128.6 22.6 %collective-permute-start.6 = (bf16[208,512]{1,0:T(8,128)(2,1)}, bf16[208,512]{1,0:T(8,128)(2,1)S(1)}, u32[]{:S(2)}, u32[]{:S(2)}) collective-permute-start(bf16[208,512]{1,0:T(8,128)(2,1)} %get-tuple-element.96), channel_id=1, source_target_pairs={{0,3},{1,4},{2,5},{3,6},{4,7},{5,0},{6,1},{7,2},{8,11},{9,12},{10,... | collective-permute-start | bytes 638984 | tf_op jit(solution)/shard_map/ppermute | solution.py:83
  132.6 22.8 %collective-permute-start.7 = (bf16[208,512]{1,0:T(8,128)(2,1)}, bf16[208,512]{1,0:T(8,128)(2,1)S(1)}, u32[]{:S(2)}, u32[]{:S(2)}) collective-permute-start(bf16[208,512]{1,0:T(8,128)(2,1)} %get-tuple-element.97), channel_id=1, source_target_pairs={{0,4},{1,5},{2,6},{3,7},{4,0},{5,1},{6,2},{7,3},{8,12},{9,13},{10,... | collective-permute-start | bytes 638984 | tf_op jit(solution)/shard_map/ppermute | solution.py:83
  137.2 24.7 %collective-permute-start.8 = (bf16[208,512]{1,0:T(8,128)(2,1)}, bf16[208,512]{1,0:T(8,128)(2,1)S(1)}, u32[]{:S(2)}, u32[]{:S(2)}) collective-permute-start(bf16[208,512]{1,0:T(8,128)(2,1)} %get-tuple-element.98), channel_id=1, source_target_pairs={{0,5},{1,6},{2,7},{3,0},{4,1},{5,2},{6,3},{7,4},{8,13},{9,14},{10,... | collective-permute-start | bytes 638984 | tf_op jit(solution)/shard_map/ppermute | solution.py:83
  141.6 31.2 %collective-permute-start.9 = (bf16[208,512]{1,0:T(8,128)(2,1)}, bf16[208,512]{1,0:T(8,128)(2,1)S(1)}, u32[]{:S(2)}, u32[]{:S(2)}) collective-permute-start(bf16[208,512]{1,0:T(8,128)(2,1)} %get-tuple-element.99), channel_id=1, source_target_pairs={{0,6},{1,7},{2,0},{3,1},{4,2},{5,3},{6,4},{7,5},{8,14},{9,15},{10,... | collective-permute-start | bytes 638984 | tf_op jit(solution)/shard_map/ppermute | solution.py:83
  146.0 29.0 %collective-permute-start.10 = (bf16[208,512]{1,0:T(8,128)(2,1)S(1)}, bf16[208,512]{1,0:T(8,128)(2,1)S(1)}, u32[]{:S(2)}, u32[]{:S(2)}) collective-permute-start(bf16[208,512]{1,0:T(8,128)(2,1)S(1)} %get-tuple-element.100), channel_id=1, source_target_pairs={{0,7},{1,0},{2,1},{3,2},{4,3},{5,4},{6,5},{7,6},{8,15},{9,8},{10,9... | collective-permute-start | bytes 638984 | tf_op jit(solution)/shard_map/ppermute | solution.py:83
  151.2 23.7 %collective-permute-start.5 = (bf16[208,512]{1,0:T(8,128)(2,1)S(1)}, bf16[208,512]{1,0:T(8,128)(2,1)S(1)}, u32[]{:S(2)}, u32[]{:S(2)}) collective-permute-start(bf16[208,512]{1,0:T(8,128)(2,1)S(1)} %get-tuple-element.101), channel_id=1, source_target_pairs={{0,2},{1,3},{2,4},{3,5},{4,6},{5,7},{6,0},{7,1},{8,10},{9,11},{10,... | collective-permute-start | bytes 638984 | tf_op jit(solution)/shard_map/ppermute | solution.py:83
  189.5 22.1 %all-to-all-start.2 = ((f32[64,1,288]{2,1,0:T(1,128)}), f32[64,1,288]{2,1,0:T(1,128)S(1)}, u32[]{:S(2)}, u32[]{:S(2)}) async-start(f32[64,1,288]{2,1,0:T(1,128)} %broadcast_in_dim.5), calls=%async_computation.2 | async-start | bytes 196608 | tf_op jit(solution)/shard_map/all_to_all | solution.py:50
Sparse Core Ops, SparseCore 0:
  10.1 45.2 all-gather.2

commit v8 on v6

--- a/solution.py
+++ b/solution.py
@@ -174,7 +174,7 @@
     ).astype(jnp.bfloat16)
     gain_portion = jnp.sum(normalized_gradient * centered_unit_rows, 1)
     last = jnp.concatenate([summed[rows * width :], gain_portion], 0)
-    finished = gather_by_exchange(last, "seq")
+    finished = lax.all_gather(last, "seq", axis=0)
     grad_taps = finished[:, :piece].reshape(-1)[: taps_rows * local_cols].reshape(
         taps_rows, local_cols
     )

time: 213 us -> 373 us (1.75)
  waiting for transfers between devices: 69.7 us -> 238 us
  starting transfers between devices: 75.2 us -> 63.7 us
    unnamed x1 -> x3, waiting for transfers between devices: 0.02 us -> 178 us
    all_to_all x2 -> x1, starting transfers between devices: 23.1 us -> 11.6 us  [gather_by_exchange(): return lax.all_to_all(copies, axis, 0, 0, tiled=False)]
    all_to_all x2 -> x1, waiting for transfers between devices: 9.88 us -> 0.01 us  [gather_by_exchange(): return lax.all_to_all(copies, axis, 0, 0, tiled=False)]
  transfers between devices with their start and end apart: 15 -> 15, of which waited for: 8 -> 8; matrix products, arithmetic and copies ran while one was open for 10% -> 6% of each run, Pallas kernels for 0% -> 0%
where the time goes in v8:
time: 373 us; the launch traced here: 372 us
  waiting for transfers between devices  238 us (64%)
  starting transfers between devices  63.7 us (17%)
  other arithmetic  32.3 us (9%)
  local copies, waits for them, and re-layouts  16.2 us (4%)
  between operations  15.2 us (4%)
  matrix products  6.16 us (2%)
    unnamed x3, waiting for transfers between devices  178 us
    all_gather x1, waiting for transfers between devices, shards(): lax.all_gather(jnp.concatenate([signal, gain_rows], 0), 'ch', axis=0)  32.1 us
    ppermute x7, waiting for transfers between devices, reduce_by_shifts(): lax.ppermute(outgoing, axis, [(i, (i + shift) % count) for i in range(cou...  24.3 us
    ppermute x7, starting transfers between devices, reduce_by_shifts(): lax.ppermute(outgoing, axis, [(i, (i + shift) % count) for i in range(cou...  23.9 us
    all_to_all x1, starting transfers between devices, shards(): summed = jnp.sum(lax.all_to_all(outgoing, 'seq', 0, 0, tiled=False), 0)  14.1 us
    all_to_all x1, starting transfers between devices, gather_by_exchange(): return lax.all_to_all(copies, axis, 0, 0, tiled=False)  11.6 us
    ppermute x2, starting transfers between devices, extended(): lax.ppermute(tail, axis, [(i, (i + 1) % count) for i in range(ends)])  9.54 us
    reduce_sum x2, other arithmetic, shards(): jnp.sum(glued_pad[:, k:k + span] * grad_pre_f, 1)  7.95 us
  transfers between devices with their start and end apart: 15, of which 8 were waited for; matrix products, arithmetic and copies ran while one was open for 6% of the time, Pallas kernels for 0%

profile of v8, /device:TPU:1, one launch (start us, length us, event | category | flops | bytes accessed | tf_op | source)
XLA Modules:
  0.0 371.8 jit_solution(17138846882478943412)
XLA Ops:
  11.6 11.6 %all-to-all-start = ((bf16[64,24,384]{2,1,0:T(8,128)(2,1)}), bf16[64,24,384]{2,1,0:T(8,128)(2,1)S(1)}, u32[]{:S(2)}, u32[]{:S(2)}) async-start(bf16[64,24,384]{2,1,0:T(8,128)(2,1)} %broadcast_in_dim.2), calls=%async_computation | async-start | bytes 2359296 | tf_op jit(solution)/shard_map/all_to_all | solution.py:50
  23.3 32.1 %all-gather.4.cloned.1.call-done = bf16[1664,512]{1,0:T(8,128)(2,1)} async-done(((bf16[208,512]{1,0:T(8,128)(2,1)}), bf16[1664,512]{1,0:T(8,128)(2,1)}) %all-gather.4.cloned.1.call-update) | async-done | bytes 1703952 | tf_op jit(solution)/shard_map/all_gather | solution.py:104
  62.6 2.6 fusion.104
  65.4 7.6 %collective-permute-start = (bf16[192,15]{1,0:T(8,128)(2,1)S(1)}, bf16[192,15]{1,0:T(8,128)(2,1)S(1)}, u32[]{:S(2)}, u32[]{:S(2)}) collective-permute-start(bf16[192,15]{1,0:T(8,128)(2,1)S(1)} %get-tuple-element.57), channel_id=1, source_target_pairs={{0,8},{8,16},{16,24},{24,32},{32,40},{40,48},{48,56},{56,64},{64,7... | collective-permute-start | bytes 17288 | tf_op jit(solution)/shard_map/ppermute | solution.py:15
  73.0 1.9 collective-permute-start.1
  75.0 3.4 collective-permute-done.1
  78.6 5.4 %fusion.34 = (f32[192]{0:T(256)S(1)}, f32[192]{0:T(256)S(1)}, f32[192]{0:T(256)S(1)}, f32[192]{0:T(256)S(1)}, f32[192]{0:T(256)S(1)}, /*index=5*/f32[192]{0:T(25...) fusion(f32[192,542]{1,0:T(8,128)S(1)} %maximum_convert_fusion, ...), kind=kLoop, calls=%fused_computation.81 | loop fusion | flops 10613376 | bytes 13013760 | tf_op jit(solution)/shard_map/reduce_sum | solution.py:135
  84.1 1.9 collective-permute-start.2
  86.0 2.6 collective-permute-start.3
  88.6 2.5 fusion.33
  92.9 4.4 %multiply_convert_fusion.5 = (bf16[192,512]{1,0:T(8,128)(2,1)S(1)}, f32[192,512]{1,0:T(8,128)S(1)}) fusion(f32[384,512]{1,0:T(8,128)S(1)} %fusion.104, f32[192,542]{1,0:T(8,128)S(1)} %maximum_convert_fusion.1, f32[192]{0:T(256)S(1)} %bitcast.113, f32[192]{0:T(256)S(1)} %bitcast.151, f32[192]{0:T(256)S(1)} %bitcast.169, f32[192]{0:T(256)S(1)} %bitcast.167, ...), kind=kLoop, calls=%fused_computation.158 | loop fusion | flops 6488064 | bytes 13196544 | tf_op jit(solution)/shard_map/convert_element_type | solution.py:137
  97.6 2.5 fusion.1
  106.3 3.1 all_to_all.10
  109.3 14.1 %all-to-all-start.1 = ((f32[64,1,9312]{2,1,0:T(1,128)}), f32[64,1,9312]{2,1,0:T(1,128)S(1)}, u32[]{:S(2)}, u32[]{:S(2)}) async-start(f32[64,1,9312]{2,1,0:T(1,128)} %all_to_all.10), calls=%async_computation.1 | async-start | bytes 4784128 | tf_op jit(solution)/shard_map/all_to_all | solution.py:155
  126.2 2.7 collective-permute-start.4
  129.0 4.0 %collective-permute-start.6 = (bf16[208,512]{1,0:T(8,128)(2,1)}, bf16[208,512]{1,0:T(8,128)(2,1)}, u32[]{:S(2)}, u32[]{:S(2)}) collective-permute-start(bf16[208,512]{1,0:T(8,128)(2,1)} %get-tuple-element.93), channel_id=1, source_target_pairs={{0,3},{1,4},{2,5},{3,6},{4,7},{5,0},{6,1},{7,2},{8,11},{9,12},{10,... | collective-permute-start | bytes 638984 | tf_op jit(solution)/shard_map/ppermute | solution.py:83
  134.9 4.6 %collective-permute-start.7 = (bf16[208,512]{1,0:T(8,128)(2,1)}, bf16[208,512]{1,0:T(8,128)(2,1)S(1)}, u32[]{:S(2)}, u32[]{:S(2)}) collective-permute-start(bf16[208,512]{1,0:T(8,128)(2,1)} %get-tuple-element.94), channel_id=1, source_target_pairs={{0,4},{1,5},{2,6},{3,7},{4,0},{5,1},{6,2},{7,3},{8,12},{9,13},{10,... | collective-permute-start | bytes 638984 | tf_op jit(solution)/shard_map/ppermute | solution.py:83
  139.5 4.4 %collective-permute-start.8 = (bf16[208,512]{1,0:T(8,128)(2,1)}, bf16[208,512]{1,0:T(8,128)(2,1)S(1)}, u32[]{:S(2)}, u32[]{:S(2)}) collective-permute-start(bf16[208,512]{1,0:T(8,128)(2,1)} %get-tuple-element.95), channel_id=1, source_target_pairs={{0,5},{1,6},{2,7},{3,0},{4,1},{5,2},{6,3},{7,4},{8,13},{9,14},{10,... | collective-permute-start | bytes 638984 | tf_op jit(solution)/shard_map/ppermute | solution.py:83
  143.9 4.3 %collective-permute-start.9 = (bf16[208,512]{1,0:T(8,128)(2,1)}, bf16[208,512]{1,0:T(8,128)(2,1)S(1)}, u32[]{:S(2)}, u32[]{:S(2)}) collective-permute-start(bf16[208,512]{1,0:T(8,128)(2,1)} %get-tuple-element.96), channel_id=1, source_target_pairs={{0,6},{1,7},{2,0},{3,1},{4,2},{5,3},{6,4},{7,5},{8,14},{9,15},{10,... | collective-permute-start | bytes 638984 | tf_op jit(solution)/shard_map/ppermute | solution.py:83
  148.2 1.9 collective-permute-start.10
  155.7 8.4 %collective-permute-done.8 = bf16[208,512]{1,0:T(8,128)(2,1)S(1)} collective-permute-done((bf16[208,512]{1,0:T(8,128)(2,1)}, bf16[208,512]{1,0:T(8,128)(2,1)S(1)}, u32[]{:S(2)}, u32[]{:S(2)}) %collective-permute-start.8) | collective-permute-done | bytes 213024 | tf_op jit(solution)/shard_map/ppermute | solution.py:83
  164.1 11.0 %collective-permute-done.9 = bf16[208,512]{1,0:T(8,128)(2,1)S(1)} collective-permute-done((bf16[208,512]{1,0:T(8,128)(2,1)}, bf16[208,512]{1,0:T(8,128)(2,1)S(1)}, u32[]{:S(2)}, u32[]{:S(2)}) %collective-permute-start.9) | collective-permute-done | bytes 213024 | tf_op jit(solution)/shard_map/ppermute | solution.py:83
  175.2 2.0 collective-permute-done.10
  184.3 178.3 %all-reduce.6.cloned.1.call-done = f32[18432]{0:T(1024)} async-done(((f32[18432]{0:T(1024)}), f32[18432]{0:T(1024)}) %all-reduce.6.cloned.1.call-update) | async-done | bytes 73744
  (86 shorter events, 38.9 us)
Async XLA Ops:
  7.2 16.1 %copy-start.6 = (f32[31,192]{1,0:T(8,128)S(1)}, f32[31,192]{1,0:T(8,128)}, u32[]{:S(2)}) copy-start(f32[31,192]{1,0:T(8,128)} %param.10) | copy-start | bytes 71428
  7.2 48.2 %all-gather.4.cloned.1.call-start = ((), (), s32[]{:S(2)}) async-start(), calls=%async_computation.2 | async-start | bytes 1916928 | tf_op jit(solution)/shard_map/all_gather | solution.py:104
  11.6 49.9 %all-to-all-start = ((bf16[64,24,384]{2,1,0:T(8,128)(2,1)}), bf16[64,24,384]{2,1,0:T(8,128)(2,1)S(1)}, u32[]{:S(2)}, u32[]{:S(2)}) async-start(bf16[64,24,384]{2,1,0:T(8,128)(2,1)} %broadcast_in_dim.2), calls=%async_computation | async-start | bytes 2359296 | tf_op jit(solution)/shard_map/all_to_all | solution.py:50
  55.3 4.5 %copy-start = (bf16[1664,512]{1,0:T(8,128)(2,1)S(1)}, bf16[1664,512]{1,0:T(8,128)(2,1)}, u32[]{:S(2)}) copy-start(bf16[1664,512]{1,0:T(8,128)(2,1)} %all-gather.4.cloned.1.call-done) | copy-start | bytes 5111812
  61.5 1.0 copy-start.2
  62.6 16.0 %copy-start.5 = (bf16[192,512]{1,0:T(8,128)(2,1)S(1)}, bf16[192,512]{1,0:T(8,128)(2,1)}, u32[]{:S(2)}) copy-start(bf16[192,512]{1,0:T(8,128)(2,1)} %param.11) | copy-start | bytes 589828
  65.4 9.7 %collective-permute-start = (bf16[192,15]{1,0:T(8,128)(2,1)S(1)}, bf16[192,15]{1,0:T(8,128)(2,1)S(1)}, u32[]{:S(2)}, u32[]{:S(2)}) collective-permute-start(bf16[192,15]{1,0:T(8,128)(2,1)S(1)} %get-tuple-element.57), channel_id=1, source_target_pairs={{0,8},{8,16},{16,24},{24,32},{32,40},{40,48},{48,56},{56,64},{64,7... | collective-permute-start | bytes 17288 | tf_op jit(solution)/shard_map/ppermute | solution.py:15
  73.0 5.4 %collective-permute-start.1 = (bf16[192,15]{1,0:T(8,128)(2,1)S(1)}, bf16[192,15]{1,0:T(8,128)(2,1)S(1)}, u32[]{:S(2)}, u32[]{:S(2)}) collective-permute-start(bf16[192,15]{1,0:T(8,128)(2,1)S(1)} %get-tuple-element.58), channel_id=1, source_target_pairs={{8,0},{16,8},{24,16},{32,24},{40,32},{48,40},{56,48},{64,56},{72,6... | collective-permute-start | bytes 17288 | tf_op jit(solution)/shard_map/ppermute | solution.py:17
  84.1 8.7 %collective-permute-start.2 = (bf16[192,15]{1,0:T(8,128)(2,1)S(1)}, bf16[192,15]{1,0:T(8,128)(2,1)S(1)}, u32[]{:S(2)}, u32[]{:S(2)}) collective-permute-start(bf16[192,15]{1,0:T(8,128)(2,1)S(1)} %get-tuple-element.55), channel_id=1, source_target_pairs={{0,8},{8,16},{16,24},{24,32},{32,40},{40,48},{48,56},{56,64},{64,7... | collective-permute-start | bytes 17288 | tf_op jit(solution)/shard_map/ppermute | solution.py:15
  86.0 5.1 %copy-start.7 = (f32[192]{0:T(256)S(1)}, f32[192]{0:T(256)}, u32[]{:S(2)}) copy-start(f32[192]{0:T(256)} %get-tuple-element.25) | copy-start | bytes 2308
  86.0 6.7 %collective-permute-start.3 = (bf16[192,15]{1,0:T(8,128)(2,1)S(1)}, bf16[192,15]{1,0:T(8,128)(2,1)S(1)}, u32[]{:S(2)}, u32[]{:S(2)}) collective-permute-start(bf16[192,15]{1,0:T(8,128)(2,1)S(1)} %get-tuple-element.56), channel_id=1, source_target_pairs={{8,0},{16,8},{24,16},{32,24},{40,32},{48,40},{56,48},{64,56},{72,6... | collective-permute-start | bytes 17288 | tf_op jit(solution)/shard_map/ppermute | solution.py:17
  92.9 4.6 %copy-start.3 = (bf16[64,24,384]{2,1,0:T(8,128)(2,1)S(1)}, bf16[64,24,384]{2,1,0:T(8,128)(2,1)}, u32[]{:S(2)}) copy-start(bf16[64,24,384]{2,1,0:T(8,128)(2,1)} %copy-done.2) | copy-start | bytes 3538948
  100.1 1.7 copy-start.1
  109.3 71.9 %all-to-all-start.1 = ((f32[64,1,9312]{2,1,0:T(1,128)}), f32[64,1,9312]{2,1,0:T(1,128)S(1)}, u32[]{:S(2)}, u32[]{:S(2)}) async-start(f32[64,1,9312]{2,1,0:T(1,128)} %all_to_all.10), calls=%async_computation.1 | async-start | bytes 4784128 | tf_op jit(solution)/shard_map/all_to_all | solution.py:155
  123.5 239.2 %all-reduce.6.cloned.1.call-start = ((), (), s32[]{:S(2)}) async-start(), calls=%async_computation.3 | async-start | bytes 147456
  125.2 54.3 %copy-start.8 = (f32[192]{0:T(256)S(1)}, f32[192]{0:T(256)}, u32[]{:S(2)}) copy-start(f32[192]{0:T(256)} %param.7) | copy-start | bytes 2308
  126.2 22.0 %collective-permute-start.4 = (bf16[208,512]{1,0:T(8,128)(2,1)}, bf16[208,512]{1,0:T(8,128)(2,1)S(1)}, u32[]{:S(2)}, u32[]{:S(2)}) collective-permute-start(bf16[208,512]{1,0:T(8,128)(2,1)} %get-tuple-element.92), channel_id=1, source_target_pairs={{0,1},{1,2},{2,3},{3,4},{4,5},{5,6},{6,7},{7,0},{8,9},{9,10},{10,1... | collective-permute-start | bytes 638984 | tf_op jit(solution)/shard_map/ppermute | solution.py:83
  129.0 22.5 %collective-permute-start.6 = (bf16[208,512]{1,0:T(8,128)(2,1)}, bf16[208,512]{1,0:T(8,128)(2,1)}, u32[]{:S(2)}, u32[]{:S(2)}) collective-permute-start(bf16[208,512]{1,0:T(8,128)(2,1)} %get-tuple-element.93), channel_id=1, source_target_pairs={{0,3},{1,4},{2,5},{3,6},{4,7},{5,0},{6,1},{7,2},{8,11},{9,12},{10,... | collective-permute-start | bytes 638984 | tf_op jit(solution)/shard_map/ppermute | solution.py:83
  134.9 20.8 %collective-permute-start.7 = (bf16[208,512]{1,0:T(8,128)(2,1)}, bf16[208,512]{1,0:T(8,128)(2,1)S(1)}, u32[]{:S(2)}, u32[]{:S(2)}) collective-permute-start(bf16[208,512]{1,0:T(8,128)(2,1)} %get-tuple-element.94), channel_id=1, source_target_pairs={{0,4},{1,5},{2,6},{3,7},{4,0},{5,1},{6,2},{7,3},{8,12},{9,13},{10,... | collective-permute-start | bytes 638984 | tf_op jit(solution)/shard_map/ppermute | solution.py:83
  139.5 24.6 %collective-permute-start.8 = (bf16[208,512]{1,0:T(8,128)(2,1)}, bf16[208,512]{1,0:T(8,128)(2,1)S(1)}, u32[]{:S(2)}, u32[]{:S(2)}) collective-permute-start(bf16[208,512]{1,0:T(8,128)(2,1)} %get-tuple-element.95), channel_id=1, source_target_pairs={{0,5},{1,6},{2,7},{3,0},{4,1},{5,2},{6,3},{7,4},{8,13},{9,14},{10,... | collective-permute-start | bytes 638984 | tf_op jit(solution)/shard_map/ppermute | solution.py:83
  143.9 31.3 %collective-permute-start.9 = (bf16[208,512]{1,0:T(8,128)(2,1)}, bf16[208,512]{1,0:T(8,128)(2,1)S(1)}, u32[]{:S(2)}, u32[]{:S(2)}) collective-permute-start(bf16[208,512]{1,0:T(8,128)(2,1)} %get-tuple-element.96), channel_id=1, source_target_pairs={{0,6},{1,7},{2,0},{3,1},{4,2},{5,3},{6,4},{7,5},{8,14},{9,15},{10,... | collective-permute-start | bytes 638984 | tf_op jit(solution)/shard_map/ppermute | solution.py:83
  148.2 29.0 %collective-permute-start.10 = (bf16[208,512]{1,0:T(8,128)(2,1)S(1)}, bf16[208,512]{1,0:T(8,128)(2,1)S(1)}, u32[]{:S(2)}, u32[]{:S(2)}) collective-permute-start(bf16[208,512]{1,0:T(8,128)(2,1)S(1)} %get-tuple-element.97), channel_id=1, source_target_pairs={{0,7},{1,0},{2,1},{3,2},{4,3},{5,4},{6,5},{7,6},{8,15},{9,8},{10,9... | collective-permute-start | bytes 638984 | tf_op jit(solution)/shard_map/ppermute | solution.py:83
  151.5 25.8 %collective-permute-start.5 = (bf16[208,512]{1,0:T(8,128)(2,1)S(1)}, bf16[208,512]{1,0:T(8,128)(2,1)S(1)}, u32[]{:S(2)}, u32[]{:S(2)}) collective-permute-start(bf16[208,512]{1,0:T(8,128)(2,1)S(1)} %get-tuple-element.98), channel_id=1, source_target_pairs={{0,2},{1,3},{2,4},{3,5},{4,6},{5,7},{6,0},{7,1},{8,10},{9,11},{10,... | collective-permute-start | bytes 638984 | tf_op jit(solution)/shard_map/ppermute | solution.py:83
  182.9 0.6 copy-start.4
Sparse Core Ops, SparseCore 0:
  10.1 45.2 all-gather.3
  183.7 178.8 all-reduce.5

commit v9 on v6

--- a/solution.py
+++ b/solution.py
@@ -151,19 +151,33 @@
     taps_rows = depth_taps.shape[0]
     taps_flat = jnp.pad(tap_partial, ((0, 1), (0, 0))).reshape(blocks, -1)
     piece = taps_flat.shape[1]
-    outgoing = jnp.concatenate([weight_partial.reshape(blocks, rows * width), taps_flat], 1)
-    summed = jnp.sum(lax.all_to_all(outgoing, "seq", 0, 0, tiled=False), 0)
-    weight_sums = summed[: rows * width].reshape(rows, width)
+    taps_row = jnp.concatenate(bf16_pieces(taps_flat, 3), 1)
+    taps_row = jnp.pad(taps_row, ((0, 0), (0, width - taps_row.shape[1])))
+    outgoing = jnp.concatenate(
+        [weight_partial.astype(jnp.bfloat16).reshape(blocks, rows, width), taps_row[:, None]], 1
+    )
+    summed = jnp.sum(lax.all_to_all(outgoing, "seq", 0, 0, tiled=False).astype(jnp.float32), 0)
+    weight_sums = summed[:rows]
+    taps_summed = (summed[rows, :piece] + summed[rows, piece : 2 * piece]) + summed[
+        rows, 2 * piece : 3 * piece
+    ]
     grad_value = weight_sums[:, :local_cols]
     grad_gate = weight_sums[:, local_cols:]
     normed_f = normed_term.astype(jnp.float32)
     weighted = normed_f * complete_gain[:, None]
     own_moments = jnp.stack([jnp.sum(weighted, 0), jnp.sum(weighted * centered_unit, 0)], 0)
     moment_rows = jnp.concatenate(bf16_pieces(own_moments, 3), 0)
+    half = frames // 2
+    moment_rows = moment_rows.reshape(-1, half)
     moment_rows = jnp.pad(moment_rows, ((0, 16 - moment_rows.shape[0]), (0, 0)))
-    normalized_gradient, moment_total = reduce_by_shifts(
-        normed_term.reshape(groups, local_cols, frames), moment_rows, "ch"
-    )
+    early_part = lax.psum_scatter(
+        normed_term[:, :half].astype(jnp.float32), "ch", scatter_dimension=0, tiled=True
+    )
+    late_part, moment_total = reduce_by_shifts(
+        normed_term[:, half:].reshape(groups, local_cols, frames - half), moment_rows, "ch"
+    )
+    normalized_gradient = jnp.concatenate([early_part, late_part], 1)
+    moment_total = moment_total[:12].reshape(6, frames)
     scaled_signal = normalized_gradient * input_norm_gain[:, None]
     moments = ((moment_total[0:2] + moment_total[2:4]) + moment_total[4:6]) * (
         1.0 / complete_signal.shape[0]
@@ -173,7 +187,7 @@
         * (scaled_signal - moments[0:1] - centered_unit_rows * moments[1:2])
     ).astype(jnp.bfloat16)
     gain_portion = jnp.sum(normalized_gradient * centered_unit_rows, 1)
-    last = jnp.concatenate([summed[rows * width :], gain_portion], 0)
+    last = jnp.concatenate([taps_summed, gain_portion], 0)
     finished = gather_by_exchange(last, "seq")
     grad_taps = finished[:, :piece].reshape(-1)[: taps_rows * local_cols].reshape(
         taps_rows, local_cols

time: 213 us -> 197 us (0.925)
  waiting for transfers between devices: 69.7 us -> 60.2 us
  local copies, waits for them, and re-layouts: 14 us -> 6.74 us
  other arithmetic: 32.2 us -> 29.9 us
    ppermute x7, waiting for transfers between devices: 24.3 us -> 12.9 us  [reduce_by_shifts(): lax.ppermute(outgoing, axis, [(i, (i + shift) % count) for i in range(cou...]
    all_to_all x1 -> x0, local copies, waits for them, and re-layouts: 3.08 us -> none  [shards(): summed = jnp.sum(lax.all_to_all(outgoing, 'seq', 0, 0, tiled=False), 0)]
  transfers between devices with their start and end apart: 15 -> 16, of which waited for: 8 -> 7; matrix products, arithmetic and copies ran while one was open for 10% -> 8% of each run, Pallas kernels for 0% -> 0%
where the time goes in v9:
time: 197 us; the launch traced here: 196 us
  starting transfers between devices  76.3 us (39%)
  waiting for transfers between devices  60.2 us (31%)
  other arithmetic  29.9 us (15%)
  between operations  14.6 us (7%)
  matrix products  8.23 us (4%)
  local copies, waits for them, and re-layouts  6.74 us (3%)
    all_gather x1, waiting for transfers between devices, shards(): lax.all_gather(jnp.concatenate([signal, gain_rows], 0), 'ch', axis=0)  32 us
    ppermute x7, starting transfers between devices, reduce_by_shifts(): lax.ppermute(outgoing, axis, [(i, (i + shift) % count) for i in range(cou...  24.3 us
    all_to_all x2, starting transfers between devices, gather_by_exchange(): return lax.all_to_all(copies, axis, 0, 0, tiled=False)  22.5 us
    all_to_all x1, starting transfers between devices, shards(): lax.all_to_all(outgoing, 'seq', 0, 0, tiled=False).astype(jnp.float32)  15.4 us
    ppermute x7, waiting for transfers between devices, reduce_by_shifts(): lax.ppermute(outgoing, axis, [(i, (i + shift) % count) for i in range(cou...  12.9 us
    all_to_all x2, waiting for transfers between devices, gather_by_exchange(): return lax.all_to_all(copies, axis, 0, 0, tiled=False)  9.88 us
    ppermute x2, starting transfers between devices, extended(): lax.ppermute(tail, axis, [(i, (i + 1) % count) for i in range(ends)])  9.55 us
    reduce_sum x2, other arithmetic, shards(): jnp.sum(glued_pad[:, k:k + span] * grad_pre_f, 1)  6.84 us
  transfers between devices with their start and end apart: 16, of which 7 were waited for; matrix products, arithmetic and copies ran while one was open for 8% of the time, Pallas kernels for 0%

profile of v9, /device:TPU:1, one launch (start us, length us, event | category | flops | bytes accessed | tf_op | source)
XLA Modules:
  0.0 196.0 jit_solution(4594739373698497576)
XLA Ops:
  11.6 11.6 %all-to-all-start = ((bf16[64,24,384]{2,1,0:T(8,128)(2,1)}), bf16[64,24,384]{2,1,0:T(8,128)(2,1)S(1)}, u32[]{:S(2)}, u32[]{:S(2)}) async-start(bf16[64,24,384]{2,1,0:T(8,128)(2,1)} %broadcast_in_dim.6), calls=%async_computation | async-start | bytes 2359296 | tf_op jit(solution)/shard_map/all_to_all | solution.py:50
  23.3 32.0 %all-gather.3.cloned.1.call-done = bf16[1664,512]{1,0:T(8,128)(2,1)} async-done(((bf16[208,512]{1,0:T(8,128)(2,1)}), bf16[1664,512]{1,0:T(8,128)(2,1)}) %all-gather.3.cloned.1.call-update) | async-done | bytes 1703952 | tf_op jit(solution)/shard_map/all_gather | solution.py:104
  62.5 2.6 %fusion.105 = f32[384,512]{1,0:T(8,128)S(1)} fusion(bf16[1536,384]{1,0:T(8,128)(2,1)} %bitcast.117, bf16[1536,512]{1,0:T(8,128)(2,1)} %bitcast.116), kind=kOutput, calls=%fused_computation.236 | convolution fusion | flops 603979776 | bytes 3538944 | tf_op jit(solution)/shard_map/dot_general | solution.py:115
  65.3 7.6 %collective-permute-start = (bf16[192,15]{1,0:T(8,128)(2,1)S(1)}, bf16[192,15]{1,0:T(8,128)(2,1)S(1)}, u32[]{:S(2)}, u32[]{:S(2)}) collective-permute-start(bf16[192,15]{1,0:T(8,128)(2,1)S(1)} %get-tuple-element.59), channel_id=1, source_target_pairs={{0,8},{8,16},{16,24},{24,32},{32,40},{40,48},{48,56},{56,64},{64,7... | collective-permute-start | bytes 17288 | tf_op jit(solution)/shard_map/ppermute | solution.py:15
  75.0 3.4 %collective-permute-done.1 = bf16[192,15]{1,0:T(8,128)(2,1)S(1)} collective-permute-done((bf16[192,15]{1,0:T(8,128)(2,1)S(1)}, bf16[192,15]{1,0:T(8,128)(2,1)S(1)}, u32[]{:S(2)}, u32[]{:S(2)}) %collective-permute-start.1) | collective-permute-done | bytes 5792 | tf_op jit(solution)/shard_map/ppermute | solution.py:17
  78.5 4.9 %fusion.33 = (f32[192]{0:T(256)S(1)}, f32[192]{0:T(256)S(1)}, f32[192]{0:T(256)S(1)}, f32[192]{0:T(256)S(1)}, f32[192]{0:T(256)S(1)}, /*index=5*/f32[192]{0:T(25...) fusion(f32[192,542]{1,0:T(8,128)S(1)} %maximum_convert_fusion, ...), kind=kLoop, calls=%fused_computation.76 | loop fusion | flops 10613376 | bytes 13013760 | tf_op jit(solution)/shard_map/reduce_sum | solution.py:135
  83.4 1.9 fusion.32
  85.7 1.9 collective-permute-start.2
  87.6 2.6 %collective-permute-start.3 = (bf16[192,15]{1,0:T(8,128)(2,1)S(1)}, bf16[192,15]{1,0:T(8,128)(2,1)S(1)}, u32[]{:S(2)}, u32[]{:S(2)}) collective-permute-start(bf16[192,15]{1,0:T(8,128)(2,1)S(1)} %get-tuple-element.58), channel_id=1, source_target_pairs={{8,0},{16,8},{24,16},{32,24},{40,32},{48,40},{56,48},{64,56},{72,6... | collective-permute-start | bytes 17288 | tf_op jit(solution)/shard_map/ppermute | solution.py:17
  91.0 2.0 %collective-permute-done.3 = bf16[192,15]{1,0:T(8,128)(2,1)S(1)} collective-permute-done((bf16[192,15]{1,0:T(8,128)(2,1)S(1)}, bf16[192,15]{1,0:T(8,128)(2,1)S(1)}, u32[]{:S(2)}, u32[]{:S(2)}) %collective-permute-start.3) | collective-permute-done | bytes 5792 | tf_op jit(solution)/shard_map/ppermute | solution.py:17
  93.2 4.4 %multiply_convert_fusion.5 = (bf16[192,512]{1,0:T(8,128)(2,1)S(1)}, f32[192,512]{1,0:T(8,128)S(1)}) fusion(f32[384,512]{1,0:T(8,128)S(1)} %fusion.105, f32[192,542]{1,0:T(8,128)S(1)} %maximum_convert_fusion.1, f32[192]{0:T(256)S(1)} %bitcast.126, f32[192]{0:T(256)S(1)} %bitcast.164, f32[192]{0:T(256)S(1)} %bitcast.182, f32[192]{0:T(256)S(1)} %bitcast.180, ...), kind=kLoop, calls=%fused_computation.147 | loop fusion | flops 6488064 | bytes 13196544 | tf_op jit(solution)/shard_map/convert_element_type | solution.py:137
  97.8 3.6 %fusion.1 = (f32[512]{0:T(512)S(1)}, f32[512]{0:T(512)}, f32[1536,512]{1,0:T(8,128)}, bf16[1536,512]{1,0:T(8,128)(2,1)S(1)}) fusion(f32[1536]{0:T(1024)S(1)} %add.437, f32[512]{0:T(512)S(1)} %add_rsqrt_fusion, f32[512]{0:T(512)S(1)} %broadcast_multiply_fusion, bf16[8,208,512]{2,1,0:T(8,128)(2,1)S(1)} %bitcast.115, bf16[1536,384]{1,0:T(8,128)(2,1)S(1)} %bitcast.118, ...), kind=kOutput, calls=%fused_computation.37 | convolution fusion | flops 611843072 | bytes 7878656 | tf_op jit(solution)/shard_map/dot_general | solution.py:146
  104.2 2.1 %convolution_convert_fusion.1 = bf16[1536,384]{1,0:T(8,128)(2,1)S(1)} fusion(f32[1536,512]{1,0:T(8,128)S(1)} %copy-done.3, f32[1536]{0:T(1024)S(1)} %add.437, bf16[192,512]{1,0:T(8,128)(2,1)} %copy-done.5, bf16[192,512]{1,0:T(8,128)(2,1)} %copy-done.6), kind=kOutput, calls=%fused_computation.42 | convolution fusion | flops 606928896 | bytes 4724736 | tf_op jit(solution)/shard_map/dot_general | solution.py:140
  107.7 15.4 %all-to-all-start.1 = ((bf16[64,25,384]{2,1,0:T(8,128)(2,1)}), bf16[64,25,384]{2,1,0:T(8,128)(2,1)S(1)}, u32[]{:S(2)}, u32[]{:S(2)}) async-start(bf16[64,25,384]{2,1,0:T(8,128)(2,1)} %pad_maximum_fusion), calls=%async_computation.2 | async-start | bytes 3145728 | tf_op jit(solution)/shard_map/all_to_all | solution.py:159
  123.4 2.8 %collective-permute-start.4 = (bf16[208,256]{1,0:T(8,128)(2,1)S(1)}, bf16[208,256]{1,0:T(8,128)(2,1)}, u32[]{:S(2)}, u32[]{:S(2)}) collective-permute-start(bf16[208,256]{1,0:T(8,128)(2,1)S(1)} %get-tuple-element.97), channel_id=1, source_target_pairs={{0,1},{1,2},{2,3},{3,4},{4,5},{5,6},{6,7},{7,0},{8,9},{9,10},{10,1... | collective-permute-start | bytes 319496 | tf_op jit(solution)/shard_map/ppermute | solution.py:83
  126.2 4.0 %collective-permute-start.6 = (bf16[208,256]{1,0:T(8,128)(2,1)S(1)}, bf16[208,256]{1,0:T(8,128)(2,1)}, u32[]{:S(2)}, u32[]{:S(2)}) collective-permute-start(bf16[208,256]{1,0:T(8,128)(2,1)S(1)} %get-tuple-element.98), channel_id=1, source_target_pairs={{0,3},{1,4},{2,5},{3,6},{4,7},{5,0},{6,1},{7,2},{8,11},{9,12},{10,... | collective-permute-start | bytes 319496 | tf_op jit(solution)/shard_map/ppermute | solution.py:83
  130.2 4.6 %collective-permute-start.7 = (bf16[208,256]{1,0:T(8,128)(2,1)S(1)}, bf16[208,256]{1,0:T(8,128)(2,1)S(1)}, u32[]{:S(2)}, u32[]{:S(2)}) collective-permute-start(bf16[208,256]{1,0:T(8,128)(2,1)S(1)} %get-tuple-element.99), channel_id=1, source_target_pairs={{0,4},{1,5},{2,6},{3,7},{4,0},{5,1},{6,2},{7,3},{8,12},{9,13},{10,... | collective-permute-start | bytes 319496 | tf_op jit(solution)/shard_map/ppermute | solution.py:83
  134.8 4.4 %collective-permute-start.8 = (bf16[208,256]{1,0:T(8,128)(2,1)S(1)}, bf16[208,256]{1,0:T(8,128)(2,1)S(1)}, u32[]{:S(2)}, u32[]{:S(2)}) collective-permute-start(bf16[208,256]{1,0:T(8,128)(2,1)S(1)} %get-tuple-element.100), channel_id=1, source_target_pairs={{0,5},{1,6},{2,7},{3,0},{4,1},{5,2},{6,3},{7,4},{8,13},{9,14},{10,... | collective-permute-start | bytes 319496 | tf_op jit(solution)/shard_map/ppermute | solution.py:83
  139.2 4.3 %collective-permute-start.9 = (bf16[208,256]{1,0:T(8,128)(2,1)S(1)}, bf16[208,256]{1,0:T(8,128)(2,1)S(1)}, u32[]{:S(2)}, u32[]{:S(2)}) collective-permute-start(bf16[208,256]{1,0:T(8,128)(2,1)S(1)} %get-tuple-element.101), channel_id=1, source_target_pairs={{0,6},{1,7},{2,0},{3,1},{4,2},{5,3},{6,4},{7,5},{8,14},{9,15},{10,... | collective-permute-start | bytes 319496 | tf_op jit(solution)/shard_map/ppermute | solution.py:83
  145.5 2.3 %collective-permute-start.5 = (bf16[208,256]{1,0:T(8,128)(2,1)S(1)}, bf16[208,256]{1,0:T(8,128)(2,1)S(1)}, u32[]{:S(2)}, u32[]{:S(2)}) collective-permute-start(bf16[208,256]{1,0:T(8,128)(2,1)S(1)} %get-tuple-element.103), channel_id=1, source_target_pairs={{0,2},{1,3},{2,4},{3,5},{4,6},{5,7},{6,0},{7,1},{8,10},{9,11},{10,... | collective-permute-start | bytes 319496 | tf_op jit(solution)/shard_map/ppermute | solution.py:83
  148.9 10.6 %collective-permute-done.9 = bf16[208,256]{1,0:T(8,128)(2,1)S(1)} collective-permute-done((bf16[208,256]{1,0:T(8,128)(2,1)S(1)}, bf16[208,256]{1,0:T(8,128)(2,1)S(1)}, u32[]{:S(2)}, u32[]{:S(2)}) %collective-permute-start.9) | collective-permute-done | bytes 106528 | tf_op jit(solution)/shard_map/ppermute | solution.py:83
  159.4 2.0 %collective-permute-done.10 = bf16[208,256]{1,0:T(8,128)(2,1)S(1)} collective-permute-done((bf16[208,256]{1,0:T(8,128)(2,1)S(1)}, bf16[208,256]{1,0:T(8,128)(2,1)S(1)}, u32[]{:S(2)}, u32[]{:S(2)}) %collective-permute-start.10) | collective-permute-done | bytes 106528 | tf_op jit(solution)/shard_map/ppermute | solution.py:83
  166.4 10.8 %all-to-all-start.2 = ((f32[64,1,288]{2,1,0:T(1,128)}), f32[64,1,288]{2,1,0:T(1,128)S(1)}, u32[]{:S(2)}, u32[]{:S(2)}) async-start(f32[64,1,288]{2,1,0:T(1,128)} %broadcast_in_dim.8), calls=%async_computation.3 | async-start | bytes 196608 | tf_op jit(solution)/shard_map/all_to_all | solution.py:50
  177.9 9.9 %all-to-all-done.2 = f32[64,1,288]{2,1,0:T(1,128)S(1)} async-done(((f32[64,1,288]{2,1,0:T(1,128)}), f32[64,1,288]{2,1,0:T(1,128)S(1)}, u32[]{:S(2)}, u32[]{:S(2)}) %all-to-all-start.2) | async-done | bytes 73760 | tf_op jit(solution)/shard_map/all_to_all | solution.py:50
  (97 shorter events, 29.6 us)
Async XLA Ops:
  7.2 48.2 %all-gather.3.cloned.1.call-start = ((), (), s32[]{:S(2)}) async-start(), calls=%async_computation.5 | async-start | bytes 1916928 | tf_op jit(solution)/shard_map/all_gather | solution.py:104
  10.5 12.8 %copy-start.9 = (f32[31,192]{1,0:T(8,128)S(1)}, f32[31,192]{1,0:T(8,128)}, u32[]{:S(2)}) copy-start(f32[31,192]{1,0:T(8,128)} %param.10) | copy-start | bytes 71428
  11.6 49.9 %all-to-all-start = ((bf16[64,24,384]{2,1,0:T(8,128)(2,1)}), bf16[64,24,384]{2,1,0:T(8,128)(2,1)S(1)}, u32[]{:S(2)}, u32[]{:S(2)}) async-start(bf16[64,24,384]{2,1,0:T(8,128)(2,1)} %broadcast_in_dim.6), calls=%async_computation | async-start | bytes 2359296 | tf_op jit(solution)/shard_map/all_to_all | solution.py:50
  23.2 140.5 %reduce-scatter.2.cloned.1.call-start = ((), (), s32[]{:S(2)}) async-start(), calls=%async_computation.4 | async-start | bytes 1769472 | tf_op jit(solution)/shard_map/reduce_scatter | solution.py:173
  55.3 4.5 %copy-start = (bf16[1664,512]{1,0:T(8,128)(2,1)S(1)}, bf16[1664,512]{1,0:T(8,128)(2,1)}, u32[]{:S(2)}) copy-start(bf16[1664,512]{1,0:T(8,128)(2,1)} %all-gather.3.cloned.1.call-done) | copy-start | bytes 5111812
  65.1 13.4 %copy-start.8 = (bf16[192,512]{1,0:T(8,128)(2,1)S(1)}, bf16[192,512]{1,0:T(8,128)(2,1)}, u32[]{:S(2)}) copy-start(bf16[192,512]{1,0:T(8,128)(2,1)} %param.11) | copy-start | bytes 589828
  65.3 9.7 %collective-permute-start = (bf16[192,15]{1,0:T(8,128)(2,1)S(1)}, bf16[192,15]{1,0:T(8,128)(2,1)S(1)}, u32[]{:S(2)}, u32[]{:S(2)}) collective-permute-start(bf16[192,15]{1,0:T(8,128)(2,1)S(1)} %get-tuple-element.59), channel_id=1, source_target_pairs={{0,8},{8,16},{16,24},{24,32},{32,40},{40,48},{48,56},{56,64},{64,7... | collective-permute-start | bytes 17288 | tf_op jit(solution)/shard_map/ppermute | solution.py:15
  73.0 5.4 %collective-permute-start.1 = (bf16[192,15]{1,0:T(8,128)(2,1)S(1)}, bf16[192,15]{1,0:T(8,128)(2,1)S(1)}, u32[]{:S(2)}, u32[]{:S(2)}) collective-permute-start(bf16[192,15]{1,0:T(8,128)(2,1)S(1)} %get-tuple-element.60), channel_id=1, source_target_pairs={{8,0},{16,8},{24,16},{32,24},{40,32},{48,40},{56,48},{64,56},{72,6... | collective-permute-start | bytes 17288 | tf_op jit(solution)/shard_map/ppermute | solution.py:17
  85.7 5.3 %collective-permute-start.2 = (bf16[192,15]{1,0:T(8,128)(2,1)S(1)}, bf16[192,15]{1,0:T(8,128)(2,1)S(1)}, u32[]{:S(2)}, u32[]{:S(2)}) collective-permute-start(bf16[192,15]{1,0:T(8,128)(2,1)S(1)} %get-tuple-element.57), channel_id=1, source_target_pairs={{0,8},{8,16},{16,24},{24,32},{32,40},{40,48},{48,56},{56,64},{64,7... | collective-permute-start | bytes 17288 | tf_op jit(solution)/shard_map/ppermute | solution.py:15
  87.6 5.4 %collective-permute-start.3 = (bf16[192,15]{1,0:T(8,128)(2,1)S(1)}, bf16[192,15]{1,0:T(8,128)(2,1)S(1)}, u32[]{:S(2)}, u32[]{:S(2)}) collective-permute-start(bf16[192,15]{1,0:T(8,128)(2,1)S(1)} %get-tuple-element.58), channel_id=1, source_target_pairs={{8,0},{16,8},{24,16},{32,24},{40,32},{48,40},{56,48},{64,56},{72,6... | collective-permute-start | bytes 17288 | tf_op jit(solution)/shard_map/ppermute | solution.py:17
  93.2 4.7 %copy-start.2 = (bf16[64,24,384]{2,1,0:T(8,128)(2,1)S(1)}, bf16[64,24,384]{2,1,0:T(8,128)(2,1)}, u32[]{:S(2)}) copy-start(bf16[64,24,384]{2,1,0:T(8,128)(2,1)} %copy-done.1) | copy-start | bytes 3538948
  97.6 3.8 %copy-start.6 = (bf16[192,512]{1,0:T(8,128)(2,1)}, bf16[192,512]{1,0:T(8,128)(2,1)S(1)}, u32[]{:S(2)}) copy-start(bf16[192,512]{1,0:T(8,128)(2,1)S(1)} %get-tuple-element.43) | copy-start | bytes 589828
  107.7 15.5 %copy-start.10 = (f32[512]{0:T(512)S(1)}, f32[512]{0:T(512)}, u32[]{:S(2)}) copy-start(f32[512]{0:T(512)} %get-tuple-element.7) | copy-start | bytes 6148
  107.7 15.6 %copy-start.4 = (bf16[1536,256]{1,0:T(8,128)(2,1)S(1)}, bf16[1536,256]{1,0:T(8,128)(2,1)}, u32[]{:S(2)}) copy-start(bf16[1536,256]{1,0:T(8,128)(2,1)} %get-tuple-element.49) | copy-start | bytes 2359300
  107.7 55.7 %all-to-all-start.1 = ((bf16[64,25,384]{2,1,0:T(8,128)(2,1)}), bf16[64,25,384]{2,1,0:T(8,128)(2,1)S(1)}, u32[]{:S(2)}, u32[]{:S(2)}) async-start(bf16[64,25,384]{2,1,0:T(8,128)(2,1)} %pad_maximum_fusion), calls=%async_computation.2 | async-start | bytes 3145728 | tf_op jit(solution)/shard_map/all_to_all | solution.py:159
  123.4 40.3 %copy-start.11 = (f32[192]{0:T(256)S(1)}, f32[192]{0:T(256)}, u32[]{:S(2)}) copy-start(f32[192]{0:T(256)} %param.7) | copy-start | bytes 2308
  123.4 20.1 %collective-permute-start.4 = (bf16[208,256]{1,0:T(8,128)(2,1)S(1)}, bf16[208,256]{1,0:T(8,128)(2,1)}, u32[]{:S(2)}, u32[]{:S(2)}) collective-permute-start(bf16[208,256]{1,0:T(8,128)(2,1)S(1)} %get-tuple-element.97), channel_id=1, source_target_pairs={{0,1},{1,2},{2,3},{3,4},{4,5},{5,6},{6,7},{7,0},{8,9},{9,10},{10,1... | collective-permute-start | bytes 319496 | tf_op jit(solution)/shard_map/ppermute | solution.py:83
  126.2 19.3 %collective-permute-start.6 = (bf16[208,256]{1,0:T(8,128)(2,1)S(1)}, bf16[208,256]{1,0:T(8,128)(2,1)}, u32[]{:S(2)}, u32[]{:S(2)}) collective-permute-start(bf16[208,256]{1,0:T(8,128)(2,1)S(1)} %get-tuple-element.98), channel_id=1, source_target_pairs={{0,3},{1,4},{2,5},{3,6},{4,7},{5,0},{6,1},{7,2},{8,11},{9,12},{10,... | collective-permute-start | bytes 319496 | tf_op jit(solution)/shard_map/ppermute | solution.py:83
  130.2 18.7 %collective-permute-start.7 = (bf16[208,256]{1,0:T(8,128)(2,1)S(1)}, bf16[208,256]{1,0:T(8,128)(2,1)S(1)}, u32[]{:S(2)}, u32[]{:S(2)}) collective-permute-start(bf16[208,256]{1,0:T(8,128)(2,1)S(1)} %get-tuple-element.99), channel_id=1, source_target_pairs={{0,4},{1,5},{2,6},{3,7},{4,0},{5,1},{6,2},{7,3},{8,12},{9,13},{10,... | collective-permute-start | bytes 319496 | tf_op jit(solution)/shard_map/ppermute | solution.py:83
  134.8 14.1 %collective-permute-start.8 = (bf16[208,256]{1,0:T(8,128)(2,1)S(1)}, bf16[208,256]{1,0:T(8,128)(2,1)S(1)}, u32[]{:S(2)}, u32[]{:S(2)}) collective-permute-start(bf16[208,256]{1,0:T(8,128)(2,1)S(1)} %get-tuple-element.100), channel_id=1, source_target_pairs={{0,5},{1,6},{2,7},{3,0},{4,1},{5,2},{6,3},{7,4},{8,13},{9,14},{10,... | collective-permute-start | bytes 319496 | tf_op jit(solution)/shard_map/ppermute | solution.py:83
  139.2 20.2 %collective-permute-start.9 = (bf16[208,256]{1,0:T(8,128)(2,1)S(1)}, bf16[208,256]{1,0:T(8,128)(2,1)S(1)}, u32[]{:S(2)}, u32[]{:S(2)}) collective-permute-start(bf16[208,256]{1,0:T(8,128)(2,1)S(1)} %get-tuple-element.101), channel_id=1, source_target_pairs={{0,6},{1,7},{2,0},{3,1},{4,2},{5,3},{6,4},{7,5},{8,14},{9,15},{10,... | collective-permute-start | bytes 319496 | tf_op jit(solution)/shard_map/ppermute | solution.py:83
  143.5 17.9 %collective-permute-start.10 = (bf16[208,256]{1,0:T(8,128)(2,1)S(1)}, bf16[208,256]{1,0:T(8,128)(2,1)S(1)}, u32[]{:S(2)}, u32[]{:S(2)}) collective-permute-start(bf16[208,256]{1,0:T(8,128)(2,1)S(1)} %get-tuple-element.102), channel_id=1, source_target_pairs={{0,7},{1,0},{2,1},{3,2},{4,3},{5,4},{6,5},{7,6},{8,15},{9,8},{10,9... | collective-permute-start | bytes 319496 | tf_op jit(solution)/shard_map/ppermute | solution.py:83
  145.5 16.0 %collective-permute-start.5 = (bf16[208,256]{1,0:T(8,128)(2,1)S(1)}, bf16[208,256]{1,0:T(8,128)(2,1)S(1)}, u32[]{:S(2)}, u32[]{:S(2)}) collective-permute-start(bf16[208,256]{1,0:T(8,128)(2,1)S(1)} %get-tuple-element.103), channel_id=1, source_target_pairs={{0,2},{1,3},{2,4},{3,5},{4,6},{5,7},{6,0},{7,1},{8,10},{9,11},{10,... | collective-permute-start | bytes 319496 | tf_op jit(solution)/shard_map/ppermute | solution.py:83
  166.4 21.4 %all-to-all-start.2 = ((f32[64,1,288]{2,1,0:T(1,128)}), f32[64,1,288]{2,1,0:T(1,128)S(1)}, u32[]{:S(2)}, u32[]{:S(2)}) async-start(f32[64,1,288]{2,1,0:T(1,128)} %broadcast_in_dim.8), calls=%async_computation.3 | async-start | bytes 196608 | tf_op jit(solution)/shard_map/all_to_all | solution.py:50
  (4 other events, 9.5 us)
Sparse Core Ops, SparseCore 0:
  10.1 45.2 all-gather.2
  103.1 57.6 reduce-scatter.1

commit v10 on v9

--- a/solution.py
+++ b/solution.py
@@ -100,9 +100,13 @@
     channel_position = lax.axis_index("ch")
     reach = depth_taps.shape[0] // 2
     gain_rows = jnp.stack(bf16_pieces(input_norm_gain, 3), 0)
-    gain_rows = jnp.pad(gain_rows, ((0, 13), (0, frames - local_cols)))
-    arrived = lax.all_gather(jnp.concatenate([signal, gain_rows], 0), "ch", axis=0)
-    complete_signal = arrived[:, :local_cols].reshape(groups * local_cols, frames)
+    half = frames // 2
+    gain_rows = jnp.pad(gain_rows, ((0, 13), (0, half - local_cols)))
+    arrived = lax.all_gather(jnp.concatenate([signal[:, :half], gain_rows], 0), "ch", axis=0)
+    arrived_late = gather_by_shifts(signal[:, half:], "ch")
+    complete_signal = jnp.concatenate([arrived[:, :local_cols], arrived_late], 2).reshape(
+        groups * local_cols, frames
+    )
     gain_parts = arrived[:, local_cols : local_cols + 3, :local_cols].astype(jnp.float32)
     complete_gain = ((gain_parts[:, 0] + gain_parts[:, 1]) + gain_parts[:, 2]).reshape(-1)
     centered_unit, inverse_deviation = standardize_rows(complete_signal)
@@ -167,7 +171,6 @@
     weighted = normed_f * complete_gain[:, None]
     own_moments = jnp.stack([jnp.sum(weighted, 0), jnp.sum(weighted * centered_unit, 0)], 0)
     moment_rows = jnp.concatenate(bf16_pieces(own_moments, 3), 0)
-    half = frames // 2
     moment_rows = moment_rows.reshape(-1, half)
     moment_rows = jnp.pad(moment_rows, ((0, 16 - moment_rows.shape[0]), (0, 0)))
     early_part = lax.psum_scatter(

time: 197 us -> 231 us (1.17)
  starting transfers between devices: 76.3 us -> 109 us
  waiting for transfers between devices: 60.2 us -> 32.6 us
  blocking collectives: 0 us -> 23 us
  local copies, waits for them, and re-layouts: 6.74 us -> 18.1 us
  other arithmetic: 29.9 us -> 26.5 us
    all_gather x1 -> x0, waiting for transfers between devices: 32 us -> none  [shards(): lax.all_gather(jnp.concatenate([signal, gain_rows], 0), 'ch', axis=0)]
    ppermute x0 -> x7, starting transfers between devices: none -> 30.9 us  [gather_by_shifts(): lax.ppermute(block, axis, [(i, (i - shift) % count) for i in range(count)])]
    all_gather x0 -> x1, blocking collectives: none -> 23 us  [shards(): lax.all_gather(jnp.concatenate([signal[:, :half], gain_rows], 0), 'ch', a...]
    unnamed x29 -> x43, local copies, waits for them, and re-layouts: 2.29 us -> 9.67 us
    ppermute x0 -> x7, waiting for transfers between devices: none -> 5.3 us  [gather_by_shifts(): lax.ppermute(block, axis, [(i, (i - shift) % count) for i in range(count)])]
  transfers between devices with their start and end apart: 16 -> 22, of which waited for: 7 -> 7; matrix products, arithmetic and copies ran while one was open for 8% -> 12% of each run, Pallas kernels for 0% -> 0%
where the time goes in v10:
time: 231 us; the launch traced here: 230 us
  starting transfers between devices  109 us (47%)
  waiting for transfers between devices  32.6 us (14%)
  other arithmetic  26.5 us (11%)
  blocking collectives  23 us (10%)
  local copies, waits for them, and re-layouts  18.1 us (8%)
  between operations  14.7 us (6%)
  matrix products  6.34 us (3%)
    ppermute x7, starting transfers between devices, gather_by_shifts(): lax.ppermute(block, axis, [(i, (i - shift) % count) for i in range(count)])  30.9 us
    ppermute x7, starting transfers between devices, reduce_by_shifts(): lax.ppermute(outgoing, axis, [(i, (i + shift) % count) for i in range(cou...  23.6 us
    all_gather x1, blocking collectives, shards(): lax.all_gather(jnp.concatenate([signal[:, :half], gain_rows], 0), 'ch', a...  23 us
    all_to_all x2, starting transfers between devices, gather_by_exchange(): return lax.all_to_all(copies, axis, 0, 0, tiled=False)  22.9 us
    all_to_all x1, starting transfers between devices, shards(): lax.all_to_all(outgoing, 'seq', 0, 0, tiled=False).astype(jnp.float32)  15.6 us
    ppermute x7, waiting for transfers between devices, reduce_by_shifts(): lax.ppermute(outgoing, axis, [(i, (i + shift) % count) for i in range(cou...  13.7 us
    ppermute x2, starting transfers between devices, extended(): lax.ppermute(tail, axis, [(i, (i + 1) % count) for i in range(ends)])  11.2 us
    all_to_all x2, waiting for transfers between devices, gather_by_exchange(): return lax.all_to_all(copies, axis, 0, 0, tiled=False)  9.88 us
  transfers between devices with their start and end apart: 22, of which 7 were waited for; matrix products, arithmetic and copies ran while one was open for 12% of the time, Pallas kernels for 0%

profile of v10, /device:TPU:1, one launch (start us, length us, event | category | flops | bytes accessed | tf_op | source)
XLA Modules:
  0.0 229.8 jit_solution(3832156412232403613)
XLA Ops:
  8.1 6.6 %collective-permute-start.5 = (bf16[192,256]{1,0:T(8,128)(2,1)S(1)}, bf16[192,256]{1,0:T(8,128)(2,1)S(1)}, u32[]{:S(2)}, u32[]{:S(2)}) collective-permute-start(bf16[192,256]{1,0:T(8,128)(2,1)S(1)} %get-tuple-element.60), channel_id=1, source_target_pairs={{0,2},{1,3},{2,4},{3,5},{4,6},{5,7},{6,0},{7,1},{8,10},{9,11},{10,... | collective-permute-start | bytes 294920 | tf_op jit(solution)/shard_map/ppermute | solution.py:69
  14.8 7.9 %collective-permute-start.4 = (bf16[192,256]{1,0:T(8,128)(2,1)S(1)}, bf16[192,256]{1,0:T(8,128)(2,1)S(1)}, u32[]{:S(2)}, u32[]{:S(2)}) collective-permute-start(bf16[192,256]{1,0:T(8,128)(2,1)S(1)} %get-tuple-element.60), channel_id=1, source_target_pairs={{0,3},{1,4},{2,5},{3,6},{4,7},{5,0},{6,1},{7,2},{8,11},{9,12},{10,... | collective-permute-start | bytes 294920 | tf_op jit(solution)/shard_map/ppermute | solution.py:69
  22.7 3.7 %collective-permute-start.3 = (bf16[192,256]{1,0:T(8,128)(2,1)S(1)}, bf16[192,256]{1,0:T(8,128)(2,1)S(1)}, u32[]{:S(2)}, u32[]{:S(2)}) collective-permute-start(bf16[192,256]{1,0:T(8,128)(2,1)S(1)} %get-tuple-element.60), channel_id=1, source_target_pairs={{0,4},{1,5},{2,6},{3,7},{4,0},{5,1},{6,2},{7,3},{8,12},{9,13},{10,... | collective-permute-start | bytes 294920 | tf_op jit(solution)/shard_map/ppermute | solution.py:69
  26.5 5.5 %collective-permute-start.2 = (bf16[192,256]{1,0:T(8,128)(2,1)S(1)}, bf16[192,256]{1,0:T(8,128)(2,1)S(1)}, u32[]{:S(2)}, u32[]{:S(2)}) collective-permute-start(bf16[192,256]{1,0:T(8,128)(2,1)S(1)} %get-tuple-element.60), channel_id=1, source_target_pairs={{0,5},{1,6},{2,7},{3,0},{4,1},{5,2},{6,3},{7,4},{8,13},{9,14},{10,... | collective-permute-start | bytes 294920 | tf_op jit(solution)/shard_map/ppermute | solution.py:69
  36.0 12.4 %all-to-all-start = ((bf16[64,24,384]{2,1,0:T(8,128)(2,1)}), bf16[64,24,384]{2,1,0:T(8,128)(2,1)}, u32[]{:S(2)}, u32[]{:S(2)}) async-start(bf16[64,24,384]{2,1,0:T(8,128)(2,1)} %broadcast_in_dim.6), calls=%async_computation | async-start | bytes 2359296 | tf_op jit(solution)/shard_map/all_to_all | solution.py:50
  48.6 23.0 %all-gather = bf16[1664,256]{1,0:T(8,128)(2,1)S(1)} all-gather(bf16[208,256]{1,0:T(8,128)(2,1)S(1)} %pad_maximum_fusion.12), channel_id=2, replica_groups=mesh['seq'=64,'ch'=8] {'ch'}, dimensions={0}, use_global_device_ids=true | all-gather | bytes 958464 | tf_op jit(solution)/shard_map/all_gather | solution.py:105
  72.4 3.1 %collective-permute-start.1 = (bf16[192,256]{1,0:T(8,128)(2,1)S(1)}, bf16[192,256]{1,0:T(8,128)(2,1)S(1)}, u32[]{:S(2)}, u32[]{:S(2)}) collective-permute-start(bf16[192,256]{1,0:T(8,128)(2,1)S(1)} %get-tuple-element.60), channel_id=1, source_target_pairs={{0,6},{1,7},{2,0},{3,1},{4,2},{5,3},{6,4},{7,5},{8,14},{9,15},{10,... | collective-permute-start | bytes 294920 | tf_op jit(solution)/shard_map/ppermute | solution.py:69
  76.2 3.9 %collective-permute-done.1 = bf16[192,256]{1,0:T(8,128)(2,1)S(1)} collective-permute-done((bf16[192,256]{1,0:T(8,128)(2,1)S(1)}, bf16[192,256]{1,0:T(8,128)(2,1)S(1)}, u32[]{:S(2)}, u32[]{:S(2)}) %collective-permute-start.1) | collective-permute-done | bytes 98336 | tf_op jit(solution)/shard_map/ppermute | solution.py:69
  96.7 9.0 %collective-permute-start.7 = (bf16[192,15]{1,0:T(8,128)(2,1)S(1)}, bf16[192,15]{1,0:T(8,128)(2,1)S(1)}, u32[]{:S(2)}, u32[]{:S(2)}) collective-permute-start(bf16[192,15]{1,0:T(8,128)(2,1)S(1)} %get-tuple-element.57), channel_id=1, source_target_pairs={{0,8},{8,16},{16,24},{24,32},{32,40},{40,48},{48,56},{56,64},{64,7... | collective-permute-start | bytes 17288 | tf_op jit(solution)/shard_map/ppermute | solution.py:15
  111.4 5.0 %fusion.41 = (f32[192]{0:T(256)S(1)}, f32[192]{0:T(256)S(1)}, f32[192]{0:T(256)S(1)}, f32[192]{0:T(256)S(1)}, f32[192]{0:T(256)S(1)}, /*index=5*/f32[192]{0:T(25...) fusion(f32[192,542]{1,0:T(8,128)S(1)} %maximum_convert_fusion.1, ...), kind=kLoop, calls=%fused_computation.84 | loop fusion | flops 10613376 | bytes 13013760 | tf_op jit(solution)/shard_map/reduce_sum | solution.py:139
  124.0 2.4 %collective-permute-done.10 = bf16[192,15]{1,0:T(8,128)(2,1)S(1)} collective-permute-done((bf16[192,15]{1,0:T(8,128)(2,1)S(1)}, bf16[192,15]{1,0:T(8,128)(2,1)S(1)}, u32[]{:S(2)}, u32[]{:S(2)}) %collective-permute-start.10) | collective-permute-done | bytes 5792 | tf_op jit(solution)/shard_map/ppermute | solution.py:17
  126.5 4.4 %multiply_convert_fusion.6 = (bf16[192,512]{1,0:T(8,128)(2,1)S(1)}, f32[192,512]{1,0:T(8,128)S(1)}) fusion(f32[384,512]{1,0:T(8,128)S(1)} %fusion.2, f32[192,542]{1,0:T(8,128)S(1)} %maximum_convert_fusion.2, f32[192]{0:T(256)S(1)} %bitcast.169, f32[192]{0:T(256)S(1)} %bitcast.145, f32[192]{0:T(256)S(1)} %bitcast.163, f32[192]{0:T(256)S(1)} %bitcast.161, ...), kind=kLoop, calls=%fused_computation.155 | loop fusion | flops 6488064 | bytes 13196544 | tf_op jit(solution)/shard_map/convert_element_type | solution.py:141
  131.1 3.2 %fusion.1 = (f32[512]{0:T(512)}, f32[512]{0:T(512)}, f32[1536,512]{1,0:T(8,128)S(1)}, bf16[1536,512]{1,0:T(8,128)(2,1)S(1)}) fusion(f32[1536]{0:T(1024)S(1)} %add.379, f32[512]{0:T(512)S(1)} %add_rsqrt_fusion, f32[512]{0:T(512)S(1)} %broadcast_multiply_fusion, f32[8,192,512]{2,1,0:T(8,128)S(1)} %copy-done, bf16[1536,384]{1,0:T(8,128)(2,1)} %bitcast.1, ...), kind=kOutput, calls=%fused_computation.37 | convolution fusion | flops 611056640 | bytes 9451520 | tf_op jit(solution)/shard_map/dot_general | solution.py:150
  138.3 15.6 %all-to-all-start.1 = ((bf16[64,25,384]{2,1,0:T(8,128)(2,1)}), bf16[64,25,384]{2,1,0:T(8,128)(2,1)}, u32[]{:S(2)}, u32[]{:S(2)}) async-start(bf16[64,25,384]{2,1,0:T(8,128)(2,1)} %pad_maximum_fusion), calls=%async_computation.2 | async-start | bytes 3145728 | tf_op jit(solution)/shard_map/all_to_all | solution.py:163
  158.1 4.2 %collective-permute-start.13 = (bf16[208,256]{1,0:T(8,128)(2,1)}, bf16[208,256]{1,0:T(8,128)(2,1)}, u32[]{:S(2)}, u32[]{:S(2)}) collective-permute-start(bf16[208,256]{1,0:T(8,128)(2,1)} %get-tuple-element.98), channel_id=1, source_target_pairs={{0,3},{1,4},{2,5},{3,6},{4,7},{5,0},{6,1},{7,2},{8,11},{9,12},{10,... | collective-permute-start | bytes 319496 | tf_op jit(solution)/shard_map/ppermute | solution.py:83
  162.2 5.3 %collective-permute-start.14 = (bf16[208,256]{1,0:T(8,128)(2,1)}, bf16[208,256]{1,0:T(8,128)(2,1)S(1)}, u32[]{:S(2)}, u32[]{:S(2)}) collective-permute-start(bf16[208,256]{1,0:T(8,128)(2,1)} %get-tuple-element.99), channel_id=1, source_target_pairs={{0,4},{1,5},{2,6},{3,7},{4,0},{5,1},{6,2},{7,3},{8,12},{9,13},{10,... | collective-permute-start | bytes 319496 | tf_op jit(solution)/shard_map/ppermute | solution.py:83
  167.5 2.7 %collective-permute-start.15 = (bf16[208,256]{1,0:T(8,128)(2,1)}, bf16[208,256]{1,0:T(8,128)(2,1)S(1)}, u32[]{:S(2)}, u32[]{:S(2)}) collective-permute-start(bf16[208,256]{1,0:T(8,128)(2,1)} %get-tuple-element.100), channel_id=1, source_target_pairs={{0,5},{1,6},{2,7},{3,0},{4,1},{5,2},{6,3},{7,4},{8,13},{9,14},{10,... | collective-permute-start | bytes 319496 | tf_op jit(solution)/shard_map/ppermute | solution.py:83
  170.3 3.6 %collective-permute-start.16 = (bf16[208,256]{1,0:T(8,128)(2,1)}, bf16[208,256]{1,0:T(8,128)(2,1)S(1)}, u32[]{:S(2)}, u32[]{:S(2)}) collective-permute-start(bf16[208,256]{1,0:T(8,128)(2,1)} %get-tuple-element.101), channel_id=1, source_target_pairs={{0,6},{1,7},{2,0},{3,1},{4,2},{5,3},{6,4},{7,5},{8,14},{9,15},{10,... | collective-permute-start | bytes 319496 | tf_op jit(solution)/shard_map/ppermute | solution.py:83
  173.8 3.4 %collective-permute-start.17 = (bf16[208,256]{1,0:T(8,128)(2,1)}, bf16[208,256]{1,0:T(8,128)(2,1)S(1)}, u32[]{:S(2)}, u32[]{:S(2)}) collective-permute-start(bf16[208,256]{1,0:T(8,128)(2,1)} %get-tuple-element.102), channel_id=1, source_target_pairs={{0,7},{1,0},{2,1},{3,2},{4,3},{5,4},{6,5},{7,6},{8,15},{9,8},{10,9... | collective-permute-start | bytes 319496 | tf_op jit(solution)/shard_map/ppermute | solution.py:83
  177.2 2.6 %collective-permute-start.12 = (bf16[208,256]{1,0:T(8,128)(2,1)}, bf16[208,256]{1,0:T(8,128)(2,1)S(1)}, u32[]{:S(2)}, u32[]{:S(2)}) collective-permute-start(bf16[208,256]{1,0:T(8,128)(2,1)} %get-tuple-element.103), channel_id=1, source_target_pairs={{0,2},{1,3},{2,4},{3,5},{4,6},{5,7},{6,0},{7,1},{8,10},{9,11},{10,... | collective-permute-start | bytes 319496 | tf_op jit(solution)/shard_map/ppermute | solution.py:83
  180.7 10.1 %collective-permute-done.16 = bf16[208,256]{1,0:T(8,128)(2,1)S(1)} collective-permute-done((bf16[208,256]{1,0:T(8,128)(2,1)}, bf16[208,256]{1,0:T(8,128)(2,1)S(1)}, u32[]{:S(2)}, u32[]{:S(2)}) %collective-permute-start.16) | collective-permute-done | bytes 106528 | tf_op jit(solution)/shard_map/ppermute | solution.py:83
  190.8 3.6 %collective-permute-done.17 = bf16[208,256]{1,0:T(8,128)(2,1)S(1)} collective-permute-done((bf16[208,256]{1,0:T(8,128)(2,1)}, bf16[208,256]{1,0:T(8,128)(2,1)S(1)}, u32[]{:S(2)}, u32[]{:S(2)}) %collective-permute-start.17) | collective-permute-done | bytes 106528 | tf_op jit(solution)/shard_map/ppermute | solution.py:83
  200.5 10.5 %all-to-all-start.2 = ((f32[64,1,288]{2,1,0:T(1,128)}), f32[64,1,288]{2,1,0:T(1,128)S(1)}, u32[]{:S(2)}, u32[]{:S(2)}) async-start(f32[64,1,288]{2,1,0:T(1,128)} %broadcast_in_dim.8), calls=%async_computation.3 | async-start | bytes 196608 | tf_op jit(solution)/shard_map/all_to_all | solution.py:50
  211.7 9.9 %all-to-all-done.2 = f32[64,1,288]{2,1,0:T(1,128)S(1)} async-done(((f32[64,1,288]{2,1,0:T(1,128)}), f32[64,1,288]{2,1,0:T(1,128)S(1)}, u32[]{:S(2)}, u32[]{:S(2)}) %all-to-all-start.2) | async-done | bytes 73760 | tf_op jit(solution)/shard_map/all_to_all | solution.py:50
  (127 shorter events, 53.8 us)
Async XLA Ops:
  8.1 76.4 %collective-permute-start.5 = (bf16[192,256]{1,0:T(8,128)(2,1)S(1)}, bf16[192,256]{1,0:T(8,128)(2,1)S(1)}, u32[]{:S(2)}, u32[]{:S(2)}) collective-permute-start(bf16[192,256]{1,0:T(8,128)(2,1)S(1)} %get-tuple-element.60), channel_id=1, source_target_pairs={{0,2},{1,3},{2,4},{3,5},{4,6},{5,7},{6,0},{7,1},{8,10},{9,11},{10,... | collective-permute-start | bytes 294920 | tf_op jit(solution)/shard_map/ppermute | solution.py:69
  14.8 69.1 %collective-permute-start.4 = (bf16[192,256]{1,0:T(8,128)(2,1)S(1)}, bf16[192,256]{1,0:T(8,128)(2,1)S(1)}, u32[]{:S(2)}, u32[]{:S(2)}) collective-permute-start(bf16[192,256]{1,0:T(8,128)(2,1)S(1)} %get-tuple-element.60), channel_id=1, source_target_pairs={{0,3},{1,4},{2,5},{3,6},{4,7},{5,0},{6,1},{7,2},{8,11},{9,12},{10,... | collective-permute-start | bytes 294920 | tf_op jit(solution)/shard_map/ppermute | solution.py:69
  22.7 60.5 %collective-permute-start.3 = (bf16[192,256]{1,0:T(8,128)(2,1)S(1)}, bf16[192,256]{1,0:T(8,128)(2,1)S(1)}, u32[]{:S(2)}, u32[]{:S(2)}) collective-permute-start(bf16[192,256]{1,0:T(8,128)(2,1)S(1)} %get-tuple-element.60), channel_id=1, source_target_pairs={{0,4},{1,5},{2,6},{3,7},{4,0},{5,1},{6,2},{7,3},{8,12},{9,13},{10,... | collective-permute-start | bytes 294920 | tf_op jit(solution)/shard_map/ppermute | solution.py:69
  26.5 56.1 %collective-permute-start.2 = (bf16[192,256]{1,0:T(8,128)(2,1)S(1)}, bf16[192,256]{1,0:T(8,128)(2,1)S(1)}, u32[]{:S(2)}, u32[]{:S(2)}) collective-permute-start(bf16[192,256]{1,0:T(8,128)(2,1)S(1)} %get-tuple-element.60), channel_id=1, source_target_pairs={{0,5},{1,6},{2,7},{3,0},{4,1},{5,2},{6,3},{7,4},{8,13},{9,14},{10,... | collective-permute-start | bytes 294920 | tf_op jit(solution)/shard_map/ppermute | solution.py:69
  31.9 40.5 %collective-permute-start = (bf16[192,256]{1,0:T(8,128)(2,1)S(1)}, bf16[192,256]{1,0:T(8,128)(2,1)S(1)}, u32[]{:S(2)}, u32[]{:S(2)}) collective-permute-start(bf16[192,256]{1,0:T(8,128)(2,1)S(1)} %get-tuple-element.60), channel_id=1, source_target_pairs={{0,7},{1,0},{2,1},{3,2},{4,3},{5,4},{6,5},{7,6},{8,15},{9,8},{10,9... | collective-permute-start | bytes 294920 | tf_op jit(solution)/shard_map/ppermute | solution.py:69
  36.0 58.3 %all-to-all-start = ((bf16[64,24,384]{2,1,0:T(8,128)(2,1)}), bf16[64,24,384]{2,1,0:T(8,128)(2,1)}, u32[]{:S(2)}, u32[]{:S(2)}) async-start(bf16[64,24,384]{2,1,0:T(8,128)(2,1)} %broadcast_in_dim.6), calls=%async_computation | async-start | bytes 2359296 | tf_op jit(solution)/shard_map/all_to_all | solution.py:50
  48.4 149.6 %reduce-scatter.2.cloned.1.call-start = ((), (), s32[]{:S(2)}) async-start(), calls=%async_computation.4 | async-start | bytes 1769472 | tf_op jit(solution)/shard_map/reduce_scatter | solution.py:176
  72.4 7.6 %collective-permute-start.1 = (bf16[192,256]{1,0:T(8,128)(2,1)S(1)}, bf16[192,256]{1,0:T(8,128)(2,1)S(1)}, u32[]{:S(2)}, u32[]{:S(2)}) collective-permute-start(bf16[192,256]{1,0:T(8,128)(2,1)S(1)} %get-tuple-element.60), channel_id=1, source_target_pairs={{0,6},{1,7},{2,0},{3,1},{4,2},{5,3},{6,4},{7,5},{8,14},{9,15},{10,... | collective-permute-start | bytes 294920 | tf_op jit(solution)/shard_map/ppermute | solution.py:69
  80.0 6.6 %collective-permute-start.6 = (bf16[192,256]{1,0:T(8,128)(2,1)S(1)}, bf16[192,256]{1,0:T(8,128)(2,1)S(1)}, u32[]{:S(2)}, u32[]{:S(2)}) collective-permute-start(bf16[192,256]{1,0:T(8,128)(2,1)S(1)} %get-tuple-element.60), channel_id=1, source_target_pairs={{0,1},{1,2},{2,3},{3,4},{4,5},{5,6},{6,7},{7,0},{8,9},{9,10},{10,1... | collective-permute-start | bytes 294920 | tf_op jit(solution)/shard_map/ppermute | solution.py:69
  94.3 36.8 %copy-start.6 = (f32[512]{0:T(512)}, f32[512]{0:T(512)S(1)}, u32[]{:S(2)}) copy-start(f32[512]{0:T(512)S(1)} %add_rsqrt_fusion) | copy-start | bytes 6148
  96.7 13.1 %collective-permute-start.7 = (bf16[192,15]{1,0:T(8,128)(2,1)S(1)}, bf16[192,15]{1,0:T(8,128)(2,1)S(1)}, u32[]{:S(2)}, u32[]{:S(2)}) collective-permute-start(bf16[192,15]{1,0:T(8,128)(2,1)S(1)} %get-tuple-element.57), channel_id=1, source_target_pairs={{0,8},{8,16},{16,24},{24,32},{32,40},{40,48},{48,56},{56,64},{64,7... | collective-permute-start | bytes 17288 | tf_op jit(solution)/shard_map/ppermute | solution.py:15
  105.7 5.5 %collective-permute-start.8 = (bf16[192,15]{1,0:T(8,128)(2,1)S(1)}, bf16[192,15]{1,0:T(8,128)(2,1)S(1)}, u32[]{:S(2)}, u32[]{:S(2)}) collective-permute-start(bf16[192,15]{1,0:T(8,128)(2,1)S(1)} %get-tuple-element.58), channel_id=1, source_target_pairs={{8,0},{16,8},{24,16},{32,24},{40,32},{48,40},{56,48},{64,56},{72,6... | collective-permute-start | bytes 17288 | tf_op jit(solution)/shard_map/ppermute | solution.py:17
  118.6 5.3 %collective-permute-start.9 = (bf16[192,15]{1,0:T(8,128)(2,1)S(1)}, bf16[192,15]{1,0:T(8,128)(2,1)S(1)}, u32[]{:S(2)}, u32[]{:S(2)}) collective-permute-start(bf16[192,15]{1,0:T(8,128)(2,1)S(1)} %get-tuple-element.55), channel_id=1, source_target_pairs={{0,8},{8,16},{16,24},{24,32},{32,40},{40,48},{48,56},{56,64},{64,7... | collective-permute-start | bytes 17288 | tf_op jit(solution)/shard_map/ppermute | solution.py:15
  120.9 5.4 %collective-permute-start.10 = (bf16[192,15]{1,0:T(8,128)(2,1)S(1)}, bf16[192,15]{1,0:T(8,128)(2,1)S(1)}, u32[]{:S(2)}, u32[]{:S(2)}) collective-permute-start(bf16[192,15]{1,0:T(8,128)(2,1)S(1)} %get-tuple-element.56), channel_id=1, source_target_pairs={{8,0},{16,8},{24,16},{32,24},{40,32},{48,40},{56,48},{64,56},{72,6... | collective-permute-start | bytes 17288 | tf_op jit(solution)/shard_map/ppermute | solution.py:17
  138.3 58.0 %all-to-all-start.1 = ((bf16[64,25,384]{2,1,0:T(8,128)(2,1)}), bf16[64,25,384]{2,1,0:T(8,128)(2,1)}, u32[]{:S(2)}, u32[]{:S(2)}) async-start(bf16[64,25,384]{2,1,0:T(8,128)(2,1)} %pad_maximum_fusion), calls=%async_computation.2 | async-start | bytes 3145728 | tf_op jit(solution)/shard_map/all_to_all | solution.py:163
  153.8 26.0 %copy-start.1 = (f32[192,512]{1,0:T(8,128)S(1)}, f32[192,512]{1,0:T(8,128)}, u32[]{:S(2)}) copy-start(f32[192,512]{1,0:T(8,128)} %get-tuple-element.40) | copy-start | bytes 1179652
  156.2 17.7 %collective-permute-start.11 = (bf16[208,256]{1,0:T(8,128)(2,1)}, bf16[208,256]{1,0:T(8,128)(2,1)}, u32[]{:S(2)}, u32[]{:S(2)}) collective-permute-start(bf16[208,256]{1,0:T(8,128)(2,1)} %get-tuple-element.97), channel_id=1, source_target_pairs={{0,1},{1,2},{2,3},{3,4},{4,5},{5,6},{6,7},{7,0},{8,9},{9,10},{10,1... | collective-permute-start | bytes 319496 | tf_op jit(solution)/shard_map/ppermute | solution.py:83
  158.1 19.2 %collective-permute-start.13 = (bf16[208,256]{1,0:T(8,128)(2,1)}, bf16[208,256]{1,0:T(8,128)(2,1)}, u32[]{:S(2)}, u32[]{:S(2)}) collective-permute-start(bf16[208,256]{1,0:T(8,128)(2,1)} %get-tuple-element.98), channel_id=1, source_target_pairs={{0,3},{1,4},{2,5},{3,6},{4,7},{5,0},{6,1},{7,2},{8,11},{9,12},{10,... | collective-permute-start | bytes 319496 | tf_op jit(solution)/shard_map/ppermute | solution.py:83
  162.2 18.4 %collective-permute-start.14 = (bf16[208,256]{1,0:T(8,128)(2,1)}, bf16[208,256]{1,0:T(8,128)(2,1)S(1)}, u32[]{:S(2)}, u32[]{:S(2)}) collective-permute-start(bf16[208,256]{1,0:T(8,128)(2,1)} %get-tuple-element.99), channel_id=1, source_target_pairs={{0,4},{1,5},{2,6},{3,7},{4,0},{5,1},{6,2},{7,3},{8,12},{9,13},{10,... | collective-permute-start | bytes 319496 | tf_op jit(solution)/shard_map/ppermute | solution.py:83
  167.5 13.1 %collective-permute-start.15 = (bf16[208,256]{1,0:T(8,128)(2,1)}, bf16[208,256]{1,0:T(8,128)(2,1)S(1)}, u32[]{:S(2)}, u32[]{:S(2)}) collective-permute-start(bf16[208,256]{1,0:T(8,128)(2,1)} %get-tuple-element.100), channel_id=1, source_target_pairs={{0,5},{1,6},{2,7},{3,0},{4,1},{5,2},{6,3},{7,4},{8,13},{9,14},{10,... | collective-permute-start | bytes 319496 | tf_op jit(solution)/shard_map/ppermute | solution.py:83
  170.3 20.5 %collective-permute-start.16 = (bf16[208,256]{1,0:T(8,128)(2,1)}, bf16[208,256]{1,0:T(8,128)(2,1)S(1)}, u32[]{:S(2)}, u32[]{:S(2)}) collective-permute-start(bf16[208,256]{1,0:T(8,128)(2,1)} %get-tuple-element.101), channel_id=1, source_target_pairs={{0,6},{1,7},{2,0},{3,1},{4,2},{5,3},{6,4},{7,5},{8,14},{9,15},{10,... | collective-permute-start | bytes 319496 | tf_op jit(solution)/shard_map/ppermute | solution.py:83
  173.8 20.5 %collective-permute-start.17 = (bf16[208,256]{1,0:T(8,128)(2,1)}, bf16[208,256]{1,0:T(8,128)(2,1)S(1)}, u32[]{:S(2)}, u32[]{:S(2)}) collective-permute-start(bf16[208,256]{1,0:T(8,128)(2,1)} %get-tuple-element.102), channel_id=1, source_target_pairs={{0,7},{1,0},{2,1},{3,2},{4,3},{5,4},{6,5},{7,6},{8,15},{9,8},{10,9... | collective-permute-start | bytes 319496 | tf_op jit(solution)/shard_map/ppermute | solution.py:83
  177.2 17.1 %collective-permute-start.12 = (bf16[208,256]{1,0:T(8,128)(2,1)}, bf16[208,256]{1,0:T(8,128)(2,1)S(1)}, u32[]{:S(2)}, u32[]{:S(2)}) collective-permute-start(bf16[208,256]{1,0:T(8,128)(2,1)} %get-tuple-element.103), channel_id=1, source_target_pairs={{0,2},{1,3},{2,4},{3,5},{4,6},{5,7},{6,0},{7,1},{8,10},{9,11},{10,... | collective-permute-start | bytes 319496 | tf_op jit(solution)/shard_map/ppermute | solution.py:83
  200.5 21.1 %all-to-all-start.2 = ((f32[64,1,288]{2,1,0:T(1,128)}), f32[64,1,288]{2,1,0:T(1,128)S(1)}, u32[]{:S(2)}, u32[]{:S(2)}) async-start(f32[64,1,288]{2,1,0:T(1,128)} %broadcast_in_dim.8), calls=%async_computation.3 | async-start | bytes 196608 | tf_op jit(solution)/shard_map/all_to_all | solution.py:50
  (10 other events, 129.5 us)
Sparse Core Ops, SparseCore 0:
  136.0 56.7 reduce-scatter.1

commit v11 on v9

--- a/solution.py
+++ b/solution.py
@@ -99,6 +99,8 @@
     blocks = lax.axis_size("seq")
     channel_position = lax.axis_index("ch")
     reach = depth_taps.shape[0] // 2
+    span = frames
+    cotangent_wide = extended(cotangent, (("seq", 1),), reach)
     gain_rows = jnp.stack(bf16_pieces(input_norm_gain, 3), 0)
     gain_rows = jnp.pad(gain_rows, ((0, 13), (0, frames - local_cols)))
     arrived = lax.all_gather(jnp.concatenate([signal, gain_rows], 0), "ch", axis=0)
@@ -119,18 +121,21 @@
     gate = mixed[local_cols:]
     sig_gate = jax.nn.sigmoid(gate)
     glued = (value * sig_gate).astype(jnp.bfloat16)
-    glued_pad = extended(glued, (("seq", 1),), reach).astype(jnp.float32)
-    span = glued.shape[1]
+    glued_wide = extended(glued, (("seq", 1),), 2 * reach).astype(jnp.float32)
+    glued_pad = glued_wide[:, reach : reach + span + 2 * reach]
     taps_count = depth_taps.shape[0]
-    pre = shifted_sum(glued_pad, depth_taps, span)
-    sig_pre = jax.nn.sigmoid(pre)
+    pre_wide = shifted_sum(glued_wide, depth_taps, span + 2 * reach)
+    sig_pre_wide = jax.nn.sigmoid(pre_wide)
+    pre = pre_wide[:, reach : reach + span]
+    sig_pre = sig_pre_wide[:, reach : reach + span]
     output = (pre * sig_pre).astype(jnp.bfloat16)
-    grad_pre = (cotangent.astype(jnp.float32) * sig_pre * (1.0 + pre * (1.0 - sig_pre))).astype(
-        jnp.bfloat16
-    )
-    grad_pre_f = grad_pre.astype(jnp.float32)
-    grad_pad = extended(grad_pre, (("seq", 1),), reach).astype(jnp.float32)
-    grad_glued = shifted_sum(grad_pad, depth_taps[::-1], span)
+    grad_pad = (
+        cotangent_wide.astype(jnp.float32)
+        * sig_pre_wide
+        * (1.0 + pre_wide * (1.0 - sig_pre_wide))
+    ).astype(jnp.bfloat16)
+    grad_pre_f = grad_pad[:, reach : reach + span].astype(jnp.float32)
+    grad_glued = shifted_sum(grad_pad.astype(jnp.float32), depth_taps[::-1], span)
     tap_partial = jnp.stack(
         [jnp.sum(glued_pad[:, k : k + span] * grad_pre_f, 1) for k in range(taps_count)], 0
     )

time: 197 us -> 197 us (level)
  other arithmetic: 29.9 us -> 36.4 us
  waiting for transfers between devices: 60.2 us -> 54.4 us
  local copies, waits for them, and re-layouts: 6.74 us -> 10.1 us
  matrix products: 8.23 us -> 4.98 us
    convert_element_type x2, other arithmetic: 0.29 us -> 6.95 us  [the longest x1 6.81 us: shards(): grad_pad.astype(jnp.float32)]
    all_gather x1, waiting for transfers between devices: 32 us -> 25.8 us  [shards(): lax.all_gather(jnp.concatenate([signal, gain_rows], 0), 'ch', axis=0)]
    all_to_all x1, starting transfers between devices: 15.4 us -> 12.2 us  [shards(): lax.all_to_all(outgoing, 'seq', 0, 0, tiled=False).astype(jnp.float32)]
    reduce_scatter x1, waiting for transfers between devices: 0.01 us -> 2.89 us  [shards(): lax.psum_scatter(normed_term[:, :half].astype(jnp.float32), 'ch', scatter...]
    ppermute x2, waiting for transfers between devices: 5.39 us -> 2.59 us  [extended(): lax.ppermute(head, axis, [((i + 1) % count, i) for i in range(ends)])]
    another operation x1, local copies, waits for them, and re-layouts: 0.1 us -> 2.81 us  [shards(): jnp.stack([jnp.sum(glued_pad[:, k:k + span] * grad_pre_f, 1) for k in ran...]
    dot_general x1, matrix products: 3.59 us -> 1.39 us  [shards(): jnp.dot(gathered, grad_both, preferred_element_type=jnp.float32)]
    reduce_sum x2 -> x3, other arithmetic: 6.84 us -> 7.32 us  [shards(): jnp.sum(glued_pad[:, k:k + span] * grad_pre_f, 1)]
  transfers between devices with their start and end apart: 16 -> 16, of which waited for: 7 -> 6; matrix products, arithmetic and copies ran while one was open for 8% -> 8% of each run, Pallas kernels for 0% -> 0%
where the time goes in v11:
time: 197 us; the launch traced here: 196 us
  starting transfers between devices  76 us (39%)
  waiting for transfers between devices  54.4 us (28%)
  other arithmetic  36.4 us (18%)
  between operations  14.6 us (7%)
  local copies, waits for them, and re-layouts  10.1 us (5%)
  matrix products  4.98 us (3%)
    all_gather x1, waiting for transfers between devices, shards(): lax.all_gather(jnp.concatenate([signal, gain_rows], 0), 'ch', axis=0)  25.8 us
    ppermute x7, starting transfers between devices, reduce_by_shifts(): lax.ppermute(outgoing, axis, [(i, (i + shift) % count) for i in range(cou...  24.3 us
    all_to_all x2, starting transfers between devices, gather_by_exchange(): return lax.all_to_all(copies, axis, 0, 0, tiled=False)  24.3 us
    ppermute x7, waiting for transfers between devices, reduce_by_shifts(): lax.ppermute(outgoing, axis, [(i, (i + shift) % count) for i in range(cou...  13.2 us
    all_to_all x1, starting transfers between devices, shards(): lax.all_to_all(outgoing, 'seq', 0, 0, tiled=False).astype(jnp.float32)  12.2 us
    ppermute x2, starting transfers between devices, extended(): lax.ppermute(tail, axis, [(i, (i + 1) % count) for i in range(ends)])  11.2 us
    all_to_all x2, waiting for transfers between devices, gather_by_exchange(): return lax.all_to_all(copies, axis, 0, 0, tiled=False)  9.88 us
    reduce_sum x3, other arithmetic, shards(): jnp.sum(glued_pad[:, k:k + span] * grad_pre_f, 1)  7.32 us
  transfers between devices with their start and end apart: 16, of which 6 were waited for; matrix products, arithmetic and copies ran while one was open for 8% of the time, Pallas kernels for 0%

profile of v11, /device:TPU:1, one launch (start us, length us, event | category | flops | bytes accessed | tf_op | source)
XLA Modules:
  0.0 196.4 jit_solution(7549118244296883520)
XLA Ops:
  11.6 11.6 %all-to-all-start = ((bf16[64,24,384]{2,1,0:T(8,128)(2,1)}), bf16[64,24,384]{2,1,0:T(8,128)(2,1)S(1)}, u32[]{:S(2)}, u32[]{:S(2)}) async-start(bf16[64,24,384]{2,1,0:T(8,128)(2,1)} %broadcast_in_dim.6), calls=%async_computation | async-start | bytes 2359296 | tf_op jit(solution)/shard_map/all_to_all | solution.py:50
  23.4 3.5 %collective-permute-start.2 = (bf16[192,15]{1,0:T(8,128)(2,1)S(1)}, bf16[192,15]{1,0:T(8,128)(2,1)S(1)}, u32[]{:S(2)}, u32[]{:S(2)}) collective-permute-start(bf16[192,15]{1,0:T(8,128)(2,1)S(1)} %get-tuple-element.64), channel_id=1, source_target_pairs={{0,8},{8,16},{16,24},{24,32},{32,40},{40,48},{48,56},{56,64},{64,7... | collective-permute-start | bytes 17288 | tf_op jit(solution)/shard_map/ppermute | solution.py:15
  29.5 25.8 %all-gather.3.cloned.1.call-done = bf16[1664,512]{1,0:T(8,128)(2,1)} async-done(((bf16[208,512]{1,0:T(8,128)(2,1)}), bf16[1664,512]{1,0:T(8,128)(2,1)}) %all-gather.3.cloned.1.call-update) | async-done | bytes 1703952 | tf_op jit(solution)/shard_map/all_gather | solution.py:106
  62.5 2.6 %fusion.138 = f32[384,512]{1,0:T(8,128)S(1)} fusion(bf16[1536,384]{1,0:T(8,128)(2,1)} %bitcast.117, bf16[1536,512]{1,0:T(8,128)(2,1)} %bitcast.116), kind=kOutput, calls=%fused_computation.297 | convolution fusion | flops 603979776 | bytes 3538944 | tf_op jit(solution)/shard_map/dot_general | solution.py:117
  65.3 7.6 %collective-permute-start = (bf16[192,30]{1,0:T(8,128)(2,1)S(1)}, bf16[192,30]{1,0:T(8,128)(2,1)S(1)}, u32[]{:S(2)}, u32[]{:S(2)}) collective-permute-start(bf16[192,30]{1,0:T(8,128)(2,1)S(1)} %get-tuple-element.62), channel_id=1, source_target_pairs={{0,8},{8,16},{16,24},{24,32},{32,40},{40,48},{48,56},{56,64},{64,7... | collective-permute-start | bytes 34568 | tf_op jit(solution)/shard_map/ppermute | solution.py:15
  75.8 2.6 %collective-permute-done.1 = bf16[192,30]{1,0:T(8,128)(2,1)S(1)} collective-permute-done((bf16[192,30]{1,0:T(8,128)(2,1)S(1)}, bf16[192,30]{1,0:T(8,128)(2,1)S(1)}, u32[]{:S(2)}, u32[]{:S(2)}) %collective-permute-start.1) | collective-permute-done | bytes 11552 | tf_op jit(solution)/shard_map/ppermute | solution.py:17
  79.2 6.8 %fusion.129 = (f32[192,542]{1,0:T(8,128)S(1)}, bf16[192,542]{1,0:T(8,128)(2,1)S(1)}, f32[192,542]{1,0:T(8,128)S(1)}) fusion(bf16[192,15]{1,0:T(8,128)(2,1)} %copy-done.5, bf16[192,512]{1,0:T(8,128)(2,1)} %param.11, bf16[192,15]{1,0:T(8,128)(2,1)S(1)} %collective-permute-done.2, f32[192,572]{1,0:T(8,128)S(1)} %maximum_convert_fusion, f32[192]{0:T(256)} %bitcast.183, ...), kind=kLoop, calls=%fused_computation.289 | loop fusion | flops 8012928 | bytes 14176512 | tf_op jit(solution)/shard_map/convert_element_type | solution.py:138
  86.0 2.2 %fusion.46 = (f32[192]{0:T(256)}, f32[192]{0:T(256)}, f32[192]{0:T(256)}, f32[192]{0:T(256)}, f32[192]{0:T(256)}, /*index=5*/f32[192]{0:T(256)}, f32[192]{0:T(256)}, f32[192]{0:T(256)}, f32[192]{0:T(256)}) fusion(f32[192,572]{1,0:T(8,128)S(1)} %maximum_convert_fusion, bf16[192,542]{1,0:T(8,128)(2,1)S(1)} %get-tuple-element.44), kind=kLoop, calls=%fused_computation.122 | loop fusion | flops 1866048 | bytes 3742464 | tf_op jit(solution)/shard_map/reduce_sum | solution.py:140
  88.2 2.1 %fusion.63 = (f32[192]{0:T(256)}, f32[192]{0:T(256)}, f32[192]{0:T(256)}, f32[192]{0:T(256)}, f32[192]{0:T(256)}, /*index=5*/f32[192]{0:T(256)}, f32[192]{0:T(256)}, f32[192]{0:T(256)}, f32[192]{0:T(256)}) fusion(f32[192,572]{1,0:T(8,128)S(1)} %maximum_convert_fusion, bf16[192,542]{1,0:T(8,128)(2,1)S(1)} %get-tuple-element.44), kind=kLoop, calls=%fused_computation.139 | loop fusion | flops 1866048 | bytes 3742464 | tf_op jit(solution)/shard_map/reduce_sum | solution.py:140
  90.3 3.0 %fusion.55 = (f32[192]{0:T(256)S(1)}, f32[192]{0:T(256)S(1)}, f32[192]{0:T(256)S(1)}, f32[192]{0:T(256)S(1)}, f32[192]{0:T(256)S(1)}, /*index=5*/f32[192]{0:T(25...) fusion(f32[192,572]{1,0:T(8,128)S(1)} %maximum_convert_fusion, ...), kind=kLoop, calls=%fused_computation.131 | loop fusion | flops 2651712 | bytes 5318400 | tf_op jit(solution)/shard_map/reduce_sum | solution.py:140
  93.3 2.8 %stack.155 = f32[31,192]{1,0:T(8,128)S(1)} concatenate(f32[1,192]{1,0:T(1,128)} %bitcast.216, f32[1,192]{1,0:T(1,128)} %bitcast.202, f32[1,192]{1,0:T(1,128)} %bitcast.203, f32[1,192]{1,0:T(1,128)} %bitcast.204, f32[1,192]{1,0:T(1,128)} %bitcast.205, f32[1,192]{1,0:T(1,128)} %bitcast.214, f32[1,192]{1,0:T(1,128)} %bitcast.213, f32[1,192]{1,0:T(1,128)} %bitcast.212, ...), dimensions={0} | concatenate | bytes 47616 | tf_op jit(solution)/shard_map/stack | solution.py:139
  96.2 5.3 %multiply_convert_fusion.6 = (bf16[192,512]{1,0:T(8,128)(2,1)S(1)}, f32[192,512]{1,0:T(8,128)S(1)}) fusion(f32[384,512]{1,0:T(8,128)S(1)} %fusion.138, f32[192,542]{1,0:T(8,128)S(1)} %get-tuple-element.43, f32[192]{0:T(256)} %bitcast.126, f32[192]{0:T(256)} %bitcast.164, f32[192]{0:T(256)} %bitcast.182, f32[192]{0:T(256)} %bitcast.180, f32[192]{0:T(256)} %bitcast.178, ...), kind=kLoop, calls=%fused_computation.212 | loop fusion | flops 6488064 | bytes 13196544 | tf_op jit(solution)/shard_map/convert_element_type | solution.py:142
  107.7 12.2 %all-to-all-start.1 = ((bf16[64,25,384]{2,1,0:T(8,128)(2,1)}), bf16[64,25,384]{2,1,0:T(8,128)(2,1)S(1)}, u32[]{:S(2)}, u32[]{:S(2)}) async-start(bf16[64,25,384]{2,1,0:T(8,128)(2,1)} %pad_maximum_fusion), calls=%async_computation.2 | async-start | bytes 3145728 | tf_op jit(solution)/shard_map/all_to_all | solution.py:164
  120.2 2.8 %collective-permute-start.4 = (bf16[208,256]{1,0:T(8,128)(2,1)S(1)}, bf16[208,256]{1,0:T(8,128)(2,1)S(1)}, u32[]{:S(2)}, u32[]{:S(2)}) collective-permute-start(bf16[208,256]{1,0:T(8,128)(2,1)S(1)} %get-tuple-element.102), channel_id=1, source_target_pairs={{0,1},{1,2},{2,3},{3,4},{4,5},{5,6},{6,7},{7,0},{8,9},{9,10},{10,1... | collective-permute-start | bytes 319496 | tf_op jit(solution)/shard_map/ppermute | solution.py:83
  123.0 4.0 %collective-permute-start.6 = (bf16[208,256]{1,0:T(8,128)(2,1)S(1)}, bf16[208,256]{1,0:T(8,128)(2,1)S(1)}, u32[]{:S(2)}, u32[]{:S(2)}) collective-permute-start(bf16[208,256]{1,0:T(8,128)(2,1)S(1)} %get-tuple-element.103), channel_id=1, source_target_pairs={{0,3},{1,4},{2,5},{3,6},{4,7},{5,0},{6,1},{7,2},{8,11},{9,12},{10,... | collective-permute-start | bytes 319496 | tf_op jit(solution)/shard_map/ppermute | solution.py:83
  127.1 4.6 %collective-permute-start.7 = (bf16[208,256]{1,0:T(8,128)(2,1)S(1)}, bf16[208,256]{1,0:T(8,128)(2,1)S(1)}, u32[]{:S(2)}, u32[]{:S(2)}) collective-permute-start(bf16[208,256]{1,0:T(8,128)(2,1)S(1)} %get-tuple-element.104), channel_id=1, source_target_pairs={{0,4},{1,5},{2,6},{3,7},{4,0},{5,1},{6,2},{7,3},{8,12},{9,13},{10,... | collective-permute-start | bytes 319496 | tf_op jit(solution)/shard_map/ppermute | solution.py:83
  131.7 4.4 %collective-permute-start.8 = (bf16[208,256]{1,0:T(8,128)(2,1)S(1)}, bf16[208,256]{1,0:T(8,128)(2,1)S(1)}, u32[]{:S(2)}, u32[]{:S(2)}) collective-permute-start(bf16[208,256]{1,0:T(8,128)(2,1)S(1)} %get-tuple-element.105), channel_id=1, source_target_pairs={{0,5},{1,6},{2,7},{3,0},{4,1},{5,2},{6,3},{7,4},{8,13},{9,14},{10,... | collective-permute-start | bytes 319496 | tf_op jit(solution)/shard_map/ppermute | solution.py:83
  136.1 4.3 %collective-permute-start.9 = (bf16[208,256]{1,0:T(8,128)(2,1)S(1)}, bf16[208,256]{1,0:T(8,128)(2,1)S(1)}, u32[]{:S(2)}, u32[]{:S(2)}) collective-permute-start(bf16[208,256]{1,0:T(8,128)(2,1)S(1)} %get-tuple-element.106), channel_id=1, source_target_pairs={{0,6},{1,7},{2,0},{3,1},{4,2},{5,3},{6,4},{7,5},{8,14},{9,15},{10,... | collective-permute-start | bytes 319496 | tf_op jit(solution)/shard_map/ppermute | solution.py:83
  142.4 2.3 %collective-permute-start.5 = (bf16[208,256]{1,0:T(8,128)(2,1)S(1)}, bf16[208,256]{1,0:T(8,128)(2,1)S(1)}, u32[]{:S(2)}, u32[]{:S(2)}) collective-permute-start(bf16[208,256]{1,0:T(8,128)(2,1)S(1)} %get-tuple-element.108), channel_id=1, source_target_pairs={{0,2},{1,3},{2,4},{3,5},{4,6},{5,7},{6,0},{7,1},{8,10},{9,11},{10,... | collective-permute-start | bytes 319496 | tf_op jit(solution)/shard_map/ppermute | solution.py:83
  145.7 10.6 %collective-permute-done.9 = bf16[208,256]{1,0:T(8,128)(2,1)S(1)} collective-permute-done((bf16[208,256]{1,0:T(8,128)(2,1)S(1)}, bf16[208,256]{1,0:T(8,128)(2,1)S(1)}, u32[]{:S(2)}, u32[]{:S(2)}) %collective-permute-start.9) | collective-permute-done | bytes 106528 | tf_op jit(solution)/shard_map/ppermute | solution.py:83
  156.3 2.6 %collective-permute-done.10 = bf16[208,256]{1,0:T(8,128)(2,1)S(1)} collective-permute-done((bf16[208,256]{1,0:T(8,128)(2,1)S(1)}, bf16[208,256]{1,0:T(8,128)(2,1)S(1)}, u32[]{:S(2)}, u32[]{:S(2)}) %collective-permute-start.10) | collective-permute-done | bytes 106528 | tf_op jit(solution)/shard_map/ppermute | solution.py:83
  159.4 2.9 %reduce-scatter.2.cloned.1.call-done = f32[192,256]{1,0:T(8,128)} async-done(((f32[1536,256]{1,0:T(8,128)}), f32[192,256]{1,0:T(8,128)}) %reduce-scatter.2.cloned.1.call-update) | async-done | bytes 196624 | tf_op jit(solution)/shard_map/reduce_scatter | solution.py:178
  165.0 12.7 %all-to-all-start.2 = ((f32[64,1,288]{2,1,0:T(1,128)}), f32[64,1,288]{2,1,0:T(1,128)S(1)}, u32[]{:S(2)}, u32[]{:S(2)}) async-start(f32[64,1,288]{2,1,0:T(1,128)} %broadcast_in_dim.8), calls=%async_computation.3 | async-start | bytes 196608 | tf_op jit(solution)/shard_map/all_to_all | solution.py:50
  178.3 9.9 %all-to-all-done.2 = f32[64,1,288]{2,1,0:T(1,128)S(1)} async-done(((f32[64,1,288]{2,1,0:T(1,128)}), f32[64,1,288]{2,1,0:T(1,128)S(1)}, u32[]{:S(2)}, u32[]{:S(2)}) %all-to-all-start.2) | async-done | bytes 73760 | tf_op jit(solution)/shard_map/all_to_all | solution.py:50
  (95 shorter events, 32.7 us)
Async XLA Ops:
  7.2 48.2 %all-gather.3.cloned.1.call-start = ((), (), s32[]{:S(2)}) async-start(), calls=%async_computation.5 | async-start | bytes 1916928 | tf_op jit(solution)/shard_map/all_gather | solution.py:106
  10.5 12.8 %copy-start.4 = (bf16[192,512]{1,0:T(8,128)(2,1)S(1)}, bf16[192,512]{1,0:T(8,128)(2,1)}, u32[]{:S(2)}) copy-start(bf16[192,512]{1,0:T(8,128)(2,1)} %param.11) | copy-start | bytes 589828
  10.5 18.4 %copy-start.6 = (f32[31,192]{1,0:T(8,128)S(1)}, f32[31,192]{1,0:T(8,128)}, u32[]{:S(2)}) copy-start(f32[31,192]{1,0:T(8,128)} %param.10) | copy-start | bytes 71428
  11.6 49.9 %all-to-all-start = ((bf16[64,24,384]{2,1,0:T(8,128)(2,1)}), bf16[64,24,384]{2,1,0:T(8,128)(2,1)S(1)}, u32[]{:S(2)}, u32[]{:S(2)}) async-start(bf16[64,24,384]{2,1,0:T(8,128)(2,1)} %broadcast_in_dim.6), calls=%async_computation | async-start | bytes 2359296 | tf_op jit(solution)/shard_map/all_to_all | solution.py:50
  23.2 139.1 %reduce-scatter.2.cloned.1.call-start = ((), (), s32[]{:S(2)}) async-start(), calls=%async_computation.4 | async-start | bytes 1769472 | tf_op jit(solution)/shard_map/reduce_scatter | solution.py:178
  23.4 55.1 %collective-permute-start.2 = (bf16[192,15]{1,0:T(8,128)(2,1)S(1)}, bf16[192,15]{1,0:T(8,128)(2,1)S(1)}, u32[]{:S(2)}, u32[]{:S(2)}) collective-permute-start(bf16[192,15]{1,0:T(8,128)(2,1)S(1)} %get-tuple-element.64), channel_id=1, source_target_pairs={{0,8},{8,16},{16,24},{24,32},{32,40},{40,48},{48,56},{56,64},{64,7... | collective-permute-start | bytes 17288 | tf_op jit(solution)/shard_map/ppermute | solution.py:15
  26.9 51.6 %collective-permute-start.3 = (bf16[192,15]{1,0:T(8,128)(2,1)S(1)}, bf16[192,15]{1,0:T(8,128)(2,1)S(1)}, u32[]{:S(2)}, u32[]{:S(2)}) collective-permute-start(bf16[192,15]{1,0:T(8,128)(2,1)S(1)} %get-tuple-element.65), channel_id=1, source_target_pairs={{8,0},{16,8},{24,16},{32,24},{40,32},{48,40},{56,48},{64,56},{72,6... | collective-permute-start | bytes 17288 | tf_op jit(solution)/shard_map/ppermute | solution.py:17
  29.5 49.7 %copy-start.7 = (f32[1,192]{1,0:T(1,128)}, f32[1,192]{1,0:T(1,128)S(1)}, u32[]{:S(2)}) copy-start(f32[1,192]{1,0:T(1,128)S(1)} %get-tuple-element.71) | copy-start | bytes 2308
  29.5 49.6 %copy-start.8 = (f32[1,192]{1,0:T(1,128)}, f32[1,192]{1,0:T(1,128)S(1)}, u32[]{:S(2)}) copy-start(f32[1,192]{1,0:T(1,128)S(1)} %get-tuple-element.72) | copy-start | bytes 2308
  55.3 4.5 %copy-start = (bf16[1664,512]{1,0:T(8,128)(2,1)S(1)}, bf16[1664,512]{1,0:T(8,128)(2,1)}, u32[]{:S(2)}) copy-start(bf16[1664,512]{1,0:T(8,128)(2,1)} %all-gather.3.cloned.1.call-done) | copy-start | bytes 5111812
  65.3 10.4 %collective-permute-start = (bf16[192,30]{1,0:T(8,128)(2,1)S(1)}, bf16[192,30]{1,0:T(8,128)(2,1)S(1)}, u32[]{:S(2)}, u32[]{:S(2)}) collective-permute-start(bf16[192,30]{1,0:T(8,128)(2,1)S(1)} %get-tuple-element.62), channel_id=1, source_target_pairs={{0,8},{8,16},{16,24},{24,32},{32,40},{40,48},{48,56},{56,64},{64,7... | collective-permute-start | bytes 34568 | tf_op jit(solution)/shard_map/ppermute | solution.py:15
  73.0 5.4 %collective-permute-start.1 = (bf16[192,30]{1,0:T(8,128)(2,1)S(1)}, bf16[192,30]{1,0:T(8,128)(2,1)S(1)}, u32[]{:S(2)}, u32[]{:S(2)}) collective-permute-start(bf16[192,30]{1,0:T(8,128)(2,1)S(1)} %get-tuple-element.63), channel_id=1, source_target_pairs={{8,0},{16,8},{24,16},{32,24},{40,32},{48,40},{56,48},{64,56},{72,6... | collective-permute-start | bytes 34568 | tf_op jit(solution)/shard_map/ppermute | solution.py:17
  96.2 5.5 %copy-start.2 = (bf16[64,24,384]{2,1,0:T(8,128)(2,1)S(1)}, bf16[64,24,384]{2,1,0:T(8,128)(2,1)}, u32[]{:S(2)}) copy-start(bf16[64,24,384]{2,1,0:T(8,128)(2,1)} %copy-done.1) | copy-start | bytes 3538948
  103.1 1.7 copy-start.3
  107.7 51.3 %all-to-all-start.1 = ((bf16[64,25,384]{2,1,0:T(8,128)(2,1)}), bf16[64,25,384]{2,1,0:T(8,128)(2,1)S(1)}, u32[]{:S(2)}, u32[]{:S(2)}) async-start(bf16[64,25,384]{2,1,0:T(8,128)(2,1)} %pad_maximum_fusion), calls=%async_computation.2 | async-start | bytes 3145728 | tf_op jit(solution)/shard_map/all_to_all | solution.py:164
  120.2 20.3 %collective-permute-start.4 = (bf16[208,256]{1,0:T(8,128)(2,1)S(1)}, bf16[208,256]{1,0:T(8,128)(2,1)S(1)}, u32[]{:S(2)}, u32[]{:S(2)}) collective-permute-start(bf16[208,256]{1,0:T(8,128)(2,1)S(1)} %get-tuple-element.102), channel_id=1, source_target_pairs={{0,1},{1,2},{2,3},{3,4},{4,5},{5,6},{6,7},{7,0},{8,9},{9,10},{10,1... | collective-permute-start | bytes 319496 | tf_op jit(solution)/shard_map/ppermute | solution.py:83
  123.0 19.4 %collective-permute-start.6 = (bf16[208,256]{1,0:T(8,128)(2,1)S(1)}, bf16[208,256]{1,0:T(8,128)(2,1)S(1)}, u32[]{:S(2)}, u32[]{:S(2)}) collective-permute-start(bf16[208,256]{1,0:T(8,128)(2,1)S(1)} %get-tuple-element.103), channel_id=1, source_target_pairs={{0,3},{1,4},{2,5},{3,6},{4,7},{5,0},{6,1},{7,2},{8,11},{9,12},{10,... | collective-permute-start | bytes 319496 | tf_op jit(solution)/shard_map/ppermute | solution.py:83
  127.1 18.6 %collective-permute-start.7 = (bf16[208,256]{1,0:T(8,128)(2,1)S(1)}, bf16[208,256]{1,0:T(8,128)(2,1)S(1)}, u32[]{:S(2)}, u32[]{:S(2)}) collective-permute-start(bf16[208,256]{1,0:T(8,128)(2,1)S(1)} %get-tuple-element.104), channel_id=1, source_target_pairs={{0,4},{1,5},{2,6},{3,7},{4,0},{5,1},{6,2},{7,3},{8,12},{9,13},{10,... | collective-permute-start | bytes 319496 | tf_op jit(solution)/shard_map/ppermute | solution.py:83
  131.7 14.0 %collective-permute-start.8 = (bf16[208,256]{1,0:T(8,128)(2,1)S(1)}, bf16[208,256]{1,0:T(8,128)(2,1)S(1)}, u32[]{:S(2)}, u32[]{:S(2)}) collective-permute-start(bf16[208,256]{1,0:T(8,128)(2,1)S(1)} %get-tuple-element.105), channel_id=1, source_target_pairs={{0,5},{1,6},{2,7},{3,0},{4,1},{5,2},{6,3},{7,4},{8,13},{9,14},{10,... | collective-permute-start | bytes 319496 | tf_op jit(solution)/shard_map/ppermute | solution.py:83
  136.1 20.1 %collective-permute-start.9 = (bf16[208,256]{1,0:T(8,128)(2,1)S(1)}, bf16[208,256]{1,0:T(8,128)(2,1)S(1)}, u32[]{:S(2)}, u32[]{:S(2)}) collective-permute-start(bf16[208,256]{1,0:T(8,128)(2,1)S(1)} %get-tuple-element.106), channel_id=1, source_target_pairs={{0,6},{1,7},{2,0},{3,1},{4,2},{5,3},{6,4},{7,5},{8,14},{9,15},{10,... | collective-permute-start | bytes 319496 | tf_op jit(solution)/shard_map/ppermute | solution.py:83
  140.5 18.4 %collective-permute-start.10 = (bf16[208,256]{1,0:T(8,128)(2,1)S(1)}, bf16[208,256]{1,0:T(8,128)(2,1)S(1)}, u32[]{:S(2)}, u32[]{:S(2)}) collective-permute-start(bf16[208,256]{1,0:T(8,128)(2,1)S(1)} %get-tuple-element.107), channel_id=1, source_target_pairs={{0,7},{1,0},{2,1},{3,2},{4,3},{5,4},{6,5},{7,6},{8,15},{9,8},{10,9... | collective-permute-start | bytes 319496 | tf_op jit(solution)/shard_map/ppermute | solution.py:83
  142.4 19.9 %copy-start.9 = (f32[192]{0:T(256)S(1)}, f32[192]{0:T(256)}, u32[]{:S(2)}) copy-start(f32[192]{0:T(256)} %param.7) | copy-start | bytes 2308
  142.4 16.5 %collective-permute-start.5 = (bf16[208,256]{1,0:T(8,128)(2,1)S(1)}, bf16[208,256]{1,0:T(8,128)(2,1)S(1)}, u32[]{:S(2)}, u32[]{:S(2)}) collective-permute-start(bf16[208,256]{1,0:T(8,128)(2,1)S(1)} %get-tuple-element.108), channel_id=1, source_target_pairs={{0,2},{1,3},{2,4},{3,5},{4,6},{5,7},{6,0},{7,1},{8,10},{9,11},{10,... | collective-permute-start | bytes 319496 | tf_op jit(solution)/shard_map/ppermute | solution.py:83
  165.0 23.2 %all-to-all-start.2 = ((f32[64,1,288]{2,1,0:T(1,128)}), f32[64,1,288]{2,1,0:T(1,128)S(1)}, u32[]{:S(2)}, u32[]{:S(2)}) async-start(f32[64,1,288]{2,1,0:T(1,128)} %broadcast_in_dim.8), calls=%async_computation.3 | async-start | bytes 196608 | tf_op jit(solution)/shard_map/all_to_all | solution.py:50
  (2 other events, 1.6 us)
Sparse Core Ops, SparseCore 0:
  10.1 45.2 all-gather.2
  106.2 56.0 reduce-scatter.1

commit v12 on v9

--- a/solution.py
+++ b/solution.py
@@ -168,16 +168,18 @@
     own_moments = jnp.stack([jnp.sum(weighted, 0), jnp.sum(weighted * centered_unit, 0)], 0)
     moment_rows = jnp.concatenate(bf16_pieces(own_moments, 3), 0)
     half = frames // 2
-    moment_rows = moment_rows.reshape(-1, half)
-    moment_rows = jnp.pad(moment_rows, ((0, 16 - moment_rows.shape[0]), (0, 0)))
+    split = frames - frames // 4
+    moment_rows = moment_rows.reshape(-1, frames - split)
+    used_rows = moment_rows.shape[0]
+    moment_rows = jnp.pad(moment_rows, ((0, 32 - used_rows), (0, 0)))
     early_part = lax.psum_scatter(
-        normed_term[:, :half].astype(jnp.float32), "ch", scatter_dimension=0, tiled=True
-    )
+        normed_term[:, :split], "ch", scatter_dimension=0, tiled=True
+    ).astype(jnp.float32)
     late_part, moment_total = reduce_by_shifts(
-        normed_term[:, half:].reshape(groups, local_cols, frames - half), moment_rows, "ch"
+        normed_term[:, split:].reshape(groups, local_cols, frames - split), moment_rows, "ch"
     )
     normalized_gradient = jnp.concatenate([early_part, late_part], 1)
-    moment_total = moment_total[:12].reshape(6, frames)
+    moment_total = moment_total[:used_rows].reshape(6, frames)
     scaled_signal = normalized_gradient * input_norm_gain[:, None]
     moments = ((moment_total[0:2] + moment_total[2:4]) + moment_total[4:6]) * (
         1.0 / complete_signal.shape[0]

time: 197 us -> 191 us (0.970)
  waiting for transfers between devices: 60.2 us -> 56.8 us
  starting transfers between devices: 76.3 us -> 72.9 us
  local copies, waits for them, and re-layouts: 6.74 us -> 9.96 us
  other arithmetic: 29.9 us -> 27.5 us
    ppermute x7, waiting for transfers between devices: 12.9 us -> 4.34 us  [reduce_by_shifts(): lax.ppermute(outgoing, axis, [(i, (i + shift) % count) for i in range(cou...]
    all_to_all x1, waiting for transfers between devices: 0.01 us -> 5.13 us  [shards(): lax.all_to_all(outgoing, 'seq', 0, 0, tiled=False).astype(jnp.float32)]
    all_to_all x2, starting transfers between devices: 22.5 us -> 19 us  [gather_by_exchange(): return lax.all_to_all(copies, axis, 0, 0, tiled=False)]
    slice x0 -> x2, local copies, waits for them, and re-layouts: none -> 2.18 us  [the longest x1 1.15 us: shards(): normed_term[:, :split]]
  transfers between devices with their start and end apart: 16 -> 16, of which waited for: 7 -> 8; matrix products, arithmetic and copies ran while one was open for 8% -> 9% of each run, Pallas kernels for 0% -> 0%
where the time goes in v12:
time: 191 us; the launch traced here: 190 us
  starting transfers between devices  72.9 us (38%)
  waiting for transfers between devices  56.8 us (30%)
  other arithmetic  27.5 us (14%)
  between operations  14.6 us (8%)
  local copies, waits for them, and re-layouts  9.96 us (5%)
  matrix products  8.23 us (4%)
    all_gather x1, waiting for transfers between devices, shards(): lax.all_gather(jnp.concatenate([signal, gain_rows], 0), 'ch', axis=0)  32 us
    ppermute x7, starting transfers between devices, reduce_by_shifts(): lax.ppermute(outgoing, axis, [(i, (i + shift) % count) for i in range(cou...  24.4 us
    all_to_all x2, starting transfers between devices, gather_by_exchange(): return lax.all_to_all(copies, axis, 0, 0, tiled=False)  19 us
    all_to_all x1, starting transfers between devices, shards(): lax.all_to_all(outgoing, 'seq', 0, 0, tiled=False).astype(jnp.float32)  15.4 us
    all_to_all x2, waiting for transfers between devices, gather_by_exchange(): return lax.all_to_all(copies, axis, 0, 0, tiled=False)  9.88 us
    ppermute x2, starting transfers between devices, extended(): lax.ppermute(tail, axis, [(i, (i + 1) % count) for i in range(ends)])  9.55 us
    reduce_sum x2, other arithmetic, shards(): jnp.sum(glued_pad[:, k:k + span] * grad_pre_f, 1)  6.84 us
    ppermute x2, waiting for transfers between devices, extended(): lax.ppermute(head, axis, [((i + 1) % count, i) for i in range(ends)])  5.39 us
  transfers between devices with their start and end apart: 16, of which 8 were waited for; matrix products, arithmetic and copies ran while one was open for 9% of the time, Pallas kernels for 0%

profile of v12, /device:TPU:1, one launch (start us, length us, event | category | flops | bytes accessed | tf_op | source)
XLA Modules:
  0.0 190.0 jit_solution(12254958359595668241)
XLA Ops:
  11.6 11.6 %all-to-all-start = ((bf16[64,24,384]{2,1,0:T(8,128)(2,1)}), bf16[64,24,384]{2,1,0:T(8,128)(2,1)S(1)}, u32[]{:S(2)}, u32[]{:S(2)}) async-start(bf16[64,24,384]{2,1,0:T(8,128)(2,1)} %broadcast_in_dim.6), calls=%async_computation | async-start | bytes 2359296 | tf_op jit(solution)/shard_map/all_to_all | solution.py:50
  23.3 32.0 %all-gather.3.cloned.1.call-done = bf16[1664,512]{1,0:T(8,128)(2,1)} async-done(((bf16[208,512]{1,0:T(8,128)(2,1)}), bf16[1664,512]{1,0:T(8,128)(2,1)}) %all-gather.3.cloned.1.call-update) | async-done | bytes 1703952 | tf_op jit(solution)/shard_map/all_gather | solution.py:104
  62.5 2.6 %fusion.105 = f32[384,512]{1,0:T(8,128)S(1)} fusion(bf16[1536,384]{1,0:T(8,128)(2,1)} %bitcast.115, bf16[1536,512]{1,0:T(8,128)(2,1)} %bitcast.114), kind=kOutput, calls=%fused_computation.235 | convolution fusion | flops 603979776 | bytes 3538944 | tf_op jit(solution)/shard_map/dot_general | solution.py:115
  65.3 7.6 %collective-permute-start = (bf16[192,15]{1,0:T(8,128)(2,1)S(1)}, bf16[192,15]{1,0:T(8,128)(2,1)S(1)}, u32[]{:S(2)}, u32[]{:S(2)}) collective-permute-start(bf16[192,15]{1,0:T(8,128)(2,1)S(1)} %get-tuple-element.57), channel_id=1, source_target_pairs={{0,8},{8,16},{16,24},{24,32},{32,40},{40,48},{48,56},{56,64},{64,7... | collective-permute-start | bytes 17288 | tf_op jit(solution)/shard_map/ppermute | solution.py:15
  75.0 3.4 %collective-permute-done.1 = bf16[192,15]{1,0:T(8,128)(2,1)S(1)} collective-permute-done((bf16[192,15]{1,0:T(8,128)(2,1)S(1)}, bf16[192,15]{1,0:T(8,128)(2,1)S(1)}, u32[]{:S(2)}, u32[]{:S(2)}) %collective-permute-start.1) | collective-permute-done | bytes 5792 | tf_op jit(solution)/shard_map/ppermute | solution.py:17
  78.5 4.9 %fusion.33 = (f32[192]{0:T(256)S(1)}, f32[192]{0:T(256)S(1)}, f32[192]{0:T(256)S(1)}, f32[192]{0:T(256)S(1)}, f32[192]{0:T(256)S(1)}, /*index=5*/f32[192]{0:T(25...) fusion(f32[192,542]{1,0:T(8,128)S(1)} %maximum_convert_fusion, ...), kind=kLoop, calls=%fused_computation.75 | loop fusion | flops 10613376 | bytes 13013760 | tf_op jit(solution)/shard_map/reduce_sum | solution.py:135
  83.4 1.9 %fusion.32 = (f32[192]{0:T(256)S(1)}, f32[192]{0:T(256)S(1)}, f32[192]{0:T(256)S(1)}, f32[192]{0:T(256)S(1)}, f32[192]{0:T(256)S(1)}, /*index=5*/f32[192]{0:T(25...) fusion(bf16[192,512]{1,0:T(8,128)(2,1)S(1)} %get-tuple-element., ...), kind=kLoop, calls=%fused_computation.74 | loop fusion | flops 2651712 | bytes 5318400 | tf_op jit(solution)/shard_map/reduce_sum | solution.py:135
  85.7 1.9 %collective-permute-start.2 = (bf16[192,15]{1,0:T(8,128)(2,1)S(1)}, bf16[192,15]{1,0:T(8,128)(2,1)S(1)}, u32[]{:S(2)}, u32[]{:S(2)}) collective-permute-start(bf16[192,15]{1,0:T(8,128)(2,1)S(1)} %get-tuple-element.55), channel_id=1, source_target_pairs={{0,8},{8,16},{16,24},{24,32},{32,40},{40,48},{48,56},{56,64},{64,7... | collective-permute-start | bytes 17288 | tf_op jit(solution)/shard_map/ppermute | solution.py:15
  87.6 2.6 %collective-permute-start.3 = (bf16[192,15]{1,0:T(8,128)(2,1)S(1)}, bf16[192,15]{1,0:T(8,128)(2,1)S(1)}, u32[]{:S(2)}, u32[]{:S(2)}) collective-permute-start(bf16[192,15]{1,0:T(8,128)(2,1)S(1)} %get-tuple-element.56), channel_id=1, source_target_pairs={{8,0},{16,8},{24,16},{32,24},{40,32},{48,40},{56,48},{64,56},{72,6... | collective-permute-start | bytes 17288 | tf_op jit(solution)/shard_map/ppermute | solution.py:17
  91.0 2.0 %collective-permute-done.3 = bf16[192,15]{1,0:T(8,128)(2,1)S(1)} collective-permute-done((bf16[192,15]{1,0:T(8,128)(2,1)S(1)}, bf16[192,15]{1,0:T(8,128)(2,1)S(1)}, u32[]{:S(2)}, u32[]{:S(2)}) %collective-permute-start.3) | collective-permute-done | bytes 5792 | tf_op jit(solution)/shard_map/ppermute | solution.py:17
  93.2 4.4 %multiply_convert_fusion.5 = (bf16[192,512]{1,0:T(8,128)(2,1)S(1)}, f32[192,512]{1,0:T(8,128)S(1)}) fusion(f32[384,512]{1,0:T(8,128)S(1)} %fusion.105, f32[192,542]{1,0:T(8,128)S(1)} %maximum_convert_fusion.1, f32[192]{0:T(256)S(1)} %bitcast.124, f32[192]{0:T(256)S(1)} %bitcast.162, f32[192]{0:T(256)S(1)} %bitcast.180, f32[192]{0:T(256)S(1)} %bitcast.178, ...), kind=kLoop, calls=%fused_computation.146 | loop fusion | flops 6488064 | bytes 13196544 | tf_op jit(solution)/shard_map/convert_element_type | solution.py:137
  97.8 3.6 %fusion.1 = (f32[512]{0:T(512)S(1)}, f32[512]{0:T(512)}, f32[1536,512]{1,0:T(8,128)}, bf16[1536,512]{1,0:T(8,128)(2,1)S(1)}) fusion(f32[1536]{0:T(1024)S(1)} %add.437, f32[512]{0:T(512)S(1)} %add_rsqrt_fusion, f32[512]{0:T(512)S(1)} %broadcast_multiply_fusion, bf16[8,208,512]{2,1,0:T(8,128)(2,1)S(1)} %bitcast.113, bf16[1536,384]{1,0:T(8,128)(2,1)S(1)} %bitcast.116, ...), kind=kOutput, calls=%fused_computation.37 | convolution fusion | flops 611843072 | bytes 7878656 | tf_op jit(solution)/shard_map/dot_general | solution.py:146
  104.9 2.1 %convolution_convert_fusion.1 = bf16[1536,384]{1,0:T(8,128)(2,1)S(1)} fusion(f32[1536,512]{1,0:T(8,128)S(1)} %copy-done.3, f32[1536]{0:T(1024)S(1)} %add.437, bf16[192,512]{1,0:T(8,128)(2,1)} %copy-done.5, bf16[192,512]{1,0:T(8,128)(2,1)} %copy-done.6), kind=kOutput, calls=%fused_computation.42 | convolution fusion | flops 606928896 | bytes 4724736 | tf_op jit(solution)/shard_map/dot_general | solution.py:140
  108.4 15.4 %all-to-all-start.1 = ((bf16[64,25,384]{2,1,0:T(8,128)(2,1)}), bf16[64,25,384]{2,1,0:T(8,128)(2,1)S(1)}, u32[]{:S(2)}, u32[]{:S(2)}) async-start(bf16[64,25,384]{2,1,0:T(8,128)(2,1)} %pad_maximum_fusion), calls=%async_computation.2 | async-start | bytes 3145728 | tf_op jit(solution)/shard_map/all_to_all | solution.py:159
  125.1 2.8 %collective-permute-start.4 = (bf16[224,128]{1,0:T(8,128)(2,1)S(1)}, bf16[224,128]{1,0:T(8,128)(2,1)S(1)}, u32[]{:S(2)}, u32[]{:S(2)}) collective-permute-start(bf16[224,128]{1,0:T(8,128)(2,1)S(1)} %get-tuple-element.95), channel_id=1, source_target_pairs={{0,1},{1,2},{2,3},{3,4},{4,5},{5,6},{6,7},{7,0},{8,9},{9,10},{10,1... | collective-permute-start | bytes 172040 | tf_op jit(solution)/shard_map/ppermute | solution.py:83
  127.9 4.0 %collective-permute-start.6 = (bf16[224,128]{1,0:T(8,128)(2,1)S(1)}, bf16[224,128]{1,0:T(8,128)(2,1)S(1)}, u32[]{:S(2)}, u32[]{:S(2)}) collective-permute-start(bf16[224,128]{1,0:T(8,128)(2,1)S(1)} %get-tuple-element.96), channel_id=1, source_target_pairs={{0,3},{1,4},{2,5},{3,6},{4,7},{5,0},{6,1},{7,2},{8,11},{9,12},{10,... | collective-permute-start | bytes 172040 | tf_op jit(solution)/shard_map/ppermute | solution.py:83
  131.9 4.6 %collective-permute-start.7 = (bf16[224,128]{1,0:T(8,128)(2,1)S(1)}, bf16[224,128]{1,0:T(8,128)(2,1)S(1)}, u32[]{:S(2)}, u32[]{:S(2)}) collective-permute-start(bf16[224,128]{1,0:T(8,128)(2,1)S(1)} %get-tuple-element.97), channel_id=1, source_target_pairs={{0,4},{1,5},{2,6},{3,7},{4,0},{5,1},{6,2},{7,3},{8,12},{9,13},{10,... | collective-permute-start | bytes 172040 | tf_op jit(solution)/shard_map/ppermute | solution.py:83
  136.5 4.4 %collective-permute-start.8 = (bf16[224,128]{1,0:T(8,128)(2,1)S(1)}, bf16[224,128]{1,0:T(8,128)(2,1)S(1)}, u32[]{:S(2)}, u32[]{:S(2)}) collective-permute-start(bf16[224,128]{1,0:T(8,128)(2,1)S(1)} %get-tuple-element.98), channel_id=1, source_target_pairs={{0,5},{1,6},{2,7},{3,0},{4,1},{5,2},{6,3},{7,4},{8,13},{9,14},{10,... | collective-permute-start | bytes 172040 | tf_op jit(solution)/shard_map/ppermute | solution.py:83
  140.9 4.3 %collective-permute-start.9 = (bf16[224,128]{1,0:T(8,128)(2,1)S(1)}, bf16[224,128]{1,0:T(8,128)(2,1)S(1)}, u32[]{:S(2)}, u32[]{:S(2)}) collective-permute-start(bf16[224,128]{1,0:T(8,128)(2,1)S(1)} %get-tuple-element.99), channel_id=1, source_target_pairs={{0,6},{1,7},{2,0},{3,1},{4,2},{5,3},{6,4},{7,5},{8,14},{9,15},{10,... | collective-permute-start | bytes 172040 | tf_op jit(solution)/shard_map/ppermute | solution.py:83
  147.2 2.4 %collective-permute-start.5 = (bf16[224,128]{1,0:T(8,128)(2,1)S(1)}, bf16[224,128]{1,0:T(8,128)(2,1)S(1)}, u32[]{:S(2)}, u32[]{:S(2)}) collective-permute-start(bf16[224,128]{1,0:T(8,128)(2,1)S(1)} %get-tuple-element.101), channel_id=1, source_target_pairs={{0,2},{1,3},{2,4},{3,5},{4,6},{5,7},{6,0},{7,1},{8,10},{9,11},{10,... | collective-permute-start | bytes 172040 | tf_op jit(solution)/shard_map/ppermute | solution.py:83
  151.7 3.0 %collective-permute-done.5 = bf16[224,128]{1,0:T(8,128)(2,1)S(1)} collective-permute-done((bf16[224,128]{1,0:T(8,128)(2,1)S(1)}, bf16[224,128]{1,0:T(8,128)(2,1)S(1)}, u32[]{:S(2)}, u32[]{:S(2)}) %collective-permute-start.5) | collective-permute-done | bytes 57376 | tf_op jit(solution)/shard_map/ppermute | solution.py:83
  157.6 5.1 %all-to-all-done.1 = bf16[64,25,384]{2,1,0:T(8,128)(2,1)S(1)} async-done(((bf16[64,25,384]{2,1,0:T(8,128)(2,1)}), bf16[64,25,384]{2,1,0:T(8,128)(2,1)S(1)}, u32[]{:S(2)}, u32[]{:S(2)}) %all-to-all-start.1) | async-done | bytes 1228832 | tf_op jit(solution)/shard_map/all_to_all | solution.py:159
  163.9 7.3 %all-to-all-start.2 = ((f32[64,1,288]{2,1,0:T(1,128)}), f32[64,1,288]{2,1,0:T(1,128)S(1)}, u32[]{:S(2)}, u32[]{:S(2)}) async-start(f32[64,1,288]{2,1,0:T(1,128)} %broadcast_in_dim.8), calls=%async_computation.3 | async-start | bytes 196608 | tf_op jit(solution)/shard_map/all_to_all | solution.py:50
  171.9 9.9 %all-to-all-done.2 = f32[64,1,288]{2,1,0:T(1,128)S(1)} async-done(((f32[64,1,288]{2,1,0:T(1,128)}), f32[64,1,288]{2,1,0:T(1,128)S(1)}, u32[]{:S(2)}, u32[]{:S(2)}) %all-to-all-start.2) | async-done | bytes 73760 | tf_op jit(solution)/shard_map/all_to_all | solution.py:50
  (97 shorter events, 31.5 us)
Async XLA Ops:
  7.2 48.2 %all-gather.3.cloned.1.call-start = ((), (), s32[]{:S(2)}) async-start(), calls=%async_computation.5 | async-start | bytes 1916928 | tf_op jit(solution)/shard_map/all_gather | solution.py:104
  10.5 12.8 %copy-start.9 = (f32[31,192]{1,0:T(8,128)S(1)}, f32[31,192]{1,0:T(8,128)}, u32[]{:S(2)}) copy-start(f32[31,192]{1,0:T(8,128)} %param.10) | copy-start | bytes 71428
  11.6 49.9 %all-to-all-start = ((bf16[64,24,384]{2,1,0:T(8,128)(2,1)}), bf16[64,24,384]{2,1,0:T(8,128)(2,1)S(1)}, u32[]{:S(2)}, u32[]{:S(2)}) async-start(bf16[64,24,384]{2,1,0:T(8,128)(2,1)} %broadcast_in_dim.6), calls=%async_computation | async-start | bytes 2359296 | tf_op jit(solution)/shard_map/all_to_all | solution.py:50
  23.2 131.6 %reduce-scatter.2.cloned.1.call-start = ((), (), s32[]{:S(2)}) async-start(), calls=%async_computation.4 | async-start | bytes 1327104 | tf_op jit(solution)/shard_map/reduce_scatter | solution.py:175
  55.3 4.5 %copy-start = (bf16[1664,512]{1,0:T(8,128)(2,1)S(1)}, bf16[1664,512]{1,0:T(8,128)(2,1)}, u32[]{:S(2)}) copy-start(bf16[1664,512]{1,0:T(8,128)(2,1)} %all-gather.3.cloned.1.call-done) | copy-start | bytes 5111812
  65.1 13.4 %copy-start.8 = (bf16[192,512]{1,0:T(8,128)(2,1)S(1)}, bf16[192,512]{1,0:T(8,128)(2,1)}, u32[]{:S(2)}) copy-start(bf16[192,512]{1,0:T(8,128)(2,1)} %param.11) | copy-start | bytes 589828
  65.3 9.7 %collective-permute-start = (bf16[192,15]{1,0:T(8,128)(2,1)S(1)}, bf16[192,15]{1,0:T(8,128)(2,1)S(1)}, u32[]{:S(2)}, u32[]{:S(2)}) collective-permute-start(bf16[192,15]{1,0:T(8,128)(2,1)S(1)} %get-tuple-element.57), channel_id=1, source_target_pairs={{0,8},{8,16},{16,24},{24,32},{32,40},{40,48},{48,56},{56,64},{64,7... | collective-permute-start | bytes 17288 | tf_op jit(solution)/shard_map/ppermute | solution.py:15
  73.0 5.4 %collective-permute-start.1 = (bf16[192,15]{1,0:T(8,128)(2,1)S(1)}, bf16[192,15]{1,0:T(8,128)(2,1)S(1)}, u32[]{:S(2)}, u32[]{:S(2)}) collective-permute-start(bf16[192,15]{1,0:T(8,128)(2,1)S(1)} %get-tuple-element.58), channel_id=1, source_target_pairs={{8,0},{16,8},{24,16},{32,24},{40,32},{48,40},{56,48},{64,56},{72,6... | collective-permute-start | bytes 17288 | tf_op jit(solution)/shard_map/ppermute | solution.py:17
  85.7 5.3 %collective-permute-start.2 = (bf16[192,15]{1,0:T(8,128)(2,1)S(1)}, bf16[192,15]{1,0:T(8,128)(2,1)S(1)}, u32[]{:S(2)}, u32[]{:S(2)}) collective-permute-start(bf16[192,15]{1,0:T(8,128)(2,1)S(1)} %get-tuple-element.55), channel_id=1, source_target_pairs={{0,8},{8,16},{16,24},{24,32},{32,40},{40,48},{48,56},{56,64},{64,7... | collective-permute-start | bytes 17288 | tf_op jit(solution)/shard_map/ppermute | solution.py:15
  87.6 5.4 %collective-permute-start.3 = (bf16[192,15]{1,0:T(8,128)(2,1)S(1)}, bf16[192,15]{1,0:T(8,128)(2,1)S(1)}, u32[]{:S(2)}, u32[]{:S(2)}) collective-permute-start(bf16[192,15]{1,0:T(8,128)(2,1)S(1)} %get-tuple-element.56), channel_id=1, source_target_pairs={{8,0},{16,8},{24,16},{32,24},{40,32},{48,40},{56,48},{64,56},{72,6... | collective-permute-start | bytes 17288 | tf_op jit(solution)/shard_map/ppermute | solution.py:17
  93.2 4.7 %copy-start.2 = (bf16[64,24,384]{2,1,0:T(8,128)(2,1)S(1)}, bf16[64,24,384]{2,1,0:T(8,128)(2,1)}, u32[]{:S(2)}) copy-start(bf16[64,24,384]{2,1,0:T(8,128)(2,1)} %copy-done.1) | copy-start | bytes 3538948
  97.6 3.8 %copy-start.6 = (bf16[192,512]{1,0:T(8,128)(2,1)}, bf16[192,512]{1,0:T(8,128)(2,1)S(1)}, u32[]{:S(2)}) copy-start(bf16[192,512]{1,0:T(8,128)(2,1)S(1)} %get-tuple-element.43) | copy-start | bytes 589828
  97.8 3.6 %copy-start.5 = (bf16[192,512]{1,0:T(8,128)(2,1)}, bf16[192,512]{1,0:T(8,128)(2,1)S(1)}, u32[]{:S(2)}) copy-start(bf16[192,512]{1,0:T(8,128)(2,1)S(1)} %multiply_convert_fusion.4) | copy-start | bytes 589828
  108.4 16.5 %copy-start.10 = (f32[512]{0:T(512)S(1)}, f32[512]{0:T(512)}, u32[]{:S(2)}) copy-start(f32[512]{0:T(512)} %get-tuple-element.7) | copy-start | bytes 6148
  108.4 54.4 %all-to-all-start.1 = ((bf16[64,25,384]{2,1,0:T(8,128)(2,1)}), bf16[64,25,384]{2,1,0:T(8,128)(2,1)S(1)}, u32[]{:S(2)}, u32[]{:S(2)}) async-start(bf16[64,25,384]{2,1,0:T(8,128)(2,1)} %pad_maximum_fusion), calls=%async_computation.2 | async-start | bytes 3145728 | tf_op jit(solution)/shard_map/all_to_all | solution.py:159
  124.9 30.9 %copy-start.11 = (f32[192]{0:T(256)S(1)}, f32[192]{0:T(256)}, u32[]{:S(2)}) copy-start(f32[192]{0:T(256)} %param.7) | copy-start | bytes 2308
  125.1 20.1 %collective-permute-start.4 = (bf16[224,128]{1,0:T(8,128)(2,1)S(1)}, bf16[224,128]{1,0:T(8,128)(2,1)S(1)}, u32[]{:S(2)}, u32[]{:S(2)}) collective-permute-start(bf16[224,128]{1,0:T(8,128)(2,1)S(1)} %get-tuple-element.95), channel_id=1, source_target_pairs={{0,1},{1,2},{2,3},{3,4},{4,5},{5,6},{6,7},{7,0},{8,9},{9,10},{10,1... | collective-permute-start | bytes 172040 | tf_op jit(solution)/shard_map/ppermute | solution.py:83
  127.9 19.3 %collective-permute-start.6 = (bf16[224,128]{1,0:T(8,128)(2,1)S(1)}, bf16[224,128]{1,0:T(8,128)(2,1)S(1)}, u32[]{:S(2)}, u32[]{:S(2)}) collective-permute-start(bf16[224,128]{1,0:T(8,128)(2,1)S(1)} %get-tuple-element.96), channel_id=1, source_target_pairs={{0,3},{1,4},{2,5},{3,6},{4,7},{5,0},{6,1},{7,2},{8,11},{9,12},{10,... | collective-permute-start | bytes 172040 | tf_op jit(solution)/shard_map/ppermute | solution.py:83
  131.9 18.4 %collective-permute-start.7 = (bf16[224,128]{1,0:T(8,128)(2,1)S(1)}, bf16[224,128]{1,0:T(8,128)(2,1)S(1)}, u32[]{:S(2)}, u32[]{:S(2)}) collective-permute-start(bf16[224,128]{1,0:T(8,128)(2,1)S(1)} %get-tuple-element.97), channel_id=1, source_target_pairs={{0,4},{1,5},{2,6},{3,7},{4,0},{5,1},{6,2},{7,3},{8,12},{9,13},{10,... | collective-permute-start | bytes 172040 | tf_op jit(solution)/shard_map/ppermute | solution.py:83
  136.5 13.8 %collective-permute-start.8 = (bf16[224,128]{1,0:T(8,128)(2,1)S(1)}, bf16[224,128]{1,0:T(8,128)(2,1)S(1)}, u32[]{:S(2)}, u32[]{:S(2)}) collective-permute-start(bf16[224,128]{1,0:T(8,128)(2,1)S(1)} %get-tuple-element.98), channel_id=1, source_target_pairs={{0,5},{1,6},{2,7},{3,0},{4,1},{5,2},{6,3},{7,4},{8,13},{9,14},{10,... | collective-permute-start | bytes 172040 | tf_op jit(solution)/shard_map/ppermute | solution.py:83
  140.9 10.7 %collective-permute-start.9 = (bf16[224,128]{1,0:T(8,128)(2,1)S(1)}, bf16[224,128]{1,0:T(8,128)(2,1)S(1)}, u32[]{:S(2)}, u32[]{:S(2)}) collective-permute-start(bf16[224,128]{1,0:T(8,128)(2,1)S(1)} %get-tuple-element.99), channel_id=1, source_target_pairs={{0,6},{1,7},{2,0},{3,1},{4,2},{5,3},{6,4},{7,5},{8,14},{9,15},{10,... | collective-permute-start | bytes 172040 | tf_op jit(solution)/shard_map/ppermute | solution.py:83
  145.2 6.5 %collective-permute-start.10 = (bf16[224,128]{1,0:T(8,128)(2,1)S(1)}, bf16[224,128]{1,0:T(8,128)(2,1)S(1)}, u32[]{:S(2)}, u32[]{:S(2)}) collective-permute-start(bf16[224,128]{1,0:T(8,128)(2,1)S(1)} %get-tuple-element.100), channel_id=1, source_target_pairs={{0,7},{1,0},{2,1},{3,2},{4,3},{5,4},{6,5},{7,6},{8,15},{9,8},{10,9... | collective-permute-start | bytes 172040 | tf_op jit(solution)/shard_map/ppermute | solution.py:83
  147.2 7.5 %collective-permute-start.5 = (bf16[224,128]{1,0:T(8,128)(2,1)S(1)}, bf16[224,128]{1,0:T(8,128)(2,1)S(1)}, u32[]{:S(2)}, u32[]{:S(2)}) collective-permute-start(bf16[224,128]{1,0:T(8,128)(2,1)S(1)} %get-tuple-element.101), channel_id=1, source_target_pairs={{0,2},{1,3},{2,4},{3,5},{4,6},{5,7},{6,0},{7,1},{8,10},{9,11},{10,... | collective-permute-start | bytes 172040 | tf_op jit(solution)/shard_map/ppermute | solution.py:83
  163.9 17.9 %all-to-all-start.2 = ((f32[64,1,288]{2,1,0:T(1,128)}), f32[64,1,288]{2,1,0:T(1,128)S(1)}, u32[]{:S(2)}, u32[]{:S(2)}) async-start(f32[64,1,288]{2,1,0:T(1,128)} %broadcast_in_dim.8), calls=%async_computation.3 | async-start | bytes 196608 | tf_op jit(solution)/shard_map/all_to_all | solution.py:50
  (4 other events, 6.6 us)
Sparse Core Ops, SparseCore 0:
  10.1 45.2 all-gather.2
  103.9 45.6 reduce-scatter.1

commit v13 on v12

--- a/solution.py
+++ b/solution.py
@@ -100,9 +100,13 @@
     channel_position = lax.axis_index("ch")
     reach = depth_taps.shape[0] // 2
     gain_rows = jnp.stack(bf16_pieces(input_norm_gain, 3), 0)
-    gain_rows = jnp.pad(gain_rows, ((0, 13), (0, frames - local_cols)))
-    arrived = lax.all_gather(jnp.concatenate([signal, gain_rows], 0), "ch", axis=0)
-    complete_signal = arrived[:, :local_cols].reshape(groups * local_cols, frames)
+    cut = frames - frames // 4
+    gain_rows = jnp.pad(gain_rows, ((0, 13), (0, cut - local_cols)))
+    arrived = lax.all_gather(jnp.concatenate([signal[:, :cut], gain_rows], 0), "ch", axis=0)
+    arrived_late = gather_by_shifts(signal[:, cut:], "ch")
+    complete_signal = jnp.concatenate([arrived[:, :local_cols], arrived_late], 2).reshape(
+        groups * local_cols, frames
+    )
     gain_parts = arrived[:, local_cols : local_cols + 3, :local_cols].astype(jnp.float32)
     complete_gain = ((gain_parts[:, 0] + gain_parts[:, 1]) + gain_parts[:, 2]).reshape(-1)
     centered_unit, inverse_deviation = standardize_rows(complete_signal)

time: 191 us -> 208 us (1.089)
  starting transfers between devices: 72.9 us -> 105 us
  waiting for transfers between devices: 56.8 us -> 40.8 us
  local copies, waits for them, and re-layouts: 9.96 us -> 14.5 us
  matrix products: 8.23 us -> 3.81 us
    ppermute x0 -> x7, starting transfers between devices: none -> 30.7 us  [gather_by_shifts(): lax.ppermute(block, axis, [(i, (i - shift) % count) for i in range(count)])]
    all_gather x1, waiting for transfers between devices: 32 us -> 7.99 us  [shards(): lax.all_gather(jnp.concatenate([signal[:, :cut], gain_rows], 0), 'ch', ax...]
    ppermute x0 -> x7, waiting for transfers between devices: none -> 10.2 us  [gather_by_shifts(): lax.ppermute(block, axis, [(i, (i - shift) % count) for i in range(count)])]
    all_to_all x2, starting transfers between devices: 19 us -> 23.6 us  [gather_by_exchange(): return lax.all_to_all(copies, axis, 0, 0, tiled=False)]
    all_to_all x1, waiting for transfers between devices: 5.13 us -> 1.72 us  [shards(): lax.all_to_all(outgoing, 'seq', 0, 0, tiled=False).astype(jnp.float32)]
    slice x0 -> x3, local copies, waits for them, and re-layouts: none -> 3.17 us  [the longest x1 1.39 us: shards(): arrived[:, :local_cols]]
    all_to_all x2, waiting for transfers between devices: 9.88 us -> 12.7 us  [gather_by_exchange(): return lax.all_to_all(copies, axis, 0, 0, tiled=False)]
    ppermute x2, starting transfers between devices: 9.55 us -> 6.92 us  [extended(): lax.ppermute(tail, axis, [(i, (i + 1) % count) for i in range(ends)])]
  transfers between devices with their start and end apart: 16 -> 23, of which waited for: 8 -> 11; matrix products, arithmetic and copies ran while one was open for 9% -> 11% of each run, Pallas kernels for 0% -> 0%
where the time goes in v13:
time: 208 us; the launch traced here: 207 us
  starting transfers between devices  105 us (50%)
  waiting for transfers between devices  40.8 us (20%)
  other arithmetic  27.6 us (13%)
  between operations  15.2 us (7%)
  local copies, waits for them, and re-layouts  14.5 us (7%)
  matrix products  3.81 us (2%)
    ppermute x7, starting transfers between devices, gather_by_shifts(): lax.ppermute(block, axis, [(i, (i - shift) % count) for i in range(count)])  30.7 us
    ppermute x7, starting transfers between devices, reduce_by_shifts(): lax.ppermute(outgoing, axis, [(i, (i + shift) % count) for i in range(cou...  23.9 us
    all_to_all x2, starting transfers between devices, gather_by_exchange(): return lax.all_to_all(copies, axis, 0, 0, tiled=False)  23.6 us
    all_to_all x1, starting transfers between devices, shards(): lax.all_to_all(outgoing, 'seq', 0, 0, tiled=False).astype(jnp.float32)  15.5 us
    all_to_all x2, waiting for transfers between devices, gather_by_exchange(): return lax.all_to_all(copies, axis, 0, 0, tiled=False)  12.7 us
    ppermute x7, waiting for transfers between devices, gather_by_shifts(): lax.ppermute(block, axis, [(i, (i - shift) % count) for i in range(count)])  10.2 us
    all_gather x1, waiting for transfers between devices, shards(): lax.all_gather(jnp.concatenate([signal[:, :cut], gain_rows], 0), 'ch', ax...  7.99 us
    reduce_sum x2, other arithmetic, shards(): jnp.sum(glued_pad[:, k:k + span] * grad_pre_f, 1)  6.97 us
  transfers between devices with their start and end apart: 23, of which 11 were waited for; matrix products, arithmetic and copies ran while one was open for 11% of the time, Pallas kernels for 0%

profile of v13, /device:TPU:1, one launch (start us, length us, event | category | flops | bytes accessed | tf_op | source)
XLA Modules:
  0.0 206.9 jit_solution(6505590085621463585)
XLA Ops:
  8.1 6.6 %collective-permute-start.5 = (bf16[192,128]{1,0:T(8,128)(2,1)S(1)}, bf16[192,128]{1,0:T(8,128)(2,1)S(1)}, u32[]{:S(2)}, u32[]{:S(2)}) collective-permute-start(bf16[192,128]{1,0:T(8,128)(2,1)S(1)} %slice.513), channel_id=1, source_target_pairs={{0,2},{1,3},{2,4},{3,5},{4,6},{5,7},{6,0},{7,1},{8,10},{9,11},{10,... | collective-permute-start | bytes 147464 | tf_op jit(solution)/shard_map/ppermute | solution.py:69
  14.7 7.9 %collective-permute-start.4 = (bf16[192,128]{1,0:T(8,128)(2,1)S(1)}, bf16[192,128]{1,0:T(8,128)(2,1)S(1)}, u32[]{:S(2)}, u32[]{:S(2)}) collective-permute-start(bf16[192,128]{1,0:T(8,128)(2,1)S(1)} %slice.513), channel_id=1, source_target_pairs={{0,3},{1,4},{2,5},{3,6},{4,7},{5,0},{6,1},{7,2},{8,11},{9,12},{10,... | collective-permute-start | bytes 147464 | tf_op jit(solution)/shard_map/ppermute | solution.py:69
  22.7 3.7 %collective-permute-start.3 = (bf16[192,128]{1,0:T(8,128)(2,1)S(1)}, bf16[192,128]{1,0:T(8,128)(2,1)S(1)}, u32[]{:S(2)}, u32[]{:S(2)}) collective-permute-start(bf16[192,128]{1,0:T(8,128)(2,1)S(1)} %slice.513), channel_id=1, source_target_pairs={{0,4},{1,5},{2,6},{3,7},{4,0},{5,1},{6,2},{7,3},{8,12},{9,13},{10,... | collective-permute-start | bytes 147464 | tf_op jit(solution)/shard_map/ppermute | solution.py:69
  26.4 5.5 %collective-permute-start.2 = (bf16[192,128]{1,0:T(8,128)(2,1)S(1)}, bf16[192,128]{1,0:T(8,128)(2,1)S(1)}, u32[]{:S(2)}, u32[]{:S(2)}) collective-permute-start(bf16[192,128]{1,0:T(8,128)(2,1)S(1)} %slice.513), channel_id=1, source_target_pairs={{0,5},{1,6},{2,7},{3,0},{4,1},{5,2},{6,3},{7,4},{8,13},{9,14},{10,... | collective-permute-start | bytes 147464 | tf_op jit(solution)/shard_map/ppermute | solution.py:69
  38.4 12.2 %all-to-all-start = ((bf16[64,24,384]{2,1,0:T(8,128)(2,1)}), bf16[64,24,384]{2,1,0:T(8,128)(2,1)S(1)}, u32[]{:S(2)}, u32[]{:S(2)}) async-start(bf16[64,24,384]{2,1,0:T(8,128)(2,1)} %broadcast_in_dim.6), calls=%async_computation | async-start | bytes 2359296 | tf_op jit(solution)/shard_map/all_to_all | solution.py:50
  52.0 2.8 %collective-permute-start.1 = (bf16[192,128]{1,0:T(8,128)(2,1)S(1)}, bf16[192,128]{1,0:T(8,128)(2,1)S(1)}, u32[]{:S(2)}, u32[]{:S(2)}) collective-permute-start(bf16[192,128]{1,0:T(8,128)(2,1)S(1)} %slice.513), channel_id=1, source_target_pairs={{0,6},{1,7},{2,0},{3,1},{4,2},{5,3},{6,4},{7,5},{8,14},{9,15},{10,... | collective-permute-start | bytes 147464 | tf_op jit(solution)/shard_map/ppermute | solution.py:69
  54.9 5.2 %collective-permute-done.1 = bf16[192,128]{1,0:T(8,128)(2,1)S(1)} collective-permute-done((bf16[192,128]{1,0:T(8,128)(2,1)S(1)}, bf16[192,128]{1,0:T(8,128)(2,1)S(1)}, u32[]{:S(2)}, u32[]{:S(2)}) %collective-permute-start.1) | collective-permute-done | bytes 49184 | tf_op jit(solution)/shard_map/ppermute | solution.py:69
  62.2 4.9 %collective-permute-done.6 = bf16[192,128]{1,0:T(8,128)(2,1)S(1)} collective-permute-done((bf16[192,128]{1,0:T(8,128)(2,1)S(1)}, bf16[192,128]{1,0:T(8,128)(2,1)S(1)}, u32[]{:S(2)}, u32[]{:S(2)}) %collective-permute-start.6) | collective-permute-done | bytes 49184 | tf_op jit(solution)/shard_map/ppermute | solution.py:69
  67.3 8.0 %all-gather.3.cloned.1.call-done = bf16[1664,384]{1,0:T(8,128)(2,1)} async-done(((bf16[208,384]{1,0:T(8,128)(2,1)}), bf16[1664,384]{1,0:T(8,128)(2,1)}) %all-gather.3.cloned.1.call-update) | async-done | bytes 1277968 | tf_op jit(solution)/shard_map/all_gather | solution.py:105
  78.4 2.8 %all-to-all-done = bf16[64,24,384]{2,1,0:T(8,128)(2,1)S(1)} async-done(((bf16[64,24,384]{2,1,0:T(8,128)(2,1)}), bf16[64,24,384]{2,1,0:T(8,128)(2,1)S(1)}, u32[]{:S(2)}, u32[]{:S(2)}) %all-to-all-start) | async-done | bytes 1179680 | tf_op jit(solution)/shard_map/all_to_all | solution.py:50
  82.8 4.8 %collective-permute-start.7 = (bf16[192,15]{1,0:T(8,128)(2,1)S(1)}, bf16[192,15]{1,0:T(8,128)(2,1)S(1)}, u32[]{:S(2)}, u32[]{:S(2)}) collective-permute-start(bf16[192,15]{1,0:T(8,128)(2,1)S(1)} %get-tuple-element.55), channel_id=1, source_target_pairs={{0,8},{8,16},{16,24},{24,32},{32,40},{40,48},{48,56},{56,64},{64,7... | collective-permute-start | bytes 17288 | tf_op jit(solution)/shard_map/ppermute | solution.py:15
  93.4 5.0 %fusion.41 = (f32[192]{0:T(256)S(1)}, f32[192]{0:T(256)S(1)}, f32[192]{0:T(256)S(1)}, f32[192]{0:T(256)S(1)}, f32[192]{0:T(256)S(1)}, /*index=5*/f32[192]{0:T(25...) fusion(f32[192,542]{1,0:T(8,128)S(1)} %maximum_convert_fusion.1, ...), kind=kLoop, calls=%fused_computation.83 | loop fusion | flops 10613376 | bytes 13013760 | tf_op jit(solution)/shard_map/reduce_sum | solution.py:139
  102.9 2.3 %collective-permute-start.10 = (bf16[192,15]{1,0:T(8,128)(2,1)S(1)}, bf16[192,15]{1,0:T(8,128)(2,1)S(1)}, u32[]{:S(2)}, u32[]{:S(2)}) collective-permute-start(bf16[192,15]{1,0:T(8,128)(2,1)S(1)} %get-tuple-element.54), channel_id=1, source_target_pairs={{8,0},{16,8},{24,16},{32,24},{40,32},{48,40},{56,48},{64,56},{72,6... | collective-permute-start | bytes 17288 | tf_op jit(solution)/shard_map/ppermute | solution.py:17
  106.0 2.2 %collective-permute-done.10 = bf16[192,15]{1,0:T(8,128)(2,1)S(1)} collective-permute-done((bf16[192,15]{1,0:T(8,128)(2,1)S(1)}, bf16[192,15]{1,0:T(8,128)(2,1)S(1)}, u32[]{:S(2)}, u32[]{:S(2)}) %collective-permute-start.10) | collective-permute-done | bytes 5792 | tf_op jit(solution)/shard_map/ppermute | solution.py:17
  108.5 4.4 %multiply_convert_fusion.6 = (bf16[192,512]{1,0:T(8,128)(2,1)S(1)}, f32[192,512]{1,0:T(8,128)S(1)}) fusion(f32[384,512]{1,0:T(8,128)S(1)} %fusion.2, f32[192,542]{1,0:T(8,128)S(1)} %maximum_convert_fusion.2, f32[192]{0:T(256)S(1)} %bitcast.145, f32[192]{0:T(256)S(1)} %bitcast.183, f32[192]{0:T(256)S(1)} %bitcast.201, f32[192]{0:T(256)S(1)} %bitcast.199, ...), kind=kLoop, calls=%fused_computation.154 | loop fusion | flops 6488064 | bytes 13196544 | tf_op jit(solution)/shard_map/convert_element_type | solution.py:141
  119.8 15.5 %all-to-all-start.1 = ((bf16[64,25,384]{2,1,0:T(8,128)(2,1)}), bf16[64,25,384]{2,1,0:T(8,128)(2,1)}, u32[]{:S(2)}, u32[]{:S(2)}) async-start(bf16[64,25,384]{2,1,0:T(8,128)(2,1)} %pad_maximum_fusion), calls=%async_computation.2 | async-start | bytes 3145728 | tf_op jit(solution)/shard_map/all_to_all | solution.py:163
  141.2 4.2 %collective-permute-start.13 = (bf16[224,128]{1,0:T(8,128)(2,1)}, bf16[224,128]{1,0:T(8,128)(2,1)}, u32[]{:S(2)}, u32[]{:S(2)}) collective-permute-start(bf16[224,128]{1,0:T(8,128)(2,1)} %get-tuple-element.94), channel_id=1, source_target_pairs={{0,3},{1,4},{2,5},{3,6},{4,7},{5,0},{6,1},{7,2},{8,11},{9,12},{10,... | collective-permute-start | bytes 172040 | tf_op jit(solution)/shard_map/ppermute | solution.py:83
  145.4 5.0 %collective-permute-start.14 = (bf16[224,128]{1,0:T(8,128)(2,1)}, bf16[224,128]{1,0:T(8,128)(2,1)S(1)}, u32[]{:S(2)}, u32[]{:S(2)}) collective-permute-start(bf16[224,128]{1,0:T(8,128)(2,1)} %get-tuple-element.95), channel_id=1, source_target_pairs={{0,4},{1,5},{2,6},{3,7},{4,0},{5,1},{6,2},{7,3},{8,12},{9,13},{10,... | collective-permute-start | bytes 172040 | tf_op jit(solution)/shard_map/ppermute | solution.py:83
  150.4 3.8 %collective-permute-start.15 = (bf16[224,128]{1,0:T(8,128)(2,1)}, bf16[224,128]{1,0:T(8,128)(2,1)S(1)}, u32[]{:S(2)}, u32[]{:S(2)}) collective-permute-start(bf16[224,128]{1,0:T(8,128)(2,1)} %get-tuple-element.96), channel_id=1, source_target_pairs={{0,5},{1,6},{2,7},{3,0},{4,1},{5,2},{6,3},{7,4},{8,13},{9,14},{10,... | collective-permute-start | bytes 172040 | tf_op jit(solution)/shard_map/ppermute | solution.py:83
  154.2 4.3 %collective-permute-start.16 = (bf16[224,128]{1,0:T(8,128)(2,1)}, bf16[224,128]{1,0:T(8,128)(2,1)S(1)}, u32[]{:S(2)}, u32[]{:S(2)}) collective-permute-start(bf16[224,128]{1,0:T(8,128)(2,1)} %get-tuple-element.97), channel_id=1, source_target_pairs={{0,6},{1,7},{2,0},{3,1},{4,2},{5,3},{6,4},{7,5},{8,14},{9,15},{10,... | collective-permute-start | bytes 172040 | tf_op jit(solution)/shard_map/ppermute | solution.py:83
  158.5 2.4 %collective-permute-start.17 = (bf16[224,128]{1,0:T(8,128)(2,1)}, bf16[224,128]{1,0:T(8,128)(2,1)S(1)}, u32[]{:S(2)}, u32[]{:S(2)}) collective-permute-start(bf16[224,128]{1,0:T(8,128)(2,1)} %get-tuple-element.98), channel_id=1, source_target_pairs={{0,7},{1,0},{2,1},{3,2},{4,3},{5,4},{6,5},{7,6},{8,15},{9,8},{10,9... | collective-permute-start | bytes 172040 | tf_op jit(solution)/shard_map/ppermute | solution.py:83
  165.9 2.4 %collective-permute-done.12 = bf16[224,128]{1,0:T(8,128)(2,1)S(1)} collective-permute-done((bf16[224,128]{1,0:T(8,128)(2,1)}, bf16[224,128]{1,0:T(8,128)(2,1)S(1)}, u32[]{:S(2)}, u32[]{:S(2)}) %collective-permute-start.12) | collective-permute-done | bytes 57376 | tf_op jit(solution)/shard_map/ppermute | solution.py:83
  176.8 11.4 %all-to-all-start.2 = ((f32[64,1,288]{2,1,0:T(1,128)}), f32[64,1,288]{2,1,0:T(1,128)S(1)}, u32[]{:S(2)}, u32[]{:S(2)}) async-start(f32[64,1,288]{2,1,0:T(1,128)} %broadcast_in_dim.8), calls=%async_computation.3 | async-start | bytes 196608 | tf_op jit(solution)/shard_map/all_to_all | solution.py:50
  188.9 9.9 %all-to-all-done.2 = f32[64,1,288]{2,1,0:T(1,128)S(1)} async-done(((f32[64,1,288]{2,1,0:T(1,128)}), f32[64,1,288]{2,1,0:T(1,128)S(1)}, u32[]{:S(2)}, u32[]{:S(2)}) %all-to-all-start.2) | async-done | bytes 73760 | tf_op jit(solution)/shard_map/all_to_all | solution.py:50
  (192 shorter events, 54.1 us)
Async XLA Ops:
  7.2 43.5 %copy-start.8 = (f32[31,192]{1,0:T(8,128)S(1)}, f32[31,192]{1,0:T(8,128)}, u32[]{:S(2)}) copy-start(f32[31,192]{1,0:T(8,128)} %param.10) | copy-start | bytes 71428
  7.2 68.1 %all-gather.3.cloned.1.call-start = ((), (), s32[]{:S(2)}) async-start(), calls=%async_computation.5 | async-start | bytes 1437696 | tf_op jit(solution)/shard_map/all_gather | solution.py:105
  8.1 54.1 %collective-permute-start.5 = (bf16[192,128]{1,0:T(8,128)(2,1)S(1)}, bf16[192,128]{1,0:T(8,128)(2,1)S(1)}, u32[]{:S(2)}, u32[]{:S(2)}) collective-permute-start(bf16[192,128]{1,0:T(8,128)(2,1)S(1)} %slice.513), channel_id=1, source_target_pairs={{0,2},{1,3},{2,4},{3,5},{4,6},{5,7},{6,0},{7,1},{8,10},{9,11},{10,... | collective-permute-start | bytes 147464 | tf_op jit(solution)/shard_map/ppermute | solution.py:69
  14.7 47.4 %collective-permute-start.4 = (bf16[192,128]{1,0:T(8,128)(2,1)S(1)}, bf16[192,128]{1,0:T(8,128)(2,1)S(1)}, u32[]{:S(2)}, u32[]{:S(2)}) collective-permute-start(bf16[192,128]{1,0:T(8,128)(2,1)S(1)} %slice.513), channel_id=1, source_target_pairs={{0,3},{1,4},{2,5},{3,6},{4,7},{5,0},{6,1},{7,2},{8,11},{9,12},{10,... | collective-permute-start | bytes 147464 | tf_op jit(solution)/shard_map/ppermute | solution.py:69
  22.7 39.4 %collective-permute-start.3 = (bf16[192,128]{1,0:T(8,128)(2,1)S(1)}, bf16[192,128]{1,0:T(8,128)(2,1)S(1)}, u32[]{:S(2)}, u32[]{:S(2)}) collective-permute-start(bf16[192,128]{1,0:T(8,128)(2,1)S(1)} %slice.513), channel_id=1, source_target_pairs={{0,4},{1,5},{2,6},{3,7},{4,0},{5,1},{6,2},{7,3},{8,12},{9,13},{10,... | collective-permute-start | bytes 147464 | tf_op jit(solution)/shard_map/ppermute | solution.py:69
  26.4 35.7 %collective-permute-start.2 = (bf16[192,128]{1,0:T(8,128)(2,1)S(1)}, bf16[192,128]{1,0:T(8,128)(2,1)S(1)}, u32[]{:S(2)}, u32[]{:S(2)}) collective-permute-start(bf16[192,128]{1,0:T(8,128)(2,1)S(1)} %slice.513), channel_id=1, source_target_pairs={{0,5},{1,6},{2,7},{3,0},{4,1},{5,2},{6,3},{7,4},{8,13},{9,14},{10,... | collective-permute-start | bytes 147464 | tf_op jit(solution)/shard_map/ppermute | solution.py:69
  31.9 20.2 %collective-permute-start = (bf16[192,128]{1,0:T(8,128)(2,1)S(1)}, bf16[192,128]{1,0:T(8,128)(2,1)S(1)}, u32[]{:S(2)}, u32[]{:S(2)}) collective-permute-start(bf16[192,128]{1,0:T(8,128)(2,1)S(1)} %slice.513), channel_id=1, source_target_pairs={{0,7},{1,0},{2,1},{3,2},{4,3},{5,4},{6,5},{7,6},{8,15},{9,8},{10,9... | collective-permute-start | bytes 147464 | tf_op jit(solution)/shard_map/ppermute | solution.py:69
  38.4 42.8 %all-to-all-start = ((bf16[64,24,384]{2,1,0:T(8,128)(2,1)}), bf16[64,24,384]{2,1,0:T(8,128)(2,1)S(1)}, u32[]{:S(2)}, u32[]{:S(2)}) async-start(bf16[64,24,384]{2,1,0:T(8,128)(2,1)} %broadcast_in_dim.6), calls=%async_computation | async-start | bytes 2359296 | tf_op jit(solution)/shard_map/all_to_all | solution.py:50
  50.6 119.4 %reduce-scatter.2.cloned.1.call-start = ((), (), s32[]{:S(2)}) async-start(), calls=%async_computation.4 | async-start | bytes 1327104 | tf_op jit(solution)/shard_map/reduce_scatter | solution.py:179
  52.0 8.1 %collective-permute-start.1 = (bf16[192,128]{1,0:T(8,128)(2,1)S(1)}, bf16[192,128]{1,0:T(8,128)(2,1)S(1)}, u32[]{:S(2)}, u32[]{:S(2)}) collective-permute-start(bf16[192,128]{1,0:T(8,128)(2,1)S(1)} %slice.513), channel_id=1, source_target_pairs={{0,6},{1,7},{2,0},{3,1},{4,2},{5,3},{6,4},{7,5},{8,14},{9,15},{10,... | collective-permute-start | bytes 147464 | tf_op jit(solution)/shard_map/ppermute | solution.py:69
  60.1 7.0 %collective-permute-start.6 = (bf16[192,128]{1,0:T(8,128)(2,1)S(1)}, bf16[192,128]{1,0:T(8,128)(2,1)S(1)}, u32[]{:S(2)}, u32[]{:S(2)}) collective-permute-start(bf16[192,128]{1,0:T(8,128)(2,1)S(1)} %slice.513), channel_id=1, source_target_pairs={{0,1},{1,2},{2,3},{3,4},{4,5},{5,6},{6,7},{7,0},{8,9},{9,10},{10,1... | collective-permute-start | bytes 147464 | tf_op jit(solution)/shard_map/ppermute | solution.py:69
  82.8 8.7 %collective-permute-start.7 = (bf16[192,15]{1,0:T(8,128)(2,1)S(1)}, bf16[192,15]{1,0:T(8,128)(2,1)S(1)}, u32[]{:S(2)}, u32[]{:S(2)}) collective-permute-start(bf16[192,15]{1,0:T(8,128)(2,1)S(1)} %get-tuple-element.55), channel_id=1, source_target_pairs={{0,8},{8,16},{16,24},{24,32},{32,40},{40,48},{48,56},{56,64},{64,7... | collective-permute-start | bytes 17288 | tf_op jit(solution)/shard_map/ppermute | solution.py:15
  87.6 5.4 %collective-permute-start.8 = (bf16[192,15]{1,0:T(8,128)(2,1)S(1)}, bf16[192,15]{1,0:T(8,128)(2,1)S(1)}, u32[]{:S(2)}, u32[]{:S(2)}) collective-permute-start(bf16[192,15]{1,0:T(8,128)(2,1)S(1)} %get-tuple-element.56), channel_id=1, source_target_pairs={{8,0},{16,8},{24,16},{32,24},{40,32},{48,40},{56,48},{64,56},{72,6... | collective-permute-start | bytes 17288 | tf_op jit(solution)/shard_map/ppermute | solution.py:17
  100.7 5.3 %collective-permute-start.9 = (bf16[192,15]{1,0:T(8,128)(2,1)S(1)}, bf16[192,15]{1,0:T(8,128)(2,1)S(1)}, u32[]{:S(2)}, u32[]{:S(2)}) collective-permute-start(bf16[192,15]{1,0:T(8,128)(2,1)S(1)} %get-tuple-element.53), channel_id=1, source_target_pairs={{0,8},{8,16},{16,24},{24,32},{32,40},{40,48},{48,56},{56,64},{64,7... | collective-permute-start | bytes 17288 | tf_op jit(solution)/shard_map/ppermute | solution.py:15
  102.9 5.4 %collective-permute-start.10 = (bf16[192,15]{1,0:T(8,128)(2,1)S(1)}, bf16[192,15]{1,0:T(8,128)(2,1)S(1)}, u32[]{:S(2)}, u32[]{:S(2)}) collective-permute-start(bf16[192,15]{1,0:T(8,128)(2,1)S(1)} %get-tuple-element.54), channel_id=1, source_target_pairs={{8,0},{16,8},{24,16},{32,24},{40,32},{48,40},{56,48},{64,56},{72,6... | collective-permute-start | bytes 17288 | tf_op jit(solution)/shard_map/ppermute | solution.py:17
  119.8 54.5 %all-to-all-start.1 = ((bf16[64,25,384]{2,1,0:T(8,128)(2,1)}), bf16[64,25,384]{2,1,0:T(8,128)(2,1)}, u32[]{:S(2)}, u32[]{:S(2)}) async-start(bf16[64,25,384]{2,1,0:T(8,128)(2,1)} %pad_maximum_fusion), calls=%async_computation.2 | async-start | bytes 3145728 | tf_op jit(solution)/shard_map/all_to_all | solution.py:163
  139.0 19.5 %collective-permute-start.11 = (bf16[224,128]{1,0:T(8,128)(2,1)}, bf16[224,128]{1,0:T(8,128)(2,1)}, u32[]{:S(2)}, u32[]{:S(2)}) collective-permute-start(bf16[224,128]{1,0:T(8,128)(2,1)} %get-tuple-element.93), channel_id=1, source_target_pairs={{0,1},{1,2},{2,3},{3,4},{4,5},{5,6},{6,7},{7,0},{8,9},{9,10},{10,1... | collective-permute-start | bytes 172040 | tf_op jit(solution)/shard_map/ppermute | solution.py:83
  141.2 19.8 %collective-permute-start.13 = (bf16[224,128]{1,0:T(8,128)(2,1)}, bf16[224,128]{1,0:T(8,128)(2,1)}, u32[]{:S(2)}, u32[]{:S(2)}) collective-permute-start(bf16[224,128]{1,0:T(8,128)(2,1)} %get-tuple-element.94), channel_id=1, source_target_pairs={{0,3},{1,4},{2,5},{3,6},{4,7},{5,0},{6,1},{7,2},{8,11},{9,12},{10,... | collective-permute-start | bytes 172040 | tf_op jit(solution)/shard_map/ppermute | solution.py:83
  145.4 18.4 %collective-permute-start.14 = (bf16[224,128]{1,0:T(8,128)(2,1)}, bf16[224,128]{1,0:T(8,128)(2,1)S(1)}, u32[]{:S(2)}, u32[]{:S(2)}) collective-permute-start(bf16[224,128]{1,0:T(8,128)(2,1)} %get-tuple-element.95), channel_id=1, source_target_pairs={{0,4},{1,5},{2,6},{3,7},{4,0},{5,1},{6,2},{7,3},{8,12},{9,13},{10,... | collective-permute-start | bytes 172040 | tf_op jit(solution)/shard_map/ppermute | solution.py:83
  150.4 13.4 %collective-permute-start.15 = (bf16[224,128]{1,0:T(8,128)(2,1)}, bf16[224,128]{1,0:T(8,128)(2,1)S(1)}, u32[]{:S(2)}, u32[]{:S(2)}) collective-permute-start(bf16[224,128]{1,0:T(8,128)(2,1)} %get-tuple-element.96), channel_id=1, source_target_pairs={{0,5},{1,6},{2,7},{3,0},{4,1},{5,2},{6,3},{7,4},{8,13},{9,14},{10,... | collective-permute-start | bytes 172040 | tf_op jit(solution)/shard_map/ppermute | solution.py:83
  154.2 11.0 %collective-permute-start.16 = (bf16[224,128]{1,0:T(8,128)(2,1)}, bf16[224,128]{1,0:T(8,128)(2,1)S(1)}, u32[]{:S(2)}, u32[]{:S(2)}) collective-permute-start(bf16[224,128]{1,0:T(8,128)(2,1)} %get-tuple-element.97), channel_id=1, source_target_pairs={{0,6},{1,7},{2,0},{3,1},{4,2},{5,3},{6,4},{7,5},{8,14},{9,15},{10,... | collective-permute-start | bytes 172040 | tf_op jit(solution)/shard_map/ppermute | solution.py:83
  158.5 7.3 %collective-permute-start.17 = (bf16[224,128]{1,0:T(8,128)(2,1)}, bf16[224,128]{1,0:T(8,128)(2,1)S(1)}, u32[]{:S(2)}, u32[]{:S(2)}) collective-permute-start(bf16[224,128]{1,0:T(8,128)(2,1)} %get-tuple-element.98), channel_id=1, source_target_pairs={{0,7},{1,0},{2,1},{3,2},{4,3},{5,4},{6,5},{7,6},{8,15},{9,8},{10,9... | collective-permute-start | bytes 172040 | tf_op jit(solution)/shard_map/ppermute | solution.py:83
  161.0 7.3 %collective-permute-start.12 = (bf16[224,128]{1,0:T(8,128)(2,1)}, bf16[224,128]{1,0:T(8,128)(2,1)S(1)}, u32[]{:S(2)}, u32[]{:S(2)}) collective-permute-start(bf16[224,128]{1,0:T(8,128)(2,1)} %get-tuple-element.99), channel_id=1, source_target_pairs={{0,2},{1,3},{2,4},{3,5},{4,6},{5,7},{6,0},{7,1},{8,10},{9,11},{10,... | collective-permute-start | bytes 172040 | tf_op jit(solution)/shard_map/ppermute | solution.py:83
  176.8 22.0 %all-to-all-start.2 = ((f32[64,1,288]{2,1,0:T(1,128)}), f32[64,1,288]{2,1,0:T(1,128)S(1)}, u32[]{:S(2)}, u32[]{:S(2)}) async-start(f32[64,1,288]{2,1,0:T(1,128)} %broadcast_in_dim.8), calls=%async_computation.3 | async-start | bytes 196608 | tf_op jit(solution)/shard_map/all_to_all | solution.py:50
  (42 other events, 515.4 us)
Sparse Core Ops, SparseCore 0:
  36.6 38.6 all-gather.2
  117.5 44.8 reduce-scatter.1

commit v14 on v12

--- a/solution.py
+++ b/solution.py
@@ -131,9 +131,8 @@
     grad_pre_f = grad_pre.astype(jnp.float32)
     grad_pad = extended(grad_pre, (("seq", 1),), reach).astype(jnp.float32)
     grad_glued = shifted_sum(grad_pad, depth_taps[::-1], span)
-    tap_partial = jnp.stack(
-        [jnp.sum(glued_pad[:, k : k + span] * grad_pre_f, 1) for k in range(taps_count)], 0
-    )
+    windows = jnp.stack([glued_pad[:, k : k + span] for k in range(taps_count)], 0)
+    tap_partial = jnp.sum(windows * grad_pre_f[None], 2)
     grad_v = (grad_glued * sig_gate).astype(jnp.bfloat16)
     grad_g = (grad_glued * value * sig_gate * (1.0 - sig_gate)).astype(jnp.bfloat16)
     grad_both = jnp.concatenate([grad_v, grad_g], 0)

time: 191 us -> 194 us (1.016)
  local copies, waits for them, and re-layouts: 9.96 us -> 15.7 us
  waiting for transfers between devices: 56.8 us -> 52.1 us
  other arithmetic: 27.5 us -> 31.3 us
    convert_element_type x0 -> x1, other arithmetic: none -> 5.98 us  [shards(): grad_pre_f = grad_pre.astype(jnp.float32)]
    reduce_sum x2 -> x1, other arithmetic: 6.84 us -> 2.64 us  [shards(): tap_partial = jnp.sum(windows * grad_pre_f[None], 2)]
    ppermute x2, waiting for transfers between devices: 5.39 us -> 2.29 us  [extended(): lax.ppermute(head, axis, [((i + 1) % count, i) for i in range(ends)])]
    unnamed x26 -> x82, local copies, waits for them, and re-layouts: 3.35 us -> 5.1 us
  transfers between devices with their start and end apart: 16 -> 16, of which waited for: 8 -> 6; matrix products, arithmetic and copies ran while one was open for 9% -> 15% of each run, Pallas kernels for 0% -> 0%
where the time goes in v14:
time: 194 us; the launch traced here: 193 us
  starting transfers between devices  71.5 us (37%)
  waiting for transfers between devices  52.1 us (27%)
  other arithmetic  31.3 us (16%)
  local copies, waits for them, and re-layouts  15.7 us (8%)
  between operations  14.9 us (8%)
  matrix products  7.17 us (4%)
    all_gather x1, waiting for transfers between devices, shards(): lax.all_gather(jnp.concatenate([signal, gain_rows], 0), 'ch', axis=0)  30.3 us
    ppermute x7, starting transfers between devices, reduce_by_shifts(): lax.ppermute(outgoing, axis, [(i, (i + shift) % count) for i in range(cou...  24.3 us
    all_to_all x2, starting transfers between devices, gather_by_exchange(): return lax.all_to_all(copies, axis, 0, 0, tiled=False)  18.9 us
    all_to_all x1, starting transfers between devices, shards(): lax.all_to_all(outgoing, 'seq', 0, 0, tiled=False).astype(jnp.float32)  13.5 us
    all_to_all x2, waiting for transfers between devices, gather_by_exchange(): return lax.all_to_all(copies, axis, 0, 0, tiled=False)  9.88 us
    ppermute x2, starting transfers between devices, extended(): lax.ppermute(tail, axis, [(i, (i + 1) % count) for i in range(ends)])  9.54 us
    convert_element_type x1, other arithmetic, shards(): grad_pre_f = grad_pre.astype(jnp.float32)  5.98 us
    convert_element_type x1, other arithmetic, shards(): grad_v = (grad_glued * sig_gate).astype(jnp.bfloat16)  5.32 us
  transfers between devices with their start and end apart: 16, of which 6 were waited for; matrix products, arithmetic and copies ran while one was open for 15% of the time, Pallas kernels for 0%

profile of v14, /device:TPU:1, one launch (start us, length us, event | category | flops | bytes accessed | tf_op | source)
XLA Modules:
  0.0 192.6 jit_solution(10333250302251031003)
XLA Ops:
  11.6 11.6 %all-to-all-start = ((bf16[64,24,384]{2,1,0:T(8,128)(2,1)}), bf16[64,24,384]{2,1,0:T(8,128)(2,1)S(1)}, u32[]{:S(2)}, u32[]{:S(2)}) async-start(bf16[64,24,384]{2,1,0:T(8,128)(2,1)} %broadcast_in_dim.6), calls=%async_computation | async-start | bytes 2359296 | tf_op jit(solution)/shard_map/all_to_all | solution.py:50
  25.0 30.3 %all-gather.3.cloned.1.call-done = bf16[1664,512]{1,0:T(8,128)(2,1)} async-done(((bf16[208,512]{1,0:T(8,128)(2,1)}), bf16[1664,512]{1,0:T(8,128)(2,1)}) %all-gather.3.cloned.1.call-update) | async-done | bytes 1703952 | tf_op jit(solution)/shard_map/all_gather | solution.py:104
  62.7 7.6 %collective-permute-start = (bf16[192,15]{1,0:T(8,128)(2,1)S(1)}, bf16[192,15]{1,0:T(8,128)(2,1)S(1)}, u32[]{:S(2)}, u32[]{:S(2)}) collective-permute-start(bf16[192,15]{1,0:T(8,128)(2,1)S(1)} %get-tuple-element.27), channel_id=1, source_target_pairs={{0,8},{8,16},{16,24},{24,32},{32,40},{40,48},{48,56},{56,64},{64,7... | collective-permute-start | bytes 17288 | tf_op jit(solution)/shard_map/ppermute | solution.py:15
  70.3 1.9 collective-permute-start.1
  73.5 2.3 %collective-permute-done.1 = bf16[192,15]{1,0:T(8,128)(2,1)S(1)} collective-permute-done((bf16[192,15]{1,0:T(8,128)(2,1)S(1)}, bf16[192,15]{1,0:T(8,128)(2,1)S(1)}, u32[]{:S(2)}, u32[]{:S(2)}) %collective-permute-start.1) | collective-permute-done | bytes 5792 | tf_op jit(solution)/shard_map/ppermute | solution.py:17
  75.9 6.0 %fusion.65 = (f32[192,512]{1,0:T(8,128)}, bf16[192,512]{1,0:T(8,128)(2,1)S(1)}, f32[192,512]{1,0:T(8,128)}) fusion(bf16[192,512]{1,0:T(8,128)(2,1)} %param.11, f32[192,542]{1,0:T(8,128)S(1)} %maximum_convert_fusion, f32[192]{0:T(256)S(1)} %bitcast.212, f32[192]{0:T(256)S(1)} %bitcast.214, f32[192]{0:T(256)} %bitcast.156, f32[192]{0:T(256)} %bitcast.158, ...), kind=kLoop, calls=%fused_computation.197 | loop fusion | flops 7077888 | bytes 13393152 | tf_op jit(solution)/shard_map/convert_element_type | solution.py:131
  84.6 3.2 %collective-permute-start.3 = (bf16[192,15]{1,0:T(8,128)(2,1)}, bf16[192,15]{1,0:T(8,128)(2,1)}, u32[]{:S(2)}, u32[]{:S(2)}) collective-permute-start(bf16[192,15]{1,0:T(8,128)(2,1)} %get-tuple-element.26), channel_id=1, source_target_pairs={{8,0},{16,8},{24,16},{32,24},{40,32},{48,40},{56,48},{64,56},{72,6... | collective-permute-start | bytes 17288 | tf_op jit(solution)/shard_map/ppermute | solution.py:17
  93.1 2.6 %multiply_reduce_fusion = f32[31,192]{1,0:T(8,128)S(1)} fusion(f32[31,192,512]{2,1,0:T(8,128)S(1)} %bitcast_dynamic-update-slice_fusion, f32[192,512]{1,0:T(8,128)} %get-tuple-element.8), kind=kLoop, calls=%fused_computation | loop fusion | flops 6088896 | bytes 12606720 | tf_op jit(solution)/shard_map/reduce_sum | solution.py:135
  97.1 5.3 %multiply_convert_fusion.5 = (bf16[192,512]{1,0:T(8,128)(2,1)S(1)}, f32[192,512]{1,0:T(8,128)S(1)}) fusion(f32[384,512]{1,0:T(8,128)S(1)} %fusion.75, f32[192,542]{1,0:T(8,128)S(1)} %maximum_convert_fusion.1, f32[192]{0:T(256)S(1)} %bitcast.155, f32[192]{0:T(256)} %bitcast.193, f32[192]{0:T(256)} %bitcast.211, f32[192]{0:T(256)} %bitcast.209, ...), kind=kLoop, calls=%fused_computation.116 | loop fusion | flops 6488064 | bytes 13196544 | tf_op jit(solution)/shard_map/convert_element_type | solution.py:136
  102.7 3.5 %fusion.1 = (f32[512]{0:T(512)S(1)}, f32[512]{0:T(512)S(1)}, f32[1536,512]{1,0:T(8,128)}, bf16[1536,512]{1,0:T(8,128)(2,1)}) fusion(f32[1536]{0:T(1024)S(1)} %add.437, f32[512]{0:T(512)S(1)} %copy-done.7, f32[512]{0:T(512)S(1)} %copy-done.9, bf16[8,208,512]{2,1,0:T(8,128)(2,1)S(1)} %bitcast.144, bf16[1536,384]{1,0:T(8,128)(2,1)S(1)} %bitcast.147, ...), kind=kOutput, calls=%fused_computation.7 | convolution fusion | flops 611843072 | bytes 7878656 | tf_op jit(solution)/shard_map/dot_general | solution.py:145
  106.2 2.4 %slice.709 = bf16[1536,384]{1,0:T(8,128)(2,1)} slice(bf16[1536,512]{1,0:T(8,128)(2,1)} %get-tuple-element.79), slice={[0:1536], [0:384]} | slice | bytes 2359296 | tf_op jit(solution)/shard_map/slice | solution.py:175
  108.6 2.9 %convolution_convert_fusion.1 = bf16[1536,384]{1,0:T(8,128)(2,1)S(1)} fusion(f32[1536,512]{1,0:T(8,128)} %get-tuple-element.17, f32[1536]{0:T(1024)S(1)} %add.437, bf16[192,512]{1,0:T(8,128)(2,1)S(1)} %multiply_convert_fusion.4, bf16[192,512]{1,0:T(8,128)(2,1)S(1)} %get-tuple-element.13), kind=kOutput, calls=%fused_computation.12 | convolution fusion | flops 606928896 | bytes 4724736 | tf_op jit(solution)/shard_map/dot_general | solution.py:139
  112.9 13.5 %all-to-all-start.1 = ((bf16[64,25,384]{2,1,0:T(8,128)(2,1)}), bf16[64,25,384]{2,1,0:T(8,128)(2,1)S(1)}, u32[]{:S(2)}, u32[]{:S(2)}) async-start(bf16[64,25,384]{2,1,0:T(8,128)(2,1)} %pad_maximum_fusion), calls=%async_computation.2 | async-start | bytes 3145728 | tf_op jit(solution)/shard_map/all_to_all | solution.py:158
  127.7 2.8 %collective-permute-start.4 = (bf16[224,128]{1,0:T(8,128)(2,1)S(1)}, bf16[224,128]{1,0:T(8,128)(2,1)S(1)}, u32[]{:S(2)}, u32[]{:S(2)}) collective-permute-start(bf16[224,128]{1,0:T(8,128)(2,1)S(1)} %get-tuple-element.65), channel_id=1, source_target_pairs={{0,1},{1,2},{2,3},{3,4},{4,5},{5,6},{6,7},{7,0},{8,9},{9,10},{10,1... | collective-permute-start | bytes 172040 | tf_op jit(solution)/shard_map/ppermute | solution.py:83
  130.5 4.0 %collective-permute-start.6 = (bf16[224,128]{1,0:T(8,128)(2,1)S(1)}, bf16[224,128]{1,0:T(8,128)(2,1)S(1)}, u32[]{:S(2)}, u32[]{:S(2)}) collective-permute-start(bf16[224,128]{1,0:T(8,128)(2,1)S(1)} %get-tuple-element.66), channel_id=1, source_target_pairs={{0,3},{1,4},{2,5},{3,6},{4,7},{5,0},{6,1},{7,2},{8,11},{9,12},{10,... | collective-permute-start | bytes 172040 | tf_op jit(solution)/shard_map/ppermute | solution.py:83
  134.5 4.6 %collective-permute-start.7 = (bf16[224,128]{1,0:T(8,128)(2,1)S(1)}, bf16[224,128]{1,0:T(8,128)(2,1)S(1)}, u32[]{:S(2)}, u32[]{:S(2)}) collective-permute-start(bf16[224,128]{1,0:T(8,128)(2,1)S(1)} %get-tuple-element.67), channel_id=1, source_target_pairs={{0,4},{1,5},{2,6},{3,7},{4,0},{5,1},{6,2},{7,3},{8,12},{9,13},{10,... | collective-permute-start | bytes 172040 | tf_op jit(solution)/shard_map/ppermute | solution.py:83
  139.2 4.4 %collective-permute-start.8 = (bf16[224,128]{1,0:T(8,128)(2,1)S(1)}, bf16[224,128]{1,0:T(8,128)(2,1)S(1)}, u32[]{:S(2)}, u32[]{:S(2)}) collective-permute-start(bf16[224,128]{1,0:T(8,128)(2,1)S(1)} %get-tuple-element.68), channel_id=1, source_target_pairs={{0,5},{1,6},{2,7},{3,0},{4,1},{5,2},{6,3},{7,4},{8,13},{9,14},{10,... | collective-permute-start | bytes 172040 | tf_op jit(solution)/shard_map/ppermute | solution.py:83
  143.6 4.3 %collective-permute-start.9 = (bf16[224,128]{1,0:T(8,128)(2,1)S(1)}, bf16[224,128]{1,0:T(8,128)(2,1)S(1)}, u32[]{:S(2)}, u32[]{:S(2)}) collective-permute-start(bf16[224,128]{1,0:T(8,128)(2,1)S(1)} %get-tuple-element.69), channel_id=1, source_target_pairs={{0,6},{1,7},{2,0},{3,1},{4,2},{5,3},{6,4},{7,5},{8,14},{9,15},{10,... | collective-permute-start | bytes 172040 | tf_op jit(solution)/shard_map/ppermute | solution.py:83
  147.9 1.9 collective-permute-start.10
  149.8 2.3 %collective-permute-start.5 = (bf16[224,128]{1,0:T(8,128)(2,1)S(1)}, bf16[224,128]{1,0:T(8,128)(2,1)S(1)}, u32[]{:S(2)}, u32[]{:S(2)}) collective-permute-start(bf16[224,128]{1,0:T(8,128)(2,1)S(1)} %get-tuple-element.71), channel_id=1, source_target_pairs={{0,2},{1,3},{2,4},{3,5},{4,6},{5,7},{6,0},{7,1},{8,10},{9,11},{10,... | collective-permute-start | bytes 172040 | tf_op jit(solution)/shard_map/ppermute | solution.py:83
  154.4 3.1 %collective-permute-done.5 = bf16[224,128]{1,0:T(8,128)(2,1)S(1)} collective-permute-done((bf16[224,128]{1,0:T(8,128)(2,1)S(1)}, bf16[224,128]{1,0:T(8,128)(2,1)S(1)}, u32[]{:S(2)}, u32[]{:S(2)}) %collective-permute-start.5) | collective-permute-done | bytes 57376 | tf_op jit(solution)/shard_map/ppermute | solution.py:83
  160.4 5.0 %all-to-all-done.1 = bf16[64,25,384]{2,1,0:T(8,128)(2,1)S(1)} async-done(((bf16[64,25,384]{2,1,0:T(8,128)(2,1)}), bf16[64,25,384]{2,1,0:T(8,128)(2,1)S(1)}, u32[]{:S(2)}, u32[]{:S(2)}) %all-to-all-start.1) | async-done | bytes 1228832 | tf_op jit(solution)/shard_map/all_to_all | solution.py:158
  166.5 7.3 %all-to-all-start.2 = ((f32[64,1,288]{2,1,0:T(1,128)}), f32[64,1,288]{2,1,0:T(1,128)S(1)}, u32[]{:S(2)}, u32[]{:S(2)}) async-start(f32[64,1,288]{2,1,0:T(1,128)} %broadcast_in_dim.8), calls=%async_computation.3 | async-start | bytes 196608 | tf_op jit(solution)/shard_map/all_to_all | solution.py:50
  174.5 9.9 %all-to-all-done.2 = f32[64,1,288]{2,1,0:T(1,128)S(1)} async-done(((f32[64,1,288]{2,1,0:T(1,128)}), f32[64,1,288]{2,1,0:T(1,128)S(1)}, u32[]{:S(2)}, u32[]{:S(2)}) %all-to-all-start.2) | async-done | bytes 73760 | tf_op jit(solution)/shard_map/all_to_all | solution.py:50
  (153 shorter events, 34.9 us)
Async XLA Ops:
  7.2 48.2 %all-gather.3.cloned.1.call-start = ((), (), s32[]{:S(2)}) async-start(), calls=%async_computation.5 | async-start | bytes 1916928 | tf_op jit(solution)/shard_map/all_gather | solution.py:104
  11.6 50.1 %all-to-all-start = ((bf16[64,24,384]{2,1,0:T(8,128)(2,1)}), bf16[64,24,384]{2,1,0:T(8,128)(2,1)S(1)}, u32[]{:S(2)}, u32[]{:S(2)}) async-start(bf16[64,24,384]{2,1,0:T(8,128)(2,1)} %broadcast_in_dim.6), calls=%async_computation | async-start | bytes 2359296 | tf_op jit(solution)/shard_map/all_to_all | solution.py:50
  23.2 134.4 %reduce-scatter.2.cloned.1.call-start = ((), (), s32[]{:S(2)}) async-start(), calls=%async_computation.4 | async-start | bytes 1327104 | tf_op jit(solution)/shard_map/reduce_scatter | solution.py:174
  61.7 31.3 %copy-start.1 = (bf16[64,24,384]{2,1,0:T(8,128)(2,1)}, bf16[64,24,384]{2,1,0:T(8,128)(2,1)S(1)}, u32[]{:S(2)}) copy-start(bf16[64,24,384]{2,1,0:T(8,128)(2,1)S(1)} %all-to-all-done) | copy-start | bytes 3538948
  62.7 10.8 %collective-permute-start = (bf16[192,15]{1,0:T(8,128)(2,1)S(1)}, bf16[192,15]{1,0:T(8,128)(2,1)S(1)}, u32[]{:S(2)}, u32[]{:S(2)}) collective-permute-start(bf16[192,15]{1,0:T(8,128)(2,1)S(1)} %get-tuple-element.27), channel_id=1, source_target_pairs={{0,8},{8,16},{16,24},{24,32},{32,40},{40,48},{48,56},{56,64},{64,7... | collective-permute-start | bytes 17288 | tf_op jit(solution)/shard_map/ppermute | solution.py:15
  70.3 5.4 %collective-permute-start.1 = (bf16[192,15]{1,0:T(8,128)(2,1)S(1)}, bf16[192,15]{1,0:T(8,128)(2,1)S(1)}, u32[]{:S(2)}, u32[]{:S(2)}) collective-permute-start(bf16[192,15]{1,0:T(8,128)(2,1)S(1)} %get-tuple-element.28), channel_id=1, source_target_pairs={{8,0},{16,8},{24,16},{32,24},{40,32},{48,40},{56,48},{64,56},{72,6... | collective-permute-start | bytes 17288 | tf_op jit(solution)/shard_map/ppermute | solution.py:17
  73.3 16.5 %copy-start.12 = (f32[1,192]{1,0:T(1,128)}, f32[1,192]{1,0:T(1,128)S(1)}, u32[]{:S(2)}) copy-start(f32[1,192]{1,0:T(1,128)S(1)} %get-tuple-element.53) | copy-start | bytes 2308
  73.3 16.5 %copy-start.13 = (f32[1,192]{1,0:T(1,128)}, f32[1,192]{1,0:T(1,128)S(1)}, u32[]{:S(2)}) copy-start(f32[1,192]{1,0:T(1,128)S(1)} %get-tuple-element.54) | copy-start | bytes 2308
  73.3 16.5 %copy-start.14 = (f32[1,192]{1,0:T(1,128)}, f32[1,192]{1,0:T(1,128)S(1)}, u32[]{:S(2)}) copy-start(f32[1,192]{1,0:T(1,128)S(1)} %get-tuple-element.55) | copy-start | bytes 2308
  73.3 16.5 %copy-start.15 = (f32[1,192]{1,0:T(1,128)}, f32[1,192]{1,0:T(1,128)S(1)}, u32[]{:S(2)}) copy-start(f32[1,192]{1,0:T(1,128)S(1)} %get-tuple-element.56) | copy-start | bytes 2308
  73.3 16.5 %copy-start.16 = (f32[1,192]{1,0:T(1,128)}, f32[1,192]{1,0:T(1,128)S(1)}, u32[]{:S(2)}) copy-start(f32[1,192]{1,0:T(1,128)S(1)} %get-tuple-element.57) | copy-start | bytes 2308
  82.6 13.4 %collective-permute-start.2 = (bf16[192,15]{1,0:T(8,128)(2,1)}, bf16[192,15]{1,0:T(8,128)(2,1)}, u32[]{:S(2)}, u32[]{:S(2)}) collective-permute-start(bf16[192,15]{1,0:T(8,128)(2,1)} %get-tuple-element.25), channel_id=1, source_target_pairs={{0,8},{8,16},{16,24},{24,32},{32,40},{40,48},{48,56},{56,64},{64,7... | collective-permute-start | bytes 17288 | tf_op jit(solution)/shard_map/ppermute | solution.py:15
  84.6 11.5 %collective-permute-start.3 = (bf16[192,15]{1,0:T(8,128)(2,1)}, bf16[192,15]{1,0:T(8,128)(2,1)}, u32[]{:S(2)}, u32[]{:S(2)}) collective-permute-start(bf16[192,15]{1,0:T(8,128)(2,1)} %get-tuple-element.26), channel_id=1, source_target_pairs={{8,0},{16,8},{24,16},{32,24},{40,32},{48,40},{56,48},{64,56},{72,6... | collective-permute-start | bytes 17288 | tf_op jit(solution)/shard_map/ppermute | solution.py:17
  102.7 49.5 %copy-start.3 = (f32[192,512]{1,0:T(8,128)S(1)}, f32[192,512]{1,0:T(8,128)}, u32[]{:S(2)}) copy-start(f32[192,512]{1,0:T(8,128)} %get-tuple-element.10) | copy-start | bytes 1179652
  102.7 55.8 %copy-start.24 = (f32[192]{0:T(256)S(1)}, f32[192]{0:T(256)}, u32[]{:S(2)}) copy-start(f32[192]{0:T(256)} %param.7) | copy-start | bytes 2308
  112.9 52.5 %all-to-all-start.1 = ((bf16[64,25,384]{2,1,0:T(8,128)(2,1)}), bf16[64,25,384]{2,1,0:T(8,128)(2,1)S(1)}, u32[]{:S(2)}, u32[]{:S(2)}) async-start(bf16[64,25,384]{2,1,0:T(8,128)(2,1)} %pad_maximum_fusion), calls=%async_computation.2 | async-start | bytes 3145728 | tf_op jit(solution)/shard_map/all_to_all | solution.py:158
  127.7 20.1 %collective-permute-start.4 = (bf16[224,128]{1,0:T(8,128)(2,1)S(1)}, bf16[224,128]{1,0:T(8,128)(2,1)S(1)}, u32[]{:S(2)}, u32[]{:S(2)}) collective-permute-start(bf16[224,128]{1,0:T(8,128)(2,1)S(1)} %get-tuple-element.65), channel_id=1, source_target_pairs={{0,1},{1,2},{2,3},{3,4},{4,5},{5,6},{6,7},{7,0},{8,9},{9,10},{10,1... | collective-permute-start | bytes 172040 | tf_op jit(solution)/shard_map/ppermute | solution.py:83
  130.5 19.3 %collective-permute-start.6 = (bf16[224,128]{1,0:T(8,128)(2,1)S(1)}, bf16[224,128]{1,0:T(8,128)(2,1)S(1)}, u32[]{:S(2)}, u32[]{:S(2)}) collective-permute-start(bf16[224,128]{1,0:T(8,128)(2,1)S(1)} %get-tuple-element.66), channel_id=1, source_target_pairs={{0,3},{1,4},{2,5},{3,6},{4,7},{5,0},{6,1},{7,2},{8,11},{9,12},{10,... | collective-permute-start | bytes 172040 | tf_op jit(solution)/shard_map/ppermute | solution.py:83
  134.5 18.4 %collective-permute-start.7 = (bf16[224,128]{1,0:T(8,128)(2,1)S(1)}, bf16[224,128]{1,0:T(8,128)(2,1)S(1)}, u32[]{:S(2)}, u32[]{:S(2)}) collective-permute-start(bf16[224,128]{1,0:T(8,128)(2,1)S(1)} %get-tuple-element.67), channel_id=1, source_target_pairs={{0,4},{1,5},{2,6},{3,7},{4,0},{5,1},{6,2},{7,3},{8,12},{9,13},{10,... | collective-permute-start | bytes 172040 | tf_op jit(solution)/shard_map/ppermute | solution.py:83
  139.2 13.8 %collective-permute-start.8 = (bf16[224,128]{1,0:T(8,128)(2,1)S(1)}, bf16[224,128]{1,0:T(8,128)(2,1)S(1)}, u32[]{:S(2)}, u32[]{:S(2)}) collective-permute-start(bf16[224,128]{1,0:T(8,128)(2,1)S(1)} %get-tuple-element.68), channel_id=1, source_target_pairs={{0,5},{1,6},{2,7},{3,0},{4,1},{5,2},{6,3},{7,4},{8,13},{9,14},{10,... | collective-permute-start | bytes 172040 | tf_op jit(solution)/shard_map/ppermute | solution.py:83
  143.6 10.8 %collective-permute-start.9 = (bf16[224,128]{1,0:T(8,128)(2,1)S(1)}, bf16[224,128]{1,0:T(8,128)(2,1)S(1)}, u32[]{:S(2)}, u32[]{:S(2)}) collective-permute-start(bf16[224,128]{1,0:T(8,128)(2,1)S(1)} %get-tuple-element.69), channel_id=1, source_target_pairs={{0,6},{1,7},{2,0},{3,1},{4,2},{5,3},{6,4},{7,5},{8,14},{9,15},{10,... | collective-permute-start | bytes 172040 | tf_op jit(solution)/shard_map/ppermute | solution.py:83
  147.9 6.5 %collective-permute-start.10 = (bf16[224,128]{1,0:T(8,128)(2,1)S(1)}, bf16[224,128]{1,0:T(8,128)(2,1)S(1)}, u32[]{:S(2)}, u32[]{:S(2)}) collective-permute-start(bf16[224,128]{1,0:T(8,128)(2,1)S(1)} %get-tuple-element.70), channel_id=1, source_target_pairs={{0,7},{1,0},{2,1},{3,2},{4,3},{5,4},{6,5},{7,6},{8,15},{9,8},{10,9... | collective-permute-start | bytes 172040 | tf_op jit(solution)/shard_map/ppermute | solution.py:83
  149.8 7.7 %collective-permute-start.5 = (bf16[224,128]{1,0:T(8,128)(2,1)S(1)}, bf16[224,128]{1,0:T(8,128)(2,1)S(1)}, u32[]{:S(2)}, u32[]{:S(2)}) collective-permute-start(bf16[224,128]{1,0:T(8,128)(2,1)S(1)} %get-tuple-element.71), channel_id=1, source_target_pairs={{0,2},{1,3},{2,4},{3,5},{4,6},{5,7},{6,0},{7,1},{8,10},{9,11},{10,... | collective-permute-start | bytes 172040 | tf_op jit(solution)/shard_map/ppermute | solution.py:83
  166.5 17.9 %all-to-all-start.2 = ((f32[64,1,288]{2,1,0:T(1,128)}), f32[64,1,288]{2,1,0:T(1,128)S(1)}, u32[]{:S(2)}, u32[]{:S(2)}) async-start(f32[64,1,288]{2,1,0:T(1,128)} %broadcast_in_dim.8), calls=%async_computation.3 | async-start | bytes 196608 | tf_op jit(solution)/shard_map/all_to_all | solution.py:50
  (17 other events, 207.2 us)
Sparse Core Ops, SparseCore 0:
  10.1 45.2 all-gather.2
  108.7 44.2 reduce-scatter.1

commit v15 on v12

--- a/solution.py
+++ b/solution.py
@@ -166,24 +166,11 @@
     normed_f = normed_term.astype(jnp.float32)
     weighted = normed_f * complete_gain[:, None]
     own_moments = jnp.stack([jnp.sum(weighted, 0), jnp.sum(weighted * centered_unit, 0)], 0)
-    moment_rows = jnp.concatenate(bf16_pieces(own_moments, 3), 0)
-    half = frames // 2
-    split = frames - frames // 4
-    moment_rows = moment_rows.reshape(-1, frames - split)
-    used_rows = moment_rows.shape[0]
-    moment_rows = jnp.pad(moment_rows, ((0, 32 - used_rows), (0, 0)))
-    early_part = lax.psum_scatter(
-        normed_term[:, :split], "ch", scatter_dimension=0, tiled=True
+    normalized_gradient = lax.psum_scatter(
+        normed_term, "ch", scatter_dimension=0, tiled=True
     ).astype(jnp.float32)
-    late_part, moment_total = reduce_by_shifts(
-        normed_term[:, split:].reshape(groups, local_cols, frames - split), moment_rows, "ch"
-    )
-    normalized_gradient = jnp.concatenate([early_part, late_part], 1)
-    moment_total = moment_total[:used_rows].reshape(6, frames)
     scaled_signal = normalized_gradient * input_norm_gain[:, None]
-    moments = ((moment_total[0:2] + moment_total[2:4]) + moment_total[4:6]) * (
-        1.0 / complete_signal.shape[0]
-    )
+    moments = lax.psum(own_moments, "ch") * (1.0 / complete_signal.shape[0])
     signal_gradient = (
         inverse_deviation
         * (scaled_signal - moments[0:1] - centered_unit_rows * moments[1:2])

time: 191 us -> 190 us (level)
  starting transfers between devices: 72.9 us -> 47.6 us
  waiting for transfers between devices: 56.8 us -> 71.5 us
  blocking collectives: 0 us -> 13.4 us
  local copies, waits for them, and re-layouts: 9.96 us -> 6.09 us
    ppermute x7 -> x0, starting transfers between devices: 24.4 us -> none  [reduce_by_shifts(): lax.ppermute(outgoing, axis, [(i, (i + shift) % count) for i in range(cou...]
    all_to_all x1, waiting for transfers between devices: 5.13 us -> 24.7 us  [shards(): lax.all_to_all(outgoing, 'seq', 0, 0, tiled=False).astype(jnp.float32)]
    psum x0 -> x1, blocking collectives: none -> 13.4 us  [shards(): moments = lax.psum(own_moments, 'ch') * (1.0 / complete_signal.shape[0])]
    ppermute x7 -> x0, waiting for transfers between devices: 4.34 us -> none  [reduce_by_shifts(): lax.ppermute(outgoing, axis, [(i, (i + shift) % count) for i in range(cou...]
    unnamed x26 -> x46, local copies, waits for them, and re-layouts: 3.35 us -> 1.13 us
    slice x2 -> x1, local copies, waits for them, and re-layouts: 2.18 us -> 0.01 us  [shards(): moments[0:1]]
  transfers between devices with their start and end apart: 16 -> 9, of which waited for: 8 -> 5; matrix products, arithmetic and copies ran while one was open for 9% -> 8% of each run, Pallas kernels for 0% -> 0%
where the time goes in v15:
time: 190 us
  waiting for transfers between devices  71.5 us (38%)
  starting transfers between devices  47.6 us (25%)
  other arithmetic  27.5 us (14%)
  between operations  14.5 us (8%)
  blocking collectives  13.4 us (7%)
  matrix products  8.98 us (5%)
  local copies, waits for them, and re-layouts  6.09 us (3%)
    all_gather x1, waiting for transfers between devices, shards(): lax.all_gather(jnp.concatenate([signal, gain_rows], 0), 'ch', axis=0)  31.4 us
    all_to_all x1, waiting for transfers between devices, shards(): lax.all_to_all(outgoing, 'seq', 0, 0, tiled=False).astype(jnp.float32)  24.7 us
    all_to_all x2, starting transfers between devices, gather_by_exchange(): return lax.all_to_all(copies, axis, 0, 0, tiled=False)  18.1 us
    all_to_all x1, starting transfers between devices, shards(): lax.all_to_all(outgoing, 'seq', 0, 0, tiled=False).astype(jnp.float32)  15.4 us
    psum x1, blocking collectives, shards(): moments = lax.psum(own_moments, 'ch') * (1.0 / complete_signal.shape[0])  13.4 us
    all_to_all x2, waiting for transfers between devices, gather_by_exchange(): return lax.all_to_all(copies, axis, 0, 0, tiled=False)  9.88 us
    ppermute x2, starting transfers between devices, extended(): lax.ppermute(tail, axis, [(i, (i + 1) % count) for i in range(ends)])  9.55 us
    reduce_sum x2, other arithmetic, shards(): jnp.sum(glued_pad[:, k:k + span] * grad_pre_f, 1)  7.75 us
  transfers between devices with their start and end apart: 9, of which 5 were waited for; matrix products, arithmetic and copies ran while one was open for 8% of the time, Pallas kernels for 0%

profile of v15, /device:TPU:1, one launch (start us, length us, event | category | flops | bytes accessed | tf_op | source)
XLA Modules:
  0.0 189.6 jit_solution(7751503122517942391)
XLA Ops:
  8.0 1.6 pad_maximum_fusion.4
  11.6 11.6 %all-to-all-start = ((bf16[64,24,384]{2,1,0:T(8,128)(2,1)}), bf16[64,24,384]{2,1,0:T(8,128)(2,1)S(1)}, u32[]{:S(2)}, u32[]{:S(2)}) async-start(bf16[64,24,384]{2,1,0:T(8,128)(2,1)} %broadcast_in_dim.6), calls=%async_computation | async-start | bytes 2359296 | tf_op jit(solution)/shard_map/all_to_all | solution.py:50
  23.9 31.4 %all-gather.3.cloned.1.call-done = bf16[1664,512]{1,0:T(8,128)(2,1)} async-done(((bf16[208,512]{1,0:T(8,128)(2,1)}), bf16[1664,512]{1,0:T(8,128)(2,1)}) %all-gather.3.cloned.1.call-update) | async-done | bytes 1703952 | tf_op jit(solution)/shard_map/all_gather | solution.py:104
  56.3 1.7 convert_reduce_fusion.1
  58.0 1.9 multiply_reduce_fusion.1
  59.9 1.6 multiply_convert_fusion.1
  62.6 2.6 %fusion.102 = f32[384,512]{1,0:T(8,128)S(1)} fusion(bf16[1536,384]{1,0:T(8,128)(2,1)} %bitcast.95, bf16[1536,512]{1,0:T(8,128)(2,1)} %bitcast.94), kind=kOutput, calls=%fused_computation.209 | convolution fusion | flops 603979776 | bytes 3538944 | tf_op jit(solution)/shard_map/dot_general | solution.py:115
  65.3 7.6 %collective-permute-start = (bf16[192,15]{1,0:T(8,128)(2,1)S(1)}, bf16[192,15]{1,0:T(8,128)(2,1)S(1)}, u32[]{:S(2)}, u32[]{:S(2)}) collective-permute-start(bf16[192,15]{1,0:T(8,128)(2,1)S(1)} %get-tuple-element.50), channel_id=1, source_target_pairs={{0,8},{8,16},{16,24},{24,32},{32,40},{40,48},{48,56},{56,64},{64,7... | collective-permute-start | bytes 17288 | tf_op jit(solution)/shard_map/ppermute | solution.py:15
  73.0 1.9 %collective-permute-start.1 = (bf16[192,15]{1,0:T(8,128)(2,1)S(1)}, bf16[192,15]{1,0:T(8,128)(2,1)S(1)}, u32[]{:S(2)}, u32[]{:S(2)}) collective-permute-start(bf16[192,15]{1,0:T(8,128)(2,1)S(1)} %get-tuple-element.51), channel_id=1, source_target_pairs={{8,0},{16,8},{24,16},{32,24},{40,32},{48,40},{56,48},{64,56},{72,6... | collective-permute-start | bytes 17288 | tf_op jit(solution)/shard_map/ppermute | solution.py:17
  75.6 2.8 %collective-permute-done.1 = bf16[192,15]{1,0:T(8,128)(2,1)S(1)} collective-permute-done((bf16[192,15]{1,0:T(8,128)(2,1)S(1)}, bf16[192,15]{1,0:T(8,128)(2,1)S(1)}, u32[]{:S(2)}, u32[]{:S(2)}) %collective-permute-start.1) | collective-permute-done | bytes 5792 | tf_op jit(solution)/shard_map/ppermute | solution.py:17
  78.5 5.8 %fusion.38 = (f32[192]{0:T(256)S(1)}, f32[192]{0:T(256)S(1)}, f32[192]{0:T(256)S(1)}, f32[192]{0:T(256)S(1)}, f32[192]{0:T(256)S(1)}, /*index=5*/f32[192]{0:T(25...) fusion(f32[192,542]{1,0:T(8,128)S(1)} %maximum_convert_fusion, ...), kind=kLoop, calls=%fused_computation.82 | loop fusion | flops 10613376 | bytes 13013760 | tf_op jit(solution)/shard_map/reduce_sum | solution.py:135
  84.5 1.9 %fusion.37 = (f32[192]{0:T(256)S(1)}, f32[192]{0:T(256)S(1)}, f32[192]{0:T(256)S(1)}, f32[192]{0:T(256)S(1)}, f32[192]{0:T(256)S(1)}, /*index=5*/f32[192]{0:T(25...) fusion(bf16[192,512]{1,0:T(8,128)(2,1)S(1)} %get-tuple-element., ...), kind=kLoop, calls=%fused_computation.81 | loop fusion | flops 2651712 | bytes 5318400 | tf_op jit(solution)/shard_map/reduce_sum | solution.py:135
  86.8 1.9 %collective-permute-start.2 = (bf16[192,15]{1,0:T(8,128)(2,1)S(1)}, bf16[192,15]{1,0:T(8,128)(2,1)S(1)}, u32[]{:S(2)}, u32[]{:S(2)}) collective-permute-start(bf16[192,15]{1,0:T(8,128)(2,1)S(1)} %get-tuple-element.48), channel_id=1, source_target_pairs={{0,8},{8,16},{16,24},{24,32},{32,40},{40,48},{48,56},{56,64},{64,7... | collective-permute-start | bytes 17288 | tf_op jit(solution)/shard_map/ppermute | solution.py:15
  88.7 2.6 %collective-permute-start.3 = (bf16[192,15]{1,0:T(8,128)(2,1)S(1)}, bf16[192,15]{1,0:T(8,128)(2,1)S(1)}, u32[]{:S(2)}, u32[]{:S(2)}) collective-permute-start(bf16[192,15]{1,0:T(8,128)(2,1)S(1)} %get-tuple-element.49), channel_id=1, source_target_pairs={{8,0},{16,8},{24,16},{32,24},{40,32},{48,40},{56,48},{64,56},{72,6... | collective-permute-start | bytes 17288 | tf_op jit(solution)/shard_map/ppermute | solution.py:17
  91.5 2.6 %collective-permute-done.3 = bf16[192,15]{1,0:T(8,128)(2,1)S(1)} collective-permute-done((bf16[192,15]{1,0:T(8,128)(2,1)S(1)}, bf16[192,15]{1,0:T(8,128)(2,1)S(1)}, u32[]{:S(2)}, u32[]{:S(2)}) %collective-permute-start.3) | collective-permute-done | bytes 5792 | tf_op jit(solution)/shard_map/ppermute | solution.py:17
  94.4 4.4 %multiply_convert_fusion.4 = (bf16[192,512]{1,0:T(8,128)(2,1)S(1)}, f32[192,512]{1,0:T(8,128)S(1)}) fusion(f32[384,512]{1,0:T(8,128)S(1)} %fusion.102, f32[192,542]{1,0:T(8,128)S(1)} %maximum_convert_fusion.1, f32[192]{0:T(256)S(1)} %bitcast.102, f32[192]{0:T(256)S(1)} %bitcast.140, f32[192]{0:T(256)S(1)} %bitcast.158, f32[192]{0:T(256)S(1)} %bitcast.156, ...), kind=kLoop, calls=%fused_computation.150 | loop fusion | flops 6488064 | bytes 13196544 | tf_op jit(solution)/shard_map/convert_element_type | solution.py:137
  99.0 3.5 %fusion.1 = (f32[512]{0:T(512)S(1)}, f32[512]{0:T(512)S(1)}, f32[1536,512]{1,0:T(8,128)}, bf16[1536,512]{1,0:T(8,128)(2,1)}) fusion(f32[1536]{0:T(1024)S(1)} %add.315, f32[512]{0:T(512)S(1)} %add_rsqrt_fusion, f32[512]{0:T(512)S(1)} %broadcast_multiply_fusion.1, bf16[8,208,512]{2,1,0:T(8,128)(2,1)S(1)} %bitcast.93, bf16[1536,384]{1,0:T(8,128)(2,1)S(1)} %bitcast.96, ...), kind=kOutput, calls=%fused_computation.37 | convolution fusion | flops 611843072 | bytes 7878656 | tf_op jit(solution)/shard_map/dot_general | solution.py:146
  102.6 2.9 %convolution_convert_fusion.1 = bf16[1536,384]{1,0:T(8,128)(2,1)S(1)} fusion(f32[1536,512]{1,0:T(8,128)} %get-tuple-element.47, f32[1536]{0:T(1024)S(1)} %add.315, bf16[192,512]{1,0:T(8,128)(2,1)S(1)} %multiply_convert_fusion.3, bf16[192,512]{1,0:T(8,128)(2,1)S(1)} %get-tuple-element.43), kind=kOutput, calls=%fused_computation.42 | convolution fusion | flops 606928896 | bytes 4724736 | tf_op jit(solution)/shard_map/dot_general | solution.py:140
  106.9 15.4 %all-to-all-start.1 = ((bf16[64,25,384]{2,1,0:T(8,128)(2,1)}), bf16[64,25,384]{2,1,0:T(8,128)(2,1)S(1)}, u32[]{:S(2)}, u32[]{:S(2)}) async-start(bf16[64,25,384]{2,1,0:T(8,128)(2,1)} %pad_maximum_fusion), calls=%async_computation.2 | async-start | bytes 3145728 | tf_op jit(solution)/shard_map/all_to_all | solution.py:159
  123.1 13.4 %psum.7 = f32[2,512]{1,0:T(2,128)S(1)} all-reduce(f32[2,512]{1,0:T(2,128)S(1)} %pad_maximum_fusion.6), channel_id=1, replica_groups=mesh['seq'=64,'ch'=8] {'ch'}, use_global_device_ids=true, to_apply=%region_5.6 | all-reduce | flops 1024 | bytes 8192 | tf_op jit(solution)/shard_map/psum | solution.py:173
  136.5 24.7 %all-to-all-done.1 = bf16[64,25,384]{2,1,0:T(8,128)(2,1)S(1)} async-done(((bf16[64,25,384]{2,1,0:T(8,128)(2,1)}), bf16[64,25,384]{2,1,0:T(8,128)(2,1)S(1)}, u32[]{:S(2)}, u32[]{:S(2)}) %all-to-all-start.1) | async-done | bytes 1228832 | tf_op jit(solution)/shard_map/all_to_all | solution.py:159
  161.6 2.0 %fusion.7 = (f32[192]{0:T(256)S(1)}, bf16[192,512]{1,0:T(8,128)(2,1)}) fusion(bf16[192,512]{1,0:T(8,128)(2,1)} %reduce-scatter.2.cloned.1.call-done, f32[1536,512]{1,0:T(8,128)} %get-tuple-element.47, s32[]{:T(128)S(6)} %select_n.3, f32[512]{0:T(512)S(1)} %bitcast.164, f32[512]{0:T(512)S(1)} %bitcast.163, f32[192]{0:T(256)S(1)} %copy-done.21, ...), kind=kLoop, calls=%fused_computation.51 | loop fusion | flops 884544 | bytes 794116 | tf_op jit(solution)/shard_map/reduce_sum | solution.py:178
  164.3 6.5 %all-to-all-start.2 = ((f32[64,1,288]{2,1,0:T(1,128)}), f32[64,1,288]{2,1,0:T(1,128)S(1)}, u32[]{:S(2)}, u32[]{:S(2)}) async-start(f32[64,1,288]{2,1,0:T(1,128)} %broadcast_in_dim.8), calls=%async_computation.3 | async-start | bytes 196608 | tf_op jit(solution)/shard_map/all_to_all | solution.py:50
  171.5 9.9 %all-to-all-done.2 = f32[64,1,288]{2,1,0:T(1,128)S(1)} async-done(((f32[64,1,288]{2,1,0:T(1,128)}), f32[64,1,288]{2,1,0:T(1,128)S(1)}, u32[]{:S(2)}, u32[]{:S(2)}) %all-to-all-start.2) | async-done | bytes 73760 | tf_op jit(solution)/shard_map/all_to_all | solution.py:50
  (93 shorter events, 12.7 us)
Async XLA Ops:
  7.2 48.2 %all-gather.3.cloned.1.call-start = ((), (), s32[]{:S(2)}) async-start(), calls=%async_computation.5 | async-start | bytes 1916928 | tf_op jit(solution)/shard_map/all_gather | solution.py:104
  10.5 12.8 %copy-start.5 = (f32[31,192]{1,0:T(8,128)S(1)}, f32[31,192]{1,0:T(8,128)}, u32[]{:S(2)}) copy-start(f32[31,192]{1,0:T(8,128)} %param.10) | copy-start | bytes 71428
  11.6 49.9 %all-to-all-start = ((bf16[64,24,384]{2,1,0:T(8,128)(2,1)}), bf16[64,24,384]{2,1,0:T(8,128)(2,1)S(1)}, u32[]{:S(2)}, u32[]{:S(2)}) async-start(bf16[64,24,384]{2,1,0:T(8,128)(2,1)} %broadcast_in_dim.6), calls=%async_computation | async-start | bytes 2359296 | tf_op jit(solution)/shard_map/all_to_all | solution.py:50
  23.2 138.4 %reduce-scatter.2.cloned.1.call-start = ((), (), s32[]{:S(2)}) async-start(), calls=%async_computation.4 | async-start | bytes 1769472 | tf_op jit(solution)/shard_map/reduce_scatter | solution.py:169
  65.1 13.4 %copy-start.4 = (bf16[192,512]{1,0:T(8,128)(2,1)S(1)}, bf16[192,512]{1,0:T(8,128)(2,1)}, u32[]{:S(2)}) copy-start(bf16[192,512]{1,0:T(8,128)(2,1)} %param.11) | copy-start | bytes 589828
  65.3 10.3 %collective-permute-start = (bf16[192,15]{1,0:T(8,128)(2,1)S(1)}, bf16[192,15]{1,0:T(8,128)(2,1)S(1)}, u32[]{:S(2)}, u32[]{:S(2)}) collective-permute-start(bf16[192,15]{1,0:T(8,128)(2,1)S(1)} %get-tuple-element.50), channel_id=1, source_target_pairs={{0,8},{8,16},{16,24},{24,32},{32,40},{40,48},{48,56},{56,64},{64,7... | collective-permute-start | bytes 17288 | tf_op jit(solution)/shard_map/ppermute | solution.py:15
  73.0 5.4 %collective-permute-start.1 = (bf16[192,15]{1,0:T(8,128)(2,1)S(1)}, bf16[192,15]{1,0:T(8,128)(2,1)S(1)}, u32[]{:S(2)}, u32[]{:S(2)}) collective-permute-start(bf16[192,15]{1,0:T(8,128)(2,1)S(1)} %get-tuple-element.51), channel_id=1, source_target_pairs={{8,0},{16,8},{24,16},{32,24},{40,32},{48,40},{56,48},{64,56},{72,6... | collective-permute-start | bytes 17288 | tf_op jit(solution)/shard_map/ppermute | solution.py:17
  84.4 9.9 %copy-start.6 = (f32[1,192]{1,0:T(1,128)S(1)}, f32[1,192]{1,0:T(1,128)}, u32[]{:S(2)}) copy-start(f32[1,192]{1,0:T(1,128)} %get-tuple-element.73) | copy-start | bytes 2308
  84.4 9.9 %copy-start.7 = (f32[1,192]{1,0:T(1,128)S(1)}, f32[1,192]{1,0:T(1,128)}, u32[]{:S(2)}) copy-start(f32[1,192]{1,0:T(1,128)} %get-tuple-element.74) | copy-start | bytes 2308
  84.4 9.9 %copy-start.8 = (f32[1,192]{1,0:T(1,128)S(1)}, f32[1,192]{1,0:T(1,128)}, u32[]{:S(2)}) copy-start(f32[1,192]{1,0:T(1,128)} %get-tuple-element.75) | copy-start | bytes 2308
  84.4 9.9 %copy-start.9 = (f32[1,192]{1,0:T(1,128)S(1)}, f32[1,192]{1,0:T(1,128)}, u32[]{:S(2)}) copy-start(f32[1,192]{1,0:T(1,128)} %get-tuple-element.76) | copy-start | bytes 2308
  84.4 9.9 %copy-start.10 = (f32[1,192]{1,0:T(1,128)S(1)}, f32[1,192]{1,0:T(1,128)}, u32[]{:S(2)}) copy-start(f32[1,192]{1,0:T(1,128)} %get-tuple-element.77) | copy-start | bytes 2308
  84.4 9.9 %copy-start.11 = (f32[1,192]{1,0:T(1,128)S(1)}, f32[1,192]{1,0:T(1,128)}, u32[]{:S(2)}) copy-start(f32[1,192]{1,0:T(1,128)} %get-tuple-element.78) | copy-start | bytes 2308
  84.4 9.9 %copy-start.12 = (f32[1,192]{1,0:T(1,128)S(1)}, f32[1,192]{1,0:T(1,128)}, u32[]{:S(2)}) copy-start(f32[1,192]{1,0:T(1,128)} %get-tuple-element.79) | copy-start | bytes 2308
  84.5 9.9 %copy-start.13 = (f32[1,192]{1,0:T(1,128)S(1)}, f32[1,192]{1,0:T(1,128)}, u32[]{:S(2)}) copy-start(f32[1,192]{1,0:T(1,128)} %get-tuple-element.80) | copy-start | bytes 2308
  84.5 9.9 %copy-start.14 = (f32[1,192]{1,0:T(1,128)S(1)}, f32[1,192]{1,0:T(1,128)}, u32[]{:S(2)}) copy-start(f32[1,192]{1,0:T(1,128)} %get-tuple-element.81) | copy-start | bytes 2308
  84.5 9.8 %copy-start.15 = (f32[1,192]{1,0:T(1,128)S(1)}, f32[1,192]{1,0:T(1,128)}, u32[]{:S(2)}) copy-start(f32[1,192]{1,0:T(1,128)} %get-tuple-element.82) | copy-start | bytes 2308
  84.5 9.8 %copy-start.16 = (f32[1,192]{1,0:T(1,128)S(1)}, f32[1,192]{1,0:T(1,128)}, u32[]{:S(2)}) copy-start(f32[1,192]{1,0:T(1,128)} %get-tuple-element.83) | copy-start | bytes 2308
  86.8 4.7 %collective-permute-start.2 = (bf16[192,15]{1,0:T(8,128)(2,1)S(1)}, bf16[192,15]{1,0:T(8,128)(2,1)S(1)}, u32[]{:S(2)}, u32[]{:S(2)}) collective-permute-start(bf16[192,15]{1,0:T(8,128)(2,1)S(1)} %get-tuple-element.48), channel_id=1, source_target_pairs={{0,8},{8,16},{16,24},{24,32},{32,40},{40,48},{48,56},{56,64},{64,7... | collective-permute-start | bytes 17288 | tf_op jit(solution)/shard_map/ppermute | solution.py:15
  88.7 5.4 %collective-permute-start.3 = (bf16[192,15]{1,0:T(8,128)(2,1)S(1)}, bf16[192,15]{1,0:T(8,128)(2,1)S(1)}, u32[]{:S(2)}, u32[]{:S(2)}) collective-permute-start(bf16[192,15]{1,0:T(8,128)(2,1)S(1)} %get-tuple-element.49), channel_id=1, source_target_pairs={{8,0},{16,8},{24,16},{32,24},{40,32},{48,40},{56,48},{64,56},{72,6... | collective-permute-start | bytes 17288 | tf_op jit(solution)/shard_map/ppermute | solution.py:17
  106.9 15.4 %copy-start.3 = (f32[192,512]{1,0:T(8,128)S(1)}, f32[192,512]{1,0:T(8,128)}, u32[]{:S(2)}) copy-start(f32[192,512]{1,0:T(8,128)} %get-tuple-element.40) | copy-start | bytes 1179652
  106.9 54.4 %all-to-all-start.1 = ((bf16[64,25,384]{2,1,0:T(8,128)(2,1)}), bf16[64,25,384]{2,1,0:T(8,128)(2,1)S(1)}, u32[]{:S(2)}, u32[]{:S(2)}) async-start(bf16[64,25,384]{2,1,0:T(8,128)(2,1)} %pad_maximum_fusion), calls=%async_computation.2 | async-start | bytes 3145728 | tf_op jit(solution)/shard_map/all_to_all | solution.py:159
  122.2 39.3 %copy-start.21 = (f32[192]{0:T(256)S(1)}, f32[192]{0:T(256)}, u32[]{:S(2)}) copy-start(f32[192]{0:T(256)} %param.7) | copy-start | bytes 2308
  164.3 17.0 %all-to-all-start.2 = ((f32[64,1,288]{2,1,0:T(1,128)}), f32[64,1,288]{2,1,0:T(1,128)S(1)}, u32[]{:S(2)}, u32[]{:S(2)}) async-start(f32[64,1,288]{2,1,0:T(1,128)} %broadcast_in_dim.8), calls=%async_computation.3 | async-start | bytes 196608 | tf_op jit(solution)/shard_map/all_to_all | solution.py:50
  (7 other events, 49.6 us)
Sparse Core Ops, SparseCore 0:
  10.1 45.2 all-gather.2
  102.7 43.0 reduce-scatter.1

commit v16 on v12

--- a/solution.py
+++ b/solution.py
@@ -100,7 +100,7 @@
     channel_position = lax.axis_index("ch")
     reach = depth_taps.shape[0] // 2
     gain_rows = jnp.stack(bf16_pieces(input_norm_gain, 3), 0)
-    gain_rows = jnp.pad(gain_rows, ((0, 13), (0, frames - local_cols)))
+    gain_rows = jnp.pad(gain_rows, ((0, 5), (0, frames - local_cols)))
     arrived = lax.all_gather(jnp.concatenate([signal, gain_rows], 0), "ch", axis=0)
     complete_signal = arrived[:, :local_cols].reshape(groups * local_cols, frames)
     gain_parts = arrived[:, local_cols : local_cols + 3, :local_cols].astype(jnp.float32)

time: 191 us -> 189 us (0.990)
  transfers between devices with their start and end apart: 16 -> 16, of which waited for: 8 -> 7; matrix products, arithmetic and copies ran while one was open for 9% -> 9% of each run, Pallas kernels for 0% -> 0%
where the time goes in v16:
time: 189 us; the launch traced here: 188 us
  starting transfers between devices  72.7 us (38%)
  waiting for transfers between devices  56.9 us (30%)
  other arithmetic  26.1 us (14%)
  between operations  14.6 us (8%)
  local copies, waits for them, and re-layouts  9.95 us (5%)
  matrix products  8.24 us (4%)
    all_gather x1, waiting for transfers between devices, shards(): lax.all_gather(jnp.concatenate([signal, gain_rows], 0), 'ch', axis=0)  32 us
    ppermute x7, starting transfers between devices, reduce_by_shifts(): lax.ppermute(outgoing, axis, [(i, (i + shift) % count) for i in range(cou...  24.3 us
    all_to_all x2, starting transfers between devices, gather_by_exchange(): return lax.all_to_all(copies, axis, 0, 0, tiled=False)  19 us
    all_to_all x1, starting transfers between devices, shards(): lax.all_to_all(outgoing, 'seq', 0, 0, tiled=False).astype(jnp.float32)  15.4 us
    all_to_all x2, waiting for transfers between devices, gather_by_exchange(): return lax.all_to_all(copies, axis, 0, 0, tiled=False)  9.88 us
    ppermute x2, starting transfers between devices, extended(): lax.ppermute(tail, axis, [(i, (i + 1) % count) for i in range(ends)])  9.43 us
    reduce_sum x2, other arithmetic, shards(): jnp.sum(glued_pad[:, k:k + span] * grad_pre_f, 1)  6.84 us
    ppermute x2, waiting for transfers between devices, extended(): lax.ppermute(head, axis, [((i + 1) % count, i) for i in range(ends)])  5.39 us
  transfers between devices with their start and end apart: 16, of which 7 were waited for; matrix products, arithmetic and copies ran while one was open for 9% of the time, Pallas kernels for 0%

profile of v16, /device:TPU:1, one launch (start us, length us, event | category | flops | bytes accessed | tf_op | source)
XLA Modules:
  0.0 188.4 jit_solution(11108739983832384376)
XLA Ops:
  11.6 11.6 %all-to-all-start = ((bf16[64,24,384]{2,1,0:T(8,128)(2,1)}), bf16[64,24,384]{2,1,0:T(8,128)(2,1)S(1)}, u32[]{:S(2)}, u32[]{:S(2)}) async-start(bf16[64,24,384]{2,1,0:T(8,128)(2,1)} %broadcast_in_dim.6), calls=%async_computation | async-start | bytes 2359296 | tf_op jit(solution)/shard_map/all_to_all | solution.py:50
  23.3 32.0 %all-gather.3.cloned.1.call-done = bf16[1600,512]{1,0:T(8,128)(2,1)} async-done(((bf16[200,512]{1,0:T(8,128)(2,1)}), bf16[1600,512]{1,0:T(8,128)(2,1)}) %all-gather.3.cloned.1.call-update) | async-done | bytes 1638416 | tf_op jit(solution)/shard_map/all_gather | solution.py:104
  61.1 2.6 %fusion.105 = f32[384,512]{1,0:T(8,128)S(1)} fusion(bf16[1536,384]{1,0:T(8,128)(2,1)} %bitcast.115, bf16[1536,512]{1,0:T(8,128)(2,1)} %bitcast.114), kind=kOutput, calls=%fused_computation.235 | convolution fusion | flops 603979776 | bytes 3538944 | tf_op jit(solution)/shard_map/dot_general | solution.py:115
  63.9 7.5 %collective-permute-start = (bf16[192,15]{1,0:T(8,128)(2,1)S(1)}, bf16[192,15]{1,0:T(8,128)(2,1)S(1)}, u32[]{:S(2)}, u32[]{:S(2)}) collective-permute-start(bf16[192,15]{1,0:T(8,128)(2,1)S(1)} %get-tuple-element.57), channel_id=1, source_target_pairs={{0,8},{8,16},{16,24},{24,32},{32,40},{40,48},{48,56},{56,64},{64,7... | collective-permute-start | bytes 17288 | tf_op jit(solution)/shard_map/ppermute | solution.py:15
  71.4 1.9 %collective-permute-start.1 = (bf16[192,15]{1,0:T(8,128)(2,1)S(1)}, bf16[192,15]{1,0:T(8,128)(2,1)S(1)}, u32[]{:S(2)}, u32[]{:S(2)}) collective-permute-start(bf16[192,15]{1,0:T(8,128)(2,1)S(1)} %get-tuple-element.58), channel_id=1, source_target_pairs={{8,0},{16,8},{24,16},{32,24},{40,32},{48,40},{56,48},{64,56},{72,6... | collective-permute-start | bytes 17288 | tf_op jit(solution)/shard_map/ppermute | solution.py:17
  73.5 3.4 %collective-permute-done.1 = bf16[192,15]{1,0:T(8,128)(2,1)S(1)} collective-permute-done((bf16[192,15]{1,0:T(8,128)(2,1)S(1)}, bf16[192,15]{1,0:T(8,128)(2,1)S(1)}, u32[]{:S(2)}, u32[]{:S(2)}) %collective-permute-start.1) | collective-permute-done | bytes 5792 | tf_op jit(solution)/shard_map/ppermute | solution.py:17
  77.0 4.9 %fusion.33 = (f32[192]{0:T(256)S(1)}, f32[192]{0:T(256)S(1)}, f32[192]{0:T(256)S(1)}, f32[192]{0:T(256)S(1)}, f32[192]{0:T(256)S(1)}, /*index=5*/f32[192]{0:T(25...) fusion(f32[192,542]{1,0:T(8,128)S(1)} %maximum_convert_fusion, ...), kind=kLoop, calls=%fused_computation.75 | loop fusion | flops 10613376 | bytes 13013760 | tf_op jit(solution)/shard_map/reduce_sum | solution.py:135
  81.9 1.9 %fusion.32 = (f32[192]{0:T(256)S(1)}, f32[192]{0:T(256)S(1)}, f32[192]{0:T(256)S(1)}, f32[192]{0:T(256)S(1)}, f32[192]{0:T(256)S(1)}, /*index=5*/f32[192]{0:T(25...) fusion(bf16[192,512]{1,0:T(8,128)(2,1)S(1)} %get-tuple-element., ...), kind=kLoop, calls=%fused_computation.74 | loop fusion | flops 2651712 | bytes 5318400 | tf_op jit(solution)/shard_map/reduce_sum | solution.py:135
  86.1 2.6 %collective-permute-start.3 = (bf16[192,15]{1,0:T(8,128)(2,1)S(1)}, bf16[192,15]{1,0:T(8,128)(2,1)S(1)}, u32[]{:S(2)}, u32[]{:S(2)}) collective-permute-start(bf16[192,15]{1,0:T(8,128)(2,1)S(1)} %get-tuple-element.56), channel_id=1, source_target_pairs={{8,0},{16,8},{24,16},{32,24},{40,32},{48,40},{56,48},{64,56},{72,6... | collective-permute-start | bytes 17288 | tf_op jit(solution)/shard_map/ppermute | solution.py:17
  89.5 2.0 %collective-permute-done.3 = bf16[192,15]{1,0:T(8,128)(2,1)S(1)} collective-permute-done((bf16[192,15]{1,0:T(8,128)(2,1)S(1)}, bf16[192,15]{1,0:T(8,128)(2,1)S(1)}, u32[]{:S(2)}, u32[]{:S(2)}) %collective-permute-start.3) | collective-permute-done | bytes 5792 | tf_op jit(solution)/shard_map/ppermute | solution.py:17
  91.6 4.4 %multiply_convert_fusion.5 = (bf16[192,512]{1,0:T(8,128)(2,1)S(1)}, f32[192,512]{1,0:T(8,128)S(1)}) fusion(f32[384,512]{1,0:T(8,128)S(1)} %fusion.105, f32[192,542]{1,0:T(8,128)S(1)} %maximum_convert_fusion.1, f32[192]{0:T(256)S(1)} %bitcast.124, f32[192]{0:T(256)S(1)} %bitcast.162, f32[192]{0:T(256)S(1)} %bitcast.180, f32[192]{0:T(256)S(1)} %bitcast.178, ...), kind=kLoop, calls=%fused_computation.146 | loop fusion | flops 6488064 | bytes 13196544 | tf_op jit(solution)/shard_map/convert_element_type | solution.py:137
  96.3 3.6 %fusion.1 = (f32[512]{0:T(512)S(1)}, f32[512]{0:T(512)}, f32[1536,512]{1,0:T(8,128)}, bf16[1536,512]{1,0:T(8,128)(2,1)S(1)}) fusion(f32[1536]{0:T(1024)S(1)} %add.437, f32[512]{0:T(512)S(1)} %add_rsqrt_fusion, f32[512]{0:T(512)S(1)} %broadcast_multiply_fusion, bf16[8,200,512]{2,1,0:T(8,128)(2,1)S(1)} %bitcast.113, bf16[1536,384]{1,0:T(8,128)(2,1)S(1)} %bitcast.116, ...), kind=kOutput, calls=%fused_computation.37 | convolution fusion | flops 611843072 | bytes 7878656 | tf_op jit(solution)/shard_map/dot_general | solution.py:146
  103.3 2.1 %convolution_convert_fusion.1 = bf16[1536,384]{1,0:T(8,128)(2,1)S(1)} fusion(f32[1536,512]{1,0:T(8,128)S(1)} %copy-done.3, f32[1536]{0:T(1024)S(1)} %add.437, bf16[192,512]{1,0:T(8,128)(2,1)} %copy-done.5, bf16[192,512]{1,0:T(8,128)(2,1)} %copy-done.6), kind=kOutput, calls=%fused_computation.42 | convolution fusion | flops 606928896 | bytes 4724736 | tf_op jit(solution)/shard_map/dot_general | solution.py:140
  106.8 15.4 %all-to-all-start.1 = ((bf16[64,25,384]{2,1,0:T(8,128)(2,1)}), bf16[64,25,384]{2,1,0:T(8,128)(2,1)S(1)}, u32[]{:S(2)}, u32[]{:S(2)}) async-start(bf16[64,25,384]{2,1,0:T(8,128)(2,1)} %pad_maximum_fusion), calls=%async_computation.2 | async-start | bytes 3145728 | tf_op jit(solution)/shard_map/all_to_all | solution.py:159
  123.6 2.7 %collective-permute-start.4 = (bf16[224,128]{1,0:T(8,128)(2,1)S(1)}, bf16[224,128]{1,0:T(8,128)(2,1)S(1)}, u32[]{:S(2)}, u32[]{:S(2)}) collective-permute-start(bf16[224,128]{1,0:T(8,128)(2,1)S(1)} %get-tuple-element.95), channel_id=1, source_target_pairs={{0,1},{1,2},{2,3},{3,4},{4,5},{5,6},{6,7},{7,0},{8,9},{9,10},{10,1... | collective-permute-start | bytes 172040 | tf_op jit(solution)/shard_map/ppermute | solution.py:83
  126.3 4.0 %collective-permute-start.6 = (bf16[224,128]{1,0:T(8,128)(2,1)S(1)}, bf16[224,128]{1,0:T(8,128)(2,1)S(1)}, u32[]{:S(2)}, u32[]{:S(2)}) collective-permute-start(bf16[224,128]{1,0:T(8,128)(2,1)S(1)} %get-tuple-element.96), channel_id=1, source_target_pairs={{0,3},{1,4},{2,5},{3,6},{4,7},{5,0},{6,1},{7,2},{8,11},{9,12},{10,... | collective-permute-start | bytes 172040 | tf_op jit(solution)/shard_map/ppermute | solution.py:83
  130.3 4.7 %collective-permute-start.7 = (bf16[224,128]{1,0:T(8,128)(2,1)S(1)}, bf16[224,128]{1,0:T(8,128)(2,1)S(1)}, u32[]{:S(2)}, u32[]{:S(2)}) collective-permute-start(bf16[224,128]{1,0:T(8,128)(2,1)S(1)} %get-tuple-element.97), channel_id=1, source_target_pairs={{0,4},{1,5},{2,6},{3,7},{4,0},{5,1},{6,2},{7,3},{8,12},{9,13},{10,... | collective-permute-start | bytes 172040 | tf_op jit(solution)/shard_map/ppermute | solution.py:83
  135.0 4.4 %collective-permute-start.8 = (bf16[224,128]{1,0:T(8,128)(2,1)S(1)}, bf16[224,128]{1,0:T(8,128)(2,1)S(1)}, u32[]{:S(2)}, u32[]{:S(2)}) collective-permute-start(bf16[224,128]{1,0:T(8,128)(2,1)S(1)} %get-tuple-element.98), channel_id=1, source_target_pairs={{0,5},{1,6},{2,7},{3,0},{4,1},{5,2},{6,3},{7,4},{8,13},{9,14},{10,... | collective-permute-start | bytes 172040 | tf_op jit(solution)/shard_map/ppermute | solution.py:83
  139.4 4.3 %collective-permute-start.9 = (bf16[224,128]{1,0:T(8,128)(2,1)S(1)}, bf16[224,128]{1,0:T(8,128)(2,1)S(1)}, u32[]{:S(2)}, u32[]{:S(2)}) collective-permute-start(bf16[224,128]{1,0:T(8,128)(2,1)S(1)} %get-tuple-element.99), channel_id=1, source_target_pairs={{0,6},{1,7},{2,0},{3,1},{4,2},{5,3},{6,4},{7,5},{8,14},{9,15},{10,... | collective-permute-start | bytes 172040 | tf_op jit(solution)/shard_map/ppermute | solution.py:83
  145.6 2.3 %collective-permute-start.5 = (bf16[224,128]{1,0:T(8,128)(2,1)S(1)}, bf16[224,128]{1,0:T(8,128)(2,1)S(1)}, u32[]{:S(2)}, u32[]{:S(2)}) collective-permute-start(bf16[224,128]{1,0:T(8,128)(2,1)S(1)} %get-tuple-element.101), channel_id=1, source_target_pairs={{0,2},{1,3},{2,4},{3,5},{4,6},{5,7},{6,0},{7,1},{8,10},{9,11},{10,... | collective-permute-start | bytes 172040 | tf_op jit(solution)/shard_map/ppermute | solution.py:83
  150.4 2.9 %collective-permute-done.5 = bf16[224,128]{1,0:T(8,128)(2,1)S(1)} collective-permute-done((bf16[224,128]{1,0:T(8,128)(2,1)S(1)}, bf16[224,128]{1,0:T(8,128)(2,1)S(1)}, u32[]{:S(2)}, u32[]{:S(2)}) %collective-permute-start.5) | collective-permute-done | bytes 57376 | tf_op jit(solution)/shard_map/ppermute | solution.py:83
  156.2 5.0 %all-to-all-done.1 = bf16[64,25,384]{2,1,0:T(8,128)(2,1)S(1)} async-done(((bf16[64,25,384]{2,1,0:T(8,128)(2,1)}), bf16[64,25,384]{2,1,0:T(8,128)(2,1)S(1)}, u32[]{:S(2)}, u32[]{:S(2)}) %all-to-all-start.1) | async-done | bytes 1228832 | tf_op jit(solution)/shard_map/all_to_all | solution.py:159
  162.3 7.4 %all-to-all-start.2 = ((f32[64,1,288]{2,1,0:T(1,128)}), f32[64,1,288]{2,1,0:T(1,128)S(1)}, u32[]{:S(2)}, u32[]{:S(2)}) async-start(f32[64,1,288]{2,1,0:T(1,128)} %broadcast_in_dim.8), calls=%async_computation.3 | async-start | bytes 196608 | tf_op jit(solution)/shard_map/all_to_all | solution.py:50
  170.4 9.9 %all-to-all-done.2 = f32[64,1,288]{2,1,0:T(1,128)S(1)} async-done(((f32[64,1,288]{2,1,0:T(1,128)}), f32[64,1,288]{2,1,0:T(1,128)S(1)}, u32[]{:S(2)}, u32[]{:S(2)}) %all-to-all-start.2) | async-done | bytes 73760 | tf_op jit(solution)/shard_map/all_to_all | solution.py:50
  (97 shorter events, 30.4 us)
Async XLA Ops:
  7.2 48.2 %all-gather.3.cloned.1.call-start = ((), (), s32[]{:S(2)}) async-start(), calls=%async_computation.5 | async-start | bytes 1843200 | tf_op jit(solution)/shard_map/all_gather | solution.py:104
  10.5 12.8 %copy-start.9 = (f32[31,192]{1,0:T(8,128)S(1)}, f32[31,192]{1,0:T(8,128)}, u32[]{:S(2)}) copy-start(f32[31,192]{1,0:T(8,128)} %param.10) | copy-start | bytes 71428
  11.6 48.5 %all-to-all-start = ((bf16[64,24,384]{2,1,0:T(8,128)(2,1)}), bf16[64,24,384]{2,1,0:T(8,128)(2,1)S(1)}, u32[]{:S(2)}, u32[]{:S(2)}) async-start(bf16[64,24,384]{2,1,0:T(8,128)(2,1)} %broadcast_in_dim.6), calls=%async_computation | async-start | bytes 2359296 | tf_op jit(solution)/shard_map/all_to_all | solution.py:50
  23.2 130.1 %reduce-scatter.2.cloned.1.call-start = ((), (), s32[]{:S(2)}) async-start(), calls=%async_computation.4 | async-start | bytes 1327104 | tf_op jit(solution)/shard_map/reduce_scatter | solution.py:175
  55.3 2.6 %copy-start = (bf16[1600,512]{1,0:T(8,128)(2,1)S(1)}, bf16[1600,512]{1,0:T(8,128)(2,1)}, u32[]{:S(2)}) copy-start(bf16[1600,512]{1,0:T(8,128)(2,1)} %all-gather.3.cloned.1.call-done) | copy-start | bytes 4915204
  63.7 13.3 %copy-start.8 = (bf16[192,512]{1,0:T(8,128)(2,1)S(1)}, bf16[192,512]{1,0:T(8,128)(2,1)}, u32[]{:S(2)}) copy-start(bf16[192,512]{1,0:T(8,128)(2,1)} %param.11) | copy-start | bytes 589828
  63.9 9.5 %collective-permute-start = (bf16[192,15]{1,0:T(8,128)(2,1)S(1)}, bf16[192,15]{1,0:T(8,128)(2,1)S(1)}, u32[]{:S(2)}, u32[]{:S(2)}) collective-permute-start(bf16[192,15]{1,0:T(8,128)(2,1)S(1)} %get-tuple-element.57), channel_id=1, source_target_pairs={{0,8},{8,16},{16,24},{24,32},{32,40},{40,48},{48,56},{56,64},{64,7... | collective-permute-start | bytes 17288 | tf_op jit(solution)/shard_map/ppermute | solution.py:15
  71.4 5.4 %collective-permute-start.1 = (bf16[192,15]{1,0:T(8,128)(2,1)S(1)}, bf16[192,15]{1,0:T(8,128)(2,1)S(1)}, u32[]{:S(2)}, u32[]{:S(2)}) collective-permute-start(bf16[192,15]{1,0:T(8,128)(2,1)S(1)} %get-tuple-element.58), channel_id=1, source_target_pairs={{8,0},{16,8},{24,16},{32,24},{40,32},{48,40},{56,48},{64,56},{72,6... | collective-permute-start | bytes 17288 | tf_op jit(solution)/shard_map/ppermute | solution.py:17
  84.1 5.3 %collective-permute-start.2 = (bf16[192,15]{1,0:T(8,128)(2,1)S(1)}, bf16[192,15]{1,0:T(8,128)(2,1)S(1)}, u32[]{:S(2)}, u32[]{:S(2)}) collective-permute-start(bf16[192,15]{1,0:T(8,128)(2,1)S(1)} %get-tuple-element.55), channel_id=1, source_target_pairs={{0,8},{8,16},{16,24},{24,32},{32,40},{40,48},{48,56},{56,64},{64,7... | collective-permute-start | bytes 17288 | tf_op jit(solution)/shard_map/ppermute | solution.py:15
  86.1 5.4 %collective-permute-start.3 = (bf16[192,15]{1,0:T(8,128)(2,1)S(1)}, bf16[192,15]{1,0:T(8,128)(2,1)S(1)}, u32[]{:S(2)}, u32[]{:S(2)}) collective-permute-start(bf16[192,15]{1,0:T(8,128)(2,1)S(1)} %get-tuple-element.56), channel_id=1, source_target_pairs={{8,0},{16,8},{24,16},{32,24},{40,32},{48,40},{56,48},{64,56},{72,6... | collective-permute-start | bytes 17288 | tf_op jit(solution)/shard_map/ppermute | solution.py:17
  91.6 4.7 %copy-start.2 = (bf16[64,24,384]{2,1,0:T(8,128)(2,1)S(1)}, bf16[64,24,384]{2,1,0:T(8,128)(2,1)}, u32[]{:S(2)}) copy-start(bf16[64,24,384]{2,1,0:T(8,128)(2,1)} %copy-done.1) | copy-start | bytes 3538948
  96.1 3.8 %copy-start.6 = (bf16[192,512]{1,0:T(8,128)(2,1)}, bf16[192,512]{1,0:T(8,128)(2,1)S(1)}, u32[]{:S(2)}) copy-start(bf16[192,512]{1,0:T(8,128)(2,1)S(1)} %get-tuple-element.43) | copy-start | bytes 589828
  96.3 3.6 %copy-start.5 = (bf16[192,512]{1,0:T(8,128)(2,1)}, bf16[192,512]{1,0:T(8,128)(2,1)S(1)}, u32[]{:S(2)}) copy-start(bf16[192,512]{1,0:T(8,128)(2,1)S(1)} %multiply_convert_fusion.4) | copy-start | bytes 589828
  106.8 16.5 %copy-start.10 = (f32[512]{0:T(512)S(1)}, f32[512]{0:T(512)}, u32[]{:S(2)}) copy-start(f32[512]{0:T(512)} %get-tuple-element.7) | copy-start | bytes 6148
  106.8 54.4 %all-to-all-start.1 = ((bf16[64,25,384]{2,1,0:T(8,128)(2,1)}), bf16[64,25,384]{2,1,0:T(8,128)(2,1)S(1)}, u32[]{:S(2)}, u32[]{:S(2)}) async-start(bf16[64,25,384]{2,1,0:T(8,128)(2,1)} %pad_maximum_fusion), calls=%async_computation.2 | async-start | bytes 3145728 | tf_op jit(solution)/shard_map/all_to_all | solution.py:159
  123.4 31.0 %copy-start.11 = (f32[192]{0:T(256)S(1)}, f32[192]{0:T(256)}, u32[]{:S(2)}) copy-start(f32[192]{0:T(256)} %param.7) | copy-start | bytes 2308
  123.6 20.1 %collective-permute-start.4 = (bf16[224,128]{1,0:T(8,128)(2,1)S(1)}, bf16[224,128]{1,0:T(8,128)(2,1)S(1)}, u32[]{:S(2)}, u32[]{:S(2)}) collective-permute-start(bf16[224,128]{1,0:T(8,128)(2,1)S(1)} %get-tuple-element.95), channel_id=1, source_target_pairs={{0,1},{1,2},{2,3},{3,4},{4,5},{5,6},{6,7},{7,0},{8,9},{9,10},{10,1... | collective-permute-start | bytes 172040 | tf_op jit(solution)/shard_map/ppermute | solution.py:83
  126.3 19.3 %collective-permute-start.6 = (bf16[224,128]{1,0:T(8,128)(2,1)S(1)}, bf16[224,128]{1,0:T(8,128)(2,1)S(1)}, u32[]{:S(2)}, u32[]{:S(2)}) collective-permute-start(bf16[224,128]{1,0:T(8,128)(2,1)S(1)} %get-tuple-element.96), channel_id=1, source_target_pairs={{0,3},{1,4},{2,5},{3,6},{4,7},{5,0},{6,1},{7,2},{8,11},{9,12},{10,... | collective-permute-start | bytes 172040 | tf_op jit(solution)/shard_map/ppermute | solution.py:83
  130.3 18.4 %collective-permute-start.7 = (bf16[224,128]{1,0:T(8,128)(2,1)S(1)}, bf16[224,128]{1,0:T(8,128)(2,1)S(1)}, u32[]{:S(2)}, u32[]{:S(2)}) collective-permute-start(bf16[224,128]{1,0:T(8,128)(2,1)S(1)} %get-tuple-element.97), channel_id=1, source_target_pairs={{0,4},{1,5},{2,6},{3,7},{4,0},{5,1},{6,2},{7,3},{8,12},{9,13},{10,... | collective-permute-start | bytes 172040 | tf_op jit(solution)/shard_map/ppermute | solution.py:83
  135.0 13.8 %collective-permute-start.8 = (bf16[224,128]{1,0:T(8,128)(2,1)S(1)}, bf16[224,128]{1,0:T(8,128)(2,1)S(1)}, u32[]{:S(2)}, u32[]{:S(2)}) collective-permute-start(bf16[224,128]{1,0:T(8,128)(2,1)S(1)} %get-tuple-element.98), channel_id=1, source_target_pairs={{0,5},{1,6},{2,7},{3,0},{4,1},{5,2},{6,3},{7,4},{8,13},{9,14},{10,... | collective-permute-start | bytes 172040 | tf_op jit(solution)/shard_map/ppermute | solution.py:83
  139.4 11.0 %collective-permute-start.9 = (bf16[224,128]{1,0:T(8,128)(2,1)S(1)}, bf16[224,128]{1,0:T(8,128)(2,1)S(1)}, u32[]{:S(2)}, u32[]{:S(2)}) collective-permute-start(bf16[224,128]{1,0:T(8,128)(2,1)S(1)} %get-tuple-element.99), channel_id=1, source_target_pairs={{0,6},{1,7},{2,0},{3,1},{4,2},{5,3},{6,4},{7,5},{8,14},{9,15},{10,... | collective-permute-start | bytes 172040 | tf_op jit(solution)/shard_map/ppermute | solution.py:83
  143.7 6.7 %collective-permute-start.10 = (bf16[224,128]{1,0:T(8,128)(2,1)S(1)}, bf16[224,128]{1,0:T(8,128)(2,1)S(1)}, u32[]{:S(2)}, u32[]{:S(2)}) collective-permute-start(bf16[224,128]{1,0:T(8,128)(2,1)S(1)} %get-tuple-element.100), channel_id=1, source_target_pairs={{0,7},{1,0},{2,1},{3,2},{4,3},{5,4},{6,5},{7,6},{8,15},{9,8},{10,9... | collective-permute-start | bytes 172040 | tf_op jit(solution)/shard_map/ppermute | solution.py:83
  145.6 7.6 %collective-permute-start.5 = (bf16[224,128]{1,0:T(8,128)(2,1)S(1)}, bf16[224,128]{1,0:T(8,128)(2,1)S(1)}, u32[]{:S(2)}, u32[]{:S(2)}) collective-permute-start(bf16[224,128]{1,0:T(8,128)(2,1)S(1)} %get-tuple-element.101), channel_id=1, source_target_pairs={{0,2},{1,3},{2,4},{3,5},{4,6},{5,7},{6,0},{7,1},{8,10},{9,11},{10,... | collective-permute-start | bytes 172040 | tf_op jit(solution)/shard_map/ppermute | solution.py:83
  162.3 17.9 %all-to-all-start.2 = ((f32[64,1,288]{2,1,0:T(1,128)}), f32[64,1,288]{2,1,0:T(1,128)S(1)}, u32[]{:S(2)}, u32[]{:S(2)}) async-start(f32[64,1,288]{2,1,0:T(1,128)} %broadcast_in_dim.8), calls=%async_computation.3 | async-start | bytes 196608 | tf_op jit(solution)/shard_map/all_to_all | solution.py:50
  (4 other events, 6.6 us)
Sparse Core Ops, SparseCore 0:
  10.1 45.1 all-gather.2
  102.3 45.5 reduce-scatter.1
